TPU v7x, 32 devices: a whole 2x2x4 slice. The times are simulated.
32 devices in a mesh: mem: 4 (over y, x), tile: 8 (over z, core).
Axes of the slice: x: 2, y: 2, z: 4, core: 2. Of those that a mesh axis runs over, the one named last changes fastest.
Arguments:
- controls: float32 [32, 128, 1792], P('mem', 'tile'), may hold values from -6 to 6
- perturbations: bfloat16 [32, 4, 128, 1792], P('mem', None, 'tile'), may hold values from -1.5 to 1.5
- jacobian: float32 [4, 128, 1792], P(None, 'tile'), may hold values from -3 to 3
- obs_weight: float32 [128, 1792], P('tile'), may hold values from 0.5 to 4
- radar_mask: int32 [128, 1792], P('tile'), may hold values 0 or 1
- row_faces: float32 [128, 1792], P('tile'), may hold values from 0.12 to 0.25
- col_faces: float32 [128, 1792], P('tile'), may hold values from 0.12 to 0.25
Outputs:
- gradient: float32 [32, 128, 1792], P('mem', 'tile')
All inputs are finite; a program needn't handle non-finite values. No bound on the sum of `radar_mask` on one device may be relied on, other than what follows from the above.
Results may differ from a plain program's by a relative error of at most 0.0003.
Values sent between devices are 32-bit elements; how exact they have to be, the bound alone decides.
No kernel may reach another device: no remote copies, remote signals or barrier semaphores. Data moves between devices by JAX's collectives and lax.ppermute only.
A program may use at most 64 MiB of HBM per device.

v0:
```python
import jax
import jax.numpy as jnp
from jax import lax
from jax.sharding import PartitionSpec as P

STEPS = 4


def padded(cells, sides, width):
    for axis, dim in sides:
        count = lax.axis_size(axis)
        ends = count - 1
        head = lax.slice_in_dim(cells, 0, width, axis=dim)
        tail = lax.slice_in_dim(cells, cells.shape[dim] - width, cells.shape[dim], axis=dim)
        cells = jnp.concatenate(
            [
                lax.ppermute(tail, axis, [(i, (i + 1) % count) for i in range(ends)]),
                cells,
                lax.ppermute(head, axis, [((i + 1) % count, i) for i in range(ends)]),
            ],
            axis=dim,
        )
    return cells


def diffuse(values, row_coef, col_coef):
    row_flux = row_coef[..., :-1, :] * (values[..., 1:, :] - values[..., :-1, :])
    col_flux = col_coef[..., :, :-1] * (values[..., :, 1:] - values[..., :, :-1])
    zeros_row = jnp.zeros_like(values[..., :1, :])
    zeros_col = jnp.zeros_like(values[..., :, :1])
    values = (
        values
        + jnp.concatenate([row_flux, zeros_row], -2)
        - jnp.concatenate([zeros_row, row_flux], -2)
    )
    return (
        values
        + jnp.concatenate([col_flux, zeros_col], -1)
        - jnp.concatenate([zeros_col, col_flux], -1)
    )


def localize(field, coef_band):
    row_count = field.shape[1]
    widened = padded(field, (("tile", 1),), STEPS)
    for repeat in range(STEPS):
        widened = diffuse(widened, coef_band[0], coef_band[1])
    field = widened[:, STEPS : STEPS + row_count]
    return field


def per_device(controls, perturbations, jacobian, obs_weight, radar_mask, row_faces, col_faces):
    row_count = controls.shape[1]
    row_index = lax.axis_index("tile") * row_count + lax.broadcasted_iota(
        jnp.int32, row_faces.shape, 0
    )
    row_coef = jnp.where(
        row_index < row_count * lax.axis_size("tile") - 1, row_faces, jnp.zeros_like(row_faces)
    )
    stacked = jnp.stack([row_coef, col_faces])
    coef_band = padded(stacked, (("tile", 1),), STEPS)
    localized = localize(controls, coef_band)
    member_sum = jnp.sum(perturbations * localized[:, None], axis=0)
    weights = radar_mask.astype(jnp.float32) * obs_weight
    increment = lax.psum(member_sum, "mem")
    reflect = jnp.sum(jacobian * increment, 0)
    adjoint_inc = jacobian * (weights * reflect)[None]
    sensitivity = jnp.sum(perturbations * adjoint_inc[None], axis=1)
    return controls + localize(sensitivity, coef_band)


def solution(mesh):
    placed = (
        P("mem", "tile", None),
        P("mem", None, "tile", None),
        P(None, "tile", None),
        P("tile", None),
        P("tile", None),
        P("tile", None),
        P("tile", None),
    )
    return jax.shard_map(
        per_device, mesh=mesh, in_specs=placed, out_specs=P("mem", "tile", None), check_vma=False
    )
```

profile of v0, /device:TPU:1, one launch (start us, length us, event | category | flops | bytes accessed | tf_op | source)
XLA Modules:
  0.0 104.9 jit_solution(15233556195645673594)
XLA Ops:
  6.5 0.0 copy-start.3
  6.5 0.0 all-reduce.34.cloned.1.call-start
  6.5 1.0 select_bitcast_fusion
  7.6 0.0 copy-start
  7.6 1.0 pad_maximum_fusion.4
  8.5 4.6 %collective-permute-start.2 = (f32[2,4,1792]{2,1,0:T(4,128)S(1)}, f32[2,4,1792]{2,1,0:T(4,128)S(1)}, u32[]{:S(2)}, u32[]{:S(2)}) collective-permute-start(f32[2,4,1792]{2,1,0:T(4,128)S(1)} %get-tuple-element.9), channel_id=1, source_target_pairs={{0,1},{1,2},{2,3},{3,4},{4,5},{5,6},{6,7},{8,9},{9,10},{10,11},{11... | collective-permute-start | bytes 172040 | tf_op jit(solution)/shard_map/ppermute | solution.py:17
  13.1 1.9 %collective-permute-start.3 = (f32[2,4,1792]{2,1,0:T(4,128)S(1)}, f32[2,4,1792]{2,1,0:T(4,128)S(1)}, u32[]{:S(2)}, u32[]{:S(2)}) collective-permute-start(f32[2,4,1792]{2,1,0:T(4,128)S(1)} %get-tuple-element.10), channel_id=1, source_target_pairs={{1,0},{2,1},{3,2},{4,3},{5,4},{6,5},{7,6},{9,8},{10,9},{11,10},{12... | collective-permute-start | bytes 172040 | tf_op jit(solution)/shard_map/ppermute | solution.py:19
  15.1 1.2 %fusion.20 = (f32[8,4,1792]{2,1,0:T(4,128)S(1)}, f32[8,4,1792]{2,1,0:T(4,128)S(1)}) fusion(f32[8,16,1792]{2,1,0:T(8,128)} %param.7), kind=kLoop, calls=%fused_computation.64 | loop fusion | bytes 917504 | tf_op jit(solution)/shard_map/slice | solution.py:14
  16.3 3.6 %collective-permute-start = (f32[8,4,1792]{2,1,0:T(4,128)S(1)}, f32[8,4,1792]{2,1,0:T(4,128)S(1)}, u32[]{:S(2)}, u32[]{:S(2)}) collective-permute-start(f32[8,4,1792]{2,1,0:T(4,128)S(1)} %get-tuple-element.7), channel_id=1, source_target_pairs={{0,1},{1,2},{2,3},{3,4},{4,5},{5,6},{6,7},{8,9},{9,10},{10,11},{11... | collective-permute-start | bytes 688136 | tf_op jit(solution)/shard_map/ppermute | solution.py:17
  19.9 1.9 %collective-permute-start.1 = (f32[8,4,1792]{2,1,0:T(4,128)S(1)}, f32[8,4,1792]{2,1,0:T(4,128)S(1)}, u32[]{:S(2)}, u32[]{:S(2)}) collective-permute-start(f32[8,4,1792]{2,1,0:T(4,128)S(1)} %get-tuple-element.8), channel_id=1, source_target_pairs={{1,0},{2,1},{3,2},{4,3},{5,4},{6,5},{7,6},{9,8},{10,9},{11,10},{12... | collective-permute-start | bytes 688136 | tf_op jit(solution)/shard_map/ppermute | solution.py:19
  21.9 0.0 collective-permute-done.2
  21.9 0.0 collective-permute-done.3
  21.9 0.0 copy-done.3
  21.9 0.1 pad_maximum_fusion.2
  22.0 0.9 collective-permute-done
  22.9 4.4 %collective-permute-done.1 = f32[8,4,1792]{2,1,0:T(4,128)S(1)} collective-permute-done((f32[8,4,1792]{2,1,0:T(4,128)S(1)}, f32[8,4,1792]{2,1,0:T(4,128)S(1)}, u32[]{:S(2)}, u32[]{:S(2)}) %collective-permute-start.1) | collective-permute-done | bytes 229408 | tf_op jit(solution)/shard_map/ppermute | solution.py:19
  27.3 0.0 copy-done
  27.3 0.2 pad_maximum_fusion
  27.5 0.2 fusion.17
  27.7 0.4 fusion.16
  28.1 0.6 pad_subtract_fusion.5
  28.7 0.2 fusion.15
  28.9 0.4 fusion.14
  29.3 0.5 pad_subtract_fusion.4
  29.8 0.2 fusion.13
  30.0 0.4 fusion.12
  30.4 0.5 pad_subtract_fusion.3
  30.9 0.2 fusion.11
  31.1 0.4 fusion.10
  31.5 0.0 copy-start.1
  31.5 0.5 pad_subtract_fusion.8
  32.1 0.9 copy-done.1
  33.0 0.0 copy-start.2
  33.0 1.1 %fusion = f32[4,16,1792]{2,1,0:T(8,128)} fusion(bf16[8,4,16,1792]{3,2,1,0:T(8,128)(2,1)S(1)} %copy-done.1, f32[8,16,1792]{2,1,0:T(8,128)S(1)} %pad_subtract_fusion.8), kind=kLoop, calls=%fused_computation.2 | loop fusion | flops 2637824 | bytes 3211264 | tf_op jit(solution)/shard_map/reduce_sum | solution.py:63
  34.2 0.0 all-reduce.34.cloned.1.call-update
  34.2 44.1 %all-reduce.34.cloned.1.call-done = f32[4,16,1792]{2,1,0:T(8,128)} async-done(((f32[4,16,1792]{2,1,0:T(8,128)}), f32[4,16,1792]{2,1,0:T(8,128)}) %all-reduce.34.cloned.1.call-update) | async-done | bytes 458768 | tf_op jit(solution)/shard_map/psum | solution.py:65
  78.3 0.0 copy-done.2
  78.3 1.1 %multiply_reduce_fusion = f32[16,1792]{1,0:T(8,128)S(1)} fusion(f32[4,16,1792]{2,1,0:T(8,128)S(1)} %copy-done.2, f32[4,16,1792]{2,1,0:T(8,128)} %all-reduce.34.cloned.1.call-done), kind=kLoop, calls=%fused_computation.53 | loop fusion | flops 200704 | bytes 1032192 | tf_op jit(solution)/shard_map/reduce_sum | solution.py:66
  79.4 1.0 multiply_multiply_fusion
  80.4 0.4 fusion.1
  80.8 0.1 fusion.19
  80.9 4.1 %collective-permute-start.4 = (f32[8,4,1792]{2,1,0:T(4,128)S(1)}, f32[8,4,1792]{2,1,0:T(4,128)S(1)}, u32[]{:S(2)}, u32[]{:S(2)}) collective-permute-start(f32[8,4,1792]{2,1,0:T(4,128)S(1)} %get-tuple-element.5), channel_id=1, source_target_pairs={{0,1},{1,2},{2,3},{3,4},{4,5},{5,6},{6,7},{8,9},{9,10},{10,11},{11... | collective-permute-start | bytes 688136 | tf_op jit(solution)/shard_map/ppermute | solution.py:17
  85.0 1.9 %collective-permute-start.5 = (f32[8,4,1792]{2,1,0:T(4,128)S(1)}, f32[8,4,1792]{2,1,0:T(4,128)S(1)}, u32[]{:S(2)}, u32[]{:S(2)}) collective-permute-start(f32[8,4,1792]{2,1,0:T(4,128)S(1)} %get-tuple-element.6), channel_id=1, source_target_pairs={{1,0},{2,1},{3,2},{4,3},{5,4},{6,5},{7,6},{9,8},{10,9},{11,10},{12... | collective-permute-start | bytes 688136 | tf_op jit(solution)/shard_map/ppermute | solution.py:19
  86.9 1.0 collective-permute-done.4
  88.0 4.4 %collective-permute-done.5 = f32[8,4,1792]{2,1,0:T(4,128)S(1)} collective-permute-done((f32[8,4,1792]{2,1,0:T(4,128)S(1)}, f32[8,4,1792]{2,1,0:T(4,128)S(1)}, u32[]{:S(2)}, u32[]{:S(2)}) %collective-permute-start.5) | collective-permute-done | bytes 229408 | tf_op jit(solution)/shard_map/ppermute | solution.py:19
  92.4 0.2 pad_maximum_fusion.1
  92.5 0.2 fusion.9
  92.7 0.4 fusion.8
  93.2 0.6 pad_subtract_fusion.2
  93.7 0.2 fusion.7
  93.9 0.4 fusion.6
  94.4 0.5 pad_subtract_fusion.1
  94.8 0.2 fusion.5
  95.0 0.4 fusion.4
  95.5 0.5 pad_subtract_fusion
  95.9 0.2 fusion.3
  96.1 0.4 fusion.2
  96.6 1.5 %fusion.18 = f32[8,16,1792]{2,1,0:T(8,128)} fusion(f32[8,16,1792]{2,1,0:T(8,128)S(1)} %copy-done, f32[8,24,1791]{2,1,0:T(8,128)S(1)} %fusion.2, f32[8,23,1792]{2,1,0:T(8,128)S(1)} %fusion.3, f32[8,24,1792]{2,1,0:T(8,128)S(1)} %pad_subtract_fusion), kind=kLoop, calls=%fused_computation.45 | loop fusion | flops 1146880 | bytes 5446912 | tf_op jit(solution)/shard_map/add | solution.py:69
  (4 shorter events, 0.1 us)
Async XLA Ops:
  6.5 15.4 %copy-start.3 = (f32[16,1792]{1,0:T(8,128)S(1)}, f32[16,1792]{1,0:T(8,128)}, u32[]{:S(2)}) copy-start(f32[16,1792]{1,0:T(8,128)} %param.13) | copy-start | bytes 344068
  6.5 71.8 %all-reduce.34.cloned.1.call-start = ((), (), s32[]{:S(2)}) async-start(), calls=%async_computation | async-start | bytes 917504 | tf_op jit(solution)/shard_map/psum | solution.py:65
  7.6 19.7 %copy-start = (f32[8,16,1792]{2,1,0:T(8,128)S(1)}, f32[8,16,1792]{2,1,0:T(8,128)}, u32[]{:S(2)}) copy-start(f32[8,16,1792]{2,1,0:T(8,128)} %param.7) | copy-start | bytes 2752516
  8.5 13.4 %collective-permute-start.2 = (f32[2,4,1792]{2,1,0:T(4,128)S(1)}, f32[2,4,1792]{2,1,0:T(4,128)S(1)}, u32[]{:S(2)}, u32[]{:S(2)}) collective-permute-start(f32[2,4,1792]{2,1,0:T(4,128)S(1)} %get-tuple-element.9), channel_id=1, source_target_pairs={{0,1},{1,2},{2,3},{3,4},{4,5},{5,6},{6,7},{8,9},{9,10},{10,11},{11... | collective-permute-start | bytes 172040 | tf_op jit(solution)/shard_map/ppermute | solution.py:17
  13.1 8.8 %collective-permute-start.3 = (f32[2,4,1792]{2,1,0:T(4,128)S(1)}, f32[2,4,1792]{2,1,0:T(4,128)S(1)}, u32[]{:S(2)}, u32[]{:S(2)}) collective-permute-start(f32[2,4,1792]{2,1,0:T(4,128)S(1)} %get-tuple-element.10), channel_id=1, source_target_pairs={{1,0},{2,1},{3,2},{4,3},{5,4},{6,5},{7,6},{9,8},{10,9},{11,10},{12... | collective-permute-start | bytes 172040 | tf_op jit(solution)/shard_map/ppermute | solution.py:19
  16.3 6.6 %collective-permute-start = (f32[8,4,1792]{2,1,0:T(4,128)S(1)}, f32[8,4,1792]{2,1,0:T(4,128)S(1)}, u32[]{:S(2)}, u32[]{:S(2)}) collective-permute-start(f32[8,4,1792]{2,1,0:T(4,128)S(1)} %get-tuple-element.7), channel_id=1, source_target_pairs={{0,1},{1,2},{2,3},{3,4},{4,5},{5,6},{6,7},{8,9},{9,10},{10,11},{11... | collective-permute-start | bytes 688136 | tf_op jit(solution)/shard_map/ppermute | solution.py:17
  19.9 7.3 %collective-permute-start.1 = (f32[8,4,1792]{2,1,0:T(4,128)S(1)}, f32[8,4,1792]{2,1,0:T(4,128)S(1)}, u32[]{:S(2)}, u32[]{:S(2)}) collective-permute-start(f32[8,4,1792]{2,1,0:T(4,128)S(1)} %get-tuple-element.8), channel_id=1, source_target_pairs={{1,0},{2,1},{3,2},{4,3},{5,4},{6,5},{7,6},{9,8},{10,9},{11,10},{12... | collective-permute-start | bytes 688136 | tf_op jit(solution)/shard_map/ppermute | solution.py:19
  31.5 1.5 %copy-start.1 = (bf16[8,4,16,1792]{3,2,1,0:T(8,128)(2,1)S(1)}, bf16[8,4,16,1792]{3,2,1,0:T(8,128)(2,1)}, u32[]{:S(2)}) copy-start(bf16[8,4,16,1792]{3,2,1,0:T(8,128)(2,1)} %param.8) | copy-start | bytes 5505028
  33.0 45.3 %copy-start.2 = (f32[4,16,1792]{2,1,0:T(8,128)S(1)}, f32[4,16,1792]{2,1,0:T(8,128)}, u32[]{:S(2)}) copy-start(f32[4,16,1792]{2,1,0:T(8,128)} %param.9) | copy-start | bytes 1376260
  80.9 7.1 %collective-permute-start.4 = (f32[8,4,1792]{2,1,0:T(4,128)S(1)}, f32[8,4,1792]{2,1,0:T(4,128)S(1)}, u32[]{:S(2)}, u32[]{:S(2)}) collective-permute-start(f32[8,4,1792]{2,1,0:T(4,128)S(1)} %get-tuple-element.5), channel_id=1, source_target_pairs={{0,1},{1,2},{2,3},{3,4},{4,5},{5,6},{6,7},{8,9},{9,10},{10,11},{11... | collective-permute-start | bytes 688136 | tf_op jit(solution)/shard_map/ppermute | solution.py:17
  85.0 7.3 %collective-permute-start.5 = (f32[8,4,1792]{2,1,0:T(4,128)S(1)}, f32[8,4,1792]{2,1,0:T(4,128)S(1)}, u32[]{:S(2)}, u32[]{:S(2)}) collective-permute-start(f32[8,4,1792]{2,1,0:T(4,128)S(1)} %get-tuple-element.6), channel_id=1, source_target_pairs={{1,0},{2,1},{3,2},{4,3},{5,4},{6,5},{7,6},{9,8},{10,9},{11,10},{12... | collective-permute-start | bytes 688136 | tf_op jit(solution)/shard_map/ppermute | solution.py:19
Sparse Core Ops, SparseCore 0:
  34.3 43.9 all-reduce.33
where the time goes:
time: 105 us
  waiting for transfers between devices  54.8 us (52%)
  starting transfers between devices  18.1 us (17%)
  other arithmetic  16 us (15%)
  between operations  13.7 us (13%)
  local copies, waits for them, and re-layouts  2.31 us (2%)
    psum x1, waiting for transfers between devices, per_device(): increment = lax.psum(member_sum, 'mem')  44.1 us
    ppermute x3, starting transfers between devices, padded(): lax.ppermute(tail, axis, [(i, (i + 1) % count) for i in range(ends)])  12.3 us
    ppermute x3, waiting for transfers between devices, padded(): lax.ppermute(head, axis, [((i + 1) % count, i) for i in range(ends)])  8.79 us
    ppermute x3, starting transfers between devices, padded(): lax.ppermute(head, axis, [((i + 1) % count, i) for i in range(ends)])  5.76 us
    sub x7, other arithmetic, diffuse(): values + jnp.concatenate([col_flux, zeros_col], -1)  3.57 us
    mul x8, other arithmetic, diffuse(): col_coef[..., :, :-1] * (values[..., :, 1:] - values[..., :, :-1])  3.38 us
  transfers between devices with their start and end apart: 7, of which 5 were waited for; matrix products, arithmetic and copies ran while one was open for 1% of the time, Pallas kernels for 0%

commit v1 on v0

--- a/solution.py
+++ b/solution.py
@@ -62,8 +62,7 @@
     localized = localize(controls, coef_band)
     member_sum = jnp.sum(perturbations * localized[:, None], axis=0)
     weights = radar_mask.astype(jnp.float32) * obs_weight
-    increment = lax.psum(member_sum, "mem")
-    reflect = jnp.sum(jacobian * increment, 0)
+    reflect = lax.psum(jnp.sum(jacobian * member_sum, 0), "mem")
     adjoint_inc = jacobian * (weights * reflect)[None]
     sensitivity = jnp.sum(perturbations * adjoint_inc[None], axis=1)
     return controls + localize(sensitivity, coef_band)

time: 105 us -> 101 us (0.962)
  waiting for transfers between devices: 54.8 us -> 51.5 us
  other arithmetic: 16 us -> 14.8 us
    psum x1, waiting for transfers between devices: 44.1 us -> 40.8 us  [per_device(): reflect = lax.psum(jnp.sum(jacobian * member_sum, 0), 'mem')]
where the time goes in v1:
time: 101 us
  waiting for transfers between devices  51.5 us (51%)
  starting transfers between devices  18.1 us (18%)
  other arithmetic  14.8 us (15%)
  between operations  13.7 us (14%)
  local copies, waits for them, and re-layouts  2.95 us (3%)
    psum x1, waiting for transfers between devices, per_device(): reflect = lax.psum(jnp.sum(jacobian * member_sum, 0), 'mem')  40.8 us
    ppermute x3, starting transfers between devices, padded(): lax.ppermute(tail, axis, [(i, (i + 1) % count) for i in range(ends)])  12.3 us
    ppermute x3, waiting for transfers between devices, padded(): lax.ppermute(head, axis, [((i + 1) % count, i) for i in range(ends)])  8.79 us
    ppermute x3, starting transfers between devices, padded(): lax.ppermute(head, axis, [((i + 1) % count, i) for i in range(ends)])  5.76 us
    sub x7, other arithmetic, diffuse(): values + jnp.concatenate([col_flux, zeros_col], -1)  3.57 us
    mul x8, other arithmetic, diffuse(): col_coef[..., :, :-1] * (values[..., :, 1:] - values[..., :, :-1])  3.38 us
  transfers between devices with their start and end apart: 7, of which 5 were waited for; matrix products, arithmetic and copies ran while one was open for 1% of the time, Pallas kernels for 0%

profile of v1, /device:TPU:1, one launch (start us, length us, event | category | flops | bytes accessed | tf_op | source)
XLA Modules:
  0.0 101.0 jit_solution(3278053175194849136)
XLA Ops:
  6.5 0.0 copy-start.3
  6.5 0.0 all-reduce.34.cloned.1.call-start
  6.5 1.0 %select_bitcast_fusion = f32[1,16,1792]{2,1,0:T(8,128)S(1)} fusion(f32[16,1792]{1,0:T(8,128)} %param.12, pred[16]{0:T(512)(128)(4,1)S(1)} %add_compare_fusion), kind=kLoop, calls=%fused_computation.58 | loop fusion | flops 28672 | bytes 229392 | tf_op jit(solution)/shard_map/stack | solution.py:60
  7.6 0.0 copy-start
  7.6 1.0 pad_maximum_fusion.4
  8.5 4.6 %collective-permute-start.2 = (f32[2,4,1792]{2,1,0:T(4,128)S(1)}, f32[2,4,1792]{2,1,0:T(4,128)S(1)}, u32[]{:S(2)}, u32[]{:S(2)}) collective-permute-start(f32[2,4,1792]{2,1,0:T(4,128)S(1)} %get-tuple-element.9), channel_id=1, source_target_pairs={{0,1},{1,2},{2,3},{3,4},{4,5},{5,6},{6,7},{8,9},{9,10},{10,11},{11... | collective-permute-start | bytes 172040 | tf_op jit(solution)/shard_map/ppermute | solution.py:17
  13.1 1.9 %collective-permute-start.3 = (f32[2,4,1792]{2,1,0:T(4,128)S(1)}, f32[2,4,1792]{2,1,0:T(4,128)S(1)}, u32[]{:S(2)}, u32[]{:S(2)}) collective-permute-start(f32[2,4,1792]{2,1,0:T(4,128)S(1)} %get-tuple-element.10), channel_id=1, source_target_pairs={{1,0},{2,1},{3,2},{4,3},{5,4},{6,5},{7,6},{9,8},{10,9},{11,10},{12... | collective-permute-start | bytes 172040 | tf_op jit(solution)/shard_map/ppermute | solution.py:19
  15.1 1.2 %fusion.20 = (f32[8,4,1792]{2,1,0:T(4,128)S(1)}, f32[8,4,1792]{2,1,0:T(4,128)S(1)}) fusion(f32[8,16,1792]{2,1,0:T(8,128)} %param.7), kind=kLoop, calls=%fused_computation.64 | loop fusion | bytes 917504 | tf_op jit(solution)/shard_map/slice | solution.py:14
  16.3 3.6 %collective-permute-start = (f32[8,4,1792]{2,1,0:T(4,128)S(1)}, f32[8,4,1792]{2,1,0:T(4,128)S(1)}, u32[]{:S(2)}, u32[]{:S(2)}) collective-permute-start(f32[8,4,1792]{2,1,0:T(4,128)S(1)} %get-tuple-element.7), channel_id=1, source_target_pairs={{0,1},{1,2},{2,3},{3,4},{4,5},{5,6},{6,7},{8,9},{9,10},{10,11},{11... | collective-permute-start | bytes 688136 | tf_op jit(solution)/shard_map/ppermute | solution.py:17
  19.9 1.9 %collective-permute-start.1 = (f32[8,4,1792]{2,1,0:T(4,128)S(1)}, f32[8,4,1792]{2,1,0:T(4,128)S(1)}, u32[]{:S(2)}, u32[]{:S(2)}) collective-permute-start(f32[8,4,1792]{2,1,0:T(4,128)S(1)} %get-tuple-element.8), channel_id=1, source_target_pairs={{1,0},{2,1},{3,2},{4,3},{5,4},{6,5},{7,6},{9,8},{10,9},{11,10},{12... | collective-permute-start | bytes 688136 | tf_op jit(solution)/shard_map/ppermute | solution.py:19
  21.9 0.0 collective-permute-done.2
  21.9 0.0 collective-permute-done.3
  21.9 0.0 copy-done.3
  21.9 0.1 pad_maximum_fusion.2
  22.0 0.9 collective-permute-done
  22.9 4.4 %collective-permute-done.1 = f32[8,4,1792]{2,1,0:T(4,128)S(1)} collective-permute-done((f32[8,4,1792]{2,1,0:T(4,128)S(1)}, f32[8,4,1792]{2,1,0:T(4,128)S(1)}, u32[]{:S(2)}, u32[]{:S(2)}) %collective-permute-start.1) | collective-permute-done | bytes 229408 | tf_op jit(solution)/shard_map/ppermute | solution.py:19
  27.3 0.0 copy-done
  27.3 0.2 pad_maximum_fusion
  27.5 0.2 fusion.17
  27.7 0.4 fusion.16
  28.1 0.6 pad_subtract_fusion.5
  28.7 0.2 fusion.15
  28.9 0.4 fusion.14
  29.3 0.5 pad_subtract_fusion.4
  29.8 0.2 fusion.13
  30.0 0.4 fusion.12
  30.4 0.5 pad_subtract_fusion.3
  30.9 0.2 fusion.11
  31.1 0.4 fusion.10
  31.5 0.0 copy-start.1
  31.5 0.5 pad_subtract_fusion.8
  32.1 0.9 copy-done.1
  33.0 0.0 copy-start.2
  33.0 0.4 fusion
  33.4 0.6 copy-done.2
  34.0 0.7 multiply_reduce_fusion
  34.7 0.0 all-reduce.34.cloned.1.call-update
  34.7 40.8 %all-reduce.34.cloned.1.call-done = f32[16,1792]{1,0:T(8,128)} async-done(((f32[16,1792]{1,0:T(8,128)}), f32[16,1792]{1,0:T(8,128)}) %all-reduce.34.cloned.1.call-update) | async-done | bytes 114704 | tf_op jit(solution)/shard_map/psum | solution.py:65
  75.5 1.0 %multiply_multiply_fusion = f32[16,1792]{1,0:T(8,128)S(1)} fusion(f32[16,1792]{1,0:T(8,128)} %all-reduce.34.cloned.1.call-done, f32[16,1792]{1,0:T(8,128)} %param.10, s32[16,1792]{1,0:T(8,128)} %param.11), kind=kLoop, calls=%fused_computation.59 | loop fusion | flops 86016 | bytes 458752 | tf_op jit(solution)/shard_map/mul | solution.py:66
  76.6 0.4 fusion.1
  77.0 0.1 fusion.19
  77.1 4.1 %collective-permute-start.4 = (f32[8,4,1792]{2,1,0:T(4,128)S(1)}, f32[8,4,1792]{2,1,0:T(4,128)S(1)}, u32[]{:S(2)}, u32[]{:S(2)}) collective-permute-start(f32[8,4,1792]{2,1,0:T(4,128)S(1)} %get-tuple-element.5), channel_id=1, source_target_pairs={{0,1},{1,2},{2,3},{3,4},{4,5},{5,6},{6,7},{8,9},{9,10},{10,11},{11... | collective-permute-start | bytes 688136 | tf_op jit(solution)/shard_map/ppermute | solution.py:17
  81.1 1.9 %collective-permute-start.5 = (f32[8,4,1792]{2,1,0:T(4,128)S(1)}, f32[8,4,1792]{2,1,0:T(4,128)S(1)}, u32[]{:S(2)}, u32[]{:S(2)}) collective-permute-start(f32[8,4,1792]{2,1,0:T(4,128)S(1)} %get-tuple-element.6), channel_id=1, source_target_pairs={{1,0},{2,1},{3,2},{4,3},{5,4},{6,5},{7,6},{9,8},{10,9},{11,10},{12... | collective-permute-start | bytes 688136 | tf_op jit(solution)/shard_map/ppermute | solution.py:19
  83.1 1.0 %collective-permute-done.4 = f32[8,4,1792]{2,1,0:T(4,128)S(1)} collective-permute-done((f32[8,4,1792]{2,1,0:T(4,128)S(1)}, f32[8,4,1792]{2,1,0:T(4,128)S(1)}, u32[]{:S(2)}, u32[]{:S(2)}) %collective-permute-start.4) | collective-permute-done | bytes 229408 | tf_op jit(solution)/shard_map/ppermute | solution.py:17
  84.1 4.4 %collective-permute-done.5 = f32[8,4,1792]{2,1,0:T(4,128)S(1)} collective-permute-done((f32[8,4,1792]{2,1,0:T(4,128)S(1)}, f32[8,4,1792]{2,1,0:T(4,128)S(1)}, u32[]{:S(2)}, u32[]{:S(2)}) %collective-permute-start.5) | collective-permute-done | bytes 229408 | tf_op jit(solution)/shard_map/ppermute | solution.py:19
  88.5 0.2 pad_maximum_fusion.1
  88.7 0.2 fusion.9
  88.9 0.4 fusion.8
  89.3 0.6 pad_subtract_fusion.2
  89.9 0.2 fusion.7
  90.0 0.4 fusion.6
  90.5 0.5 pad_subtract_fusion.1
  91.0 0.2 fusion.5
  91.2 0.4 fusion.4
  91.6 0.5 pad_subtract_fusion
  92.1 0.2 fusion.3
  92.3 0.4 fusion.2
  92.7 1.5 %fusion.18 = f32[8,16,1792]{2,1,0:T(8,128)} fusion(f32[8,16,1792]{2,1,0:T(8,128)S(1)} %copy-done, f32[8,24,1791]{2,1,0:T(8,128)S(1)} %fusion.2, f32[8,23,1792]{2,1,0:T(8,128)S(1)} %fusion.3, f32[8,24,1792]{2,1,0:T(8,128)S(1)} %pad_subtract_fusion), kind=kLoop, calls=%fused_computation.45 | loop fusion | flops 1146880 | bytes 5446912 | tf_op jit(solution)/shard_map/add | solution.py:68
  (4 shorter events, 0.1 us)
Async XLA Ops:
  6.5 15.4 %copy-start.3 = (f32[16,1792]{1,0:T(8,128)S(1)}, f32[16,1792]{1,0:T(8,128)}, u32[]{:S(2)}) copy-start(f32[16,1792]{1,0:T(8,128)} %param.13) | copy-start | bytes 344068
  6.5 69.0 %all-reduce.34.cloned.1.call-start = ((), (), s32[]{:S(2)}) async-start(), calls=%async_computation | async-start | bytes 229376 | tf_op jit(solution)/shard_map/psum | solution.py:65
  7.6 19.7 %copy-start = (f32[8,16,1792]{2,1,0:T(8,128)S(1)}, f32[8,16,1792]{2,1,0:T(8,128)}, u32[]{:S(2)}) copy-start(f32[8,16,1792]{2,1,0:T(8,128)} %param.7) | copy-start | bytes 2752516
  8.5 13.4 %collective-permute-start.2 = (f32[2,4,1792]{2,1,0:T(4,128)S(1)}, f32[2,4,1792]{2,1,0:T(4,128)S(1)}, u32[]{:S(2)}, u32[]{:S(2)}) collective-permute-start(f32[2,4,1792]{2,1,0:T(4,128)S(1)} %get-tuple-element.9), channel_id=1, source_target_pairs={{0,1},{1,2},{2,3},{3,4},{4,5},{5,6},{6,7},{8,9},{9,10},{10,11},{11... | collective-permute-start | bytes 172040 | tf_op jit(solution)/shard_map/ppermute | solution.py:17
  13.1 8.8 %collective-permute-start.3 = (f32[2,4,1792]{2,1,0:T(4,128)S(1)}, f32[2,4,1792]{2,1,0:T(4,128)S(1)}, u32[]{:S(2)}, u32[]{:S(2)}) collective-permute-start(f32[2,4,1792]{2,1,0:T(4,128)S(1)} %get-tuple-element.10), channel_id=1, source_target_pairs={{1,0},{2,1},{3,2},{4,3},{5,4},{6,5},{7,6},{9,8},{10,9},{11,10},{12... | collective-permute-start | bytes 172040 | tf_op jit(solution)/shard_map/ppermute | solution.py:19
  16.3 6.6 %collective-permute-start = (f32[8,4,1792]{2,1,0:T(4,128)S(1)}, f32[8,4,1792]{2,1,0:T(4,128)S(1)}, u32[]{:S(2)}, u32[]{:S(2)}) collective-permute-start(f32[8,4,1792]{2,1,0:T(4,128)S(1)} %get-tuple-element.7), channel_id=1, source_target_pairs={{0,1},{1,2},{2,3},{3,4},{4,5},{5,6},{6,7},{8,9},{9,10},{10,11},{11... | collective-permute-start | bytes 688136 | tf_op jit(solution)/shard_map/ppermute | solution.py:17
  19.9 7.3 %collective-permute-start.1 = (f32[8,4,1792]{2,1,0:T(4,128)S(1)}, f32[8,4,1792]{2,1,0:T(4,128)S(1)}, u32[]{:S(2)}, u32[]{:S(2)}) collective-permute-start(f32[8,4,1792]{2,1,0:T(4,128)S(1)} %get-tuple-element.8), channel_id=1, source_target_pairs={{1,0},{2,1},{3,2},{4,3},{5,4},{6,5},{7,6},{9,8},{10,9},{11,10},{12... | collective-permute-start | bytes 688136 | tf_op jit(solution)/shard_map/ppermute | solution.py:19
  31.5 1.5 %copy-start.1 = (bf16[8,4,16,1792]{3,2,1,0:T(8,128)(2,1)S(1)}, bf16[8,4,16,1792]{3,2,1,0:T(8,128)(2,1)}, u32[]{:S(2)}) copy-start(bf16[8,4,16,1792]{3,2,1,0:T(8,128)(2,1)} %param.8) | copy-start | bytes 5505028
  33.0 1.0 %copy-start.2 = (f32[4,16,1792]{2,1,0:T(8,128)S(1)}, f32[4,16,1792]{2,1,0:T(8,128)}, u32[]{:S(2)}) copy-start(f32[4,16,1792]{2,1,0:T(8,128)} %param.9) | copy-start | bytes 1376260
  77.1 7.0 %collective-permute-start.4 = (f32[8,4,1792]{2,1,0:T(4,128)S(1)}, f32[8,4,1792]{2,1,0:T(4,128)S(1)}, u32[]{:S(2)}, u32[]{:S(2)}) collective-permute-start(f32[8,4,1792]{2,1,0:T(4,128)S(1)} %get-tuple-element.5), channel_id=1, source_target_pairs={{0,1},{1,2},{2,3},{3,4},{4,5},{5,6},{6,7},{8,9},{9,10},{10,11},{11... | collective-permute-start | bytes 688136 | tf_op jit(solution)/shard_map/ppermute | solution.py:17
  81.1 7.3 %collective-permute-start.5 = (f32[8,4,1792]{2,1,0:T(4,128)S(1)}, f32[8,4,1792]{2,1,0:T(4,128)S(1)}, u32[]{:S(2)}, u32[]{:S(2)}) collective-permute-start(f32[8,4,1792]{2,1,0:T(4,128)S(1)} %get-tuple-element.6), channel_id=1, source_target_pairs={{1,0},{2,1},{3,2},{4,3},{5,4},{6,5},{7,6},{9,8},{10,9},{11,10},{12... | collective-permute-start | bytes 688136 | tf_op jit(solution)/shard_map/ppermute | solution.py:19
Sparse Core Ops, SparseCore 0:
  34.9 40.5 all-reduce.33

commit v2 on v1

--- a/solution.py
+++ b/solution.py
@@ -21,6 +21,17 @@
             axis=dim,
         )
     return cells
+
+
+def mem_sum(part):
+    count = lax.axis_size("mem")
+    if count & (count - 1):
+        return lax.psum(part, "mem")
+    stride = 1
+    while stride < count:
+        part = part + lax.ppermute(part, "mem", [(i, i ^ stride) for i in range(count)])
+        stride *= 2
+    return part
 
 
 def diffuse(values, row_coef, col_coef):
@@ -62,7 +73,7 @@
     localized = localize(controls, coef_band)
     member_sum = jnp.sum(perturbations * localized[:, None], axis=0)
     weights = radar_mask.astype(jnp.float32) * obs_weight
-    reflect = lax.psum(jnp.sum(jacobian * member_sum, 0), "mem")
+    reflect = mem_sum(jnp.sum(jacobian * member_sum, 0))
     adjoint_inc = jacobian * (weights * reflect)[None]
     sensitivity = jnp.sum(perturbations * adjoint_inc[None], axis=1)
     return controls + localize(sensitivity, coef_band)

time: 101 us -> 54.3 us (0.54)
  waiting for transfers between devices: 51.5 us -> 15.5 us
  between operations: 13.7 us -> 0.28 us
  starting transfers between devices: 18.1 us -> 21.9 us
  other arithmetic: 14.8 us -> 13.2 us
    psum x1 -> x0, waiting for transfers between devices: 40.8 us -> none  [per_device(): reflect = lax.psum(jnp.sum(jacobian * member_sum, 0), 'mem')]
    ppermute x0 -> x2, waiting for transfers between devices: none -> 4.83 us  [mem_sum(): lax.ppermute(part, 'mem', [(i, i ^ stride) for i in range(count)])]
    ppermute x0 -> x2, starting transfers between devices: none -> 2.58 us  [mem_sum(): lax.ppermute(part, 'mem', [(i, i ^ stride) for i in range(count)])]
    ppermute x3, starting transfers between devices: 12.3 us -> 13.6 us  [padded(): lax.ppermute(tail, axis, [(i, (i + 1) % count) for i in range(ends)])]
  transfers between devices with their start and end apart: 7 -> 8, of which waited for: 5 -> 6; matrix products, arithmetic and copies ran while one was open for 1% -> 2% of each run, Pallas kernels for 0% -> 0%
where the time goes in v2:
time: 54.3 us; the launch traced here: 53.9 us
  starting transfers between devices  21.9 us (40%)
  waiting for transfers between devices  15.5 us (29%)
  other arithmetic  13.2 us (24%)
  local copies, waits for them, and re-layouts  2.99 us (6%)
    ppermute x3, starting transfers between devices, padded(): lax.ppermute(tail, axis, [(i, (i + 1) % count) for i in range(ends)])  13.6 us
    ppermute x3, waiting for transfers between devices, padded(): lax.ppermute(head, axis, [((i + 1) % count, i) for i in range(ends)])  8.79 us
    ppermute x3, starting transfers between devices, padded(): lax.ppermute(head, axis, [((i + 1) % count, i) for i in range(ends)])  5.76 us
    ppermute x2, waiting for transfers between devices, mem_sum(): lax.ppermute(part, 'mem', [(i, i ^ stride) for i in range(count)])  4.83 us
    sub x7, other arithmetic, diffuse(): values + jnp.concatenate([col_flux, zeros_col], -1)  3.54 us
    mul x8, other arithmetic, diffuse(): col_coef[..., :, :-1] * (values[..., :, 1:] - values[..., :, :-1])  3.38 us
    ppermute x2, starting transfers between devices, mem_sum(): lax.ppermute(part, 'mem', [(i, i ^ stride) for i in range(count)])  2.58 us
    ppermute x3, waiting for transfers between devices, padded(): lax.ppermute(tail, axis, [(i, (i + 1) % count) for i in range(ends)])  1.9 us
  transfers between devices with their start and end apart: 8, of which 6 were waited for; matrix products, arithmetic and copies ran while one was open for 2% of the time, Pallas kernels for 0%

profile of v2, /device:TPU:1, one launch (start us, length us, event | category | flops | bytes accessed | tf_op | source)
XLA Modules:
  0.0 53.9 jit_solution(11897420206027700757)
XLA Ops:
  0.0 0.0 copy-start.3
  0.0 1.0 %select_bitcast_fusion = f32[1,16,1792]{2,1,0:T(8,128)S(1)} fusion(f32[16,1792]{1,0:T(8,128)} %param.12, pred[16]{0:T(512)(128)(4,1)S(1)} %add_compare_fusion), kind=kLoop, calls=%fused_computation.59 | loop fusion | flops 28672 | bytes 229392 | tf_op jit(solution)/shard_map/stack | solution.py:71
  1.0 0.0 copy-start
  1.0 1.0 %pad_maximum_fusion.4 = (f32[2,4,1792]{2,1,0:T(4,128)S(1)}, f32[2,4,1792]{2,1,0:T(4,128)S(1)}) fusion(f32[1,16,1792]{2,1,0:T(8,128)} %bitcast.16, f32[1,16,1792]{2,1,0:T(8,128)S(1)} %select_bitcast_fusion), kind=kLoop, calls=%fused_computation.61 | loop fusion | flops 28672 | bytes 344064 | tf_op jit(solution)/shard_map/slice | solution.py:14
  2.0 4.6 %collective-permute-start.2 = (f32[2,4,1792]{2,1,0:T(4,128)S(1)}, f32[2,4,1792]{2,1,0:T(4,128)S(1)}, u32[]{:S(2)}, u32[]{:S(2)}) collective-permute-start(f32[2,4,1792]{2,1,0:T(4,128)S(1)} %get-tuple-element.9), channel_id=1, source_target_pairs={{0,1},{1,2},{2,3},{3,4},{4,5},{5,6},{6,7},{8,9},{9,10},{10,11},{11... | collective-permute-start | bytes 172040 | tf_op jit(solution)/shard_map/ppermute | solution.py:17
  6.6 1.9 %collective-permute-start.3 = (f32[2,4,1792]{2,1,0:T(4,128)S(1)}, f32[2,4,1792]{2,1,0:T(4,128)S(1)}, u32[]{:S(2)}, u32[]{:S(2)}) collective-permute-start(f32[2,4,1792]{2,1,0:T(4,128)S(1)} %get-tuple-element.10), channel_id=1, source_target_pairs={{1,0},{2,1},{3,2},{4,3},{5,4},{6,5},{7,6},{9,8},{10,9},{11,10},{12... | collective-permute-start | bytes 172040 | tf_op jit(solution)/shard_map/ppermute | solution.py:19
  8.5 1.2 %fusion.20 = (f32[8,4,1792]{2,1,0:T(4,128)S(1)}, f32[8,4,1792]{2,1,0:T(4,128)S(1)}) fusion(f32[8,16,1792]{2,1,0:T(8,128)} %param.7), kind=kLoop, calls=%fused_computation.64 | loop fusion | bytes 917504 | tf_op jit(solution)/shard_map/slice | solution.py:14
  9.8 3.6 %collective-permute-start = (f32[8,4,1792]{2,1,0:T(4,128)S(1)}, f32[8,4,1792]{2,1,0:T(4,128)S(1)}, u32[]{:S(2)}, u32[]{:S(2)}) collective-permute-start(f32[8,4,1792]{2,1,0:T(4,128)S(1)} %get-tuple-element.7), channel_id=1, source_target_pairs={{0,1},{1,2},{2,3},{3,4},{4,5},{5,6},{6,7},{8,9},{9,10},{10,11},{11... | collective-permute-start | bytes 688136 | tf_op jit(solution)/shard_map/ppermute | solution.py:17
  13.4 1.9 %collective-permute-start.1 = (f32[8,4,1792]{2,1,0:T(4,128)S(1)}, f32[8,4,1792]{2,1,0:T(4,128)S(1)}, u32[]{:S(2)}, u32[]{:S(2)}) collective-permute-start(f32[8,4,1792]{2,1,0:T(4,128)S(1)} %get-tuple-element.8), channel_id=1, source_target_pairs={{1,0},{2,1},{3,2},{4,3},{5,4},{6,5},{7,6},{9,8},{10,9},{11,10},{12... | collective-permute-start | bytes 688136 | tf_op jit(solution)/shard_map/ppermute | solution.py:19
  15.3 0.0 collective-permute-done.2
  15.4 0.0 collective-permute-done.3
  15.4 0.0 copy-done.3
  15.4 0.1 pad_maximum_fusion.2
  15.5 0.9 %collective-permute-done = f32[8,4,1792]{2,1,0:T(4,128)S(1)} collective-permute-done((f32[8,4,1792]{2,1,0:T(4,128)S(1)}, f32[8,4,1792]{2,1,0:T(4,128)S(1)}, u32[]{:S(2)}, u32[]{:S(2)}) %collective-permute-start) | collective-permute-done | bytes 229408 | tf_op jit(solution)/shard_map/ppermute | solution.py:17
  16.4 4.4 %collective-permute-done.1 = f32[8,4,1792]{2,1,0:T(4,128)S(1)} collective-permute-done((f32[8,4,1792]{2,1,0:T(4,128)S(1)}, f32[8,4,1792]{2,1,0:T(4,128)S(1)}, u32[]{:S(2)}, u32[]{:S(2)}) %collective-permute-start.1) | collective-permute-done | bytes 229408 | tf_op jit(solution)/shard_map/ppermute | solution.py:19
  20.8 0.0 copy-done
  20.8 0.2 pad_maximum_fusion
  20.9 0.2 fusion.17
  21.1 0.4 fusion.16
  21.6 0.6 %pad_subtract_fusion.5 = f32[8,24,1792]{2,1,0:T(8,128)S(1)} fusion(f32[8,24,1791]{2,1,0:T(8,128)S(1)} %fusion.16, f32[8,23,1792]{2,1,0:T(8,128)S(1)} %fusion.17, f32[8,4,1792]{2,1,0:T(4,128)S(1)} %collective-permute-done.1, f32[8,16,1792]{2,1,0:T(8,128)S(1)} %copy-done, f32[8,4,1792]{2,1,0:T(4,128)S(1)} %collective-permute-done), kind=kLoop, calls=%fused_computation.43 | loop fusion | flops 2064384 | bytes 5446912 | tf_op jit(solution)/shard_map/sub | solution.py:48
  22.1 0.2 fusion.15
  22.3 0.4 fusion.14
  22.8 0.5 pad_subtract_fusion.4
  23.2 0.2 fusion.13
  23.4 0.4 fusion.12
  23.9 0.5 pad_subtract_fusion.3
  24.3 0.2 fusion.11
  24.5 0.4 fusion.10
  25.0 0.0 copy-start.1
  25.0 0.5 pad_subtract_fusion.8
  25.5 1.0 %copy-done.1 = bf16[8,4,16,1792]{3,2,1,0:T(8,128)(2,1)S(1)} copy-done((bf16[8,4,16,1792]{3,2,1,0:T(8,128)(2,1)S(1)}, bf16[8,4,16,1792]{3,2,1,0:T(8,128)(2,1)}, u32[]{:S(2)}) %copy-start.1) | copy-done | bytes 1835032
  26.5 0.0 copy-start.2
  26.5 0.4 fusion
  26.9 0.6 %copy-done.2 = f32[4,16,1792]{2,1,0:T(8,128)S(1)} copy-done((f32[4,16,1792]{2,1,0:T(8,128)S(1)}, f32[4,16,1792]{2,1,0:T(8,128)}, u32[]{:S(2)}) %copy-start.2) | copy-done | bytes 458776
  27.5 0.0 copy-start.4
  27.5 0.0 copy-start.5
  27.5 1.3 %collective-permute-start.4 = (f32[16,1792]{1,0:T(8,128)S(1)}, f32[16,1792]{1,0:T(8,128)S(1)}, u32[]{:S(2)}, u32[]{:S(2)}) collective-permute-start(f32[16,1792]{1,0:T(8,128)S(1)} %multiply_reduce_fusion), channel_id=1, source_target_pairs={{0,8},{8,0},{16,24},{24,16},{1,9},{9,1},{17,25},{25,17},{2,10},{10... | collective-permute-start | bytes 344072 | tf_op jit(solution)/shard_map/ppermute | solution.py:32
  28.8 2.4 %collective-permute-done.4 = f32[16,1792]{1,0:T(8,128)S(1)} collective-permute-done((f32[16,1792]{1,0:T(8,128)S(1)}, f32[16,1792]{1,0:T(8,128)S(1)}, u32[]{:S(2)}, u32[]{:S(2)}) %collective-permute-start.4) | collective-permute-done | bytes 114720 | tf_op jit(solution)/shard_map/ppermute | solution.py:32
  31.3 1.3 %collective-permute-start.5 = (f32[16,1792]{1,0:T(8,128)S(1)}, f32[16,1792]{1,0:T(8,128)S(1)}, u32[]{:S(2)}, u32[]{:S(2)}) collective-permute-start(f32[16,1792]{1,0:T(8,128)S(1)} %add.138), channel_id=1, source_target_pairs={{0,16},{8,24},{16,0},{24,8},{1,17},{9,25},{17,1},{25,9},{2,18},{10... | collective-permute-start | bytes 344072 | tf_op jit(solution)/shard_map/ppermute | solution.py:32
  32.6 2.4 %collective-permute-done.5 = f32[16,1792]{1,0:T(8,128)S(1)} collective-permute-done((f32[16,1792]{1,0:T(8,128)S(1)}, f32[16,1792]{1,0:T(8,128)S(1)}, u32[]{:S(2)}, u32[]{:S(2)}) %collective-permute-start.5) | collective-permute-done | bytes 114720 | tf_op jit(solution)/shard_map/ppermute | solution.py:32
  35.0 0.0 copy-done.4
  35.0 0.0 copy-done.5
  35.1 0.4 fusion.1
  35.4 0.1 fusion.19
  35.5 5.4 %collective-permute-start.6 = (f32[8,4,1792]{2,1,0:T(4,128)S(1)}, f32[8,4,1792]{2,1,0:T(4,128)S(1)}, u32[]{:S(2)}, u32[]{:S(2)}) collective-permute-start(f32[8,4,1792]{2,1,0:T(4,128)S(1)} %get-tuple-element.5), channel_id=1, source_target_pairs={{0,1},{1,2},{2,3},{3,4},{4,5},{5,6},{6,7},{8,9},{9,10},{10,11},{11... | collective-permute-start | bytes 688136 | tf_op jit(solution)/shard_map/ppermute | solution.py:17
  40.9 1.9 %collective-permute-start.7 = (f32[8,4,1792]{2,1,0:T(4,128)S(1)}, f32[8,4,1792]{2,1,0:T(4,128)S(1)}, u32[]{:S(2)}, u32[]{:S(2)}) collective-permute-start(f32[8,4,1792]{2,1,0:T(4,128)S(1)} %get-tuple-element.6), channel_id=1, source_target_pairs={{1,0},{2,1},{3,2},{4,3},{5,4},{6,5},{7,6},{9,8},{10,9},{11,10},{12... | collective-permute-start | bytes 688136 | tf_op jit(solution)/shard_map/ppermute | solution.py:19
  42.8 1.0 %collective-permute-done.6 = f32[8,4,1792]{2,1,0:T(4,128)S(1)} collective-permute-done((f32[8,4,1792]{2,1,0:T(4,128)S(1)}, f32[8,4,1792]{2,1,0:T(4,128)S(1)}, u32[]{:S(2)}, u32[]{:S(2)}) %collective-permute-start.6) | collective-permute-done | bytes 229408 | tf_op jit(solution)/shard_map/ppermute | solution.py:17
  43.8 4.4 %collective-permute-done.7 = f32[8,4,1792]{2,1,0:T(4,128)S(1)} collective-permute-done((f32[8,4,1792]{2,1,0:T(4,128)S(1)}, f32[8,4,1792]{2,1,0:T(4,128)S(1)}, u32[]{:S(2)}, u32[]{:S(2)}) %collective-permute-start.7) | collective-permute-done | bytes 229408 | tf_op jit(solution)/shard_map/ppermute | solution.py:19
  48.2 0.2 pad_maximum_fusion.1
  48.4 0.2 fusion.9
  48.6 0.4 fusion.8
  49.0 0.6 %pad_subtract_fusion.2 = f32[8,24,1792]{2,1,0:T(8,128)S(1)} fusion(f32[8,24,1791]{2,1,0:T(8,128)S(1)} %fusion.8, f32[8,23,1792]{2,1,0:T(8,128)S(1)} %fusion.9, f32[8,4,1792]{2,1,0:T(4,128)S(1)} %collective-permute-done.7, f32[8,16,1792]{2,1,0:T(8,128)S(1)} %fusion.1, f32[8,4,1792]{2,1,0:T(4,128)S(1)} %collective-permute-done.6), kind=kLoop, calls=%fused_computation.40 | loop fusion | flops 2064384 | bytes 5446912 | tf_op jit(solution)/shard_map/sub | solution.py:48
  49.6 0.2 fusion.7
  49.8 0.4 fusion.6
  50.2 0.5 pad_subtract_fusion.1
  50.7 0.2 fusion.5
  50.9 0.4 fusion.4
  51.3 0.5 pad_subtract_fusion
  51.8 0.2 fusion.3
  52.0 0.4 fusion.2
  52.5 1.5 %fusion.18 = f32[8,16,1792]{2,1,0:T(8,128)} fusion(f32[8,16,1792]{2,1,0:T(8,128)S(1)} %copy-done, f32[8,24,1791]{2,1,0:T(8,128)S(1)} %fusion.2, f32[8,23,1792]{2,1,0:T(8,128)S(1)} %fusion.3, f32[8,24,1792]{2,1,0:T(8,128)S(1)} %pad_subtract_fusion), kind=kLoop, calls=%fused_computation.45 | loop fusion | flops 1146880 | bytes 5446912 | tf_op jit(solution)/shard_map/add | solution.py:79
  (7 shorter events, 0.2 us)
Async XLA Ops:
  0.0 15.4 %copy-start.3 = (f32[16,1792]{1,0:T(8,128)S(1)}, f32[16,1792]{1,0:T(8,128)}, u32[]{:S(2)}) copy-start(f32[16,1792]{1,0:T(8,128)} %param.13) | copy-start | bytes 344068
  1.0 19.7 %copy-start = (f32[8,16,1792]{2,1,0:T(8,128)S(1)}, f32[8,16,1792]{2,1,0:T(8,128)}, u32[]{:S(2)}) copy-start(f32[8,16,1792]{2,1,0:T(8,128)} %param.7) | copy-start | bytes 2752516
  2.0 13.4 %collective-permute-start.2 = (f32[2,4,1792]{2,1,0:T(4,128)S(1)}, f32[2,4,1792]{2,1,0:T(4,128)S(1)}, u32[]{:S(2)}, u32[]{:S(2)}) collective-permute-start(f32[2,4,1792]{2,1,0:T(4,128)S(1)} %get-tuple-element.9), channel_id=1, source_target_pairs={{0,1},{1,2},{2,3},{3,4},{4,5},{5,6},{6,7},{8,9},{9,10},{10,11},{11... | collective-permute-start | bytes 172040 | tf_op jit(solution)/shard_map/ppermute | solution.py:17
  6.6 8.8 %collective-permute-start.3 = (f32[2,4,1792]{2,1,0:T(4,128)S(1)}, f32[2,4,1792]{2,1,0:T(4,128)S(1)}, u32[]{:S(2)}, u32[]{:S(2)}) collective-permute-start(f32[2,4,1792]{2,1,0:T(4,128)S(1)} %get-tuple-element.10), channel_id=1, source_target_pairs={{1,0},{2,1},{3,2},{4,3},{5,4},{6,5},{7,6},{9,8},{10,9},{11,10},{12... | collective-permute-start | bytes 172040 | tf_op jit(solution)/shard_map/ppermute | solution.py:19
  9.8 6.6 %collective-permute-start = (f32[8,4,1792]{2,1,0:T(4,128)S(1)}, f32[8,4,1792]{2,1,0:T(4,128)S(1)}, u32[]{:S(2)}, u32[]{:S(2)}) collective-permute-start(f32[8,4,1792]{2,1,0:T(4,128)S(1)} %get-tuple-element.7), channel_id=1, source_target_pairs={{0,1},{1,2},{2,3},{3,4},{4,5},{5,6},{6,7},{8,9},{9,10},{10,11},{11... | collective-permute-start | bytes 688136 | tf_op jit(solution)/shard_map/ppermute | solution.py:17
  13.4 7.3 %collective-permute-start.1 = (f32[8,4,1792]{2,1,0:T(4,128)S(1)}, f32[8,4,1792]{2,1,0:T(4,128)S(1)}, u32[]{:S(2)}, u32[]{:S(2)}) collective-permute-start(f32[8,4,1792]{2,1,0:T(4,128)S(1)} %get-tuple-element.8), channel_id=1, source_target_pairs={{1,0},{2,1},{3,2},{4,3},{5,4},{6,5},{7,6},{9,8},{10,9},{11,10},{12... | collective-permute-start | bytes 688136 | tf_op jit(solution)/shard_map/ppermute | solution.py:19
  25.0 1.5 %copy-start.1 = (bf16[8,4,16,1792]{3,2,1,0:T(8,128)(2,1)S(1)}, bf16[8,4,16,1792]{3,2,1,0:T(8,128)(2,1)}, u32[]{:S(2)}) copy-start(bf16[8,4,16,1792]{3,2,1,0:T(8,128)(2,1)} %param.8) | copy-start | bytes 5505028
  26.5 1.0 %copy-start.2 = (f32[4,16,1792]{2,1,0:T(8,128)S(1)}, f32[4,16,1792]{2,1,0:T(8,128)}, u32[]{:S(2)}) copy-start(f32[4,16,1792]{2,1,0:T(8,128)} %param.9) | copy-start | bytes 1376260
  27.5 7.5 %copy-start.4 = (f32[16,1792]{1,0:T(8,128)S(1)}, f32[16,1792]{1,0:T(8,128)}, u32[]{:S(2)}) copy-start(f32[16,1792]{1,0:T(8,128)} %param.10) | copy-start | bytes 344068
  27.5 7.5 %copy-start.5 = (s32[16,1792]{1,0:T(8,128)S(1)}, s32[16,1792]{1,0:T(8,128)}, u32[]{:S(2)}) copy-start(s32[16,1792]{1,0:T(8,128)} %param.11) | copy-start | bytes 344068
  27.5 3.7 %collective-permute-start.4 = (f32[16,1792]{1,0:T(8,128)S(1)}, f32[16,1792]{1,0:T(8,128)S(1)}, u32[]{:S(2)}, u32[]{:S(2)}) collective-permute-start(f32[16,1792]{1,0:T(8,128)S(1)} %multiply_reduce_fusion), channel_id=1, source_target_pairs={{0,8},{8,0},{16,24},{24,16},{1,9},{9,1},{17,25},{25,17},{2,10},{10... | collective-permute-start | bytes 344072 | tf_op jit(solution)/shard_map/ppermute | solution.py:32
  31.3 3.7 %collective-permute-start.5 = (f32[16,1792]{1,0:T(8,128)S(1)}, f32[16,1792]{1,0:T(8,128)S(1)}, u32[]{:S(2)}, u32[]{:S(2)}) collective-permute-start(f32[16,1792]{1,0:T(8,128)S(1)} %add.138), channel_id=1, source_target_pairs={{0,16},{8,24},{16,0},{24,8},{1,17},{9,25},{17,1},{25,9},{2,18},{10... | collective-permute-start | bytes 344072 | tf_op jit(solution)/shard_map/ppermute | solution.py:32
  35.5 8.3 %collective-permute-start.6 = (f32[8,4,1792]{2,1,0:T(4,128)S(1)}, f32[8,4,1792]{2,1,0:T(4,128)S(1)}, u32[]{:S(2)}, u32[]{:S(2)}) collective-permute-start(f32[8,4,1792]{2,1,0:T(4,128)S(1)} %get-tuple-element.5), channel_id=1, source_target_pairs={{0,1},{1,2},{2,3},{3,4},{4,5},{5,6},{6,7},{8,9},{9,10},{10,11},{11... | collective-permute-start | bytes 688136 | tf_op jit(solution)/shard_map/ppermute | solution.py:17
  40.9 7.3 %collective-permute-start.7 = (f32[8,4,1792]{2,1,0:T(4,128)S(1)}, f32[8,4,1792]{2,1,0:T(4,128)S(1)}, u32[]{:S(2)}, u32[]{:S(2)}) collective-permute-start(f32[8,4,1792]{2,1,0:T(4,128)S(1)} %get-tuple-element.6), channel_id=1, source_target_pairs={{1,0},{2,1},{3,2},{4,3},{5,4},{6,5},{7,6},{9,8},{10,9},{11,10},{12... | collective-permute-start | bytes 688136 | tf_op jit(solution)/shard_map/ppermute | solution.py:19

commit v3 on v2

--- a/solution.py
+++ b/solution.py
@@ -6,21 +6,23 @@
 STEPS = 4
 
 
-def padded(cells, sides, width):
-    for axis, dim in sides:
-        count = lax.axis_size(axis)
-        ends = count - 1
-        head = lax.slice_in_dim(cells, 0, width, axis=dim)
-        tail = lax.slice_in_dim(cells, cells.shape[dim] - width, cells.shape[dim], axis=dim)
-        cells = jnp.concatenate(
-            [
-                lax.ppermute(tail, axis, [(i, (i + 1) % count) for i in range(ends)]),
-                cells,
-                lax.ppermute(head, axis, [((i + 1) % count, i) for i in range(ends)]),
-            ],
-            axis=dim,
-        )
-    return cells
+def exchange(parts, width):
+    count = lax.axis_size("tile")
+    cols = parts[0].shape[-1]
+    sizes = [part[..., :width, :].size // cols for part in parts]
+    head = jnp.concatenate([part[..., :width, :].reshape(-1, cols) for part in parts], 0)
+    tail = jnp.concatenate([part[..., -width:, :].reshape(-1, cols) for part in parts], 0)
+    above = lax.ppermute(tail, "tile", [(i, i + 1) for i in range(count - 1)])
+    below = lax.ppermute(head, "tile", [(i + 1, i) for i in range(count - 1)])
+    bands = []
+    start = 0
+    for part, size in zip(parts, sizes):
+        shape = part.shape[:-2] + (width, cols)
+        top = above[start : start + size].reshape(shape)
+        bottom = below[start : start + size].reshape(shape)
+        bands.append(jnp.concatenate([top, part, bottom], -2))
+        start += size
+    return bands
 
 
 def mem_sum(part):
@@ -52,11 +54,8 @@
 
 
 def localize(field, coef_band):
-    row_count = field.shape[1]
-    widened = padded(field, (("tile", 1),), STEPS)
     for repeat in range(STEPS):
-        widened = diffuse(widened, coef_band[0], coef_band[1])
-    field = widened[:, STEPS : STEPS + row_count]
+        field = diffuse(field, coef_band[0], coef_band[1])
     return field
 
 
@@ -69,14 +68,15 @@
         row_index < row_count * lax.axis_size("tile") - 1, row_faces, jnp.zeros_like(row_faces)
     )
     stacked = jnp.stack([row_coef, col_faces])
-    coef_band = padded(stacked, (("tile", 1),), STEPS)
-    localized = localize(controls, coef_band)
-    member_sum = jnp.sum(perturbations * localized[:, None], axis=0)
-    weights = radar_mask.astype(jnp.float32) * obs_weight
-    reflect = mem_sum(jnp.sum(jacobian * member_sum, 0))
-    adjoint_inc = jacobian * (weights * reflect)[None]
-    sensitivity = jnp.sum(perturbations * adjoint_inc[None], axis=1)
-    return controls + localize(sensitivity, coef_band)
+    field, coef_band = exchange([controls, stacked], STEPS)
+    localized = localize(field, coef_band)[:, STEPS : STEPS + row_count]
+    mix = jnp.sum(perturbations.astype(jnp.float32) * jacobian[None], axis=1)
+    (mix_band,) = exchange([mix], STEPS)
+    reflect = mem_sum(jnp.sum(mix * localized, 0))
+    weighted = radar_mask.astype(jnp.float32) * obs_weight * reflect
+    (weighted_band,) = exchange([weighted[None]], STEPS)
+    sensitivity = mix_band * weighted_band
+    return controls + localize(sensitivity, coef_band)[:, STEPS : STEPS + row_count]
 
 
 def solution(mesh):

time: 54.3 us -> 52.7 us (0.971)
  waiting for transfers between devices: 15.5 us -> 10.8 us
  local copies, waits for them, and re-layouts: 2.99 us -> 5.83 us
  other arithmetic: 13.2 us -> 15.1 us
  starting transfers between devices: 21.9 us -> 20 us
    slice x2 -> x6, local copies, waits for them, and re-layouts: 1.32 us -> 5.1 us  [the longest x2 1.85 us: exchange(): top = above[start:start + size].reshape(shape)]
    ppermute x6, waiting for transfers between devices: 10.7 us -> 8.01 us  [the longest x3 7.43 us: exchange(): below = lax.ppermute(head, 'tile', [(i + 1, i) for i in range(count - 1)])]
    ppermute x2, waiting for transfers between devices: 4.83 us -> 2.83 us  [mem_sum(): lax.ppermute(part, 'mem', [(i, i ^ stride) for i in range(count)])]
    ppermute x6, starting transfers between devices: 19.4 us -> 17.4 us  [the longest x3 11.4 us: exchange(): above = lax.ppermute(tail, 'tile', [(i, i + 1) for i in range(count - 1)])]
    unnamed x12 -> x8, local copies, waits for them, and re-layouts: 1.64 us -> 0.02 us
    concatenate x3 -> x4, other arithmetic: 0.42 us -> 1.71 us  [the longest x1 0.73 us: exchange(): jnp.concatenate([part[..., -width:, :].reshape(-1, cols) for part in part...]
    broadcast_in_dim x0 -> x1, other arithmetic: none -> 1.04 us  [per_device(): weighted_band, = exchange([weighted[None]], STEPS)]
    reshape x0 -> x13, local copies, waits for them, and re-layouts: none -> 0.69 us  [the longest x4 0.2 us: exchange(): part[..., -width:, :].reshape(-1, cols)]
  transfers between devices with their start and end apart: 8 -> 8, of which waited for: 6 -> 4; matrix products, arithmetic and copies ran while one was open for 2% -> 7% of each run, Pallas kernels for 0% -> 0%
where the time goes in v3:
time: 52.7 us; the launch traced here: 52.2 us
  starting transfers between devices  20 us (38%)
  other arithmetic  15.1 us (29%)
  waiting for transfers between devices  10.8 us (20%)
  local copies, waits for them, and re-layouts  5.83 us (11%)
    ppermute x3, starting transfers between devices, exchange(): above = lax.ppermute(tail, 'tile', [(i, i + 1) for i in range(count - 1)])  11.4 us
    ppermute x3, waiting for transfers between devices, exchange(): below = lax.ppermute(head, 'tile', [(i + 1, i) for i in range(count - 1)])  7.43 us
    ppermute x3, starting transfers between devices, exchange(): below = lax.ppermute(head, 'tile', [(i + 1, i) for i in range(count - 1)])  6.06 us
    mul x8, other arithmetic, diffuse(): col_coef[..., :, :-1] * (values[..., :, 1:] - values[..., :, :-1])  3.38 us
    sub x6, other arithmetic, diffuse(): values + jnp.concatenate([col_flux, zeros_col], -1)  2.95 us
    ppermute x2, waiting for transfers between devices, mem_sum(): lax.ppermute(part, 'mem', [(i, i ^ stride) for i in range(count)])  2.83 us
    ppermute x2, starting transfers between devices, mem_sum(): lax.ppermute(part, 'mem', [(i, i ^ stride) for i in range(count)])  2.58 us
    slice x2, local copies, waits for them, and re-layouts, exchange(): top = above[start:start + size].reshape(shape)  1.85 us
  transfers between devices with their start and end apart: 8, of which 4 were waited for; matrix products, arithmetic and copies ran while one was open for 7% of the time, Pallas kernels for 0%

profile of v3, /device:TPU:1, one launch (start us, length us, event | category | flops | bytes accessed | tf_op | source)
XLA Modules:
  0.0 52.2 jit_solution(6028657806695804598)
XLA Ops:
  0.0 1.0 %select_bitcast_fusion = f32[1,16,1792]{2,1,0:T(8,128)S(1)} fusion(f32[16,1792]{1,0:T(8,128)} %param.12, pred[16]{0:T(512)(128)(4,1)S(1)} %add_compare_fusion), kind=kLoop, calls=%fused_computation.59 | loop fusion | flops 28672 | bytes 229392 | tf_op jit(solution)/shard_map/stack | solution.py:70
  1.0 0.9 %pad_maximum_fusion.5 = (f32[2,4,1792]{2,1,0:T(4,128)S(1)}, f32[2,4,1792]{2,1,0:T(4,128)S(1)}) fusion(f32[1,16,1792]{2,1,0:T(8,128)} %bitcast.26, f32[1,16,1792]{2,1,0:T(8,128)S(1)} %select_bitcast_fusion), kind=kLoop, calls=%fused_computation.61 | loop fusion | flops 28672 | bytes 344064 | tf_op jit(solution)/shard_map/slice | solution.py:14
  1.9 0.0 copy-start.1
  1.9 0.0 copy-start.2
  1.9 1.4 %fusion.19 = (f32[8,4,1792]{2,1,0:T(4,128)S(1)}, f32[8,4,1792]{2,1,0:T(4,128)S(1)}) fusion(f32[8,16,1792]{2,1,0:T(8,128)} %param.7), kind=kLoop, calls=%fused_computation.65 | loop fusion | bytes 917504 | tf_op jit(solution)/shard_map/slice | solution.py:14
  3.3 0.1 reshape.56
  3.4 0.7 %pad_maximum_fusion.2 = f32[40,1792]{1,0:T(8,128)} fusion(f32[8,1792]{1,0:T(8,128)S(1)} %reshape.57, f32[32,1792]{1,0:T(8,128)S(1)} %reshape.56), kind=kLoop, calls=%fused_computation.53 | loop fusion | flops 71680 | bytes 573440 | tf_op jit(solution)/shard_map/concatenate | solution.py:14
  4.1 4.6 %collective-permute-start.2 = (f32[40,1792]{1,0:T(8,128)}, f32[40,1792]{1,0:T(8,128)}, u32[]{:S(2)}, u32[]{:S(2)}) collective-permute-start(f32[40,1792]{1,0:T(8,128)} %pad_maximum_fusion.2), channel_id=1, source_target_pairs={{0,1},{1,2},{2,3},{3,4},{4,5},{5,6},{6,7},{8,9},{9,10},{10,11},{11... | collective-permute-start | bytes 860168 | tf_op jit(solution)/shard_map/ppermute | solution.py:15
  8.7 0.1 reshape.59
  8.8 0.7 %pad_maximum_fusion.3 = f32[40,1792]{1,0:T(8,128)} fusion(f32[8,1792]{1,0:T(8,128)S(1)} %reshape.60, f32[32,1792]{1,0:T(8,128)S(1)} %reshape.59), kind=kLoop, calls=%fused_computation.54 | loop fusion | flops 71680 | bytes 573440 | tf_op jit(solution)/shard_map/concatenate | solution.py:13
  9.6 2.0 %collective-permute-start.3 = (f32[40,1792]{1,0:T(8,128)}, f32[40,1792]{1,0:T(8,128)}, u32[]{:S(2)}, u32[]{:S(2)}) collective-permute-start(f32[40,1792]{1,0:T(8,128)} %pad_maximum_fusion.3), channel_id=1, source_target_pairs={{1,0},{2,1},{3,2},{4,3},{5,4},{6,5},{7,6},{9,8},{10,9},{11,10},{12... | collective-permute-start | bytes 860168 | tf_op jit(solution)/shard_map/ppermute | solution.py:16
  11.6 0.4 multiply_reduce_fusion
  12.0 0.6 %collective-permute-done.2 = f32[40,1792]{1,0:T(8,128)} collective-permute-done((f32[40,1792]{1,0:T(8,128)}, f32[40,1792]{1,0:T(8,128)}, u32[]{:S(2)}, u32[]{:S(2)}) %collective-permute-start.2) | collective-permute-done | bytes 286752 | tf_op jit(solution)/shard_map/ppermute | solution.py:15
  12.6 0.8 %slice.231 = f32[8,1792]{1,0:T(8,128)S(1)} slice(f32[40,1792]{1,0:T(8,128)} %collective-permute-done.2), slice={[32:40], [0:1792]} | slice | bytes 114688 | tf_op jit(solution)/shard_map/slice | solution.py:21
  13.4 4.5 %collective-permute-done.3 = f32[40,1792]{1,0:T(8,128)} collective-permute-done((f32[40,1792]{1,0:T(8,128)}, f32[40,1792]{1,0:T(8,128)}, u32[]{:S(2)}, u32[]{:S(2)}) %collective-permute-start.3) | collective-permute-done | bytes 286752 | tf_op jit(solution)/shard_map/ppermute | solution.py:16
  18.0 0.8 %slice.232 = f32[8,1792]{1,0:T(8,128)S(1)} slice(f32[40,1792]{1,0:T(8,128)} %collective-permute-done.3), slice={[32:40], [0:1792]} | slice | bytes 114688 | tf_op jit(solution)/shard_map/slice | solution.py:22
  18.8 0.1 pad_maximum_fusion.1
  18.9 0.0 copy-start
  18.9 1.0 %slice.229 = f32[32,1792]{1,0:T(8,128)S(1)} slice(f32[40,1792]{1,0:T(8,128)} %collective-permute-done.2), slice={[0:32], [0:1792]} | slice | bytes 458752 | tf_op jit(solution)/shard_map/slice | solution.py:21
  20.0 0.1 reshape.58
  20.0 1.0 %slice.230 = f32[32,1792]{1,0:T(8,128)S(1)} slice(f32[40,1792]{1,0:T(8,128)} %collective-permute-done.3), slice={[0:32], [0:1792]} | slice | bytes 458752 | tf_op jit(solution)/shard_map/slice | solution.py:22
  21.0 0.1 reshape.61
  21.1 0.2 pad_maximum_fusion
  21.3 0.2 fusion.15
  21.5 0.4 fusion.14
  21.9 0.6 %pad_subtract_fusion.5 = f32[8,24,1792]{2,1,0:T(8,128)S(1)} fusion(f32[8,24,1791]{2,1,0:T(8,128)S(1)} %fusion.14, f32[8,23,1792]{2,1,0:T(8,128)S(1)} %fusion.15, f32[8,4,1792]{2,1,0:T(4,128)S(1)} %reshape.61, f32[8,16,1792]{2,1,0:T(8,128)S(1)} %copy-done, f32[8,4,1792]{2,1,0:T(4,128)S(1)} %reshape.58), kind=kLoop, calls=%fused_computation.40 | loop fusion | flops 2064384 | bytes 5446912 | tf_op jit(solution)/shard_map/sub | solution.py:50
  22.5 0.2 fusion.13
  22.7 0.4 fusion.12
  23.1 0.5 pad_subtract_fusion.4
  23.6 0.2 fusion.11
  23.8 0.4 fusion.10
  24.2 0.5 pad_subtract_fusion.3
  24.7 0.2 fusion.9
  24.9 0.4 fusion.8
  25.3 0.6 %fusion.18 = f32[16,1792]{1,0:T(8,128)S(1)} fusion(f32[8,16,1792]{2,1,0:T(8,128)S(1)} %multiply_reduce_fusion, f32[8,24,1791]{2,1,0:T(8,128)S(1)} %fusion.8, f32[8,23,1792]{2,1,0:T(8,128)S(1)} %fusion.9, f32[8,24,1792]{2,1,0:T(8,128)S(1)} %pad_subtract_fusion.3), kind=kLoop, calls=%fused_computation.48 | loop fusion | flops 1347584 | bytes 4644096 | tf_op jit(solution)/shard_map/reduce_sum | solution.py:75
  25.9 1.3 %collective-permute-start.4 = (f32[16,1792]{1,0:T(8,128)S(1)}, f32[16,1792]{1,0:T(8,128)S(1)}, u32[]{:S(2)}, u32[]{:S(2)}) collective-permute-start(f32[16,1792]{1,0:T(8,128)S(1)} %fusion.18), channel_id=1, source_target_pairs={{0,8},{8,0},{16,24},{24,16},{1,9},{9,1},{17,25},{25,17},{2,10},{10... | collective-permute-start | bytes 344072 | tf_op jit(solution)/shard_map/ppermute | solution.py:34
  27.1 2.8 %collective-permute-done.4 = f32[16,1792]{1,0:T(8,128)S(1)} collective-permute-done((f32[16,1792]{1,0:T(8,128)S(1)}, f32[16,1792]{1,0:T(8,128)S(1)}, u32[]{:S(2)}, u32[]{:S(2)}) %collective-permute-start.4) | collective-permute-done | bytes 114720 | tf_op jit(solution)/shard_map/ppermute | solution.py:34
  30.0 1.3 %collective-permute-start.5 = (f32[16,1792]{1,0:T(8,128)S(1)}, f32[16,1792]{1,0:T(8,128)}, u32[]{:S(2)}, u32[]{:S(2)}) collective-permute-start(f32[16,1792]{1,0:T(8,128)S(1)} %add.138), channel_id=1, source_target_pairs={{0,16},{8,24},{16,0},{24,8},{1,17},{9,25},{17,1},{25,9},{2,18},{10... | collective-permute-start | bytes 344072 | tf_op jit(solution)/shard_map/ppermute | solution.py:34
  31.3 0.1 fusion.20
  31.4 0.1 reshape.52
  31.5 3.1 %collective-permute-start = (f32[32,1792]{1,0:T(8,128)S(1)}, f32[32,1792]{1,0:T(8,128)S(1)}, u32[]{:S(2)}, u32[]{:S(2)}) collective-permute-start(f32[32,1792]{1,0:T(8,128)S(1)} %reshape.52), channel_id=1, source_target_pairs={{0,1},{1,2},{2,3},{3,4},{4,5},{5,6},{6,7},{8,9},{9,10},{10,11},{11... | collective-permute-start | bytes 688136 | tf_op jit(solution)/shard_map/ppermute | solution.py:15
  34.6 0.1 reshape.54
  34.7 1.9 %collective-permute-start.1 = (f32[32,1792]{1,0:T(8,128)S(1)}, f32[32,1792]{1,0:T(8,128)S(1)}, u32[]{:S(2)}, u32[]{:S(2)}) collective-permute-start(f32[32,1792]{1,0:T(8,128)S(1)} %reshape.54), channel_id=1, source_target_pairs={{1,0},{2,1},{3,2},{4,3},{5,4},{6,5},{7,6},{9,8},{10,9},{11,10},{12... | collective-permute-start | bytes 688136 | tf_op jit(solution)/shard_map/ppermute | solution.py:16
  36.6 0.0 collective-permute-done.5
  36.6 1.0 %multiply_bitcast_fusion = f32[1,16,1792]{2,1,0:T(8,128)S(1)} fusion(f32[16,1792]{1,0:T(8,128)S(1)} %add.138, f32[16,1792]{1,0:T(8,128)} %collective-permute-done.5, f32[16,1792]{1,0:T(8,128)} %param.10, s32[16,1792]{1,0:T(8,128)} %param.11), kind=kLoop, calls=%fused_computation.58 | loop fusion | flops 114688 | bytes 573440 | tf_op jit(solution)/shard_map/broadcast_in_dim | solution.py:77
  37.7 3.6 %collective-permute-start.6 = (f32[4,1792]{1,0:T(4,128)S(1)}, f32[4,1792]{1,0:T(4,128)S(1)}, u32[]{:S(2)}, u32[]{:S(2)}) collective-permute-start(f32[4,1792]{1,0:T(4,128)S(1)} %get-tuple-element.11), channel_id=1, source_target_pairs={{0,1},{1,2},{2,3},{3,4},{4,5},{5,6},{6,7},{8,9},{9,10},{10,11},{11... | collective-permute-start | bytes 86024 | tf_op jit(solution)/shard_map/ppermute | solution.py:15
  41.3 2.1 %collective-permute-start.7 = (f32[4,1792]{1,0:T(4,128)S(1)}, f32[4,1792]{1,0:T(4,128)S(1)}, u32[]{:S(2)}, u32[]{:S(2)}) collective-permute-start(f32[4,1792]{1,0:T(4,128)S(1)} %get-tuple-element.12), channel_id=1, source_target_pairs={{1,0},{2,1},{3,2},{4,3},{5,4},{6,5},{7,6},{9,8},{10,9},{11,10},{12... | collective-permute-start | bytes 86024 | tf_op jit(solution)/shard_map/ppermute | solution.py:16
  43.5 0.0 collective-permute-done
  43.5 0.1 reshape.53
  43.6 0.1 reshape.55
  43.6 2.9 %collective-permute-done.7 = f32[4,1792]{1,0:T(4,128)S(1)} collective-permute-done((f32[4,1792]{1,0:T(4,128)S(1)}, f32[4,1792]{1,0:T(4,128)S(1)}, u32[]{:S(2)}, u32[]{:S(2)}) %collective-permute-start.7) | collective-permute-done | bytes 28704 | tf_op jit(solution)/shard_map/ppermute | solution.py:16
  46.6 0.2 maximum_multiply_fusion
  46.8 0.2 fusion.7
  47.0 0.4 fusion.6
  47.4 0.5 pad_subtract_fusion.2
  47.9 0.2 fusion.5
  48.1 0.4 fusion.4
  48.5 0.5 pad_subtract_fusion.1
  49.0 0.2 fusion.3
  49.2 0.4 fusion.2
  49.6 0.5 pad_subtract_fusion
  50.1 0.2 fusion.1
  50.3 0.4 fusion
  50.7 1.5 %fusion.16 = f32[8,16,1792]{2,1,0:T(8,128)} fusion(f32[8,16,1792]{2,1,0:T(8,128)S(1)} %copy-done, f32[8,24,1791]{2,1,0:T(8,128)S(1)} %fusion, f32[8,23,1792]{2,1,0:T(8,128)S(1)} %fusion.1, f32[8,24,1792]{2,1,0:T(8,128)S(1)} %pad_subtract_fusion), kind=kLoop, calls=%fused_computation.42 | loop fusion | flops 1146880 | bytes 5446912 | tf_op jit(solution)/shard_map/add | solution.py:79
  (17 shorter events, 0.2 us)
Async XLA Ops:
  1.9 9.7 %copy-start.1 = (bf16[8,4,16,1792]{3,2,1,0:T(8,128)(2,1)S(1)}, bf16[8,4,16,1792]{3,2,1,0:T(8,128)(2,1)}, u32[]{:S(2)}) copy-start(bf16[8,4,16,1792]{3,2,1,0:T(8,128)(2,1)} %param.8) | copy-start | bytes 5505028
  1.9 9.7 %copy-start.2 = (f32[4,16,1792]{2,1,0:T(8,128)S(1)}, f32[4,16,1792]{2,1,0:T(8,128)}, u32[]{:S(2)}) copy-start(f32[4,16,1792]{2,1,0:T(8,128)} %param.9) | copy-start | bytes 1376260
  4.1 8.5 %collective-permute-start.2 = (f32[40,1792]{1,0:T(8,128)}, f32[40,1792]{1,0:T(8,128)}, u32[]{:S(2)}, u32[]{:S(2)}) collective-permute-start(f32[40,1792]{1,0:T(8,128)} %pad_maximum_fusion.2), channel_id=1, source_target_pairs={{0,1},{1,2},{2,3},{3,4},{4,5},{5,6},{6,7},{8,9},{9,10},{10,11},{11... | collective-permute-start | bytes 860168 | tf_op jit(solution)/shard_map/ppermute | solution.py:15
  9.6 9.2 %copy-start.3 = (f32[16,1792]{1,0:T(8,128)S(1)}, f32[16,1792]{1,0:T(8,128)}, u32[]{:S(2)}) copy-start(f32[16,1792]{1,0:T(8,128)} %param.13) | copy-start | bytes 344068
  9.6 8.4 %collective-permute-start.3 = (f32[40,1792]{1,0:T(8,128)}, f32[40,1792]{1,0:T(8,128)}, u32[]{:S(2)}, u32[]{:S(2)}) collective-permute-start(f32[40,1792]{1,0:T(8,128)} %pad_maximum_fusion.3), channel_id=1, source_target_pairs={{1,0},{2,1},{3,2},{4,3},{5,4},{6,5},{7,6},{9,8},{10,9},{11,10},{12... | collective-permute-start | bytes 860168 | tf_op jit(solution)/shard_map/ppermute | solution.py:16
  18.9 2.2 %copy-start = (f32[8,16,1792]{2,1,0:T(8,128)S(1)}, f32[8,16,1792]{2,1,0:T(8,128)}, u32[]{:S(2)}) copy-start(f32[8,16,1792]{2,1,0:T(8,128)} %param.7) | copy-start | bytes 2752516
  25.9 4.1 %collective-permute-start.4 = (f32[16,1792]{1,0:T(8,128)S(1)}, f32[16,1792]{1,0:T(8,128)S(1)}, u32[]{:S(2)}, u32[]{:S(2)}) collective-permute-start(f32[16,1792]{1,0:T(8,128)S(1)} %fusion.18), channel_id=1, source_target_pairs={{0,8},{8,0},{16,24},{24,16},{1,9},{9,1},{17,25},{25,17},{2,10},{10... | collective-permute-start | bytes 344072 | tf_op jit(solution)/shard_map/ppermute | solution.py:34
  30.0 6.6 %collective-permute-start.5 = (f32[16,1792]{1,0:T(8,128)S(1)}, f32[16,1792]{1,0:T(8,128)}, u32[]{:S(2)}, u32[]{:S(2)}) collective-permute-start(f32[16,1792]{1,0:T(8,128)S(1)} %add.138), channel_id=1, source_target_pairs={{0,16},{8,24},{16,0},{24,8},{1,17},{9,25},{17,1},{25,9},{2,18},{10... | collective-permute-start | bytes 344072 | tf_op jit(solution)/shard_map/ppermute | solution.py:34
  31.5 12.0 %collective-permute-start = (f32[32,1792]{1,0:T(8,128)S(1)}, f32[32,1792]{1,0:T(8,128)S(1)}, u32[]{:S(2)}, u32[]{:S(2)}) collective-permute-start(f32[32,1792]{1,0:T(8,128)S(1)} %reshape.52), channel_id=1, source_target_pairs={{0,1},{1,2},{2,3},{3,4},{4,5},{5,6},{6,7},{8,9},{9,10},{10,11},{11... | collective-permute-start | bytes 688136 | tf_op jit(solution)/shard_map/ppermute | solution.py:15
  34.7 8.8 %collective-permute-start.1 = (f32[32,1792]{1,0:T(8,128)S(1)}, f32[32,1792]{1,0:T(8,128)S(1)}, u32[]{:S(2)}, u32[]{:S(2)}) collective-permute-start(f32[32,1792]{1,0:T(8,128)S(1)} %reshape.54), channel_id=1, source_target_pairs={{1,0},{2,1},{3,2},{4,3},{5,4},{6,5},{7,6},{9,8},{10,9},{11,10},{12... | collective-permute-start | bytes 688136 | tf_op jit(solution)/shard_map/ppermute | solution.py:16
  37.7 5.9 %collective-permute-start.6 = (f32[4,1792]{1,0:T(4,128)S(1)}, f32[4,1792]{1,0:T(4,128)S(1)}, u32[]{:S(2)}, u32[]{:S(2)}) collective-permute-start(f32[4,1792]{1,0:T(4,128)S(1)} %get-tuple-element.11), channel_id=1, source_target_pairs={{0,1},{1,2},{2,3},{3,4},{4,5},{5,6},{6,7},{8,9},{9,10},{10,11},{11... | collective-permute-start | bytes 86024 | tf_op jit(solution)/shard_map/ppermute | solution.py:15
  41.3 5.2 %collective-permute-start.7 = (f32[4,1792]{1,0:T(4,128)S(1)}, f32[4,1792]{1,0:T(4,128)S(1)}, u32[]{:S(2)}, u32[]{:S(2)}) collective-permute-start(f32[4,1792]{1,0:T(4,128)S(1)} %get-tuple-element.12), channel_id=1, source_target_pairs={{1,0},{2,1},{3,2},{4,3},{5,4},{6,5},{7,6},{9,8},{10,9},{11,10},{12... | collective-permute-start | bytes 86024 | tf_op jit(solution)/shard_map/ppermute | solution.py:16

commit v4 on v3

--- a/solution.py
+++ b/solution.py
@@ -27,13 +27,19 @@
 
 def mem_sum(part):
     count = lax.axis_size("mem")
-    if count & (count - 1):
+    if count & (count - 1) or part.shape[-1] % 256:
         return lax.psum(part, "mem")
+    half = part.shape[-1] // 2
+    first, second = part[..., :half], part[..., half:]
+    strides = []
     stride = 1
     while stride < count:
-        part = part + lax.ppermute(part, "mem", [(i, i ^ stride) for i in range(count)])
+        strides.append(stride)
         stride *= 2
-    return part
+    for up, down in zip(strides, strides[::-1]):
+        first = first + lax.ppermute(first, "mem", [(i, i ^ up) for i in range(count)])
+        second = second + lax.ppermute(second, "mem", [(i, i ^ down) for i in range(count)])
+    return jnp.concatenate([first, second], -1)
 
 
 def diffuse(values, row_coef, col_coef):
@@ -68,15 +74,16 @@
         row_index < row_count * lax.axis_size("tile") - 1, row_faces, jnp.zeros_like(row_faces)
     )
     stacked = jnp.stack([row_coef, col_faces])
-    field, coef_band = exchange([controls, stacked], STEPS)
-    localized = localize(field, coef_band)[:, STEPS : STEPS + row_count]
     mix = jnp.sum(perturbations.astype(jnp.float32) * jacobian[None], axis=1)
-    (mix_band,) = exchange([mix], STEPS)
-    reflect = mem_sum(jnp.sum(mix * localized, 0))
-    weighted = radar_mask.astype(jnp.float32) * obs_weight * reflect
-    (weighted_band,) = exchange([weighted[None]], STEPS)
-    sensitivity = mix_band * weighted_band
-    return controls + localize(sensitivity, coef_band)[:, STEPS : STEPS + row_count]
+    weights = radar_mask.astype(jnp.float32) * obs_weight
+    field, coef_band = exchange([controls, stacked], 2 * STEPS)
+    mix_band, weights_band = exchange([mix, weights[None]], STEPS)
+    reach = row_count + 2 * STEPS
+    localized = localize(field, coef_band)[:, STEPS : STEPS + reach]
+    reflect = mem_sum(jnp.sum(mix_band * localized, 0))
+    sensitivity = mix_band * (weights_band[0] * reflect)
+    spread = localize(sensitivity, coef_band[:, STEPS : STEPS + reach])
+    return controls + spread[:, STEPS : STEPS + row_count]
 
 
 def solution(mesh):

time: 52.7 us -> 51.9 us (0.985)
  the two profiles are of different devices: /device:TPU:1 before, /device:TPU:8 now
where the time goes in v4:
time: 51.9 us; the launch traced here: 51.5 us
  other arithmetic  16.8 us (32%)
  starting transfers between devices  14.5 us (28%)
  waiting for transfers between devices  14.2 us (27%)
  local copies, waits for them, and re-layouts  5.48 us (11%)
    ppermute x2, waiting for transfers between devices, exchange(): above = lax.ppermute(tail, 'tile', [(i, i + 1) for i in range(count - 1)])  6.69 us
    ppermute x2, starting transfers between devices, exchange(): below = lax.ppermute(head, 'tile', [(i + 1, i) for i in range(count - 1)])  5.05 us
    ppermute x2, starting transfers between devices, exchange(): above = lax.ppermute(tail, 'tile', [(i, i + 1) for i in range(count - 1)])  4.3 us
    sub x6, other arithmetic, diffuse(): values + jnp.concatenate([col_flux, zeros_col], -1)  4.21 us
    mul x8, other arithmetic, diffuse(): col_coef[..., :, :-1] * (values[..., :, 1:] - values[..., :, :-1])  4.02 us
    ppermute x2, waiting for transfers between devices, mem_sum(): lax.ppermute(first, 'mem', [(i, i ^ up) for i in range(count)])  3.86 us
    ppermute x2, starting transfers between devices, mem_sum(): lax.ppermute(first, 'mem', [(i, i ^ up) for i in range(count)])  3.14 us
    ppermute x2, waiting for transfers between devices, mem_sum(): lax.ppermute(second, 'mem', [(i, i ^ down) for i in range(count)])  3 us
  transfers between devices with their start and end apart: 8, of which 6 were waited for; matrix products, arithmetic and copies ran while one was open for 10% of the time, Pallas kernels for 0%

profile of v4, /device:TPU:8, one launch (start us, length us, event | category | flops | bytes accessed | tf_op | source)
XLA Modules:
  0.0 51.5 jit_solution(15022692518247098289)
XLA Ops:
  0.0 0.0 copy-start.2
  0.0 1.3 %slice_bitcast_fusion.3 = (f32[64,1792]{1,0:T(8,128)S(1)}, f32[64,1792]{1,0:T(8,128)S(1)}) fusion(f32[8,16,1792]{2,1,0:T(8,128)} %param.7), kind=kLoop, calls=%fused_computation.59 | loop fusion | bytes 1835008 | tf_op jit(solution)/shard_map/reshape | solution.py:14
  1.3 0.0 copy-start.1
  1.3 0.1 select_bitcast_fusion
  1.4 0.8 %pad_maximum_fusion.3 = f32[80,1792]{1,0:T(8,128)} fusion(f32[16,1792]{1,0:T(8,128)S(1)} %get-tuple-element.10, f32[64,1792]{1,0:T(8,128)S(1)} %get-tuple-element.6), kind=kLoop, calls=%fused_computation.54 | loop fusion | flops 143360 | bytes 1146880 | tf_op jit(solution)/shard_map/concatenate | solution.py:13
  2.3 1.9 %collective-permute-start.3 = (f32[80,1792]{1,0:T(8,128)}, f32[80,1792]{1,0:T(8,128)S(1)}, u32[]{:S(2)}, u32[]{:S(2)}) collective-permute-start(f32[80,1792]{1,0:T(8,128)} %pad_maximum_fusion.3), channel_id=1, source_target_pairs={{1,0},{2,1},{3,2},{4,3},{5,4},{6,5},{7,6},{9,8},{10,9},{11,10},{12... | collective-permute-start | bytes 1720328 | tf_op jit(solution)/shard_map/ppermute | solution.py:16
  4.2 0.4 multiply_reduce_fusion
  4.6 0.0 copy-start.6
  4.6 0.0 copy-start.7
  4.6 0.1 fusion.23
  4.7 0.1 reshape.84
  4.8 0.7 %copy-done.6 = f32[16,1792]{1,0:T(8,128)S(1)} copy-done((f32[16,1792]{1,0:T(8,128)S(1)}, f32[16,1792]{1,0:T(8,128)}, u32[]{:S(2)}) %copy-start.6) | copy-done | bytes 114712
  5.5 0.1 copy-done.7
  5.6 0.7 %pad_maximum_fusion.5 = f32[36,1792]{1,0:T(8,128)} fusion(f32[4,1792]{1,0:T(4,128)S(1)} %get-tuple-element.15, f32[32,1792]{1,0:T(8,128)S(1)} %reshape.84), kind=kLoop, calls=%fused_computation.60 | loop fusion | flops 64512 | bytes 516096 | tf_op jit(solution)/shard_map/concatenate | solution.py:14
  6.4 2.4 %collective-permute-start = (f32[36,1792]{1,0:T(8,128)}, f32[36,1792]{1,0:T(8,128)}, u32[]{:S(2)}, u32[]{:S(2)}) collective-permute-start(f32[36,1792]{1,0:T(8,128)} %pad_maximum_fusion.5), channel_id=1, source_target_pairs={{0,1},{1,2},{2,3},{3,4},{4,5},{5,6},{6,7},{8,9},{9,10},{10,11},{11... | collective-permute-start | bytes 774152 | tf_op jit(solution)/shard_map/ppermute | solution.py:15
  8.8 0.1 reshape.87
  8.8 0.7 %pad_maximum_fusion.6 = f32[36,1792]{1,0:T(8,128)} fusion(f32[4,1792]{1,0:T(4,128)S(1)} %get-tuple-element.16, f32[32,1792]{1,0:T(8,128)S(1)} %reshape.87), kind=kLoop, calls=%fused_computation.61 | loop fusion | flops 64512 | bytes 516096 | tf_op jit(solution)/shard_map/concatenate | solution.py:13
  9.6 3.1 %collective-permute-start.1 = (f32[36,1792]{1,0:T(8,128)}, f32[36,1792]{1,0:T(8,128)S(1)}, u32[]{:S(2)}, u32[]{:S(2)}) collective-permute-start(f32[36,1792]{1,0:T(8,128)} %pad_maximum_fusion.6), channel_id=1, source_target_pairs={{1,0},{2,1},{3,2},{4,3},{5,4},{6,5},{7,6},{9,8},{10,9},{11,10},{12... | collective-permute-start | bytes 774152 | tf_op jit(solution)/shard_map/ppermute | solution.py:16
  12.7 0.9 %pad_maximum_fusion.2 = f32[80,1792]{1,0:T(8,128)} fusion(f32[16,1792]{1,0:T(8,128)S(1)} %get-tuple-element.9, f32[64,1792]{1,0:T(8,128)S(1)} %get-tuple-element.5), kind=kLoop, calls=%fused_computation.53 | loop fusion | flops 143360 | bytes 1146880 | tf_op jit(solution)/shard_map/concatenate | solution.py:14
  13.6 1.9 %collective-permute-start.2 = (f32[80,1792]{1,0:T(8,128)}, f32[80,1792]{1,0:T(8,128)S(1)}, u32[]{:S(2)}, u32[]{:S(2)}) collective-permute-start(f32[80,1792]{1,0:T(8,128)} %pad_maximum_fusion.2), channel_id=1, source_target_pairs={{0,1},{1,2},{2,3},{3,4},{4,5},{5,6},{6,7},{8,9},{9,10},{10,11},{11... | collective-permute-start | bytes 1720328 | tf_op jit(solution)/shard_map/ppermute | solution.py:15
  15.5 0.0 collective-permute-done
  15.5 1.0 %slice.267 = f32[32,1792]{1,0:T(8,128)S(1)} slice(f32[36,1792]{1,0:T(8,128)} %collective-permute-done), slice={[0:32], [0:1792]} | slice | bytes 458752 | tf_op jit(solution)/shard_map/slice | solution.py:21
  16.5 0.1 reshape.86
  16.6 0.6 %collective-permute-done.1 = f32[36,1792]{1,0:T(8,128)S(1)} collective-permute-done((f32[36,1792]{1,0:T(8,128)}, f32[36,1792]{1,0:T(8,128)S(1)}, u32[]{:S(2)}, u32[]{:S(2)}) %collective-permute-start.1) | collective-permute-done | bytes 258080 | tf_op jit(solution)/shard_map/ppermute | solution.py:16
  17.2 0.1 reshape.89
  17.3 0.8 %slice.271 = f32[4,1792]{1,0:T(4,128)S(1)} slice(f32[36,1792]{1,0:T(8,128)} %collective-permute-done), slice={[32:36], [0:1792]} | slice | bytes 57344 | tf_op jit(solution)/shard_map/slice | solution.py:21
  18.1 6.7 %collective-permute-done.2 = f32[80,1792]{1,0:T(8,128)S(1)} collective-permute-done((f32[80,1792]{1,0:T(8,128)}, f32[80,1792]{1,0:T(8,128)S(1)}, u32[]{:S(2)}, u32[]{:S(2)}) %collective-permute-start.2) | collective-permute-done | bytes 573472 | tf_op jit(solution)/shard_map/ppermute | solution.py:15
  24.9 0.0 copy-start
  25.0 1.0 %copy-done = f32[8,16,1792]{2,1,0:T(8,128)S(1)} copy-done((f32[8,16,1792]{2,1,0:T(8,128)S(1)}, f32[8,16,1792]{2,1,0:T(8,128)}, u32[]{:S(2)}) %copy-start) | copy-done | bytes 917528
  26.1 0.1 pad_maximum_fusion
  26.2 0.2 fusion.7
  26.5 0.6 %fusion.6 = f32[8,32,1791]{2,1,0:T(8,128)S(1)} fusion(f32[8,32,1792]{2,1,0:T(8,128)S(1)} %pad_maximum_fusion, f32[32,1791]{1,0:T(8,128)S(1)} %bitcast.34), kind=kLoop, calls=%fused_computation.14 | loop fusion | flops 916992 | bytes 5731200 | tf_op jit(solution)/shard_map/mul | solution.py:47
  27.0 0.9 %pad_subtract_fusion.2 = f32[8,32,1792]{2,1,0:T(8,128)S(1)} fusion(f32[8,32,1791]{2,1,0:T(8,128)S(1)} %fusion.6, f32[8,31,1792]{2,1,0:T(8,128)S(1)} %fusion.7, f32[8,8,1792]{2,1,0:T(8,128)S(1)} %slice_bitcast_fusion, f32[8,16,1792]{2,1,0:T(8,128)S(1)} %copy-done, f32[8,8,1792]{2,1,0:T(8,128)S(1)} %slice_bitcast_fusion.1), kind=kLoop, calls=%fused_computation.20 | loop fusion | flops 2752512 | bytes 7281664 | tf_op jit(solution)/shard_map/sub | solution.py:56
  27.9 0.2 fusion.5
  28.2 0.6 %fusion.4 = f32[8,32,1791]{2,1,0:T(8,128)S(1)} fusion(f32[8,32,1792]{2,1,0:T(8,128)S(1)} %pad_subtract_fusion.2, f32[32,1791]{1,0:T(8,128)S(1)} %bitcast.35), kind=kLoop, calls=%fused_computation.10 | loop fusion | flops 916992 | bytes 5731200 | tf_op jit(solution)/shard_map/mul | solution.py:47
  28.8 0.9 %pad_subtract_fusion.1 = f32[8,32,1792]{2,1,0:T(8,128)S(1)} fusion(f32[8,32,1791]{2,1,0:T(8,128)S(1)} %fusion.4, f32[8,31,1792]{2,1,0:T(8,128)S(1)} %fusion.5, f32[8,32,1792]{2,1,0:T(8,128)S(1)} %pad_subtract_fusion.2), kind=kLoop, calls=%fused_computation.19 | loop fusion | flops 1835008 | bytes 7281664 | tf_op jit(solution)/shard_map/sub | solution.py:56
  29.7 0.2 fusion.3
  30.0 0.6 %fusion.2 = f32[8,32,1791]{2,1,0:T(8,128)S(1)} fusion(f32[8,32,1792]{2,1,0:T(8,128)S(1)} %pad_subtract_fusion.1, f32[32,1791]{1,0:T(8,128)S(1)} %bitcast.36), kind=kLoop, calls=%fused_computation.6 | loop fusion | flops 916992 | bytes 5731200 | tf_op jit(solution)/shard_map/mul | solution.py:47
  30.6 0.9 %pad_subtract_fusion = f32[8,32,1792]{2,1,0:T(8,128)S(1)} fusion(f32[8,32,1791]{2,1,0:T(8,128)S(1)} %fusion.2, f32[8,31,1792]{2,1,0:T(8,128)S(1)} %fusion.3, f32[8,32,1792]{2,1,0:T(8,128)S(1)} %pad_subtract_fusion.1), kind=kLoop, calls=%fused_computation.18 | loop fusion | flops 1835008 | bytes 7281664 | tf_op jit(solution)/shard_map/sub | solution.py:56
  31.5 0.2 fusion.1
  31.8 0.6 %fusion = f32[8,32,1791]{2,1,0:T(8,128)S(1)} fusion(f32[8,32,1792]{2,1,0:T(8,128)S(1)} %pad_subtract_fusion, f32[32,1791]{1,0:T(8,128)S(1)} %bitcast.37), kind=kLoop, calls=%fused_computation.2 | loop fusion | flops 916992 | bytes 5731200 | tf_op jit(solution)/shard_map/mul | solution.py:47
  32.3 1.2 %fusion.17 = f32[24,1792]{1,0:T(8,128)S(1)} fusion(f32[8,32,1791]{2,1,0:T(8,128)S(1)} %fusion, f32[8,31,1792]{2,1,0:T(8,128)S(1)} %fusion.1, f32[8,32,1792]{2,1,0:T(8,128)S(1)} %pad_subtract_fusion, f32[8,4,1792]{2,1,0:T(4,128)S(1)} %reshape.89, f32[8,16,1792]{2,1,0:T(8,128)S(1)} %multiply_reduce_fusion, f32[8,4,1792]{2,1,0:T(4,128)S(1)} %reshape.86), kind=kLoop, calls=%fused_computation.39 | loop fusion | flops 2709504 | bytes 6536192 | tf_op jit(solution)/shard_map/reduce_sum | solution.py:83
  33.6 0.0 slice-start
  33.6 1.6 %collective-permute-start.4 = (f32[24,896]{1,0:T(8,128)S(1)}, f32[24,896]{1,0:T(8,128)S(1)}, u32[]{:S(2)}, u32[]{:S(2)}) collective-permute-start(f32[24,896]{1,0:T(8,128)S(1)} %get-tuple-element.13), channel_id=1, source_target_pairs={{0,8},{8,0},{16,24},{24,16},{1,9},{9,1},{17,25},{25,17},{2,10},{10... | collective-permute-start | bytes 258056 | tf_op jit(solution)/shard_map/ppermute | solution.py:40
  35.2 1.5 %collective-permute-start.6 = (f32[24,896]{1,0:T(8,128)S(1)}, f32[24,896]{1,0:T(8,128)S(1)}, u32[]{:S(2)}, u32[]{:S(2)}) collective-permute-start(f32[24,896]{1,0:T(8,128)S(1)} %get-tuple-element.14), channel_id=1, source_target_pairs={{0,16},{8,24},{16,0},{24,8},{1,17},{9,25},{17,1},{25,9},{2,18},{10... | collective-permute-start | bytes 258056 | tf_op jit(solution)/shard_map/ppermute | solution.py:41
  36.7 1.5 %collective-permute-done.4 = f32[24,896]{1,0:T(8,128)S(1)} collective-permute-done((f32[24,896]{1,0:T(8,128)S(1)}, f32[24,896]{1,0:T(8,128)S(1)}, u32[]{:S(2)}, u32[]{:S(2)}) %collective-permute-start.4) | collective-permute-done | bytes 86048 | tf_op jit(solution)/shard_map/ppermute | solution.py:40
  38.1 1.5 %collective-permute-done.6 = f32[24,896]{1,0:T(8,128)S(1)} collective-permute-done((f32[24,896]{1,0:T(8,128)S(1)}, f32[24,896]{1,0:T(8,128)S(1)}, u32[]{:S(2)}, u32[]{:S(2)}) %collective-permute-start.6) | collective-permute-done | bytes 86048 | tf_op jit(solution)/shard_map/ppermute | solution.py:41
  39.7 1.6 %collective-permute-start.5 = (f32[24,896]{1,0:T(8,128)S(1)}, f32[24,896]{1,0:T(8,128)S(1)}, u32[]{:S(2)}, u32[]{:S(2)}) collective-permute-start(f32[24,896]{1,0:T(8,128)S(1)} %get-tuple-element.11), channel_id=1, source_target_pairs={{0,16},{8,24},{16,0},{24,8},{1,17},{9,25},{17,1},{25,9},{2,18},{10... | collective-permute-start | bytes 258056 | tf_op jit(solution)/shard_map/ppermute | solution.py:40
  41.2 0.5 %collective-permute-start.7 = (f32[24,896]{1,0:T(8,128)S(1)}, f32[24,896]{1,0:T(8,128)S(1)}, u32[]{:S(2)}, u32[]{:S(2)}) collective-permute-start(f32[24,896]{1,0:T(8,128)S(1)} %get-tuple-element.12), channel_id=1, source_target_pairs={{0,8},{8,0},{16,24},{24,16},{1,9},{9,1},{17,25},{25,17},{2,10},{10... | collective-permute-start | bytes 258056 | tf_op jit(solution)/shard_map/ppermute | solution.py:41
  41.8 2.4 %collective-permute-done.5 = f32[24,896]{1,0:T(8,128)S(1)} collective-permute-done((f32[24,896]{1,0:T(8,128)S(1)}, f32[24,896]{1,0:T(8,128)S(1)}, u32[]{:S(2)}, u32[]{:S(2)}) %collective-permute-start.5) | collective-permute-done | bytes 86048 | tf_op jit(solution)/shard_map/ppermute | solution.py:40
  44.2 1.5 %collective-permute-done.7 = f32[24,896]{1,0:T(8,128)S(1)} collective-permute-done((f32[24,896]{1,0:T(8,128)S(1)}, f32[24,896]{1,0:T(8,128)S(1)}, u32[]{:S(2)}, u32[]{:S(2)}) %collective-permute-start.7) | collective-permute-done | bytes 86048 | tf_op jit(solution)/shard_map/ppermute | solution.py:41
  45.8 0.2 fusion.18
  46.0 0.2 fusion.15
  46.2 0.4 fusion.14
  46.7 0.5 pad_subtract_fusion.7
  47.1 0.2 fusion.13
  47.3 0.4 fusion.12
  47.8 0.5 pad_subtract_fusion.6
  48.2 0.2 fusion.11
  48.4 0.4 fusion.10
  48.9 0.5 pad_subtract_fusion.5
  49.4 0.2 fusion.9
  49.5 0.4 fusion.8
  50.0 1.5 %fusion.19 = f32[8,16,1792]{2,1,0:T(8,128)} fusion(f32[8,16,1792]{2,1,0:T(8,128)S(1)} %copy-done, f32[8,24,1791]{2,1,0:T(8,128)S(1)} %fusion.8, f32[8,23,1792]{2,1,0:T(8,128)S(1)} %fusion.9, f32[8,24,1792]{2,1,0:T(8,128)S(1)} %pad_subtract_fusion.5), kind=kLoop, calls=%fused_computation.49 | loop fusion | flops 1146880 | bytes 5446912 | tf_op jit(solution)/shard_map/add | solution.py:86
  (29 shorter events, 0.4 us)
Async XLA Ops:
  0.0 1.3 %copy-start.5 = (f32[16,1792]{1,0:T(8,128)S(1)}, f32[16,1792]{1,0:T(8,128)}, u32[]{:S(2)}) copy-start(f32[16,1792]{1,0:T(8,128)} %param.12) | copy-start | bytes 344068
  0.0 1.4 %copy-start.3 = (f32[16,1792]{1,0:T(8,128)S(1)}, f32[16,1792]{1,0:T(8,128)}, u32[]{:S(2)}) copy-start(f32[16,1792]{1,0:T(8,128)} %param.13) | copy-start | bytes 344068
  0.0 4.2 %copy-start.2 = (f32[4,16,1792]{2,1,0:T(8,128)S(1)}, f32[4,16,1792]{2,1,0:T(8,128)}, u32[]{:S(2)}) copy-start(f32[4,16,1792]{2,1,0:T(8,128)} %param.9) | copy-start | bytes 1376260
  1.3 2.9 %copy-start.1 = (bf16[8,4,16,1792]{3,2,1,0:T(8,128)(2,1)S(1)}, bf16[8,4,16,1792]{3,2,1,0:T(8,128)(2,1)}, u32[]{:S(2)}) copy-start(bf16[8,4,16,1792]{3,2,1,0:T(8,128)(2,1)} %param.8) | copy-start | bytes 5505028
  2.3 15.8 %collective-permute-start.3 = (f32[80,1792]{1,0:T(8,128)}, f32[80,1792]{1,0:T(8,128)S(1)}, u32[]{:S(2)}, u32[]{:S(2)}) collective-permute-start(f32[80,1792]{1,0:T(8,128)} %pad_maximum_fusion.3), channel_id=1, source_target_pairs={{1,0},{2,1},{3,2},{4,3},{5,4},{6,5},{7,6},{9,8},{10,9},{11,10},{12... | collective-permute-start | bytes 1720328 | tf_op jit(solution)/shard_map/ppermute | solution.py:16
  4.6 0.9 %copy-start.6 = (f32[16,1792]{1,0:T(8,128)S(1)}, f32[16,1792]{1,0:T(8,128)}, u32[]{:S(2)}) copy-start(f32[16,1792]{1,0:T(8,128)} %param.10) | copy-start | bytes 344068
  4.6 0.9 %copy-start.7 = (s32[16,1792]{1,0:T(8,128)S(1)}, s32[16,1792]{1,0:T(8,128)}, u32[]{:S(2)}) copy-start(s32[16,1792]{1,0:T(8,128)} %param.11) | copy-start | bytes 344068
  6.4 9.2 %collective-permute-start = (f32[36,1792]{1,0:T(8,128)}, f32[36,1792]{1,0:T(8,128)}, u32[]{:S(2)}, u32[]{:S(2)}) collective-permute-start(f32[36,1792]{1,0:T(8,128)} %pad_maximum_fusion.5), channel_id=1, source_target_pairs={{0,1},{1,2},{2,3},{3,4},{4,5},{5,6},{6,7},{8,9},{9,10},{10,11},{11... | collective-permute-start | bytes 774152 | tf_op jit(solution)/shard_map/ppermute | solution.py:15
  9.6 7.6 %collective-permute-start.1 = (f32[36,1792]{1,0:T(8,128)}, f32[36,1792]{1,0:T(8,128)S(1)}, u32[]{:S(2)}, u32[]{:S(2)}) collective-permute-start(f32[36,1792]{1,0:T(8,128)} %pad_maximum_fusion.6), channel_id=1, source_target_pairs={{1,0},{2,1},{3,2},{4,3},{5,4},{6,5},{7,6},{9,8},{10,9},{11,10},{12... | collective-permute-start | bytes 774152 | tf_op jit(solution)/shard_map/ppermute | solution.py:16
  13.6 11.2 %collective-permute-start.2 = (f32[80,1792]{1,0:T(8,128)}, f32[80,1792]{1,0:T(8,128)S(1)}, u32[]{:S(2)}, u32[]{:S(2)}) collective-permute-start(f32[80,1792]{1,0:T(8,128)} %pad_maximum_fusion.2), channel_id=1, source_target_pairs={{0,1},{1,2},{2,3},{3,4},{4,5},{5,6},{6,7},{8,9},{9,10},{10,11},{11... | collective-permute-start | bytes 1720328 | tf_op jit(solution)/shard_map/ppermute | solution.py:15
  17.2 7.7 %copy-start.4 = (f32[36,1792]{1,0:T(8,128)}, f32[36,1792]{1,0:T(8,128)S(1)}, u32[]{:S(2)}) copy-start(f32[36,1792]{1,0:T(8,128)S(1)} %collective-permute-done.1) | copy-start | bytes 774148
  24.9 1.2 %copy-start = (f32[8,16,1792]{2,1,0:T(8,128)S(1)}, f32[8,16,1792]{2,1,0:T(8,128)}, u32[]{:S(2)}) copy-start(f32[8,16,1792]{2,1,0:T(8,128)} %param.7) | copy-start | bytes 2752516
  33.6 12.2 %slice-start = ((f32[36,1792]{1,0:T(8,128)}), f32[4,1792]{1,0:T(4,128)S(1)}, s32[]{:S(2)}) async-start(f32[36,1792]{1,0:T(8,128)} %copy-done.4), calls=%async_computation | async-start | bytes 57344 | tf_op jit(solution)/shard_map/slice | solution.py:22
  33.6 4.6 %collective-permute-start.4 = (f32[24,896]{1,0:T(8,128)S(1)}, f32[24,896]{1,0:T(8,128)S(1)}, u32[]{:S(2)}, u32[]{:S(2)}) collective-permute-start(f32[24,896]{1,0:T(8,128)S(1)} %get-tuple-element.13), channel_id=1, source_target_pairs={{0,8},{8,0},{16,24},{24,16},{1,9},{9,1},{17,25},{25,17},{2,10},{10... | collective-permute-start | bytes 258056 | tf_op jit(solution)/shard_map/ppermute | solution.py:40
  35.2 4.5 %collective-permute-start.6 = (f32[24,896]{1,0:T(8,128)S(1)}, f32[24,896]{1,0:T(8,128)S(1)}, u32[]{:S(2)}, u32[]{:S(2)}) collective-permute-start(f32[24,896]{1,0:T(8,128)S(1)} %get-tuple-element.14), channel_id=1, source_target_pairs={{0,16},{8,24},{16,0},{24,8},{1,17},{9,25},{17,1},{25,9},{2,18},{10... | collective-permute-start | bytes 258056 | tf_op jit(solution)/shard_map/ppermute | solution.py:41
  39.7 4.6 %collective-permute-start.5 = (f32[24,896]{1,0:T(8,128)S(1)}, f32[24,896]{1,0:T(8,128)S(1)}, u32[]{:S(2)}, u32[]{:S(2)}) collective-permute-start(f32[24,896]{1,0:T(8,128)S(1)} %get-tuple-element.11), channel_id=1, source_target_pairs={{0,16},{8,24},{16,0},{24,8},{1,17},{9,25},{17,1},{25,9},{2,18},{10... | collective-permute-start | bytes 258056 | tf_op jit(solution)/shard_map/ppermute | solution.py:40
  41.2 4.5 %collective-permute-start.7 = (f32[24,896]{1,0:T(8,128)S(1)}, f32[24,896]{1,0:T(8,128)S(1)}, u32[]{:S(2)}, u32[]{:S(2)}) collective-permute-start(f32[24,896]{1,0:T(8,128)S(1)} %get-tuple-element.12), channel_id=1, source_target_pairs={{0,8},{8,0},{16,24},{24,16},{1,9},{9,1},{17,25},{25,17},{2,10},{10... | collective-permute-start | bytes 258056 | tf_op jit(solution)/shard_map/ppermute | solution.py:41

commit v5 on v4

--- a/solution.py
+++ b/solution.py
@@ -6,18 +6,18 @@
 STEPS = 4
 
 
-def exchange(parts, width):
+def exchange(parts):
     count = lax.axis_size("tile")
-    cols = parts[0].shape[-1]
-    sizes = [part[..., :width, :].size // cols for part in parts]
-    head = jnp.concatenate([part[..., :width, :].reshape(-1, cols) for part in parts], 0)
-    tail = jnp.concatenate([part[..., -width:, :].reshape(-1, cols) for part in parts], 0)
+    cols = parts[0][0].shape[-1]
+    head = jnp.concatenate([part[..., :width, :].reshape(-1, cols) for part, width in parts], 0)
+    tail = jnp.concatenate([part[..., -width:, :].reshape(-1, cols) for part, width in parts], 0)
     above = lax.ppermute(tail, "tile", [(i, i + 1) for i in range(count - 1)])
     below = lax.ppermute(head, "tile", [(i + 1, i) for i in range(count - 1)])
     bands = []
     start = 0
-    for part, size in zip(parts, sizes):
+    for part, width in parts:
         shape = part.shape[:-2] + (width, cols)
+        size = part[..., :width, :].size // cols
         top = above[start : start + size].reshape(shape)
         bottom = below[start : start + size].reshape(shape)
         bands.append(jnp.concatenate([top, part, bottom], -2))
@@ -27,19 +27,13 @@
 
 def mem_sum(part):
     count = lax.axis_size("mem")
-    if count & (count - 1) or part.shape[-1] % 256:
+    if count & (count - 1):
         return lax.psum(part, "mem")
-    half = part.shape[-1] // 2
-    first, second = part[..., :half], part[..., half:]
-    strides = []
     stride = 1
     while stride < count:
-        strides.append(stride)
+        part = part + lax.ppermute(part, "mem", [(i, i ^ stride) for i in range(count)])
         stride *= 2
-    for up, down in zip(strides, strides[::-1]):
-        first = first + lax.ppermute(first, "mem", [(i, i ^ up) for i in range(count)])
-        second = second + lax.ppermute(second, "mem", [(i, i ^ down) for i in range(count)])
-    return jnp.concatenate([first, second], -1)
+    return part
 
 
 def diffuse(values, row_coef, col_coef):
@@ -76,8 +70,9 @@
     stacked = jnp.stack([row_coef, col_faces])
     mix = jnp.sum(perturbations.astype(jnp.float32) * jacobian[None], axis=1)
     weights = radar_mask.astype(jnp.float32) * obs_weight
-    field, coef_band = exchange([controls, stacked], 2 * STEPS)
-    mix_band, weights_band = exchange([mix, weights[None]], STEPS)
+    field, coef_band, mix_band, weights_band = exchange(
+        [(controls, 2 * STEPS), (stacked, 2 * STEPS), (mix, STEPS), (weights[None], STEPS)]
+    )
     reach = row_count + 2 * STEPS
     localized = localize(field, coef_band)[:, STEPS : STEPS + reach]
     reflect = mem_sum(jnp.sum(mix_band * localized, 0))

time: 51.9 us -> 58 us (1.12)
  starting transfers between devices: 14.5 us -> 7.46 us
  other arithmetic: 16.8 us -> 23.2 us
  waiting for transfers between devices: 14.2 us -> 18.7 us
  local copies, waits for them, and re-layouts: 5.48 us -> 7.87 us
    ppermute x2 -> x1, waiting for transfers between devices: 0.63 us -> 8.02 us  [exchange(): below = lax.ppermute(head, 'tile', [(i + 1, i) for i in range(count - 1)])]
    reduce_sum x1, other arithmetic: 1.22 us -> 4.54 us  [per_device(): reflect = mem_sum(jnp.sum(mix_band * localized, 0))]
    ppermute x2 -> x1, starting transfers between devices: 5.05 us -> 1.91 us  [exchange(): below = lax.ppermute(head, 'tile', [(i + 1, i) for i in range(count - 1)])]
    ppermute x2 -> x1, waiting for transfers between devices: 6.69 us -> 3.65 us  [exchange(): above = lax.ppermute(tail, 'tile', [(i, i + 1) for i in range(count - 1)])]
    concatenate x4 -> x2, other arithmetic: 3.18 us -> 1.04 us  [the longest x1 0.96 us: exchange(): jnp.concatenate([part[..., :width, :].reshape(-1, cols) for part, width i...]
    ppermute x4 -> x2, starting transfers between devices: 5.2 us -> 3.14 us  [mem_sum(): lax.ppermute(part, 'mem', [(i, i ^ stride) for i in range(count)])]
    unnamed x16 -> x22, local copies, waits for them, and re-layouts: 1.82 us -> 3.86 us
    ppermute x2 -> x1, starting transfers between devices: 4.3 us -> 2.41 us  [exchange(): above = lax.ppermute(tail, 'tile', [(i, i + 1) for i in range(count - 1)])]
  transfers between devices with their start and end apart: 8 -> 4, of which waited for: 6 -> 4; matrix products, arithmetic and copies ran while one was open for 10% -> 2% of each run, Pallas kernels for 0% -> 0%
where the time goes in v5:
time: 58 us; the launch traced here: 57.6 us
  other arithmetic  23.2 us (40%)
  waiting for transfers between devices  18.7 us (32%)
  local copies, waits for them, and re-layouts  7.87 us (14%)
  starting transfers between devices  7.46 us (13%)
    ppermute x1, waiting for transfers between devices, exchange(): below = lax.ppermute(head, 'tile', [(i + 1, i) for i in range(count - 1)])  8.02 us
    ppermute x2, waiting for transfers between devices, mem_sum(): lax.ppermute(part, 'mem', [(i, i ^ stride) for i in range(count)])  7.06 us
    mul x8, other arithmetic, diffuse(): col_coef[..., :, :-1] * (values[..., :, 1:] - values[..., :, :-1])  5.25 us
    reduce_sum x1, other arithmetic, per_device(): reflect = mem_sum(jnp.sum(mix_band * localized, 0))  4.54 us
    sub x6, other arithmetic, diffuse(): values + jnp.concatenate([col_flux, zeros_col], -1)  4.27 us
    unnamed x22, local copies, waits for them, and re-layouts  3.86 us
    ppermute x1, waiting for transfers between devices, exchange(): above = lax.ppermute(tail, 'tile', [(i, i + 1) for i in range(count - 1)])  3.65 us
    ppermute x2, starting transfers between devices, mem_sum(): lax.ppermute(part, 'mem', [(i, i ^ stride) for i in range(count)])  3.14 us
  transfers between devices with their start and end apart: 4, of which 4 were waited for; matrix products, arithmetic and copies ran while one was open for 2% of the time, Pallas kernels for 0%

profile of v5, /device:TPU:8, one launch (start us, length us, event | category | flops | bytes accessed | tf_op | source)
XLA Modules:
  0.0 57.6 jit_solution(18360787017166970213)
XLA Ops:
  0.0 1.0 %multiply_bitcast_fusion = f32[1,16,1792]{2,1,0:T(8,128)S(1)} fusion(f32[16,1792]{1,0:T(8,128)} %param.10, s32[16,1792]{1,0:T(8,128)} %param.11), kind=kLoop, calls=%fused_computation.74 | loop fusion | flops 57344 | bytes 344064 | tf_op jit(solution)/shard_map/broadcast_in_dim | solution.py:74
  1.0 0.0 copy-start.7
  1.0 0.6 %copy-done.7 = f32[1,16,1792]{2,1,0:T(8,128)} copy-done((f32[1,16,1792]{2,1,0:T(8,128)}, f32[1,16,1792]{2,1,0:T(8,128)S(1)}, u32[]{:S(2)}) %copy-start.7) | copy-done | bytes 114712
  1.6 2.1 %multiply_reduce_fusion = f32[8,16,1792]{2,1,0:T(8,128)S(1)} fusion(bf16[8,4,16,1792]{3,2,1,0:T(8,128)(2,1)} %param.8, f32[4,16,1792]{2,1,0:T(8,128)} %param.9), kind=kLoop, calls=%fused_computation | loop fusion | flops 2523136 | bytes 3211264 | tf_op jit(solution)/shard_map/reduce_sum | solution.py:71
  3.7 0.0 copy-start.1
  3.7 0.9 %copy-done.1 = f32[8,16,1792]{2,1,0:T(8,128)} copy-done((f32[8,16,1792]{2,1,0:T(8,128)}, f32[8,16,1792]{2,1,0:T(8,128)S(1)}, u32[]{:S(2)}) %copy-start.1) | copy-done | bytes 917528
  4.6 0.1 fusion.24
  4.7 0.0 copy-start.10
  4.7 0.0 copy-start.9
  4.7 0.1 reshape.63
  4.8 1.0 %copy-done = f32[8,16,1792]{2,1,0:T(8,128)S(1)} copy-done((f32[8,16,1792]{2,1,0:T(8,128)S(1)}, f32[8,16,1792]{2,1,0:T(8,128)}, u32[]{:S(2)}) %copy-start) | copy-done | bytes 917528
  5.8 0.1 slice_bitcast_fusion.3
  5.9 0.0 copy-done.10
  5.9 0.1 select_bitcast_fusion
  6.0 0.0 copy-done.9
  6.0 1.0 %pad_maximum_fusion.3 = f32[116,1792]{1,0:T(8,128)} fusion(f32[4,1792]{1,0:T(4,128)S(1)} %get-tuple-element.12, f32[32,1792]{1,0:T(8,128)S(1)} %reshape.63, f32[16,1792]{1,0:T(8,128)S(1)} %get-tuple-element.10, f32[64,1792]{1,0:T(8,128)S(1)} %get-tuple-element.6), kind=kLoop, calls=%fused_computation.54 | loop fusion | flops 623616 | bytes 1662976 | tf_op jit(solution)/shard_map/concatenate | solution.py:12
  7.0 1.9 %collective-permute-start.1 = (f32[116,1792]{1,0:T(8,128)}, f32[116,1792]{1,0:T(8,128)S(1)}, u32[]{:S(2)}, u32[]{:S(2)}) collective-permute-start(f32[116,1792]{1,0:T(8,128)} %pad_maximum_fusion.3), channel_id=1, source_target_pairs={{1,0},{2,1},{3,2},{4,3},{5,4},{6,5},{7,6},{9,8},{10,9},{11,10},{12... | collective-permute-start | bytes 2494472 | tf_op jit(solution)/shard_map/ppermute | solution.py:15
  8.9 0.1 reshape.58
  9.0 0.1 pad_maximum_fusion.2
  9.0 2.4 %collective-permute-start = (f32[116,1792]{1,0:T(8,128)S(1)}, f32[116,1792]{1,0:T(8,128)S(1)}, u32[]{:S(2)}, u32[]{:S(2)}) collective-permute-start(f32[116,1792]{1,0:T(8,128)S(1)} %pad_maximum_fusion.2), channel_id=1, source_target_pairs={{0,1},{1,2},{2,3},{3,4},{4,5},{5,6},{6,7},{8,9},{9,10},{10,11},{11... | collective-permute-start | bytes 2494472 | tf_op jit(solution)/shard_map/ppermute | solution.py:14
  11.5 8.0 %collective-permute-done.1 = f32[116,1792]{1,0:T(8,128)S(1)} collective-permute-done((f32[116,1792]{1,0:T(8,128)}, f32[116,1792]{1,0:T(8,128)S(1)}, u32[]{:S(2)}, u32[]{:S(2)}) %collective-permute-start.1) | collective-permute-done | bytes 831520 | tf_op jit(solution)/shard_map/ppermute | solution.py:15
  19.5 3.7 %collective-permute-done = f32[116,1792]{1,0:T(8,128)S(1)} collective-permute-done((f32[116,1792]{1,0:T(8,128)S(1)}, f32[116,1792]{1,0:T(8,128)S(1)}, u32[]{:S(2)}, u32[]{:S(2)}) %collective-permute-start) | collective-permute-done | bytes 831520 | tf_op jit(solution)/shard_map/ppermute | solution.py:14
  23.2 0.1 pad_maximum_fusion.4
  23.2 0.0 copy-done.3
  23.2 0.0 copy-start.4
  23.3 1.3 %copy-done.4 = f32[116,1792]{1,0:T(8,128)S(1)} copy-done((f32[116,1792]{1,0:T(8,128)S(1)}, f32[116,1792]{1,0:T(8,128)}, u32[]{:S(2)}) %copy-start.4) | copy-done | bytes 831512
  24.7 0.0 copy-done.6
  24.7 0.1 pad_maximum_fusion
  24.9 0.2 fusion.7
  25.1 0.6 %fusion.6 = f32[8,32,1791]{2,1,0:T(8,128)S(1)} fusion(f32[8,32,1792]{2,1,0:T(8,128)S(1)} %pad_maximum_fusion, f32[32,1791]{1,0:T(8,128)S(1)} %bitcast.43), kind=kLoop, calls=%fused_computation.14 | loop fusion | flops 916992 | bytes 5731200 | tf_op jit(solution)/shard_map/mul | solution.py:41
  25.7 0.9 %pad_subtract_fusion.2 = f32[8,32,1792]{2,1,0:T(8,128)S(1)} fusion(f32[8,32,1791]{2,1,0:T(8,128)S(1)} %fusion.6, f32[8,31,1792]{2,1,0:T(8,128)S(1)} %fusion.7, f32[8,8,1792]{2,1,0:T(8,128)S(1)} %slice_bitcast_fusion, f32[8,16,1792]{2,1,0:T(8,128)S(1)} %copy-done, f32[8,8,1792]{2,1,0:T(8,128)S(1)} %slice_bitcast_fusion.1), kind=kLoop, calls=%fused_computation.20 | loop fusion | flops 2752512 | bytes 7281664 | tf_op jit(solution)/shard_map/sub | solution.py:50
  26.6 0.2 fusion.5
  26.9 0.6 %fusion.4 = f32[8,32,1791]{2,1,0:T(8,128)S(1)} fusion(f32[8,32,1792]{2,1,0:T(8,128)S(1)} %pad_subtract_fusion.2, f32[32,1791]{1,0:T(8,128)S(1)} %bitcast.44), kind=kLoop, calls=%fused_computation.10 | loop fusion | flops 916992 | bytes 5731200 | tf_op jit(solution)/shard_map/mul | solution.py:41
  27.5 0.9 %pad_subtract_fusion.1 = f32[8,32,1792]{2,1,0:T(8,128)S(1)} fusion(f32[8,32,1791]{2,1,0:T(8,128)S(1)} %fusion.4, f32[8,31,1792]{2,1,0:T(8,128)S(1)} %fusion.5, f32[8,32,1792]{2,1,0:T(8,128)S(1)} %pad_subtract_fusion.2), kind=kLoop, calls=%fused_computation.19 | loop fusion | flops 1835008 | bytes 7281664 | tf_op jit(solution)/shard_map/sub | solution.py:50
  28.4 0.2 fusion.3
  28.7 0.6 %fusion.2 = f32[8,32,1791]{2,1,0:T(8,128)S(1)} fusion(f32[8,32,1792]{2,1,0:T(8,128)S(1)} %pad_subtract_fusion.1, f32[32,1791]{1,0:T(8,128)S(1)} %bitcast.45), kind=kLoop, calls=%fused_computation.6 | loop fusion | flops 916992 | bytes 5731200 | tf_op jit(solution)/shard_map/mul | solution.py:41
  29.3 0.9 %pad_subtract_fusion = f32[8,32,1792]{2,1,0:T(8,128)S(1)} fusion(f32[8,32,1791]{2,1,0:T(8,128)S(1)} %fusion.2, f32[8,31,1792]{2,1,0:T(8,128)S(1)} %fusion.3, f32[8,32,1792]{2,1,0:T(8,128)S(1)} %pad_subtract_fusion.1), kind=kLoop, calls=%fused_computation.18 | loop fusion | flops 1835008 | bytes 7281664 | tf_op jit(solution)/shard_map/sub | solution.py:50
  30.2 1.5 %fusion.1 = f32[8,31,1792]{2,1,0:T(8,128)} fusion(f32[8,32,1792]{2,1,0:T(8,128)S(1)} %pad_subtract_fusion, f32[31,1792]{1,0:T(8,128)S(1)} %slice_bitcast_fusion.5), kind=kLoop, calls=%fused_computation.4 | loop fusion | flops 888832 | bytes 5555200 | tf_op jit(solution)/shard_map/mul | solution.py:40
  31.7 1.8 %fusion = f32[8,32,1791]{2,1,0:T(8,128)} fusion(f32[8,32,1792]{2,1,0:T(8,128)S(1)} %pad_subtract_fusion, f32[32,1791]{1,0:T(8,128)S(1)} %bitcast.46), kind=kLoop, calls=%fused_computation.2 | loop fusion | flops 916992 | bytes 5731200 | tf_op jit(solution)/shard_map/mul | solution.py:41
  33.5 0.0 slice-done
  33.5 0.1 reshape.65
  33.6 1.6 %slice.261 = f32[32,1792]{1,0:T(8,128)} slice(f32[116,1792]{1,0:T(8,128)} %copy-done.6), slice={[80:112], [0:1792]} | slice | bytes 458752 | tf_op jit(solution)/shard_map/slice | solution.py:21
  35.2 1.0 %reshape.60 = f32[8,4,1792]{2,1,0:T(4,128)S(1)} reshape(f32[32,1792]{1,0:T(8,128)} %slice.261) | data formatting | bytes 458752 | tf_op jit(solution)/shard_map/reshape | solution.py:21
  36.3 0.0 copy-start.5
  36.3 4.5 %fusion.17 = f32[24,1792]{1,0:T(8,128)S(1)} fusion(f32[8,32,1791]{2,1,0:T(8,128)} %fusion, f32[8,31,1792]{2,1,0:T(8,128)} %fusion.1, f32[8,32,1792]{2,1,0:T(8,128)S(1)} %pad_subtract_fusion, f32[8,4,1792]{2,1,0:T(4,128)S(1)} %reshape.65, f32[8,16,1792]{2,1,0:T(8,128)} %copy-done.1, f32[8,4,1792]{2,1,0:T(4,128)S(1)} %reshape.60), kind=kLoop, calls=%fused_computation.39 | loop fusion | flops 2709504 | bytes 6536192 | tf_op jit(solution)/shard_map/reduce_sum | solution.py:78
  40.8 0.0 copy-start.2
  40.8 1.6 %collective-permute-start.2 = (f32[24,1792]{1,0:T(8,128)S(1)}, f32[24,1792]{1,0:T(8,128)S(1)}, u32[]{:S(2)}, u32[]{:S(2)}) collective-permute-start(f32[24,1792]{1,0:T(8,128)S(1)} %fusion.17), channel_id=1, source_target_pairs={{0,8},{8,0},{16,24},{24,16},{1,9},{9,1},{17,25},{25,17},{2,10},{10... | collective-permute-start | bytes 516104 | tf_op jit(solution)/shard_map/ppermute | solution.py:34
  42.4 4.0 %collective-permute-done.2 = f32[24,1792]{1,0:T(8,128)S(1)} collective-permute-done((f32[24,1792]{1,0:T(8,128)S(1)}, f32[24,1792]{1,0:T(8,128)S(1)}, u32[]{:S(2)}, u32[]{:S(2)}) %collective-permute-start.2) | collective-permute-done | bytes 172064 | tf_op jit(solution)/shard_map/ppermute | solution.py:34
  46.4 1.6 %collective-permute-start.3 = (f32[24,1792]{1,0:T(8,128)S(1)}, f32[24,1792]{1,0:T(8,128)S(1)}, u32[]{:S(2)}, u32[]{:S(2)}) collective-permute-start(f32[24,1792]{1,0:T(8,128)S(1)} %add.138), channel_id=1, source_target_pairs={{0,16},{8,24},{16,0},{24,8},{1,17},{9,25},{17,1},{25,9},{2,18},{10... | collective-permute-start | bytes 516104 | tf_op jit(solution)/shard_map/ppermute | solution.py:34
  48.0 0.8 %slice_bitcast_fusion.11 = f32[1,4,1792]{2,1,0:T(4,128)S(1)} fusion(f32[116,1792]{1,0:T(8,128)} %copy-done.6), kind=kLoop, calls=%fused_computation.77 | loop fusion | bytes 57344 | tf_op jit(solution)/shard_map/reshape | solution.py:21
  48.8 3.1 %collective-permute-done.3 = f32[24,1792]{1,0:T(8,128)S(1)} collective-permute-done((f32[24,1792]{1,0:T(8,128)S(1)}, f32[24,1792]{1,0:T(8,128)S(1)}, u32[]{:S(2)}, u32[]{:S(2)}) %collective-permute-start.3) | collective-permute-done | bytes 172064 | tf_op jit(solution)/shard_map/ppermute | solution.py:34
  51.9 0.2 fusion.18
  52.2 0.2 fusion.15
  52.4 0.4 fusion.14
  52.8 0.5 pad_subtract_fusion.7
  53.3 0.2 fusion.13
  53.5 0.4 fusion.12
  53.9 0.5 pad_subtract_fusion.6
  54.4 0.2 fusion.11
  54.6 0.4 fusion.10
  55.0 0.5 pad_subtract_fusion.5
  55.5 0.2 fusion.9
  55.7 0.4 fusion.8
  56.1 1.5 %fusion.19 = f32[8,16,1792]{2,1,0:T(8,128)} fusion(f32[8,16,1792]{2,1,0:T(8,128)S(1)} %copy-done, f32[8,24,1791]{2,1,0:T(8,128)S(1)} %fusion.8, f32[8,23,1792]{2,1,0:T(8,128)S(1)} %fusion.9, f32[8,24,1792]{2,1,0:T(8,128)S(1)} %pad_subtract_fusion.5), kind=kLoop, calls=%fused_computation.49 | loop fusion | flops 1146880 | bytes 5446912 | tf_op jit(solution)/shard_map/add | solution.py:81
  (22 shorter events, 0.3 us)
Async XLA Ops:
  1.0 0.7 %copy-start.7 = (f32[1,16,1792]{2,1,0:T(8,128)}, f32[1,16,1792]{2,1,0:T(8,128)S(1)}, u32[]{:S(2)}) copy-start(f32[1,16,1792]{2,1,0:T(8,128)S(1)} %multiply_bitcast_fusion) | copy-start | bytes 344068
  3.7 0.9 %copy-start.1 = (f32[8,16,1792]{2,1,0:T(8,128)}, f32[8,16,1792]{2,1,0:T(8,128)S(1)}, u32[]{:S(2)}) copy-start(f32[8,16,1792]{2,1,0:T(8,128)S(1)} %multiply_reduce_fusion) | copy-start | bytes 2752516
  4.6 1.2 %copy-start = (f32[8,16,1792]{2,1,0:T(8,128)S(1)}, f32[8,16,1792]{2,1,0:T(8,128)}, u32[]{:S(2)}) copy-start(f32[8,16,1792]{2,1,0:T(8,128)} %param.7) | copy-start | bytes 2752516
  4.7 1.2 %copy-start.10 = (f32[16,1792]{1,0:T(8,128)S(1)}, f32[16,1792]{1,0:T(8,128)}, u32[]{:S(2)}) copy-start(f32[16,1792]{1,0:T(8,128)} %param.12) | copy-start | bytes 344068
  4.7 1.2 %copy-start.9 = (f32[16,1792]{1,0:T(8,128)S(1)}, f32[16,1792]{1,0:T(8,128)}, u32[]{:S(2)}) copy-start(f32[16,1792]{1,0:T(8,128)} %param.13) | copy-start | bytes 344068
  7.0 12.5 %collective-permute-start.1 = (f32[116,1792]{1,0:T(8,128)}, f32[116,1792]{1,0:T(8,128)S(1)}, u32[]{:S(2)}, u32[]{:S(2)}) collective-permute-start(f32[116,1792]{1,0:T(8,128)} %pad_maximum_fusion.3), channel_id=1, source_target_pairs={{1,0},{2,1},{3,2},{4,3},{5,4},{6,5},{7,6},{9,8},{10,9},{11,10},{12... | collective-permute-start | bytes 2494472 | tf_op jit(solution)/shard_map/ppermute | solution.py:15
  9.0 14.1 %collective-permute-start = (f32[116,1792]{1,0:T(8,128)S(1)}, f32[116,1792]{1,0:T(8,128)S(1)}, u32[]{:S(2)}, u32[]{:S(2)}) collective-permute-start(f32[116,1792]{1,0:T(8,128)S(1)} %pad_maximum_fusion.2), channel_id=1, source_target_pairs={{0,1},{1,2},{2,3},{3,4},{4,5},{5,6},{6,7},{8,9},{9,10},{10,11},{11... | collective-permute-start | bytes 2494472 | tf_op jit(solution)/shard_map/ppermute | solution.py:14
  19.5 3.7 %copy-start.3 = (f32[116,1792]{1,0:T(8,128)}, f32[116,1792]{1,0:T(8,128)S(1)}, u32[]{:S(2)}) copy-start(f32[116,1792]{1,0:T(8,128)S(1)} %collective-permute-done.1) | copy-start | bytes 2494468
  23.1 1.5 %copy-start.6 = (f32[116,1792]{1,0:T(8,128)}, f32[116,1792]{1,0:T(8,128)S(1)}, u32[]{:S(2)}) copy-start(f32[116,1792]{1,0:T(8,128)S(1)} %collective-permute-done) | copy-start | bytes 2494468
  23.2 1.4 %copy-start.4 = (f32[116,1792]{1,0:T(8,128)S(1)}, f32[116,1792]{1,0:T(8,128)}, u32[]{:S(2)}) copy-start(f32[116,1792]{1,0:T(8,128)} %copy-done.3) | copy-start | bytes 2494468
  31.7 1.8 %slice-start = ((f32[116,1792]{1,0:T(8,128)}), f32[32,1792]{1,0:T(8,128)S(1)}, s32[]{:S(2)}) async-start(f32[116,1792]{1,0:T(8,128)} %copy-done.3), calls=%async_computation | async-start | bytes 458752 | tf_op jit(solution)/shard_map/slice | solution.py:22
  36.3 6.1 %copy-start.5 = (f32[116,1792]{1,0:T(8,128)S(1)}, f32[116,1792]{1,0:T(8,128)}, u32[]{:S(2)}) copy-start(f32[116,1792]{1,0:T(8,128)} %copy-done.3) | copy-start | bytes 2494468
  36.3 15.6 %copy-start.8 = (f32[1,16,1792]{2,1,0:T(8,128)S(1)}, f32[1,16,1792]{2,1,0:T(8,128)}, u32[]{:S(2)}) copy-start(f32[1,16,1792]{2,1,0:T(8,128)} %copy-done.7) | copy-start | bytes 344068
  40.8 11.1 %copy-start.2 = (f32[8,16,1792]{2,1,0:T(8,128)S(1)}, f32[8,16,1792]{2,1,0:T(8,128)}, u32[]{:S(2)}) copy-start(f32[8,16,1792]{2,1,0:T(8,128)} %copy-done.1) | copy-start | bytes 2752516
  40.8 5.6 %collective-permute-start.2 = (f32[24,1792]{1,0:T(8,128)S(1)}, f32[24,1792]{1,0:T(8,128)S(1)}, u32[]{:S(2)}, u32[]{:S(2)}) collective-permute-start(f32[24,1792]{1,0:T(8,128)S(1)} %fusion.17), channel_id=1, source_target_pairs={{0,8},{8,0},{16,24},{24,16},{1,9},{9,1},{17,25},{25,17},{2,10},{10... | collective-permute-start | bytes 516104 | tf_op jit(solution)/shard_map/ppermute | solution.py:34
  46.4 5.5 %collective-permute-start.3 = (f32[24,1792]{1,0:T(8,128)S(1)}, f32[24,1792]{1,0:T(8,128)S(1)}, u32[]{:S(2)}, u32[]{:S(2)}) collective-permute-start(f32[24,1792]{1,0:T(8,128)S(1)} %add.138), channel_id=1, source_target_pairs={{0,16},{8,24},{16,0},{24,8},{1,17},{9,25},{17,1},{25,9},{2,18},{10... | collective-permute-start | bytes 516104 | tf_op jit(solution)/shard_map/ppermute | solution.py:34

commit v6 on v3

--- a/solution.py
+++ b/solution.py
@@ -1,7 +1,10 @@
 import jax
 import jax.numpy as jnp
 from jax import lax
+from jax.experimental import pallas as pl
+from jax.experimental.pallas import tpu as pltpu
 from jax.sharding import PartitionSpec as P
+import functools
 
 STEPS = 4
 
@@ -36,6 +39,76 @@
     return part
 
 
+def diffuse_block(values, row_coef, col_coef):
+    rows, cols = values.shape
+    row_flux = row_coef * (pltpu.roll(values, rows - 1, 0) - values)
+    col_flux = col_coef * (pltpu.roll(values, cols - 1, 1) - values)
+    values = values + row_flux - pltpu.roll(row_flux, 1, 0)
+    return values + col_flux - pltpu.roll(col_flux, 1, 1)
+
+
+def forward_kernel(band_ref, coef_ref, mix_ref, out_ref):
+    member = pl.program_id(0)
+    values = band_ref[0]
+    for repeat in range(STEPS):
+        values = diffuse_block(values, coef_ref[0], coef_ref[1])
+    keep = out_ref.shape[0]
+    term = mix_ref[0] * pltpu.roll(values, values.shape[0] - STEPS, 0)[:keep]
+
+    @pl.when(member == 0)
+    def _():
+        out_ref[...] = term
+
+    @pl.when(member > 0)
+    def _():
+        out_ref[...] = out_ref[...] + term
+
+
+def backward_kernel(mix_ref, weighted_ref, coef_ref, controls_ref, out_ref):
+    rows = mix_ref.shape[1]
+    shift = coef_ref.shape[1] - STEPS
+    row_coef = pltpu.roll(coef_ref[0], shift, 0)[:rows]
+    col_coef = pltpu.roll(coef_ref[1], shift, 0)[:rows]
+    values = mix_ref[0] * weighted_ref[...]
+    for repeat in range(STEPS):
+        values = diffuse_block(values, row_coef, col_coef)
+    keep = out_ref.shape[1]
+    out_ref[0] = controls_ref[0] + pltpu.roll(values, rows - STEPS, 0)[:keep]
+
+
+def forward(band, coef, mix):
+    members, rows, cols = band.shape
+    keep = mix.shape[1]
+    return pl.pallas_call(
+        forward_kernel,
+        grid=(members,),
+        in_specs=[
+            pl.BlockSpec((1, rows, cols), lambda k: (k, 0, 0)),
+            pl.BlockSpec((2, rows, cols), lambda k: (0, 0, 0)),
+            pl.BlockSpec((1, keep, cols), lambda k: (k, 0, 0)),
+        ],
+        out_specs=pl.BlockSpec((keep, cols), lambda k: (0, 0)),
+        out_shape=jax.ShapeDtypeStruct((keep, cols), jnp.float32),
+    )(band, coef, mix)
+
+
+def backward(mix, weighted, coef, controls):
+    members, rows, cols = mix.shape
+    keep = controls.shape[1]
+    return pl.pallas_call(
+        backward_kernel,
+        grid=(members,),
+        in_specs=[
+            pl.BlockSpec((1, rows, cols), lambda k: (k, 0, 0)),
+            pl.BlockSpec((rows, cols), lambda k: (0, 0)),
+            pl.BlockSpec((2, coef.shape[1], cols), lambda k: (0, 0, 0)),
+            pl.BlockSpec((1, keep, cols), lambda k: (k, 0, 0)),
+        ],
+        out_specs=pl.BlockSpec((1, keep, cols), lambda k: (k, 0, 0)),
+        out_shape=jax.ShapeDtypeStruct(controls.shape, jnp.float32),
+    )(mix, weighted, coef, controls)
+
+
 def diffuse(values, row_coef, col_coef):
     row_flux = row_coef[..., :-1, :] * (values[..., 1:, :] - values[..., :-1, :])
     col_flux = col_coef[..., :, :-1] * (values[..., :, 1:] - values[..., :, :-1])
@@ -60,23 +133,22 @@
 
 
 def per_device(controls, perturbations, jacobian, obs_weight, radar_mask, row_faces, col_faces):
-    row_count = controls.shape[1]
+    row_count, col_count = controls.shape[1:]
     row_index = lax.axis_index("tile") * row_count + lax.broadcasted_iota(
         jnp.int32, row_faces.shape, 0
     )
     row_coef = jnp.where(
         row_index < row_count * lax.axis_size("tile") - 1, row_faces, jnp.zeros_like(row_faces)
     )
-    stacked = jnp.stack([row_coef, col_faces])
-    field, coef_band = exchange([controls, stacked], STEPS)
-    localized = localize(field, coef_band)[:, STEPS : STEPS + row_count]
+    col_index = lax.broadcasted_iota(jnp.int32, col_faces.shape, 1)
+    col_coef = jnp.where(col_index < col_count - 1, col_faces, jnp.zeros_like(col_faces))
+    stacked = jnp.stack([row_coef, col_coef])
     mix = jnp.sum(perturbations.astype(jnp.float32) * jacobian[None], axis=1)
-    (mix_band,) = exchange([mix], STEPS)
-    reflect = mem_sum(jnp.sum(mix * localized, 0))
-    weighted = radar_mask.astype(jnp.float32) * obs_weight * reflect
-    (weighted_band,) = exchange([weighted[None]], STEPS)
-    sensitivity = mix_band * weighted_band
-    return controls + localize(sensitivity, coef_band)[:, STEPS : STEPS + row_count]
+    weights = radar_mask.astype(jnp.float32) * obs_weight
+    field, coef_band = exchange([controls, stacked], 2 * STEPS)
+    mix_band, weights_band = exchange([mix, weights[None]], STEPS)
+    reflect = mem_sum(forward(field, coef_band, mix_band))
+    return backward(mix_band, weights_band[0] * reflect, coef_band, controls)
 
 
 def solution(mesh):

time: 52.7 us -> 60.5 us (1.15)
  the two profiles are of different devices: /device:TPU:1 before, /device:TPU:16 now
where the time goes in v6:
time: 60.5 us; the launch traced here: 59.7 us
  Pallas kernels  18.3 us (30%)
  starting transfers between devices  12.9 us (21%)
  other arithmetic  11.5 us (19%)
  waiting for transfers between devices  10.8 us (18%)
  local copies, waits for them, and re-layouts  6.02 us (10%)
    pallas_call x1, Pallas kernels, forward(): pl.pallas_call(forward_kernel, grid=(members,), in_specs=[pl.BlockSpec((1...  9.37 us
    pallas_call x1, Pallas kernels, backward(): pl.pallas_call(backward_kernel, grid=(members,), in_specs=[pl.BlockSpec((...  8.9 us
    ppermute x2, waiting for transfers between devices, mem_sum(): lax.ppermute(part, 'mem', [(i, i ^ stride) for i in range(count)])  7.08 us
    ppermute x2, starting transfers between devices, exchange(): above = lax.ppermute(tail, 'tile', [(i, i + 1) for i in range(count - 1)])  5.48 us
    ppermute x2, starting transfers between devices, exchange(): below = lax.ppermute(head, 'tile', [(i + 1, i) for i in range(count - 1)])  4.36 us
    ppermute x2, waiting for transfers between devices, exchange(): above = lax.ppermute(tail, 'tile', [(i, i + 1) for i in range(count - 1)])  3.69 us
    concatenate x3, other arithmetic, exchange(): bands.append(jnp.concatenate([top, part, bottom], -2))  3.5 us
    ppermute x2, starting transfers between devices, mem_sum(): lax.ppermute(part, 'mem', [(i, i ^ stride) for i in range(count)])  3.08 us
  transfers between devices with their start and end apart: 6, of which 4 were waited for; matrix products, arithmetic and copies ran while one was open for 14% of the time, Pallas kernels for 0%

profile of v6, /device:TPU:16, one launch (start us, length us, event | category | flops | bytes accessed | tf_op | source)
XLA Modules:
  0.0 59.7 jit_solution(1567839430405804706)
XLA Ops:
  0.0 1.0 %multiply_bitcast_fusion = f32[1,16,1792]{2,1,0:T(8,128)S(1)} fusion(f32[16,1792]{1,0:T(8,128)} %param.10, s32[16,1792]{1,0:T(8,128)} %param.11), kind=kLoop, calls=%fused_computation.24 | loop fusion | flops 57344 | bytes 344064 | tf_op jit(solution)/shard_map/broadcast_in_dim | solution.py:149
  1.0 0.0 copy-start
  1.0 2.1 %multiply_reduce_fusion = f32[8,16,1792]{2,1,0:T(8,128)S(1)} fusion(bf16[8,4,16,1792]{3,2,1,0:T(8,128)(2,1)} %param.8, f32[4,16,1792]{2,1,0:T(8,128)} %param.9), kind=kLoop, calls=%fused_computation | loop fusion | flops 2523136 | bytes 3211264 | tf_op jit(solution)/shard_map/reduce_sum | solution.py:146
  3.1 0.0 copy-start.1
  3.1 0.0 copy-start.2
  3.1 0.1 fusion.4
  3.2 0.1 reshape.52
  3.3 0.7 %pad_maximum_fusion.6 = f32[36,1792]{1,0:T(8,128)} fusion(f32[4,1792]{1,0:T(4,128)S(1)} %get-tuple-element.12, f32[32,1792]{1,0:T(8,128)S(1)} %reshape.52), kind=kLoop, calls=%fused_computation.11 | loop fusion | flops 64512 | bytes 516096 | tf_op jit(solution)/shard_map/concatenate | solution.py:16
  4.1 1.9 %collective-permute-start.1 = (f32[36,1792]{1,0:T(8,128)}, f32[36,1792]{1,0:T(8,128)}, u32[]{:S(2)}, u32[]{:S(2)}) collective-permute-start(f32[36,1792]{1,0:T(8,128)} %pad_maximum_fusion.6), channel_id=1, source_target_pairs={{1,0},{2,1},{3,2},{4,3},{5,4},{6,5},{7,6},{9,8},{10,9},{11,10},{12... | collective-permute-start | bytes 774152 | tf_op jit(solution)/shard_map/ppermute | solution.py:19
  6.0 0.0 copy-done
  6.0 0.1 slice_bitcast_fusion.3
  6.1 0.0 copy-done.1
  6.1 0.0 copy-done.2
  6.1 0.1 select_bitcast_fusion
  6.2 0.8 %pad_maximum_fusion.3 = f32[80,1792]{1,0:T(8,128)} fusion(f32[16,1792]{1,0:T(8,128)S(1)} %get-tuple-element.10, f32[64,1792]{1,0:T(8,128)S(1)} %get-tuple-element.6), kind=kLoop, calls=%fused_computation.4 | loop fusion | flops 143360 | bytes 1146880 | tf_op jit(solution)/shard_map/concatenate | solution.py:16
  7.1 2.5 %collective-permute-start.3 = (f32[80,1792]{1,0:T(8,128)}, f32[80,1792]{1,0:T(8,128)}, u32[]{:S(2)}, u32[]{:S(2)}) collective-permute-start(f32[80,1792]{1,0:T(8,128)} %pad_maximum_fusion.3), channel_id=1, source_target_pairs={{1,0},{2,1},{3,2},{4,3},{5,4},{6,5},{7,6},{9,8},{10,9},{11,10},{12... | collective-permute-start | bytes 1720328 | tf_op jit(solution)/shard_map/ppermute | solution.py:19
  9.5 0.1 reshape.49
  9.6 0.7 %pad_maximum_fusion.5 = f32[36,1792]{1,0:T(8,128)} fusion(f32[4,1792]{1,0:T(4,128)S(1)} %get-tuple-element.11, f32[32,1792]{1,0:T(8,128)S(1)} %reshape.49), kind=kLoop, calls=%fused_computation.10 | loop fusion | flops 64512 | bytes 516096 | tf_op jit(solution)/shard_map/concatenate | solution.py:17
  10.3 1.9 %collective-permute-start = (f32[36,1792]{1,0:T(8,128)}, f32[36,1792]{1,0:T(8,128)}, u32[]{:S(2)}, u32[]{:S(2)}) collective-permute-start(f32[36,1792]{1,0:T(8,128)} %pad_maximum_fusion.5), channel_id=1, source_target_pairs={{0,1},{1,2},{2,3},{3,4},{4,5},{5,6},{6,7},{8,9},{9,10},{10,11},{11... | collective-permute-start | bytes 774152 | tf_op jit(solution)/shard_map/ppermute | solution.py:18
  12.2 0.9 %pad_maximum_fusion.2 = f32[80,1792]{1,0:T(8,128)} fusion(f32[16,1792]{1,0:T(8,128)S(1)} %get-tuple-element.9, f32[64,1792]{1,0:T(8,128)S(1)} %get-tuple-element.5), kind=kLoop, calls=%fused_computation.3 | loop fusion | flops 143360 | bytes 1146880 | tf_op jit(solution)/shard_map/concatenate | solution.py:17
  13.1 3.6 %collective-permute-start.2 = (f32[80,1792]{1,0:T(8,128)}, f32[80,1792]{1,0:T(8,128)S(1)}, u32[]{:S(2)}, u32[]{:S(2)}) collective-permute-start(f32[80,1792]{1,0:T(8,128)} %pad_maximum_fusion.2), channel_id=1, source_target_pairs={{0,1},{1,2},{2,3},{3,4},{4,5},{5,6},{6,7},{8,9},{9,10},{10,11},{11... | collective-permute-start | bytes 1720328 | tf_op jit(solution)/shard_map/ppermute | solution.py:18
  16.7 0.0 collective-permute-done.1
  16.7 1.0 %slice.69 = f32[32,1792]{1,0:T(8,128)S(1)} slice(f32[36,1792]{1,0:T(8,128)} %collective-permute-done.1), slice={[0:32], [0:1792]} | slice | bytes 458752 | tf_op jit(solution)/shard_map/slice | solution.py:25
  17.7 0.1 reshape.54
  17.7 0.9 %collective-permute-done = f32[36,1792]{1,0:T(8,128)} collective-permute-done((f32[36,1792]{1,0:T(8,128)}, f32[36,1792]{1,0:T(8,128)}, u32[]{:S(2)}, u32[]{:S(2)}) %collective-permute-start) | collective-permute-done | bytes 258080 | tf_op jit(solution)/shard_map/ppermute | solution.py:18
  18.6 1.0 %slice.66 = f32[32,1792]{1,0:T(8,128)S(1)} slice(f32[36,1792]{1,0:T(8,128)} %collective-permute-done), slice={[0:32], [0:1792]} | slice | bytes 458752 | tf_op jit(solution)/shard_map/slice | solution.py:24
  19.5 0.1 reshape.51
  19.6 1.3 %pad_maximum_fusion.1.mix_ref = f32[8,24,1792]{2,1,0:T(8,128)} fusion(f32[8,4,1792]{2,1,0:T(4,128)S(1)} %reshape.54, f32[8,16,1792]{2,1,0:T(8,128)S(1)} %multiply_reduce_fusion, f32[8,4,1792]{2,1,0:T(4,128)S(1)} %reshape.51), kind=kLoop, calls=%fused_computation.2 | loop fusion | flops 688128 | bytes 2752512 | tf_op jit(solution)/shard_map/concatenate | solution.py:26
  20.9 0.0 collective-permute-done.3
  20.9 0.9 %slice_bitcast_fusion.4 = f32[2,8,1792]{2,1,0:T(8,128)S(1)} fusion(f32[80,1792]{1,0:T(8,128)} %collective-permute-done.3), kind=kLoop, calls=%fused_computation.18 | loop fusion | bytes 229376 | tf_op jit(solution)/shard_map/reshape | solution.py:25
  21.8 2.8 %collective-permute-done.2 = f32[80,1792]{1,0:T(8,128)S(1)} collective-permute-done((f32[80,1792]{1,0:T(8,128)}, f32[80,1792]{1,0:T(8,128)S(1)}, u32[]{:S(2)}, u32[]{:S(2)}) %collective-permute-start.2) | collective-permute-done | bytes 573472 | tf_op jit(solution)/shard_map/ppermute | solution.py:18
  24.6 0.8 %pad_maximum_fusion.4.coef_ref = f32[2,32,1792]{2,1,0:T(8,128)} fusion(f32[2,8,1792]{2,1,0:T(8,128)S(1)} %slice_bitcast_fusion.4, f32[1,16,1792]{2,1,0:T(8,128)S(1)} %get-tuple-element.13, f32[1,16,1792]{2,1,0:T(8,128)S(1)} %get-tuple-element.14, f32[2,8,1792]{2,1,0:T(8,128)S(1)} %slice_bitcast_fusion.5), kind=kLoop, calls=%fused_computation.7 | loop fusion | flops 344064 | bytes 917504 | tf_op jit(solution)/shard_map/concatenate | solution.py:26
  25.5 1.0 %slice_bitcast_fusion = f32[8,8,1792]{2,1,0:T(8,128)S(1)} fusion(f32[80,1792]{1,0:T(8,128)} %collective-permute-done.3), kind=kLoop, calls=%fused_computation.5 | loop fusion | bytes 917504 | tf_op jit(solution)/shard_map/reshape | solution.py:25
  26.6 1.4 %pad_maximum_fusion.band_ref = f32[8,32,1792]{2,1,0:T(8,128)} fusion(f32[8,8,1792]{2,1,0:T(8,128)S(1)} %slice_bitcast_fusion, f32[8,16,1792]{2,1,0:T(8,128)S(1)} %copy-done, f32[8,8,1792]{2,1,0:T(8,128)S(1)} %slice_bitcast_fusion.1), kind=kLoop, calls=%fused_computation.1 | loop fusion | flops 917504 | bytes 3670016 | tf_op jit(solution)/shard_map/concatenate | solution.py:26
  28.0 9.4 %shard_map.73 = f32[24,1792]{1,0:T(8,128)} custom-call(f32[8,32,1792]{2,1,0:T(8,128)} %pad_maximum_fusion.band_ref, f32[2,32,1792]{2,1,0:T(8,128)} %pad_maximum_fusion.4.coef_ref, f32[8,24,1792]{2,1,0:T(8,128)} %pad_maximum_fusion.1.mix_ref), custom_call_target="tpu_custom_call" | custom-call | tf_op jit(solution)/shard_map/pallas_call | solution.py:82
  37.3 1.5 %collective-permute-start.4 = (f32[24,1792]{1,0:T(8,128)}, f32[24,1792]{1,0:T(8,128)S(1)}, u32[]{:S(2)}, u32[]{:S(2)}) collective-permute-start(f32[24,1792]{1,0:T(8,128)} %shard_map.73), channel_id=1, source_target_pairs={{0,8},{8,0},{16,24},{24,16},{1,9},{9,1},{17,25},{25,17},{2,10},{10... | collective-permute-start | bytes 516104 | tf_op jit(solution)/shard_map/ppermute | solution.py:37
  38.8 0.8 %slice_bitcast_fusion.6 = f32[1,4,1792]{2,1,0:T(4,128)S(1)} fusion(f32[36,1792]{1,0:T(8,128)} %collective-permute-done.1), kind=kLoop, calls=%fused_computation.25 | loop fusion | bytes 57344 | tf_op jit(solution)/shard_map/reshape | solution.py:25
  39.6 4.0 %collective-permute-done.4 = f32[24,1792]{1,0:T(8,128)S(1)} collective-permute-done((f32[24,1792]{1,0:T(8,128)}, f32[24,1792]{1,0:T(8,128)S(1)}, u32[]{:S(2)}, u32[]{:S(2)}) %collective-permute-start.4) | collective-permute-done | bytes 172064 | tf_op jit(solution)/shard_map/ppermute | solution.py:37
  43.7 0.9 %add.15 = f32[24,1792]{1,0:T(8,128)S(1)} add(f32[24,1792]{1,0:T(8,128)} %shard_map.73, f32[24,1792]{1,0:T(8,128)S(1)} %collective-permute-done.4) | non-fusion elementwise | flops 43008 | bytes 516096 | tf_op jit(solution)/shard_map/add | solution.py:37
  44.6 1.6 %collective-permute-start.5 = (f32[24,1792]{1,0:T(8,128)S(1)}, f32[24,1792]{1,0:T(8,128)S(1)}, u32[]{:S(2)}, u32[]{:S(2)}) collective-permute-start(f32[24,1792]{1,0:T(8,128)S(1)} %add.15), channel_id=1, source_target_pairs={{0,16},{8,24},{16,0},{24,8},{1,17},{9,25},{17,1},{25,9},{2,18},{10... | collective-permute-start | bytes 516104 | tf_op jit(solution)/shard_map/ppermute | solution.py:37
  46.2 0.8 %slice_bitcast_fusion.7 = f32[1,4,1792]{2,1,0:T(4,128)S(1)} fusion(f32[36,1792]{1,0:T(8,128)} %collective-permute-done), kind=kLoop, calls=%fused_computation.26 | loop fusion | bytes 57344 | tf_op jit(solution)/shard_map/reshape | solution.py:24
  47.0 3.1 %collective-permute-done.5 = f32[24,1792]{1,0:T(8,128)S(1)} collective-permute-done((f32[24,1792]{1,0:T(8,128)S(1)}, f32[24,1792]{1,0:T(8,128)S(1)}, u32[]{:S(2)}, u32[]{:S(2)}) %collective-permute-start.5) | collective-permute-done | bytes 172064 | tf_op jit(solution)/shard_map/ppermute | solution.py:37
  50.1 0.7 %fusion.weighted_ref = f32[24,1792]{1,0:T(8,128)} fusion(f32[1,4,1792]{2,1,0:T(4,128)S(1)} %slice_bitcast_fusion.6, f32[1,16,1792]{2,1,0:T(8,128)S(1)} %multiply_bitcast_fusion, f32[1,4,1792]{2,1,0:T(4,128)S(1)} %slice_bitcast_fusion.7, f32[24,1792]{1,0:T(8,128)S(1)} %add.15, f32[24,1792]{1,0:T(8,128)S(1)} %collective-permute-done.5), kind=kLoop, calls=%fused_computation.15 | loop fusion | flops 172032 | bytes 688128 | tf_op jit(solution)/shard_map/mul | solution.py:151
  50.8 8.9 %shard_map.74 = f32[8,16,1792]{2,1,0:T(8,128)} custom-call(f32[8,24,1792]{2,1,0:T(8,128)} %pad_maximum_fusion.1.mix_ref, f32[24,1792]{1,0:T(8,128)} %fusion.weighted_ref, f32[2,32,1792]{2,1,0:T(8,128)} %pad_maximum_fusion.4.coef_ref, f32[8,16,1792]{2,1,0:T(8,128)} %controls_ref.1), custom_call_target="tpu_custom_call" | custom-call | tf_op jit(solution)/shard_map/pallas_call | solution.py:98
  (6 shorter events, 0.1 us)
Async XLA Ops:
  1.0 5.0 %copy-start = (f32[8,16,1792]{2,1,0:T(8,128)S(1)}, f32[8,16,1792]{2,1,0:T(8,128)}, u32[]{:S(2)}) copy-start(f32[8,16,1792]{2,1,0:T(8,128)} %controls_ref.1) | copy-start | bytes 2752516
  3.1 3.0 %copy-start.1 = (f32[16,1792]{1,0:T(8,128)S(1)}, f32[16,1792]{1,0:T(8,128)}, u32[]{:S(2)}) copy-start(f32[16,1792]{1,0:T(8,128)} %param.13) | copy-start | bytes 344068
  3.1 3.0 %copy-start.2 = (f32[16,1792]{1,0:T(8,128)S(1)}, f32[16,1792]{1,0:T(8,128)}, u32[]{:S(2)}) copy-start(f32[16,1792]{1,0:T(8,128)} %param.12) | copy-start | bytes 344068
  4.1 12.6 %collective-permute-start.1 = (f32[36,1792]{1,0:T(8,128)}, f32[36,1792]{1,0:T(8,128)}, u32[]{:S(2)}, u32[]{:S(2)}) collective-permute-start(f32[36,1792]{1,0:T(8,128)} %pad_maximum_fusion.6), channel_id=1, source_target_pairs={{1,0},{2,1},{3,2},{4,3},{5,4},{6,5},{7,6},{9,8},{10,9},{11,10},{12... | collective-permute-start | bytes 774152 | tf_op jit(solution)/shard_map/ppermute | solution.py:19
  7.1 13.8 %collective-permute-start.3 = (f32[80,1792]{1,0:T(8,128)}, f32[80,1792]{1,0:T(8,128)}, u32[]{:S(2)}, u32[]{:S(2)}) collective-permute-start(f32[80,1792]{1,0:T(8,128)} %pad_maximum_fusion.3), channel_id=1, source_target_pairs={{1,0},{2,1},{3,2},{4,3},{5,4},{6,5},{7,6},{9,8},{10,9},{11,10},{12... | collective-permute-start | bytes 1720328 | tf_op jit(solution)/shard_map/ppermute | solution.py:19
  10.3 8.3 %collective-permute-start = (f32[36,1792]{1,0:T(8,128)}, f32[36,1792]{1,0:T(8,128)}, u32[]{:S(2)}, u32[]{:S(2)}) collective-permute-start(f32[36,1792]{1,0:T(8,128)} %pad_maximum_fusion.5), channel_id=1, source_target_pairs={{0,1},{1,2},{2,3},{3,4},{4,5},{5,6},{6,7},{8,9},{9,10},{10,11},{11... | collective-permute-start | bytes 774152 | tf_op jit(solution)/shard_map/ppermute | solution.py:18
  13.1 11.5 %collective-permute-start.2 = (f32[80,1792]{1,0:T(8,128)}, f32[80,1792]{1,0:T(8,128)S(1)}, u32[]{:S(2)}, u32[]{:S(2)}) collective-permute-start(f32[80,1792]{1,0:T(8,128)} %pad_maximum_fusion.2), channel_id=1, source_target_pairs={{0,1},{1,2},{2,3},{3,4},{4,5},{5,6},{6,7},{8,9},{9,10},{10,11},{11... | collective-permute-start | bytes 1720328 | tf_op jit(solution)/shard_map/ppermute | solution.py:18
  37.3 6.3 %collective-permute-start.4 = (f32[24,1792]{1,0:T(8,128)}, f32[24,1792]{1,0:T(8,128)S(1)}, u32[]{:S(2)}, u32[]{:S(2)}) collective-permute-start(f32[24,1792]{1,0:T(8,128)} %shard_map.73), channel_id=1, source_target_pairs={{0,8},{8,0},{16,24},{24,16},{1,9},{9,1},{17,25},{25,17},{2,10},{10... | collective-permute-start | bytes 516104 | tf_op jit(solution)/shard_map/ppermute | solution.py:37
  44.6 5.5 %collective-permute-start.5 = (f32[24,1792]{1,0:T(8,128)S(1)}, f32[24,1792]{1,0:T(8,128)S(1)}, u32[]{:S(2)}, u32[]{:S(2)}) collective-permute-start(f32[24,1792]{1,0:T(8,128)S(1)} %add.15), channel_id=1, source_target_pairs={{0,16},{8,24},{16,0},{24,8},{1,17},{9,25},{17,1},{25,9},{2,18},{10... | collective-permute-start | bytes 516104 | tf_op jit(solution)/shard_map/ppermute | solution.py:37

commit v7 on v4

--- a/solution.py
+++ b/solution.py
@@ -27,41 +27,42 @@
 
 def mem_sum(part):
     count = lax.axis_size("mem")
-    if count & (count - 1) or part.shape[-1] % 256:
+    if count & (count - 1):
         return lax.psum(part, "mem")
-    half = part.shape[-1] // 2
-    first, second = part[..., :half], part[..., half:]
-    strides = []
     stride = 1
     while stride < count:
-        strides.append(stride)
+        part = part + lax.ppermute(part, "mem", [(i, i ^ stride) for i in range(count)])
         stride *= 2
-    for up, down in zip(strides, strides[::-1]):
-        first = first + lax.ppermute(first, "mem", [(i, i ^ up) for i in range(count)])
-        second = second + lax.ppermute(second, "mem", [(i, i ^ down) for i in range(count)])
-    return jnp.concatenate([first, second], -1)
+    return part
 
 
-def diffuse(values, row_coef, col_coef):
-    row_flux = row_coef[..., :-1, :] * (values[..., 1:, :] - values[..., :-1, :])
-    col_flux = col_coef[..., :, :-1] * (values[..., :, 1:] - values[..., :, :-1])
-    zeros_row = jnp.zeros_like(values[..., :1, :])
-    zeros_col = jnp.zeros_like(values[..., :, :1])
-    values = (
-        values
-        + jnp.concatenate([row_flux, zeros_row], -2)
-        - jnp.concatenate([zeros_row, row_flux], -2)
-    )
-    return (
-        values
-        + jnp.concatenate([col_flux, zeros_col], -1)
-        - jnp.concatenate([zeros_col, col_flux], -1)
-    )
+def shifted(values, axis, step):
+    zero = jnp.zeros_like(lax.slice_in_dim(values, 0, 1, axis=axis))
+    if step > 0:
+        return jnp.concatenate([lax.slice_in_dim(values, 1, None, axis=axis), zero], axis)
+    return jnp.concatenate([zero, lax.slice_in_dim(values, 0, -1, axis=axis)], axis)
+
+
+def coefficients(coef_band):
+    row_coef, col_coef = coef_band[0], coef_band[1]
+    row_next = shifted(shifted(row_coef, 0, -1), 0, 1)
+    col_next = shifted(shifted(col_coef, 1, -1), 1, 1)
+    return row_next, shifted(row_coef, 0, -1), col_next, shifted(col_coef, 1, -1)
+
+
+def diffuse(values, coefs):
+    row_next, row_prev, col_next, col_prev = coefs
+    row_in = row_next * (shifted(values, 1, 1) - values)
+    row_out = row_prev * (values - shifted(values, 1, -1))
+    col_in = col_next * (shifted(values, 2, 1) - values)
+    col_out = col_prev * (values - shifted(values, 2, -1))
+    return values + row_in - row_out + col_in - col_out
 
 
 def localize(field, coef_band):
+    coefs = coefficients(coef_band)
     for repeat in range(STEPS):
-        field = diffuse(field, coef_band[0], coef_band[1])
+        field = diffuse(field, coefs)
     return field
 
 

time: 51.9 us -> 53.9 us (1.039)
  local copies, waits for them, and re-layouts: 5.48 us -> 11.7 us
  other arithmetic: 16.8 us -> 12.4 us
  waiting for transfers between devices: 14.2 us -> 15.1 us
  starting transfers between devices: 14.5 us -> 13.8 us
    slice x1 -> x23, local copies, waits for them, and re-layouts: 0.01 us -> 6.65 us  [the longest x16 6.35 us: shifted(): lax.slice_in_dim(values, 1, None, axis=axis)]
    mul x17 -> x0, other arithmetic: 5.74 us -> none  [the longest x8 4.02 us: diffuse(): col_coef[..., :, :-1] * (values[..., :, 1:] - values[..., :, :-1])]
    slice x2 -> x1, local copies, waits for them, and re-layouts: 1.8 us -> 0.02 us  [exchange(): top = above[start:start + size].reshape(shape)]
    ppermute x2, starting transfers between devices: 4.3 us -> 6.04 us  [exchange(): above = lax.ppermute(tail, 'tile', [(i, i + 1) for i in range(count - 1)])]
    ppermute x4 -> x2, starting transfers between devices: 5.2 us -> 3.68 us  [mem_sum(): lax.ppermute(part, 'mem', [(i, i ^ stride) for i in range(count)])]
    sub x6, other arithmetic: 4.21 us -> 5.63 us  [diffuse(): return values + row_in - row_out + col_in - col_out]
    ppermute x2, starting transfers between devices: 5.05 us -> 4.08 us  [exchange(): below = lax.ppermute(head, 'tile', [(i + 1, i) for i in range(count - 1)])]
    ppermute x2, waiting for transfers between devices: 6.69 us -> 7.49 us  [exchange(): above = lax.ppermute(tail, 'tile', [(i, i + 1) for i in range(count - 1)])]
  transfers between devices with their start and end apart: 8 -> 6, of which waited for: 6 -> 3; matrix products, arithmetic and copies ran while one was open for 10% -> 8% of each run, Pallas kernels for 0% -> 0%
where the time goes in v7:
time: 53.9 us; the launch traced here: 53.6 us
  waiting for transfers between devices  15.1 us (28%)
  starting transfers between devices  13.8 us (26%)
  other arithmetic  12.4 us (23%)
  local copies, waits for them, and re-layouts  11.7 us (22%)
  between operations  0.55 us (1%)
    ppermute x2, waiting for transfers between devices, mem_sum(): lax.ppermute(part, 'mem', [(i, i ^ stride) for i in range(count)])  7.6 us
    ppermute x2, waiting for transfers between devices, exchange(): above = lax.ppermute(tail, 'tile', [(i, i + 1) for i in range(count - 1)])  7.49 us
    slice x16, local copies, waits for them, and re-layouts, shifted(): lax.slice_in_dim(values, 1, None, axis=axis)  6.35 us
    ppermute x2, starting transfers between devices, exchange(): above = lax.ppermute(tail, 'tile', [(i, i + 1) for i in range(count - 1)])  6.04 us
    sub x6, other arithmetic, diffuse(): return values + row_in - row_out + col_in - col_out  5.63 us
    ppermute x2, starting transfers between devices, exchange(): below = lax.ppermute(head, 'tile', [(i + 1, i) for i in range(count - 1)])  4.08 us
    ppermute x2, starting transfers between devices, mem_sum(): lax.ppermute(part, 'mem', [(i, i ^ stride) for i in range(count)])  3.68 us
    reshape x3, local copies, waits for them, and re-layouts, exchange(): part[..., -width:, :].reshape(-1, cols)  1.99 us
  transfers between devices with their start and end apart: 6, of which 3 were waited for; matrix products, arithmetic and copies ran while one was open for 8% of the time, Pallas kernels for 0%

profile of v7, /device:TPU:8, one launch (start us, length us, event | category | flops | bytes accessed | tf_op | source)
XLA Modules:
  0.0 53.6 jit_solution(13978102001261407956)
XLA Ops:
  0.0 0.0 copy-start.2
  0.0 1.3 %slice_bitcast_fusion.3 = (f32[64,1792]{1,0:T(8,128)S(1)}, f32[64,1792]{1,0:T(8,128)S(1)}) fusion(f32[8,16,1792]{2,1,0:T(8,128)} %param.7), kind=kLoop, calls=%fused_computation.43 | loop fusion | bytes 1835008 | tf_op jit(solution)/shard_map/reshape | solution.py:14
  1.3 0.0 copy-start.1
  1.3 0.1 select_bitcast_fusion
  1.4 0.0 copy-done.3
  1.4 0.8 %pad_maximum_fusion.3 = f32[80,1792]{1,0:T(8,128)} fusion(f32[16,1792]{1,0:T(8,128)S(1)} %get-tuple-element.46, f32[64,1792]{1,0:T(8,128)S(1)} %get-tuple-element.38), kind=kLoop, calls=%fused_computation.38 | loop fusion | flops 143360 | bytes 1146880 | tf_op jit(solution)/shard_map/concatenate | solution.py:13
  2.3 2.0 %collective-permute-start.3 = (f32[80,1792]{1,0:T(8,128)}, f32[80,1792]{1,0:T(8,128)S(1)}, u32[]{:S(2)}, u32[]{:S(2)}) collective-permute-start(f32[80,1792]{1,0:T(8,128)} %pad_maximum_fusion.3), channel_id=1, source_target_pairs={{1,0},{2,1},{3,2},{4,3},{5,4},{6,5},{7,6},{9,8},{10,9},{11,10},{12... | collective-permute-start | bytes 1720328 | tf_op jit(solution)/shard_map/ppermute | solution.py:16
  4.4 0.4 multiply_reduce_fusion
  4.8 0.1 fusion.40
  4.9 0.6 %slice_bitcast_fusion.13 = (f32[4,1792]{1,0:T(4,128)}, f32[4,1792]{1,0:T(4,128)S(1)}) fusion(f32[1,16,1792]{2,1,0:T(8,128)S(1)} %multiply_bitcast_fusion), kind=kLoop, calls=%fused_computation.67 | loop fusion | bytes 114688 | tf_op jit(solution)/shard_map/reshape | solution.py:14
  5.5 0.1 reshape.63
  5.6 0.7 %pad_maximum_fusion.6 = f32[36,1792]{1,0:T(8,128)} fusion(f32[4,1792]{1,0:T(4,128)S(1)} %get-tuple-element.52, f32[32,1792]{1,0:T(8,128)S(1)} %reshape.63), kind=kLoop, calls=%fused_computation.45 | loop fusion | flops 64512 | bytes 516096 | tf_op jit(solution)/shard_map/concatenate | solution.py:13
  6.3 2.0 %collective-permute-start.1 = (f32[36,1792]{1,0:T(8,128)}, f32[36,1792]{1,0:T(8,128)S(1)}, u32[]{:S(2)}, u32[]{:S(2)}) collective-permute-start(f32[36,1792]{1,0:T(8,128)} %pad_maximum_fusion.6), channel_id=1, source_target_pairs={{1,0},{2,1},{3,2},{4,3},{5,4},{6,5},{7,6},{9,8},{10,9},{11,10},{12... | collective-permute-start | bytes 774152 | tf_op jit(solution)/shard_map/ppermute | solution.py:16
  8.4 0.8 %pad_maximum_fusion.2 = f32[80,1792]{1,0:T(8,128)} fusion(f32[16,1792]{1,0:T(8,128)S(1)} %get-tuple-element.45, f32[64,1792]{1,0:T(8,128)S(1)} %get-tuple-element.37), kind=kLoop, calls=%fused_computation.37 | loop fusion | flops 143360 | bytes 1146880 | tf_op jit(solution)/shard_map/concatenate | solution.py:14
  9.2 2.4 %collective-permute-start.2 = (f32[80,1792]{1,0:T(8,128)}, f32[80,1792]{1,0:T(8,128)S(1)}, u32[]{:S(2)}, u32[]{:S(2)}) collective-permute-start(f32[80,1792]{1,0:T(8,128)} %pad_maximum_fusion.2), channel_id=1, source_target_pairs={{0,1},{1,2},{2,3},{3,4},{4,5},{5,6},{6,7},{8,9},{9,10},{10,11},{11... | collective-permute-start | bytes 1720328 | tf_op jit(solution)/shard_map/ppermute | solution.py:15
  11.6 0.1 reshape.60
  11.8 3.6 %collective-permute-start = (f32[36,1792]{1,0:T(8,128)S(1)}, f32[36,1792]{1,0:T(8,128)S(1)}, u32[]{:S(2)}, u32[]{:S(2)}) collective-permute-start(f32[36,1792]{1,0:T(8,128)S(1)} %pad_maximum_fusion.5), channel_id=1, source_target_pairs={{0,1},{1,2},{2,3},{3,4},{4,5},{5,6},{6,7},{8,9},{9,10},{10,11},{11... | collective-permute-start | bytes 774152 | tf_op jit(solution)/shard_map/ppermute | solution.py:15
  15.4 0.0 collective-permute-done.1
  15.4 0.6 %slice_bitcast_fusion.10 = f32[1,4,1792]{2,1,0:T(4,128)} fusion(f32[36,1792]{1,0:T(8,128)S(1)} %collective-permute-done.1), kind=kLoop, calls=%fused_computation.64 | loop fusion | bytes 57344 | tf_op jit(solution)/shard_map/reshape | solution.py:22
  16.0 7.5 %collective-permute-done = f32[36,1792]{1,0:T(8,128)S(1)} collective-permute-done((f32[36,1792]{1,0:T(8,128)S(1)}, f32[36,1792]{1,0:T(8,128)S(1)}, u32[]{:S(2)}, u32[]{:S(2)}) %collective-permute-start) | collective-permute-done | bytes 258080 | tf_op jit(solution)/shard_map/ppermute | solution.py:15
  23.5 0.6 %slice_bitcast_fusion.11 = f32[1,4,1792]{2,1,0:T(4,128)} fusion(f32[36,1792]{1,0:T(8,128)S(1)} %collective-permute-done), kind=kLoop, calls=%fused_computation.65 | loop fusion | bytes 57344 | tf_op jit(solution)/shard_map/reshape | solution.py:21
  24.1 0.1 reshape.62
  24.2 0.1 reshape.65
  24.3 0.0 collective-permute-done.3
  24.3 0.0 collective-permute-done.2
  24.4 0.0 copy-start
  24.6 1.0 %copy-done = f32[8,16,1792]{2,1,0:T(8,128)S(1)} copy-done((f32[8,16,1792]{2,1,0:T(8,128)S(1)}, f32[8,16,1792]{2,1,0:T(8,128)}, u32[]{:S(2)}) %copy-start) | copy-done | bytes 917528
  25.6 0.1 pad_maximum_fusion
  25.7 0.3 fusion.30
  26.1 0.0 copy-start.10
  26.1 0.6 %fusion.31 = (f32[8,32,1791]{2,1,0:T(8,128)S(1)}, f32[8,32,1791]{2,1,0:T(8,128)S(1)}) fusion(f32[8,32,1792]{2,1,0:T(8,128)S(1)} %pad_maximum_fusion), kind=kLoop, calls=%fused_computation.82 | loop fusion | bytes 7335936 | tf_op jit(solution)/shard_map/slice | solution.py:42
  26.8 0.0 copy-done.10
  26.8 0.1 concatenate.158
  26.9 1.0 %multiply_subtract_fusion.2 = f32[8,32,1792]{2,1,0:T(8,128)S(1)} fusion(f32[8,32,1791]{2,1,0:T(8,128)S(1)} %get-tuple-element.20, f32[8,32,1791]{2,1,0:T(8,128)S(1)} %get-tuple-element.19, f32[8,31,1792]{2,1,0:T(8,128)S(1)} %get-tuple-element.18, f32[8,31,1792]{2,1,0:T(8,128)S(1)} %get-tuple-element.17, f32[32,1792]{1,0:T(8,128)S(1)} %concatenate.158, ...), kind=kLoop, calls=%fused_computation.4 | loop fusion | flops 6422528 | bytes 11810816 | tf_op jit(solution)/shard_map/sub | solution.py:59
  27.9 0.3 fusion.28
  28.3 0.6 %fusion.29 = (f32[8,32,1791]{2,1,0:T(8,128)S(1)}, f32[8,32,1791]{2,1,0:T(8,128)S(1)}) fusion(f32[8,32,1792]{2,1,0:T(8,128)S(1)} %multiply_subtract_fusion.2), kind=kLoop, calls=%fused_computation.80 | loop fusion | bytes 7335936 | tf_op jit(solution)/shard_map/slice | solution.py:42
  28.9 1.1 %multiply_subtract_fusion.1 = f32[8,32,1792]{2,1,0:T(8,128)S(1)} fusion(f32[8,32,1792]{2,1,0:T(8,128)S(1)} %multiply_subtract_fusion.2, f32[8,32,1791]{2,1,0:T(8,128)S(1)} %get-tuple-element.16, f32[8,32,1791]{2,1,0:T(8,128)S(1)} %get-tuple-element.15, f32[8,31,1792]{2,1,0:T(8,128)S(1)} %get-tuple-element.14, f32[8,31,1792]{2,1,0:T(8,128)S(1)} %get-tuple-element.13, ...), kind=kLoop, calls=%fused_computation.3 | loop fusion | flops 5505024 | bytes 11810816 | tf_op jit(solution)/shard_map/sub | solution.py:59
  29.9 0.3 fusion.26
  30.3 0.6 %fusion.27 = (f32[8,32,1791]{2,1,0:T(8,128)S(1)}, f32[8,32,1791]{2,1,0:T(8,128)S(1)}) fusion(f32[8,32,1792]{2,1,0:T(8,128)S(1)} %multiply_subtract_fusion.1), kind=kLoop, calls=%fused_computation.78 | loop fusion | bytes 7335936 | tf_op jit(solution)/shard_map/slice | solution.py:42
  30.9 1.1 %multiply_subtract_fusion = f32[8,32,1792]{2,1,0:T(8,128)S(1)} fusion(f32[8,32,1792]{2,1,0:T(8,128)S(1)} %multiply_subtract_fusion.1, f32[8,32,1791]{2,1,0:T(8,128)S(1)} %get-tuple-element.12, f32[8,32,1791]{2,1,0:T(8,128)S(1)} %get-tuple-element.11, f32[8,31,1792]{2,1,0:T(8,128)S(1)} %get-tuple-element.10, f32[8,31,1792]{2,1,0:T(8,128)S(1)} %get-tuple-element.9, ...), kind=kLoop, calls=%fused_computation.2 | loop fusion | flops 5505024 | bytes 11810816 | tf_op jit(solution)/shard_map/sub | solution.py:59
  32.0 0.3 fusion.24
  32.3 0.6 %fusion.25 = (f32[8,32,1791]{2,1,0:T(8,128)S(1)}, f32[8,32,1791]{2,1,0:T(8,128)S(1)}) fusion(f32[8,32,1792]{2,1,0:T(8,128)S(1)} %multiply_subtract_fusion), kind=kLoop, calls=%fused_computation.76 | loop fusion | bytes 7335936 | tf_op jit(solution)/shard_map/slice | solution.py:42
  32.9 0.1 pad_slice_fusion.7
  33.2 1.6 %fusion.3 = f32[24,1792]{1,0:T(8,128)S(1)} fusion(f32[8,32,1791]{2,1,0:T(8,128)S(1)} %get-tuple-element.8, f32[8,32,1791]{2,1,0:T(8,128)S(1)} %get-tuple-element.7, f32[8,31,1792]{2,1,0:T(8,128)S(1)} %get-tuple-element.6, f32[8,31,1792]{2,1,0:T(8,128)S(1)} %get-tuple-element.5, f32[8,32,1792]{2,1,0:T(8,128)S(1)} %multiply_subtract_fusion, ...), kind=kLoop, calls=%fused_computation.9 | loop fusion | flops 5462016 | bytes 10835968 | tf_op jit(solution)/shard_map/reduce_sum | solution.py:84
  34.8 2.1 %collective-permute-start.4 = (f32[24,1792]{1,0:T(8,128)S(1)}, f32[24,1792]{1,0:T(8,128)S(1)}, u32[]{:S(2)}, u32[]{:S(2)}) collective-permute-start(f32[24,1792]{1,0:T(8,128)S(1)} %fusion.3), channel_id=1, source_target_pairs={{0,8},{8,0},{16,24},{24,16},{1,9},{9,1},{17,25},{25,17},{2,10},{10... | collective-permute-start | bytes 516104 | tf_op jit(solution)/shard_map/ppermute | solution.py:34
  36.9 0.1 concatenate.178
  37.0 3.8 %collective-permute-done.4 = f32[24,1792]{1,0:T(8,128)S(1)} collective-permute-done((f32[24,1792]{1,0:T(8,128)S(1)}, f32[24,1792]{1,0:T(8,128)S(1)}, u32[]{:S(2)}, u32[]{:S(2)}) %collective-permute-start.4) | collective-permute-done | bytes 172064 | tf_op jit(solution)/shard_map/ppermute | solution.py:34
  40.9 1.6 %collective-permute-start.5 = (f32[24,1792]{1,0:T(8,128)S(1)}, f32[24,1792]{1,0:T(8,128)S(1)}, u32[]{:S(2)}, u32[]{:S(2)}) collective-permute-start(f32[24,1792]{1,0:T(8,128)S(1)} %add.150), channel_id=1, source_target_pairs={{0,16},{8,24},{16,0},{24,8},{1,17},{9,25},{17,1},{25,9},{2,18},{10... | collective-permute-start | bytes 516104 | tf_op jit(solution)/shard_map/ppermute | solution.py:34
  42.5 0.1 pad_slice_fusion.2
  42.6 3.8 %collective-permute-done.5 = f32[24,1792]{1,0:T(8,128)S(1)} collective-permute-done((f32[24,1792]{1,0:T(8,128)S(1)}, f32[24,1792]{1,0:T(8,128)S(1)}, u32[]{:S(2)}, u32[]{:S(2)}) %collective-permute-start.5) | collective-permute-done | bytes 172064 | tf_op jit(solution)/shard_map/ppermute | solution.py:34
  46.4 0.1 fusion.20
  46.4 0.2 fusion.10
  46.7 0.2 fusion.38
  46.9 0.4 fusion.39
  47.3 0.8 %multiply_subtract_fusion.5 = f32[8,24,1792]{2,1,0:T(8,128)S(1)} fusion(f32[8,24,1792]{2,1,0:T(8,128)S(1)} %fusion.10, f32[8,24,1791]{2,1,0:T(8,128)S(1)} %get-tuple-element.36, f32[8,24,1791]{2,1,0:T(8,128)S(1)} %get-tuple-element.35, f32[8,23,1792]{2,1,0:T(8,128)S(1)} %get-tuple-element.34, f32[8,23,1792]{2,1,0:T(8,128)S(1)} %get-tuple-element.33, ...), kind=kLoop, calls=%fused_computation.22 | loop fusion | flops 4128768 | bytes 8829440 | tf_op jit(solution)/shard_map/sub | solution.py:59
  48.1 0.2 fusion.36
  48.3 0.4 fusion.37
  48.7 1.0 %multiply_subtract_fusion.4 = f32[8,24,1792]{2,1,0:T(8,128)S(1)} fusion(f32[8,24,1792]{2,1,0:T(8,128)S(1)} %multiply_subtract_fusion.5, f32[8,24,1791]{2,1,0:T(8,128)S(1)} %get-tuple-element.32, f32[8,24,1791]{2,1,0:T(8,128)S(1)} %get-tuple-element.31, f32[8,23,1792]{2,1,0:T(8,128)S(1)} %get-tuple-element.30, f32[8,23,1792]{2,1,0:T(8,128)S(1)} %get-tuple-element.29, ...), kind=kLoop, calls=%fused_computation.21 | loop fusion | flops 4128768 | bytes 8829440 | tf_op jit(solution)/shard_map/sub | solution.py:59
  49.7 0.2 fusion.34
  49.9 0.4 fusion.35
  50.3 0.8 %multiply_subtract_fusion.3 = f32[8,24,1792]{2,1,0:T(8,128)S(1)} fusion(f32[8,24,1792]{2,1,0:T(8,128)S(1)} %multiply_subtract_fusion.4, f32[8,24,1791]{2,1,0:T(8,128)S(1)} %get-tuple-element.28, f32[8,24,1791]{2,1,0:T(8,128)S(1)} %get-tuple-element.27, f32[8,23,1792]{2,1,0:T(8,128)S(1)} %get-tuple-element.26, f32[8,23,1792]{2,1,0:T(8,128)S(1)} %get-tuple-element.25, ...), kind=kLoop, calls=%fused_computation.20 | loop fusion | flops 4128768 | bytes 8829440 | tf_op jit(solution)/shard_map/sub | solution.py:59
  51.1 0.2 fusion.32
  51.3 0.4 fusion.33
  51.8 1.8 %fusion.13 = f32[8,16,1792]{2,1,0:T(8,128)} fusion(f32[8,16,1792]{2,1,0:T(8,128)S(1)} %copy-done, f32[8,24,1791]{2,1,0:T(8,128)S(1)} %get-tuple-element.24, f32[8,24,1791]{2,1,0:T(8,128)S(1)} %get-tuple-element.23, f32[8,23,1792]{2,1,0:T(8,128)S(1)} %get-tuple-element.22, f32[8,23,1792]{2,1,0:T(8,128)S(1)} %get-tuple-element.21, ...), kind=kLoop, calls=%fused_computation.27 | loop fusion | flops 2981888 | bytes 8600064 | tf_op jit(solution)/shard_map/add | solution.py:87
  (38 shorter events, 0.5 us)
Async XLA Ops:
  0.0 1.3 %copy-start.4 = (f32[16,1792]{1,0:T(8,128)S(1)}, f32[16,1792]{1,0:T(8,128)}, u32[]{:S(2)}) copy-start(f32[16,1792]{1,0:T(8,128)} %param.12) | copy-start | bytes 344068
  0.0 1.4 %copy-start.3 = (f32[16,1792]{1,0:T(8,128)S(1)}, f32[16,1792]{1,0:T(8,128)}, u32[]{:S(2)}) copy-start(f32[16,1792]{1,0:T(8,128)} %param.13) | copy-start | bytes 344068
  0.0 4.3 %copy-start.2 = (f32[4,16,1792]{2,1,0:T(8,128)S(1)}, f32[4,16,1792]{2,1,0:T(8,128)}, u32[]{:S(2)}) copy-start(f32[4,16,1792]{2,1,0:T(8,128)} %param.9) | copy-start | bytes 1376260
  1.3 3.0 %copy-start.1 = (bf16[8,4,16,1792]{3,2,1,0:T(8,128)(2,1)S(1)}, bf16[8,4,16,1792]{3,2,1,0:T(8,128)(2,1)}, u32[]{:S(2)}) copy-start(bf16[8,4,16,1792]{3,2,1,0:T(8,128)(2,1)} %param.8) | copy-start | bytes 5505028
  2.3 2.6 %copy-start.6 = (f32[16,1792]{1,0:T(8,128)S(1)}, f32[16,1792]{1,0:T(8,128)}, u32[]{:S(2)}) copy-start(f32[16,1792]{1,0:T(8,128)} %param.10) | copy-start | bytes 344068
  2.3 2.6 %copy-start.7 = (s32[16,1792]{1,0:T(8,128)S(1)}, s32[16,1792]{1,0:T(8,128)}, u32[]{:S(2)}) copy-start(s32[16,1792]{1,0:T(8,128)} %param.11) | copy-start | bytes 344068
  2.3 22.0 %collective-permute-start.3 = (f32[80,1792]{1,0:T(8,128)}, f32[80,1792]{1,0:T(8,128)S(1)}, u32[]{:S(2)}, u32[]{:S(2)}) collective-permute-start(f32[80,1792]{1,0:T(8,128)} %pad_maximum_fusion.3), channel_id=1, source_target_pairs={{1,0},{2,1},{3,2},{4,3},{5,4},{6,5},{7,6},{9,8},{10,9},{11,10},{12... | collective-permute-start | bytes 1720328 | tf_op jit(solution)/shard_map/ppermute | solution.py:16
  6.3 5.4 %copy-start.5 = (f32[4,1792]{1,0:T(4,128)S(1)}, f32[4,1792]{1,0:T(4,128)}, u32[]{:S(2)}) copy-start(f32[4,1792]{1,0:T(4,128)} %get-tuple-element.51) | copy-start | bytes 86020
  6.3 9.1 %collective-permute-start.1 = (f32[36,1792]{1,0:T(8,128)}, f32[36,1792]{1,0:T(8,128)S(1)}, u32[]{:S(2)}, u32[]{:S(2)}) collective-permute-start(f32[36,1792]{1,0:T(8,128)} %pad_maximum_fusion.6), channel_id=1, source_target_pairs={{1,0},{2,1},{3,2},{4,3},{5,4},{6,5},{7,6},{9,8},{10,9},{11,10},{12... | collective-permute-start | bytes 774152 | tf_op jit(solution)/shard_map/ppermute | solution.py:16
  9.2 15.1 %collective-permute-start.2 = (f32[80,1792]{1,0:T(8,128)}, f32[80,1792]{1,0:T(8,128)S(1)}, u32[]{:S(2)}, u32[]{:S(2)}) collective-permute-start(f32[80,1792]{1,0:T(8,128)} %pad_maximum_fusion.2), channel_id=1, source_target_pairs={{0,1},{1,2},{2,3},{3,4},{4,5},{5,6},{6,7},{8,9},{9,10},{10,11},{11... | collective-permute-start | bytes 1720328 | tf_op jit(solution)/shard_map/ppermute | solution.py:15
  11.8 11.8 %collective-permute-start = (f32[36,1792]{1,0:T(8,128)S(1)}, f32[36,1792]{1,0:T(8,128)S(1)}, u32[]{:S(2)}, u32[]{:S(2)}) collective-permute-start(f32[36,1792]{1,0:T(8,128)S(1)} %pad_maximum_fusion.5), channel_id=1, source_target_pairs={{0,1},{1,2},{2,3},{3,4},{4,5},{5,6},{6,7},{8,9},{9,10},{10,11},{11... | collective-permute-start | bytes 774152 | tf_op jit(solution)/shard_map/ppermute | solution.py:15
  24.4 1.2 %copy-start = (f32[8,16,1792]{2,1,0:T(8,128)S(1)}, f32[8,16,1792]{2,1,0:T(8,128)}, u32[]{:S(2)}) copy-start(f32[8,16,1792]{2,1,0:T(8,128)} %param.7) | copy-start | bytes 2752516
  26.1 0.7 %copy-start.10 = (pred[1792]{0:T(1024)(128)(4,1)S(1)}, pred[1792]{0:T(1024)(128)(4,1)}, u32[]{:S(2)}) copy-start(pred[1792]{0:T(1024)(128)(4,1)} %constant.9.clone.1) | copy-start | bytes 5380
  34.7 11.6 %copy-start.8 = (f32[1,4,1792]{2,1,0:T(4,128)S(1)}, f32[1,4,1792]{2,1,0:T(4,128)}, u32[]{:S(2)}) copy-start(f32[1,4,1792]{2,1,0:T(4,128)} %slice_bitcast_fusion.10) | copy-start | bytes 86020
  34.8 11.6 %copy-start.9 = (f32[1,4,1792]{2,1,0:T(4,128)S(1)}, f32[1,4,1792]{2,1,0:T(4,128)}, u32[]{:S(2)}) copy-start(f32[1,4,1792]{2,1,0:T(4,128)} %slice_bitcast_fusion.11) | copy-start | bytes 86020
  34.8 6.1 %collective-permute-start.4 = (f32[24,1792]{1,0:T(8,128)S(1)}, f32[24,1792]{1,0:T(8,128)S(1)}, u32[]{:S(2)}, u32[]{:S(2)}) collective-permute-start(f32[24,1792]{1,0:T(8,128)S(1)} %fusion.3), channel_id=1, source_target_pairs={{0,8},{8,0},{16,24},{24,16},{1,9},{9,1},{17,25},{25,17},{2,10},{10... | collective-permute-start | bytes 516104 | tf_op jit(solution)/shard_map/ppermute | solution.py:34
  40.9 5.5 %collective-permute-start.5 = (f32[24,1792]{1,0:T(8,128)S(1)}, f32[24,1792]{1,0:T(8,128)S(1)}, u32[]{:S(2)}, u32[]{:S(2)}) collective-permute-start(f32[24,1792]{1,0:T(8,128)S(1)} %add.150), channel_id=1, source_target_pairs={{0,16},{8,24},{16,0},{24,8},{1,17},{9,25},{17,1},{25,9},{2,18},{10... | collective-permute-start | bytes 516104 | tf_op jit(solution)/shard_map/ppermute | solution.py:34

commit v8 on v4

--- a/solution.py
+++ b/solution.py
@@ -27,19 +27,22 @@
 
 def mem_sum(part):
     count = lax.axis_size("mem")
-    if count & (count - 1) or part.shape[-1] % 256:
+    if count & (count - 1):
         return lax.psum(part, "mem")
-    half = part.shape[-1] // 2
-    first, second = part[..., :half], part[..., half:]
-    strides = []
+
+    def partner(stride):
+        return lax.ppermute(part, "mem", [(i, i ^ stride) for i in range(count)])
+
     stride = 1
     while stride < count:
-        strides.append(stride)
-        stride *= 2
-    for up, down in zip(strides, strides[::-1]):
-        first = first + lax.ppermute(first, "mem", [(i, i ^ up) for i in range(count)])
-        second = second + lax.ppermute(second, "mem", [(i, i ^ down) for i in range(count)])
-    return jnp.concatenate([first, second], -1)
+        if stride * 2 < count:
+            near, far, both = partner(stride), partner(2 * stride), partner(3 * stride)
+            part = (part + near) + (far + both)
+            stride *= 4
+        else:
+            part = part + partner(stride)
+            stride *= 2
+    return part
 
 
 def diffuse(values, row_coef, col_coef):

time: 51.9 us -> 49.8 us (0.960)
  local copies, waits for them, and re-layouts: 5.48 us -> 3.56 us
  waiting for transfers between devices: 14.2 us -> 15.6 us
  other arithmetic: 16.8 us -> 16.1 us
  starting transfers between devices: 14.5 us -> 13.8 us
    slice x2 -> x1, local copies, waits for them, and re-layouts: 1.8 us -> 0.02 us  [exchange(): top = above[start:start + size].reshape(shape)]
    ppermute x2, starting transfers between devices: 4.3 us -> 6.04 us  [exchange(): above = lax.ppermute(tail, 'tile', [(i, i + 1) for i in range(count - 1)])]
    ppermute x4 -> x3, starting transfers between devices: 5.2 us -> 3.64 us  [partner(): return lax.ppermute(part, 'mem', [(i, i ^ stride) for i in range(count)])]
    ppermute x2, waiting for transfers between devices: 6.69 us -> 8.1 us  [exchange(): above = lax.ppermute(tail, 'tile', [(i, i + 1) for i in range(count - 1)])]
    ppermute x2, starting transfers between devices: 5.05 us -> 4.08 us  [exchange(): below = lax.ppermute(head, 'tile', [(i + 1, i) for i in range(count - 1)])]
    unnamed x16, local copies, waits for them, and re-layouts: 1.82 us -> 1.08 us
    concatenate x2, other arithmetic: 1.6 us -> 0.87 us  [exchange(): jnp.concatenate([part[..., -width:, :].reshape(-1, cols) for part in part...]
    ppermute x4 -> x3, waiting for transfers between devices: 6.86 us -> 7.51 us  [partner(): return lax.ppermute(part, 'mem', [(i, i ^ stride) for i in range(count)])]
  transfers between devices with their start and end apart: 8 -> 7, of which waited for: 6 -> 3; matrix products, arithmetic and copies ran while one was open for 10% -> 6% of each run, Pallas kernels for 0% -> 0%
where the time goes in v8:
time: 49.8 us; the launch traced here: 49.5 us
  other arithmetic  16.1 us (32%)
  waiting for transfers between devices  15.6 us (31%)
  starting transfers between devices  13.8 us (28%)
  local copies, waits for them, and re-layouts  3.56 us (7%)
    ppermute x2, waiting for transfers between devices, exchange(): above = lax.ppermute(tail, 'tile', [(i, i + 1) for i in range(count - 1)])  8.1 us
    ppermute x3, waiting for transfers between devices, partner(): return lax.ppermute(part, 'mem', [(i, i ^ stride) for i in range(count)])  7.51 us
    ppermute x2, starting transfers between devices, exchange(): above = lax.ppermute(tail, 'tile', [(i, i + 1) for i in range(count - 1)])  6.04 us
    sub x6, other arithmetic, diffuse(): values + jnp.concatenate([col_flux, zeros_col], -1)  4.21 us
    ppermute x2, starting transfers between devices, exchange(): below = lax.ppermute(head, 'tile', [(i + 1, i) for i in range(count - 1)])  4.08 us
    mul x8, other arithmetic, diffuse(): col_coef[..., :, :-1] * (values[..., :, 1:] - values[..., :, :-1])  4.01 us
    ppermute x3, starting transfers between devices, partner(): return lax.ppermute(part, 'mem', [(i, i ^ stride) for i in range(count)])  3.64 us
    reshape x3, local copies, waits for them, and re-layouts, exchange(): part[..., -width:, :].reshape(-1, cols)  2 us
  transfers between devices with their start and end apart: 7, of which 3 were waited for; matrix products, arithmetic and copies ran while one was open for 6% of the time, Pallas kernels for 0%

profile of v8, /device:TPU:8, one launch (start us, length us, event | category | flops | bytes accessed | tf_op | source)
XLA Modules:
  0.0 49.5 jit_solution(6057297879123049254)
XLA Ops:
  0.0 0.0 copy-start.2
  0.0 1.3 %slice_bitcast_fusion.3 = (f32[64,1792]{1,0:T(8,128)S(1)}, f32[64,1792]{1,0:T(8,128)S(1)}) fusion(f32[8,16,1792]{2,1,0:T(8,128)} %param.7), kind=kLoop, calls=%fused_computation.59 | loop fusion | bytes 1835008 | tf_op jit(solution)/shard_map/reshape | solution.py:14
  1.3 0.0 copy-done.4
  1.3 0.0 copy-start.1
  1.3 0.1 select_bitcast_fusion
  1.4 0.0 copy-done.3
  1.4 0.8 %pad_maximum_fusion.3 = f32[80,1792]{1,0:T(8,128)} fusion(f32[16,1792]{1,0:T(8,128)S(1)} %get-tuple-element.10, f32[64,1792]{1,0:T(8,128)S(1)} %get-tuple-element.6), kind=kLoop, calls=%fused_computation.54 | loop fusion | flops 143360 | bytes 1146880 | tf_op jit(solution)/shard_map/concatenate | solution.py:13
  2.3 2.0 %collective-permute-start.3 = (f32[80,1792]{1,0:T(8,128)}, f32[80,1792]{1,0:T(8,128)S(1)}, u32[]{:S(2)}, u32[]{:S(2)}) collective-permute-start(f32[80,1792]{1,0:T(8,128)} %pad_maximum_fusion.3), channel_id=1, source_target_pairs={{1,0},{2,1},{3,2},{4,3},{5,4},{6,5},{7,6},{9,8},{10,9},{11,10},{12... | collective-permute-start | bytes 1720328 | tf_op jit(solution)/shard_map/ppermute | solution.py:16
  4.3 0.0 copy-done.2
  4.4 0.0 copy-done.1
  4.4 0.4 multiply_reduce_fusion
  4.8 0.1 fusion.24
  4.8 0.0 copy-done.6
  4.9 0.0 copy-done.7
  4.9 0.6 %slice_bitcast_fusion.13 = (f32[4,1792]{1,0:T(4,128)}, f32[4,1792]{1,0:T(4,128)S(1)}) fusion(f32[1,16,1792]{2,1,0:T(8,128)S(1)} %multiply_bitcast_fusion), kind=kLoop, calls=%fused_computation.81 | loop fusion | bytes 114688 | tf_op jit(solution)/shard_map/reshape | solution.py:14
  5.5 0.1 reshape.59
  5.6 0.7 %pad_maximum_fusion.6 = f32[36,1792]{1,0:T(8,128)} fusion(f32[4,1792]{1,0:T(4,128)S(1)} %get-tuple-element.12, f32[32,1792]{1,0:T(8,128)S(1)} %reshape.59), kind=kLoop, calls=%fused_computation.61 | loop fusion | flops 64512 | bytes 516096 | tf_op jit(solution)/shard_map/concatenate | solution.py:13
  6.3 2.0 %collective-permute-start.1 = (f32[36,1792]{1,0:T(8,128)}, f32[36,1792]{1,0:T(8,128)S(1)}, u32[]{:S(2)}, u32[]{:S(2)}) collective-permute-start(f32[36,1792]{1,0:T(8,128)} %pad_maximum_fusion.6), channel_id=1, source_target_pairs={{1,0},{2,1},{3,2},{4,3},{5,4},{6,5},{7,6},{9,8},{10,9},{11,10},{12... | collective-permute-start | bytes 774152 | tf_op jit(solution)/shard_map/ppermute | solution.py:16
  8.4 0.9 %pad_maximum_fusion.2 = f32[80,1792]{1,0:T(8,128)} fusion(f32[16,1792]{1,0:T(8,128)S(1)} %get-tuple-element.9, f32[64,1792]{1,0:T(8,128)S(1)} %get-tuple-element.5), kind=kLoop, calls=%fused_computation.53 | loop fusion | flops 143360 | bytes 1146880 | tf_op jit(solution)/shard_map/concatenate | solution.py:14
  9.2 2.4 %collective-permute-start.2 = (f32[80,1792]{1,0:T(8,128)}, f32[80,1792]{1,0:T(8,128)S(1)}, u32[]{:S(2)}, u32[]{:S(2)}) collective-permute-start(f32[80,1792]{1,0:T(8,128)} %pad_maximum_fusion.2), channel_id=1, source_target_pairs={{0,1},{1,2},{2,3},{3,4},{4,5},{5,6},{6,7},{8,9},{9,10},{10,11},{11... | collective-permute-start | bytes 1720328 | tf_op jit(solution)/shard_map/ppermute | solution.py:15
  11.6 0.1 reshape.56
  11.7 0.0 copy-done.5
  11.8 3.6 %collective-permute-start = (f32[36,1792]{1,0:T(8,128)S(1)}, f32[36,1792]{1,0:T(8,128)S(1)}, u32[]{:S(2)}, u32[]{:S(2)}) collective-permute-start(f32[36,1792]{1,0:T(8,128)S(1)} %pad_maximum_fusion.5), channel_id=1, source_target_pairs={{0,1},{1,2},{2,3},{3,4},{4,5},{5,6},{6,7},{8,9},{9,10},{10,11},{11... | collective-permute-start | bytes 774152 | tf_op jit(solution)/shard_map/ppermute | solution.py:15
  15.4 0.0 collective-permute-done.1
  15.4 8.1 %collective-permute-done = f32[36,1792]{1,0:T(8,128)S(1)} collective-permute-done((f32[36,1792]{1,0:T(8,128)S(1)}, f32[36,1792]{1,0:T(8,128)S(1)}, u32[]{:S(2)}, u32[]{:S(2)}) %collective-permute-start) | collective-permute-done | bytes 258080 | tf_op jit(solution)/shard_map/ppermute | solution.py:15
  23.6 0.1 reshape.58
  23.7 0.1 reshape.61
  23.7 0.0 collective-permute-done.3
  23.8 0.0 collective-permute-done.2
  23.8 0.0 copy-start
  24.0 1.0 %copy-done = f32[8,16,1792]{2,1,0:T(8,128)S(1)} copy-done((f32[8,16,1792]{2,1,0:T(8,128)S(1)}, f32[8,16,1792]{2,1,0:T(8,128)}, u32[]{:S(2)}) %copy-start) | copy-done | bytes 917528
  25.0 0.1 pad_maximum_fusion
  25.2 0.2 fusion.7
  25.4 0.6 %fusion.6 = f32[8,32,1791]{2,1,0:T(8,128)S(1)} fusion(f32[8,32,1792]{2,1,0:T(8,128)S(1)} %pad_maximum_fusion, f32[32,1791]{1,0:T(8,128)S(1)} %bitcast.43), kind=kLoop, calls=%fused_computation.14 | loop fusion | flops 916992 | bytes 5731200 | tf_op jit(solution)/shard_map/mul | solution.py:50
  26.0 0.9 %pad_subtract_fusion.2 = f32[8,32,1792]{2,1,0:T(8,128)S(1)} fusion(f32[8,32,1791]{2,1,0:T(8,128)S(1)} %fusion.6, f32[8,31,1792]{2,1,0:T(8,128)S(1)} %fusion.7, f32[8,8,1792]{2,1,0:T(8,128)S(1)} %slice_bitcast_fusion, f32[8,16,1792]{2,1,0:T(8,128)S(1)} %copy-done, f32[8,8,1792]{2,1,0:T(8,128)S(1)} %slice_bitcast_fusion.1), kind=kLoop, calls=%fused_computation.20 | loop fusion | flops 2752512 | bytes 7281664 | tf_op jit(solution)/shard_map/sub | solution.py:59
  26.9 0.2 fusion.5
  27.1 0.6 %fusion.4 = f32[8,32,1791]{2,1,0:T(8,128)S(1)} fusion(f32[8,32,1792]{2,1,0:T(8,128)S(1)} %pad_subtract_fusion.2, f32[32,1791]{1,0:T(8,128)S(1)} %bitcast.44), kind=kLoop, calls=%fused_computation.10 | loop fusion | flops 916992 | bytes 5731200 | tf_op jit(solution)/shard_map/mul | solution.py:50
  27.7 0.9 %pad_subtract_fusion.1 = f32[8,32,1792]{2,1,0:T(8,128)S(1)} fusion(f32[8,32,1791]{2,1,0:T(8,128)S(1)} %fusion.4, f32[8,31,1792]{2,1,0:T(8,128)S(1)} %fusion.5, f32[8,32,1792]{2,1,0:T(8,128)S(1)} %pad_subtract_fusion.2), kind=kLoop, calls=%fused_computation.19 | loop fusion | flops 1835008 | bytes 7281664 | tf_op jit(solution)/shard_map/sub | solution.py:59
  28.7 0.2 fusion.3
  28.9 0.6 %fusion.2 = f32[8,32,1791]{2,1,0:T(8,128)S(1)} fusion(f32[8,32,1792]{2,1,0:T(8,128)S(1)} %pad_subtract_fusion.1, f32[32,1791]{1,0:T(8,128)S(1)} %bitcast.45), kind=kLoop, calls=%fused_computation.6 | loop fusion | flops 916992 | bytes 5731200 | tf_op jit(solution)/shard_map/mul | solution.py:50
  29.5 0.9 %pad_subtract_fusion = f32[8,32,1792]{2,1,0:T(8,128)S(1)} fusion(f32[8,32,1791]{2,1,0:T(8,128)S(1)} %fusion.2, f32[8,31,1792]{2,1,0:T(8,128)S(1)} %fusion.3, f32[8,32,1792]{2,1,0:T(8,128)S(1)} %pad_subtract_fusion.1), kind=kLoop, calls=%fused_computation.18 | loop fusion | flops 1835008 | bytes 7281664 | tf_op jit(solution)/shard_map/sub | solution.py:59
  30.5 0.2 fusion.1
  30.7 0.6 %fusion = f32[8,32,1791]{2,1,0:T(8,128)S(1)} fusion(f32[8,32,1792]{2,1,0:T(8,128)S(1)} %pad_subtract_fusion, f32[32,1791]{1,0:T(8,128)S(1)} %bitcast.46), kind=kLoop, calls=%fused_computation.2 | loop fusion | flops 916992 | bytes 5731200 | tf_op jit(solution)/shard_map/mul | solution.py:50
  31.3 1.2 %fusion.17 = f32[24,1792]{1,0:T(8,128)S(1)} fusion(f32[8,32,1791]{2,1,0:T(8,128)S(1)} %fusion, f32[8,31,1792]{2,1,0:T(8,128)S(1)} %fusion.1, f32[8,32,1792]{2,1,0:T(8,128)S(1)} %pad_subtract_fusion, f32[8,4,1792]{2,1,0:T(4,128)S(1)} %reshape.61, f32[8,16,1792]{2,1,0:T(8,128)S(1)} %multiply_reduce_fusion, f32[8,4,1792]{2,1,0:T(4,128)S(1)} %reshape.58), kind=kLoop, calls=%fused_computation.39 | loop fusion | flops 2709504 | bytes 6536192 | tf_op jit(solution)/shard_map/reduce_sum | solution.py:86
  32.5 2.1 %collective-permute-start.4 = (f32[24,1792]{1,0:T(8,128)S(1)}, f32[24,1792]{1,0:T(8,128)S(1)}, u32[]{:S(2)}, u32[]{:S(2)}) collective-permute-start(f32[24,1792]{1,0:T(8,128)S(1)} %fusion.17), channel_id=1, source_target_pairs={{0,8},{8,0},{16,24},{24,16},{1,9},{9,1},{17,25},{25,17},{2,10},{10... | collective-permute-start | bytes 516104 | tf_op jit(solution)/shard_map/ppermute | solution.py:34
  34.6 1.5 %collective-permute-start.5 = (f32[24,1792]{1,0:T(8,128)S(1)}, f32[24,1792]{1,0:T(8,128)S(1)}, u32[]{:S(2)}, u32[]{:S(2)}) collective-permute-start(f32[24,1792]{1,0:T(8,128)S(1)} %fusion.17), channel_id=1, source_target_pairs={{0,16},{8,24},{16,0},{24,8},{1,17},{9,25},{17,1},{25,9},{2,18},{10... | collective-permute-start | bytes 516104 | tf_op jit(solution)/shard_map/ppermute | solution.py:34
  36.1 0.0 collective-permute-start.6
  36.2 3.7 %collective-permute-done.4 = f32[24,1792]{1,0:T(8,128)S(1)} collective-permute-done((f32[24,1792]{1,0:T(8,128)S(1)}, f32[24,1792]{1,0:T(8,128)S(1)}, u32[]{:S(2)}, u32[]{:S(2)}) %collective-permute-start.4) | collective-permute-done | bytes 172064 | tf_op jit(solution)/shard_map/ppermute | solution.py:34
  39.9 3.8 %collective-permute-done.5 = f32[24,1792]{1,0:T(8,128)S(1)} collective-permute-done((f32[24,1792]{1,0:T(8,128)S(1)}, f32[24,1792]{1,0:T(8,128)S(1)}, u32[]{:S(2)}, u32[]{:S(2)}) %collective-permute-start.5) | collective-permute-done | bytes 172064 | tf_op jit(solution)/shard_map/ppermute | solution.py:34
  43.7 0.0 collective-permute-done.6
  43.7 0.1 fusion.20
  43.8 0.2 fusion.18
  44.0 0.2 fusion.15
  44.2 0.4 fusion.14
  44.6 0.5 pad_subtract_fusion.7
  45.1 0.2 fusion.13
  45.3 0.4 fusion.12
  45.7 0.5 pad_subtract_fusion.6
  46.2 0.2 fusion.11
  46.4 0.4 fusion.10
  46.9 0.5 pad_subtract_fusion.5
  47.3 0.2 fusion.9
  47.5 0.4 fusion.8
  48.0 1.5 %fusion.19 = f32[8,16,1792]{2,1,0:T(8,128)} fusion(f32[8,16,1792]{2,1,0:T(8,128)S(1)} %copy-done, f32[8,24,1791]{2,1,0:T(8,128)S(1)} %fusion.8, f32[8,23,1792]{2,1,0:T(8,128)S(1)} %fusion.9, f32[8,24,1792]{2,1,0:T(8,128)S(1)} %pad_subtract_fusion.5), kind=kLoop, calls=%fused_computation.49 | loop fusion | flops 1146880 | bytes 5446912 | tf_op jit(solution)/shard_map/add | solution.py:89
  (22 shorter events, 0.3 us)
Async XLA Ops:
  0.0 1.3 %copy-start.4 = (f32[16,1792]{1,0:T(8,128)S(1)}, f32[16,1792]{1,0:T(8,128)}, u32[]{:S(2)}) copy-start(f32[16,1792]{1,0:T(8,128)} %param.12) | copy-start | bytes 344068
  0.0 1.4 %copy-start.3 = (f32[16,1792]{1,0:T(8,128)S(1)}, f32[16,1792]{1,0:T(8,128)}, u32[]{:S(2)}) copy-start(f32[16,1792]{1,0:T(8,128)} %param.13) | copy-start | bytes 344068
  0.0 4.3 %copy-start.2 = (f32[4,16,1792]{2,1,0:T(8,128)S(1)}, f32[4,16,1792]{2,1,0:T(8,128)}, u32[]{:S(2)}) copy-start(f32[4,16,1792]{2,1,0:T(8,128)} %param.9) | copy-start | bytes 1376260
  1.3 3.0 %copy-start.1 = (bf16[8,4,16,1792]{3,2,1,0:T(8,128)(2,1)S(1)}, bf16[8,4,16,1792]{3,2,1,0:T(8,128)(2,1)}, u32[]{:S(2)}) copy-start(bf16[8,4,16,1792]{3,2,1,0:T(8,128)(2,1)} %param.8) | copy-start | bytes 5505028
  2.3 2.6 %copy-start.6 = (f32[16,1792]{1,0:T(8,128)S(1)}, f32[16,1792]{1,0:T(8,128)}, u32[]{:S(2)}) copy-start(f32[16,1792]{1,0:T(8,128)} %param.10) | copy-start | bytes 344068
  2.3 2.6 %copy-start.7 = (s32[16,1792]{1,0:T(8,128)S(1)}, s32[16,1792]{1,0:T(8,128)}, u32[]{:S(2)}) copy-start(s32[16,1792]{1,0:T(8,128)} %param.11) | copy-start | bytes 344068
  2.3 21.4 %collective-permute-start.3 = (f32[80,1792]{1,0:T(8,128)}, f32[80,1792]{1,0:T(8,128)S(1)}, u32[]{:S(2)}, u32[]{:S(2)}) collective-permute-start(f32[80,1792]{1,0:T(8,128)} %pad_maximum_fusion.3), channel_id=1, source_target_pairs={{1,0},{2,1},{3,2},{4,3},{5,4},{6,5},{7,6},{9,8},{10,9},{11,10},{12... | collective-permute-start | bytes 1720328 | tf_op jit(solution)/shard_map/ppermute | solution.py:16
  6.3 5.4 %copy-start.5 = (f32[4,1792]{1,0:T(4,128)S(1)}, f32[4,1792]{1,0:T(4,128)}, u32[]{:S(2)}) copy-start(f32[4,1792]{1,0:T(4,128)} %get-tuple-element.11) | copy-start | bytes 86020
  6.3 9.1 %collective-permute-start.1 = (f32[36,1792]{1,0:T(8,128)}, f32[36,1792]{1,0:T(8,128)S(1)}, u32[]{:S(2)}, u32[]{:S(2)}) collective-permute-start(f32[36,1792]{1,0:T(8,128)} %pad_maximum_fusion.6), channel_id=1, source_target_pairs={{1,0},{2,1},{3,2},{4,3},{5,4},{6,5},{7,6},{9,8},{10,9},{11,10},{12... | collective-permute-start | bytes 774152 | tf_op jit(solution)/shard_map/ppermute | solution.py:16
  9.2 14.5 %collective-permute-start.2 = (f32[80,1792]{1,0:T(8,128)}, f32[80,1792]{1,0:T(8,128)S(1)}, u32[]{:S(2)}, u32[]{:S(2)}) collective-permute-start(f32[80,1792]{1,0:T(8,128)} %pad_maximum_fusion.2), channel_id=1, source_target_pairs={{0,1},{1,2},{2,3},{3,4},{4,5},{5,6},{6,7},{8,9},{9,10},{10,11},{11... | collective-permute-start | bytes 1720328 | tf_op jit(solution)/shard_map/ppermute | solution.py:15
  11.8 11.8 %collective-permute-start = (f32[36,1792]{1,0:T(8,128)S(1)}, f32[36,1792]{1,0:T(8,128)S(1)}, u32[]{:S(2)}, u32[]{:S(2)}) collective-permute-start(f32[36,1792]{1,0:T(8,128)S(1)} %pad_maximum_fusion.5), channel_id=1, source_target_pairs={{0,1},{1,2},{2,3},{3,4},{4,5},{5,6},{6,7},{8,9},{9,10},{10,11},{11... | collective-permute-start | bytes 774152 | tf_op jit(solution)/shard_map/ppermute | solution.py:15
  23.8 1.2 %copy-start = (f32[8,16,1792]{2,1,0:T(8,128)S(1)}, f32[8,16,1792]{2,1,0:T(8,128)}, u32[]{:S(2)}) copy-start(f32[8,16,1792]{2,1,0:T(8,128)} %param.7) | copy-start | bytes 2752516
  32.5 7.4 %collective-permute-start.4 = (f32[24,1792]{1,0:T(8,128)S(1)}, f32[24,1792]{1,0:T(8,128)S(1)}, u32[]{:S(2)}, u32[]{:S(2)}) collective-permute-start(f32[24,1792]{1,0:T(8,128)S(1)} %fusion.17), channel_id=1, source_target_pairs={{0,8},{8,0},{16,24},{24,16},{1,9},{9,1},{17,25},{25,17},{2,10},{10... | collective-permute-start | bytes 516104 | tf_op jit(solution)/shard_map/ppermute | solution.py:34
  34.6 9.1 %collective-permute-start.5 = (f32[24,1792]{1,0:T(8,128)S(1)}, f32[24,1792]{1,0:T(8,128)S(1)}, u32[]{:S(2)}, u32[]{:S(2)}) collective-permute-start(f32[24,1792]{1,0:T(8,128)S(1)} %fusion.17), channel_id=1, source_target_pairs={{0,16},{8,24},{16,0},{24,8},{1,17},{9,25},{17,1},{25,9},{2,18},{10... | collective-permute-start | bytes 516104 | tf_op jit(solution)/shard_map/ppermute | solution.py:34
  36.1 7.6 %collective-permute-start.6 = (f32[24,1792]{1,0:T(8,128)S(1)}, f32[24,1792]{1,0:T(8,128)S(1)}, u32[]{:S(2)}, u32[]{:S(2)}) collective-permute-start(f32[24,1792]{1,0:T(8,128)S(1)} %fusion.17), channel_id=1, source_target_pairs={{0,24},{8,16},{16,8},{24,0},{1,25},{9,17},{17,9},{25,1},{2,26},{10... | collective-permute-start | bytes 516104 | tf_op jit(solution)/shard_map/ppermute | solution.py:34

commit v9 on v8

--- a/solution.py
+++ b/solution.py
@@ -80,6 +80,7 @@
     mix = jnp.sum(perturbations.astype(jnp.float32) * jacobian[None], axis=1)
     weights = radar_mask.astype(jnp.float32) * obs_weight
     field, coef_band = exchange([controls, stacked], 2 * STEPS)
+    field, mix, weights = lax.optimization_barrier((field, mix, weights))
     mix_band, weights_band = exchange([mix, weights[None]], STEPS)
     reach = row_count + 2 * STEPS
     localized = localize(field, coef_band)[:, STEPS : STEPS + reach]

time: 49.8 us -> 68.9 us (1.38)
  the two profiles are of different devices: /device:TPU:8 before, /device:TPU:9 now
where the time goes in v9:
time: 68.9 us; the launch traced here: 68.3 us
  other arithmetic  22.7 us (33%)
  waiting for transfers between devices  17.4 us (25%)
  starting transfers between devices  15 us (22%)
  local copies, waits for them, and re-layouts  12.8 us (19%)
    ppermute x2, waiting for transfers between devices, exchange(): below = lax.ppermute(head, 'tile', [(i + 1, i) for i in range(count - 1)])  10.3 us
    ppermute x2, starting transfers between devices, exchange(): above = lax.ppermute(tail, 'tile', [(i, i + 1) for i in range(count - 1)])  7.48 us
    ppermute x3, waiting for transfers between devices, partner(): return lax.ppermute(part, 'mem', [(i, i ^ stride) for i in range(count)])  6.1 us
    mul x8, other arithmetic, diffuse(): col_coef[..., :, :-1] * (values[..., :, 1:] - values[..., :, :-1])  5.25 us
    ppermute x2, starting transfers between devices, exchange(): below = lax.ppermute(head, 'tile', [(i + 1, i) for i in range(count - 1)])  4.81 us
    reduce_sum x1, other arithmetic, per_device(): reflect = mem_sum(jnp.sum(mix_band * localized, 0))  4.37 us
    sub x6, other arithmetic, diffuse(): values + jnp.concatenate([col_flux, zeros_col], -1)  4.28 us
    reshape x3, local copies, waits for them, and re-layouts, exchange(): part[..., -width:, :].reshape(-1, cols)  2.98 us
  transfers between devices with their start and end apart: 7, of which 5 were waited for; matrix products, arithmetic and copies ran while one was open for 10% of the time, Pallas kernels for 0%

profile of v9, /device:TPU:9, one launch (start us, length us, event | category | flops | bytes accessed | tf_op | source)
XLA Modules:
  0.0 68.3 jit_solution(17128495370572294007)
XLA Ops:
  0.0 1.3 %slice_bitcast_fusion.3 = (f32[64,1792]{1,0:T(8,128)S(1)}, f32[64,1792]{1,0:T(8,128)S(1)}) fusion(f32[8,16,1792]{2,1,0:T(8,128)} %param.7), kind=kLoop, calls=%fused_computation.57 | loop fusion | bytes 1835008 | tf_op jit(solution)/shard_map/reshape | solution.py:14
  1.3 0.1 select_bitcast_fusion
  1.4 0.0 copy-start.8
  1.4 0.0 copy-start.9
  1.4 0.0 copy-start.2
  1.4 0.0 copy-start.5
  1.5 2.7 %collective-permute-start.1 = (f32[80,1792]{1,0:T(8,128)S(1)}, f32[80,1792]{1,0:T(8,128)S(1)}, u32[]{:S(2)}, u32[]{:S(2)}) collective-permute-start(f32[80,1792]{1,0:T(8,128)S(1)} %pad_maximum_fusion.3), channel_id=1, source_target_pairs={{1,0},{2,1},{3,2},{4,3},{5,4},{6,5},{7,6},{9,8},{10,9},{11,10},{12... | collective-permute-start | bytes 1720328 | tf_op jit(solution)/shard_map/ppermute | solution.py:16
  4.3 3.1 %collective-permute-start = (f32[80,1792]{1,0:T(8,128)S(1)}, f32[80,1792]{1,0:T(8,128)S(1)}, u32[]{:S(2)}, u32[]{:S(2)}) collective-permute-start(f32[80,1792]{1,0:T(8,128)S(1)} %pad_maximum_fusion.2), channel_id=1, source_target_pairs={{0,1},{1,2},{2,3},{3,4},{4,5},{5,6},{6,7},{8,9},{9,10},{10,11},{11... | collective-permute-start | bytes 1720328 | tf_op jit(solution)/shard_map/ppermute | solution.py:15
  7.4 0.0 copy-done.2
  7.4 0.4 multiply_reduce_fusion
  7.8 5.2 %collective-permute-done.1 = f32[80,1792]{1,0:T(8,128)S(1)} collective-permute-done((f32[80,1792]{1,0:T(8,128)S(1)}, f32[80,1792]{1,0:T(8,128)S(1)}, u32[]{:S(2)}, u32[]{:S(2)}) %collective-permute-start.1) | collective-permute-done | bytes 573472 | tf_op jit(solution)/shard_map/ppermute | solution.py:16
  13.1 0.9 %collective-permute-done = f32[80,1792]{1,0:T(8,128)S(1)} collective-permute-done((f32[80,1792]{1,0:T(8,128)S(1)}, f32[80,1792]{1,0:T(8,128)S(1)}, u32[]{:S(2)}, u32[]{:S(2)}) %collective-permute-start) | collective-permute-done | bytes 573472 | tf_op jit(solution)/shard_map/ppermute | solution.py:15
  14.1 0.0 copy-start
  14.2 1.0 %copy-done = f32[8,16,1792]{2,1,0:T(8,128)S(1)} copy-done((f32[8,16,1792]{2,1,0:T(8,128)S(1)}, f32[8,16,1792]{2,1,0:T(8,128)}, u32[]{:S(2)}) %copy-start) | copy-done | bytes 917528
  15.2 0.1 pad_maximum_fusion
  15.4 0.2 subtract_multiply_fusion.1
  15.6 0.6 subtract_multiply_fusion
  16.2 0.9 %pad_subtract_fusion.2 = f32[8,32,1792]{2,1,0:T(8,128)S(1)} fusion(f32[8,32,1791]{2,1,0:T(8,128)S(1)} %subtract_multiply_fusion, f32[8,31,1792]{2,1,0:T(8,128)S(1)} %subtract_multiply_fusion.1, f32[8,32,1792]{2,1,0:T(8,128)S(1)} %pad_maximum_fusion), kind=kLoop, calls=%fused_computation.16 | loop fusion | flops 1835008 | bytes 7281664 | tf_op jit(solution)/shard_map/sub | solution.py:59
  17.2 0.2 fusion.5
  17.4 0.6 fusion.4
  18.0 0.9 %pad_subtract_fusion.1 = f32[8,32,1792]{2,1,0:T(8,128)S(1)} fusion(f32[8,32,1791]{2,1,0:T(8,128)S(1)} %fusion.4, f32[8,31,1792]{2,1,0:T(8,128)S(1)} %fusion.5, f32[8,32,1792]{2,1,0:T(8,128)S(1)} %pad_subtract_fusion.2), kind=kLoop, calls=%fused_computation.15 | loop fusion | flops 1835008 | bytes 7281664 | tf_op jit(solution)/shard_map/sub | solution.py:59
  19.0 0.2 fusion.3
  19.2 0.6 fusion.2
  19.8 0.9 %pad_subtract_fusion = f32[8,32,1792]{2,1,0:T(8,128)S(1)} fusion(f32[8,32,1791]{2,1,0:T(8,128)S(1)} %fusion.2, f32[8,31,1792]{2,1,0:T(8,128)S(1)} %fusion.3, f32[8,32,1792]{2,1,0:T(8,128)S(1)} %pad_subtract_fusion.1), kind=kLoop, calls=%fused_computation.14 | loop fusion | flops 1835008 | bytes 7281664 | tf_op jit(solution)/shard_map/sub | solution.py:59
  20.7 1.5 %fusion.1 = f32[8,31,1792]{2,1,0:T(8,128)} fusion(f32[8,32,1792]{2,1,0:T(8,128)S(1)} %pad_subtract_fusion, f32[31,1792]{1,0:T(8,128)S(1)} %slice_bitcast_fusion.5), kind=kLoop, calls=%fused_computation.4 | loop fusion | flops 888832 | bytes 5555200 | tf_op jit(solution)/shard_map/mul | solution.py:49
  22.2 1.8 %fusion = f32[8,32,1791]{2,1,0:T(8,128)} fusion(f32[8,32,1792]{2,1,0:T(8,128)S(1)} %pad_subtract_fusion, f32[32,1791]{1,0:T(8,128)S(1)} %bitcast.45), kind=kLoop, calls=%fused_computation.2 | loop fusion | flops 916992 | bytes 5731200 | tf_op jit(solution)/shard_map/mul | solution.py:50
  24.1 0.8 %fusion.22 = (f32[8,4,1792]{2,1,0:T(4,128)}, f32[8,4,1792]{2,1,0:T(4,128)}) fusion(f32[8,16,1792]{2,1,0:T(8,128)S(1)} %multiply_reduce_fusion), kind=kLoop, calls=%fused_computation.81 | loop fusion | bytes 917504 | tf_op jit(solution)/shard_map/slice | solution.py:14
  24.9 1.7 %reshape.62 = f32[32,1792]{1,0:T(8,128)} reshape(f32[8,4,1792]{2,1,0:T(4,128)} %get-tuple-element.11) | data formatting | bytes 458752 | tf_op jit(solution)/shard_map/reshape | solution.py:14
  26.7 1.7 %pad_maximum_fusion.5 = f32[36,1792]{1,0:T(8,128)} fusion(f32[4,1792]{1,0:T(4,128)S(1)} %get-tuple-element.17, f32[32,1792]{1,0:T(8,128)} %reshape.62), kind=kLoop, calls=%fused_computation.58 | loop fusion | flops 64512 | bytes 516096 | tf_op jit(solution)/shard_map/concatenate | solution.py:14
  28.3 4.4 %collective-permute-start.2 = (f32[36,1792]{1,0:T(8,128)}, f32[36,1792]{1,0:T(8,128)}, u32[]{:S(2)}, u32[]{:S(2)}) collective-permute-start(f32[36,1792]{1,0:T(8,128)} %pad_maximum_fusion.5), channel_id=1, source_target_pairs={{0,1},{1,2},{2,3},{3,4},{4,5},{5,6},{6,7},{8,9},{9,10},{10,11},{11... | collective-permute-start | bytes 774152 | tf_op jit(solution)/shard_map/ppermute | solution.py:15
  32.7 1.7 %reshape.65 = f32[32,1792]{1,0:T(8,128)} reshape(f32[8,4,1792]{2,1,0:T(4,128)} %get-tuple-element.12) | data formatting | bytes 458752 | tf_op jit(solution)/shard_map/reshape | solution.py:13
  34.4 1.7 %pad_maximum_fusion.6 = f32[36,1792]{1,0:T(8,128)} fusion(f32[4,1792]{1,0:T(4,128)S(1)} %get-tuple-element.18, f32[32,1792]{1,0:T(8,128)} %reshape.65), kind=kLoop, calls=%fused_computation.59 | loop fusion | flops 64512 | bytes 516096 | tf_op jit(solution)/shard_map/concatenate | solution.py:13
  36.1 2.1 %collective-permute-start.3 = (f32[36,1792]{1,0:T(8,128)}, f32[36,1792]{1,0:T(8,128)}, u32[]{:S(2)}, u32[]{:S(2)}) collective-permute-start(f32[36,1792]{1,0:T(8,128)} %pad_maximum_fusion.6), channel_id=1, source_target_pairs={{1,0},{2,1},{3,2},{4,3},{5,4},{6,5},{7,6},{9,8},{10,9},{11,10},{12... | collective-permute-start | bytes 774152 | tf_op jit(solution)/shard_map/ppermute | solution.py:16
  38.2 0.0 collective-permute-done.2
  38.2 1.0 %slice.262 = f32[32,1792]{1,0:T(8,128)S(1)} slice(f32[36,1792]{1,0:T(8,128)} %collective-permute-done.2), slice={[0:32], [0:1792]} | slice | bytes 458752 | tf_op jit(solution)/shard_map/slice | solution.py:21
  39.2 0.1 reshape.64
  39.3 5.1 %collective-permute-done.3 = f32[36,1792]{1,0:T(8,128)} collective-permute-done((f32[36,1792]{1,0:T(8,128)}, f32[36,1792]{1,0:T(8,128)}, u32[]{:S(2)}, u32[]{:S(2)}) %collective-permute-start.3) | collective-permute-done | bytes 258080 | tf_op jit(solution)/shard_map/ppermute | solution.py:16
  44.3 1.6 %slice.264 = f32[32,1792]{1,0:T(8,128)} slice(f32[36,1792]{1,0:T(8,128)} %collective-permute-done.3), slice={[0:32], [0:1792]} | slice | bytes 458752 | tf_op jit(solution)/shard_map/slice | solution.py:22
  46.0 1.0 %reshape.67 = f32[8,4,1792]{2,1,0:T(4,128)S(1)} reshape(f32[32,1792]{1,0:T(8,128)} %slice.264) | data formatting | bytes 458752 | tf_op jit(solution)/shard_map/reshape | solution.py:22
  47.0 4.4 %fusion.15 = f32[24,1792]{1,0:T(8,128)S(1)} fusion(f32[8,32,1791]{2,1,0:T(8,128)} %fusion, f32[8,31,1792]{2,1,0:T(8,128)} %fusion.1, f32[8,32,1792]{2,1,0:T(8,128)S(1)} %pad_subtract_fusion, f32[8,4,1792]{2,1,0:T(4,128)S(1)} %reshape.67, f32[8,16,1792]{2,1,0:T(8,128)S(1)} %multiply_reduce_fusion, f32[8,4,1792]{2,1,0:T(4,128)S(1)} %reshape.64), kind=kLoop, calls=%fused_computation.37 | loop fusion | flops 2709504 | bytes 6536192 | tf_op jit(solution)/shard_map/reduce_sum | solution.py:87
  51.4 1.3 %collective-permute-start.4 = (f32[24,1792]{1,0:T(8,128)S(1)}, f32[24,1792]{1,0:T(8,128)S(1)}, u32[]{:S(2)}, u32[]{:S(2)}) collective-permute-start(f32[24,1792]{1,0:T(8,128)S(1)} %fusion.15), channel_id=1, source_target_pairs={{0,8},{8,0},{16,24},{24,16},{1,9},{9,1},{17,25},{25,17},{2,10},{10... | collective-permute-start | bytes 516104 | tf_op jit(solution)/shard_map/ppermute | solution.py:34
  52.6 1.2 %collective-permute-start.5 = (f32[24,1792]{1,0:T(8,128)S(1)}, f32[24,1792]{1,0:T(8,128)S(1)}, u32[]{:S(2)}, u32[]{:S(2)}) collective-permute-start(f32[24,1792]{1,0:T(8,128)S(1)} %fusion.15), channel_id=1, source_target_pairs={{0,16},{8,24},{16,0},{24,8},{1,17},{9,25},{17,1},{25,9},{2,18},{10... | collective-permute-start | bytes 516104 | tf_op jit(solution)/shard_map/ppermute | solution.py:34
  53.9 0.2 collective-permute-start.6
  54.1 0.8 %slice_bitcast_fusion.11 = f32[1,4,1792]{2,1,0:T(4,128)S(1)} fusion(f32[36,1792]{1,0:T(8,128)} %collective-permute-done.2), kind=kLoop, calls=%fused_computation.77 | loop fusion | bytes 57344 | tf_op jit(solution)/shard_map/reshape | solution.py:21
  54.9 0.8 %slice_bitcast_fusion.10 = f32[1,4,1792]{2,1,0:T(4,128)S(1)} fusion(f32[36,1792]{1,0:T(8,128)} %collective-permute-done.3), kind=kLoop, calls=%fused_computation.76 | loop fusion | bytes 57344 | tf_op jit(solution)/shard_map/reshape | solution.py:22
  55.7 1.9 %collective-permute-done.4 = f32[24,1792]{1,0:T(8,128)S(1)} collective-permute-done((f32[24,1792]{1,0:T(8,128)S(1)}, f32[24,1792]{1,0:T(8,128)S(1)}, u32[]{:S(2)}, u32[]{:S(2)}) %collective-permute-start.4) | collective-permute-done | bytes 172064 | tf_op jit(solution)/shard_map/ppermute | solution.py:34
  57.6 4.2 %collective-permute-done.5 = f32[24,1792]{1,0:T(8,128)S(1)} collective-permute-done((f32[24,1792]{1,0:T(8,128)S(1)}, f32[24,1792]{1,0:T(8,128)S(1)}, u32[]{:S(2)}, u32[]{:S(2)}) %collective-permute-start.5) | collective-permute-done | bytes 172064 | tf_op jit(solution)/shard_map/ppermute | solution.py:34
  61.8 0.0 collective-permute-done.6
  61.8 0.1 fusion.18
  61.9 0.2 fusion.16
  62.2 0.2 fusion.13
  62.4 0.4 fusion.12
  62.8 0.5 pad_subtract_fusion.7
  63.3 0.2 fusion.11
  63.5 0.4 fusion.10
  63.9 0.5 pad_subtract_fusion.6
  64.4 0.2 fusion.9
  64.6 0.4 fusion.8
  65.0 0.5 pad_subtract_fusion.5
  65.5 0.2 fusion.7
  65.7 0.0 copy-start.1
  65.7 0.4 fusion.6
  66.1 0.7 %copy-done.1 = f32[8,16,1792]{2,1,0:T(8,128)S(1)} copy-done((f32[8,16,1792]{2,1,0:T(8,128)S(1)}, f32[8,16,1792]{2,1,0:T(8,128)}, u32[]{:S(2)}) %copy-start.1) | copy-done | bytes 917528
  66.8 1.5 %fusion.17 = f32[8,16,1792]{2,1,0:T(8,128)} fusion(f32[8,16,1792]{2,1,0:T(8,128)S(1)} %copy-done.1, f32[8,24,1791]{2,1,0:T(8,128)S(1)} %fusion.6, f32[8,23,1792]{2,1,0:T(8,128)S(1)} %fusion.7, f32[8,24,1792]{2,1,0:T(8,128)S(1)} %pad_subtract_fusion.5), kind=kLoop, calls=%fused_computation.47 | loop fusion | flops 1146880 | bytes 5446912 | tf_op jit(solution)/shard_map/add | solution.py:90
  (26 shorter events, 0.4 us)
Async XLA Ops:
  0.0 1.3 %copy-start.7 = (f32[16,1792]{1,0:T(8,128)S(1)}, f32[16,1792]{1,0:T(8,128)}, u32[]{:S(2)}) copy-start(f32[16,1792]{1,0:T(8,128)} %param.12) | copy-start | bytes 344068
  0.0 1.4 %copy-start.6 = (f32[16,1792]{1,0:T(8,128)S(1)}, f32[16,1792]{1,0:T(8,128)}, u32[]{:S(2)}) copy-start(f32[16,1792]{1,0:T(8,128)} %param.13) | copy-start | bytes 344068
  1.4 6.0 %copy-start.8 = (f32[16,1792]{1,0:T(8,128)S(1)}, f32[16,1792]{1,0:T(8,128)}, u32[]{:S(2)}) copy-start(f32[16,1792]{1,0:T(8,128)} %param.10) | copy-start | bytes 344068
  1.4 6.0 %copy-start.9 = (s32[16,1792]{1,0:T(8,128)S(1)}, s32[16,1792]{1,0:T(8,128)}, u32[]{:S(2)}) copy-start(s32[16,1792]{1,0:T(8,128)} %param.11) | copy-start | bytes 344068
  1.4 6.0 %copy-start.2 = (bf16[8,4,16,1792]{3,2,1,0:T(8,128)(2,1)S(1)}, bf16[8,4,16,1792]{3,2,1,0:T(8,128)(2,1)}, u32[]{:S(2)}) copy-start(bf16[8,4,16,1792]{3,2,1,0:T(8,128)(2,1)} %param.8) | copy-start | bytes 5505028
  1.4 6.0 %copy-start.5 = (f32[4,16,1792]{2,1,0:T(8,128)S(1)}, f32[4,16,1792]{2,1,0:T(8,128)}, u32[]{:S(2)}) copy-start(f32[4,16,1792]{2,1,0:T(8,128)} %param.9) | copy-start | bytes 1376260
  1.5 11.6 %collective-permute-start.1 = (f32[80,1792]{1,0:T(8,128)S(1)}, f32[80,1792]{1,0:T(8,128)S(1)}, u32[]{:S(2)}, u32[]{:S(2)}) collective-permute-start(f32[80,1792]{1,0:T(8,128)S(1)} %pad_maximum_fusion.3), channel_id=1, source_target_pairs={{1,0},{2,1},{3,2},{4,3},{5,4},{6,5},{7,6},{9,8},{10,9},{11,10},{12... | collective-permute-start | bytes 1720328 | tf_op jit(solution)/shard_map/ppermute | solution.py:16
  4.3 9.7 %collective-permute-start = (f32[80,1792]{1,0:T(8,128)S(1)}, f32[80,1792]{1,0:T(8,128)S(1)}, u32[]{:S(2)}, u32[]{:S(2)}) collective-permute-start(f32[80,1792]{1,0:T(8,128)S(1)} %pad_maximum_fusion.2), channel_id=1, source_target_pairs={{0,1},{1,2},{2,3},{3,4},{4,5},{5,6},{6,7},{8,9},{9,10},{10,11},{11... | collective-permute-start | bytes 1720328 | tf_op jit(solution)/shard_map/ppermute | solution.py:15
  7.4 19.2 %copy-start.3 = (f32[16,1792]{1,0:T(8,128)}, f32[16,1792]{1,0:T(8,128)S(1)}, u32[]{:S(2)}) copy-start(f32[16,1792]{1,0:T(8,128)S(1)} %convert_multiply_fusion) | copy-start | bytes 344068
  14.1 1.2 %copy-start = (f32[8,16,1792]{2,1,0:T(8,128)S(1)}, f32[8,16,1792]{2,1,0:T(8,128)}, u32[]{:S(2)}) copy-start(f32[8,16,1792]{2,1,0:T(8,128)} %param.7) | copy-start | bytes 2752516
  28.3 9.9 %collective-permute-start.2 = (f32[36,1792]{1,0:T(8,128)}, f32[36,1792]{1,0:T(8,128)}, u32[]{:S(2)}, u32[]{:S(2)}) collective-permute-start(f32[36,1792]{1,0:T(8,128)} %pad_maximum_fusion.5), channel_id=1, source_target_pairs={{0,1},{1,2},{2,3},{3,4},{4,5},{5,6},{6,7},{8,9},{9,10},{10,11},{11... | collective-permute-start | bytes 774152 | tf_op jit(solution)/shard_map/ppermute | solution.py:15
  36.1 8.3 %collective-permute-start.3 = (f32[36,1792]{1,0:T(8,128)}, f32[36,1792]{1,0:T(8,128)}, u32[]{:S(2)}, u32[]{:S(2)}) collective-permute-start(f32[36,1792]{1,0:T(8,128)} %pad_maximum_fusion.6), channel_id=1, source_target_pairs={{1,0},{2,1},{3,2},{4,3},{5,4},{6,5},{7,6},{9,8},{10,9},{11,10},{12... | collective-permute-start | bytes 774152 | tf_op jit(solution)/shard_map/ppermute | solution.py:16
  47.0 14.8 %copy-start.4 = (f32[16,1792]{1,0:T(8,128)S(1)}, f32[16,1792]{1,0:T(8,128)}, u32[]{:S(2)}) copy-start(f32[16,1792]{1,0:T(8,128)} %copy-done.3) | copy-start | bytes 344068
  51.4 6.2 %collective-permute-start.4 = (f32[24,1792]{1,0:T(8,128)S(1)}, f32[24,1792]{1,0:T(8,128)S(1)}, u32[]{:S(2)}, u32[]{:S(2)}) collective-permute-start(f32[24,1792]{1,0:T(8,128)S(1)} %fusion.15), channel_id=1, source_target_pairs={{0,8},{8,0},{16,24},{24,16},{1,9},{9,1},{17,25},{25,17},{2,10},{10... | collective-permute-start | bytes 516104 | tf_op jit(solution)/shard_map/ppermute | solution.py:34
  52.6 9.2 %collective-permute-start.5 = (f32[24,1792]{1,0:T(8,128)S(1)}, f32[24,1792]{1,0:T(8,128)S(1)}, u32[]{:S(2)}, u32[]{:S(2)}) collective-permute-start(f32[24,1792]{1,0:T(8,128)S(1)} %fusion.15), channel_id=1, source_target_pairs={{0,16},{8,24},{16,0},{24,8},{1,17},{9,25},{17,1},{25,9},{2,18},{10... | collective-permute-start | bytes 516104 | tf_op jit(solution)/shard_map/ppermute | solution.py:34
  53.9 7.9 %collective-permute-start.6 = (f32[24,1792]{1,0:T(8,128)S(1)}, f32[24,1792]{1,0:T(8,128)S(1)}, u32[]{:S(2)}, u32[]{:S(2)}) collective-permute-start(f32[24,1792]{1,0:T(8,128)S(1)} %fusion.15), channel_id=1, source_target_pairs={{0,24},{8,16},{16,8},{24,0},{1,25},{9,17},{17,9},{25,1},{2,26},{10... | collective-permute-start | bytes 516104 | tf_op jit(solution)/shard_map/ppermute | solution.py:34
  65.7 1.2 %copy-start.1 = (f32[8,16,1792]{2,1,0:T(8,128)S(1)}, f32[8,16,1792]{2,1,0:T(8,128)}, u32[]{:S(2)}) copy-start(f32[8,16,1792]{2,1,0:T(8,128)} %param.7) | copy-start | bytes 2752516

commit v10 on v8

--- a/solution.py
+++ b/solution.py
@@ -77,16 +77,13 @@
         row_index < row_count * lax.axis_size("tile") - 1, row_faces, jnp.zeros_like(row_faces)
     )
     stacked = jnp.stack([row_coef, col_faces])
+    field, coef_band = exchange([controls, stacked], STEPS)
+    localized = localize(field, coef_band)[:, STEPS : STEPS + row_count]
     mix = jnp.sum(perturbations.astype(jnp.float32) * jacobian[None], axis=1)
-    weights = radar_mask.astype(jnp.float32) * obs_weight
-    field, coef_band = exchange([controls, stacked], 2 * STEPS)
-    mix_band, weights_band = exchange([mix, weights[None]], STEPS)
-    reach = row_count + 2 * STEPS
-    localized = localize(field, coef_band)[:, STEPS : STEPS + reach]
-    reflect = mem_sum(jnp.sum(mix_band * localized, 0))
-    sensitivity = mix_band * (weights_band[0] * reflect)
-    spread = localize(sensitivity, coef_band[:, STEPS : STEPS + reach])
-    return controls + spread[:, STEPS : STEPS + row_count]
+    reflect = mem_sum(jnp.sum(mix * localized, 0))
+    weighted = radar_mask.astype(jnp.float32) * obs_weight * reflect
+    (sensitivity,) = exchange([mix * weighted[None]], STEPS)
+    return controls + localize(sensitivity, coef_band)[:, STEPS : STEPS + row_count]
 
 
 def solution(mesh):

time: 49.8 us -> 47.2 us (0.948)
  the two profiles are of different devices: /device:TPU:8 before, /device:TPU:1 now
where the time goes in v10:
time: 47.2 us; the launch traced here: 46.8 us
  starting transfers between devices  16.8 us (36%)
  other arithmetic  14.2 us (30%)
  waiting for transfers between devices  9.59 us (20%)
  local copies, waits for them, and re-layouts  5.83 us (12%)
    ppermute x2, starting transfers between devices, exchange(): above = lax.ppermute(tail, 'tile', [(i, i + 1) for i in range(count - 1)])  10.2 us
    ppermute x3, waiting for transfers between devices, partner(): return lax.ppermute(part, 'mem', [(i, i ^ stride) for i in range(count)])  4.27 us
    ppermute x2, starting transfers between devices, exchange(): below = lax.ppermute(head, 'tile', [(i + 1, i) for i in range(count - 1)])  3.88 us
    mul x8, other arithmetic, diffuse(): col_coef[..., :, :-1] * (values[..., :, 1:] - values[..., :, :-1])  3.38 us
    sub x6, other arithmetic, diffuse(): values + jnp.concatenate([col_flux, zeros_col], -1)  3.04 us
    ppermute x2, waiting for transfers between devices, exchange(): below = lax.ppermute(head, 'tile', [(i + 1, i) for i in range(count - 1)])  2.81 us
    ppermute x3, starting transfers between devices, partner(): return lax.ppermute(part, 'mem', [(i, i ^ stride) for i in range(count)])  2.71 us
    ppermute x2, waiting for transfers between devices, exchange(): above = lax.ppermute(tail, 'tile', [(i, i + 1) for i in range(count - 1)])  2.51 us
  transfers between devices with their start and end apart: 7, of which 7 were waited for; matrix products, arithmetic and copies ran while one was open for 5% of the time, Pallas kernels for 0%

profile of v10, /device:TPU:1, one launch (start us, length us, event | category | flops | bytes accessed | tf_op | source)
XLA Modules:
  0.0 46.8 jit_solution(8694324238088647187)
XLA Ops:
  0.0 1.0 %select_bitcast_fusion = f32[1,16,1792]{2,1,0:T(8,128)S(1)} fusion(f32[16,1792]{1,0:T(8,128)} %param.12, pred[16]{0:T(512)(128)(4,1)S(1)} %add_compare_fusion), kind=kLoop, calls=%fused_computation.59 | loop fusion | flops 28672 | bytes 229392 | tf_op jit(solution)/shard_map/stack | solution.py:79
  1.0 0.9 %pad_maximum_fusion.6 = (f32[2,4,1792]{2,1,0:T(4,128)S(1)}, f32[2,4,1792]{2,1,0:T(4,128)S(1)}) fusion(f32[1,16,1792]{2,1,0:T(8,128)} %bitcast.16, f32[1,16,1792]{2,1,0:T(8,128)S(1)} %select_bitcast_fusion), kind=kLoop, calls=%fused_computation.61 | loop fusion | flops 28672 | bytes 344064 | tf_op jit(solution)/shard_map/slice | solution.py:14
  1.9 1.4 %fusion.20 = (f32[8,4,1792]{2,1,0:T(4,128)S(1)}, f32[8,4,1792]{2,1,0:T(4,128)S(1)}) fusion(f32[8,16,1792]{2,1,0:T(8,128)} %param.7), kind=kLoop, calls=%fused_computation.64 | loop fusion | bytes 917504 | tf_op jit(solution)/shard_map/slice | solution.py:14
  3.3 0.1 reshape.44
  3.4 0.7 %pad_maximum_fusion.4 = f32[40,1792]{1,0:T(8,128)} fusion(f32[8,1792]{1,0:T(8,128)S(1)} %reshape.45, f32[32,1792]{1,0:T(8,128)S(1)} %reshape.44), kind=kLoop, calls=%fused_computation.55 | loop fusion | flops 71680 | bytes 573440 | tf_op jit(solution)/shard_map/concatenate | solution.py:13
  4.1 2.0 %collective-permute-start.1 = (f32[40,1792]{1,0:T(8,128)}, f32[40,1792]{1,0:T(8,128)}, u32[]{:S(2)}, u32[]{:S(2)}) collective-permute-start(f32[40,1792]{1,0:T(8,128)} %pad_maximum_fusion.4), channel_id=1, source_target_pairs={{1,0},{2,1},{3,2},{4,3},{5,4},{6,5},{7,6},{9,8},{10,9},{11,10},{12... | collective-permute-start | bytes 860168 | tf_op jit(solution)/shard_map/ppermute | solution.py:16
  6.1 0.1 reshape.41
  6.2 0.7 %pad_maximum_fusion.3 = f32[40,1792]{1,0:T(8,128)} fusion(f32[8,1792]{1,0:T(8,128)S(1)} %reshape.42, f32[32,1792]{1,0:T(8,128)S(1)} %reshape.41), kind=kLoop, calls=%fused_computation.54 | loop fusion | flops 71680 | bytes 573440 | tf_op jit(solution)/shard_map/concatenate | solution.py:14
  6.9 4.7 %collective-permute-start = (f32[40,1792]{1,0:T(8,128)}, f32[40,1792]{1,0:T(8,128)}, u32[]{:S(2)}, u32[]{:S(2)}) collective-permute-start(f32[40,1792]{1,0:T(8,128)} %pad_maximum_fusion.3), channel_id=1, source_target_pairs={{0,1},{1,2},{2,3},{3,4},{4,5},{5,6},{6,7},{8,9},{9,10},{10,11},{11... | collective-permute-start | bytes 860168 | tf_op jit(solution)/shard_map/ppermute | solution.py:15
  11.6 0.4 multiply_reduce_fusion
  12.0 1.3 %collective-permute-done.1 = f32[40,1792]{1,0:T(8,128)} collective-permute-done((f32[40,1792]{1,0:T(8,128)}, f32[40,1792]{1,0:T(8,128)}, u32[]{:S(2)}, u32[]{:S(2)}) %collective-permute-start.1) | collective-permute-done | bytes 286752 | tf_op jit(solution)/shard_map/ppermute | solution.py:16
  13.3 0.8 %slice.222 = f32[8,1792]{1,0:T(8,128)S(1)} slice(f32[40,1792]{1,0:T(8,128)} %collective-permute-done.1), slice={[32:40], [0:1792]} | slice | bytes 114688 | tf_op jit(solution)/shard_map/slice | solution.py:22
  14.2 1.3 %collective-permute-done = f32[40,1792]{1,0:T(8,128)} collective-permute-done((f32[40,1792]{1,0:T(8,128)}, f32[40,1792]{1,0:T(8,128)}, u32[]{:S(2)}, u32[]{:S(2)}) %collective-permute-start) | collective-permute-done | bytes 286752 | tf_op jit(solution)/shard_map/ppermute | solution.py:15
  15.5 0.8 %slice.221 = f32[8,1792]{1,0:T(8,128)S(1)} slice(f32[40,1792]{1,0:T(8,128)} %collective-permute-done), slice={[32:40], [0:1792]} | slice | bytes 114688 | tf_op jit(solution)/shard_map/slice | solution.py:21
  16.4 0.1 pad_maximum_fusion.2
  16.4 0.0 copy-start
  16.5 1.0 %slice.220 = f32[32,1792]{1,0:T(8,128)S(1)} slice(f32[40,1792]{1,0:T(8,128)} %collective-permute-done.1), slice={[0:32], [0:1792]} | slice | bytes 458752 | tf_op jit(solution)/shard_map/slice | solution.py:22
  17.5 0.1 reshape.46
  17.6 1.0 %slice.219 = f32[32,1792]{1,0:T(8,128)S(1)} slice(f32[40,1792]{1,0:T(8,128)} %collective-permute-done), slice={[0:32], [0:1792]} | slice | bytes 458752 | tf_op jit(solution)/shard_map/slice | solution.py:21
  18.5 0.1 reshape.43
  18.6 0.2 pad_maximum_fusion
  18.8 0.2 fusion.15
  19.0 0.4 fusion.14
  19.4 0.6 %pad_subtract_fusion.5 = f32[8,24,1792]{2,1,0:T(8,128)S(1)} fusion(f32[8,24,1791]{2,1,0:T(8,128)S(1)} %fusion.14, f32[8,23,1792]{2,1,0:T(8,128)S(1)} %fusion.15, f32[8,4,1792]{2,1,0:T(4,128)S(1)} %reshape.46, f32[8,16,1792]{2,1,0:T(8,128)S(1)} %copy-done, f32[8,4,1792]{2,1,0:T(4,128)S(1)} %reshape.43), kind=kLoop, calls=%fused_computation.40 | loop fusion | flops 2064384 | bytes 5446912 | tf_op jit(solution)/shard_map/sub | solution.py:59
  20.0 0.2 fusion.13
  20.2 0.4 fusion.12
  20.6 0.5 %pad_subtract_fusion.4 = f32[8,24,1792]{2,1,0:T(8,128)S(1)} fusion(f32[8,24,1791]{2,1,0:T(8,128)S(1)} %fusion.12, f32[8,23,1792]{2,1,0:T(8,128)S(1)} %fusion.13, f32[8,24,1792]{2,1,0:T(8,128)S(1)} %pad_subtract_fusion.5), kind=kLoop, calls=%fused_computation.39 | loop fusion | flops 1376256 | bytes 5446912 | tf_op jit(solution)/shard_map/sub | solution.py:59
  21.1 0.2 fusion.11
  21.3 0.4 fusion.10
  21.7 0.5 %pad_subtract_fusion.3 = f32[8,24,1792]{2,1,0:T(8,128)S(1)} fusion(f32[8,24,1791]{2,1,0:T(8,128)S(1)} %fusion.10, f32[8,23,1792]{2,1,0:T(8,128)S(1)} %fusion.11, f32[8,24,1792]{2,1,0:T(8,128)S(1)} %pad_subtract_fusion.4), kind=kLoop, calls=%fused_computation.38 | loop fusion | flops 1376256 | bytes 5446912 | tf_op jit(solution)/shard_map/sub | solution.py:59
  22.2 0.2 fusion.9
  22.4 0.4 fusion.8
  22.8 0.0 copy-start.4
  22.8 0.0 copy-start.5
  22.9 0.6 %fusion.18 = f32[16,1792]{1,0:T(8,128)S(1)} fusion(f32[8,16,1792]{2,1,0:T(8,128)S(1)} %multiply_reduce_fusion, f32[8,24,1791]{2,1,0:T(8,128)S(1)} %fusion.8, f32[8,23,1792]{2,1,0:T(8,128)S(1)} %fusion.9, f32[8,24,1792]{2,1,0:T(8,128)S(1)} %pad_subtract_fusion.3), kind=kLoop, calls=%fused_computation.48 | loop fusion | flops 1347584 | bytes 4644096 | tf_op jit(solution)/shard_map/reduce_sum | solution.py:83
  23.4 2.2 %collective-permute-start.4 = (f32[16,1792]{1,0:T(8,128)S(1)}, f32[16,1792]{1,0:T(8,128)S(1)}, u32[]{:S(2)}, u32[]{:S(2)}) collective-permute-start(f32[16,1792]{1,0:T(8,128)S(1)} %fusion.18), channel_id=1, source_target_pairs={{0,24},{8,16},{16,8},{24,0},{1,25},{9,17},{17,9},{25,1},{2,26},{10... | collective-permute-start | bytes 344072 | tf_op jit(solution)/shard_map/ppermute | solution.py:34
  25.7 0.2 collective-permute-start.3
  25.9 0.3 collective-permute-start.2
  26.1 2.3 %collective-permute-done.4 = f32[16,1792]{1,0:T(8,128)S(1)} collective-permute-done((f32[16,1792]{1,0:T(8,128)S(1)}, f32[16,1792]{1,0:T(8,128)S(1)}, u32[]{:S(2)}, u32[]{:S(2)}) %collective-permute-start.4) | collective-permute-done | bytes 114720 | tf_op jit(solution)/shard_map/ppermute | solution.py:34
  28.4 1.5 %collective-permute-done.3 = f32[16,1792]{1,0:T(8,128)S(1)} collective-permute-done((f32[16,1792]{1,0:T(8,128)S(1)}, f32[16,1792]{1,0:T(8,128)S(1)}, u32[]{:S(2)}, u32[]{:S(2)}) %collective-permute-start.3) | collective-permute-done | bytes 114720 | tf_op jit(solution)/shard_map/ppermute | solution.py:34
  29.9 0.5 %collective-permute-done.2 = f32[16,1792]{1,0:T(8,128)S(1)} collective-permute-done((f32[16,1792]{1,0:T(8,128)S(1)}, f32[16,1792]{1,0:T(8,128)S(1)}, u32[]{:S(2)}, u32[]{:S(2)}) %collective-permute-start.2) | collective-permute-done | bytes 114720 | tf_op jit(solution)/shard_map/ppermute | solution.py:34
  30.4 0.1 broadcast_multiply_fusion
  30.5 0.1 fusion.19
  30.6 0.1 reshape.51
  30.7 1.9 %collective-permute-start.6 = (f32[32,1792]{1,0:T(8,128)S(1)}, f32[32,1792]{1,0:T(8,128)S(1)}, u32[]{:S(2)}, u32[]{:S(2)}) collective-permute-start(f32[32,1792]{1,0:T(8,128)S(1)} %reshape.51), channel_id=1, source_target_pairs={{1,0},{2,1},{3,2},{4,3},{5,4},{6,5},{7,6},{9,8},{10,9},{11,10},{12... | collective-permute-start | bytes 688136 | tf_op jit(solution)/shard_map/ppermute | solution.py:16
  32.6 0.1 reshape.49
  32.7 5.5 %collective-permute-start.5 = (f32[32,1792]{1,0:T(8,128)S(1)}, f32[32,1792]{1,0:T(8,128)S(1)}, u32[]{:S(2)}, u32[]{:S(2)}) collective-permute-start(f32[32,1792]{1,0:T(8,128)S(1)} %reshape.49), channel_id=1, source_target_pairs={{0,1},{1,2},{2,3},{3,4},{4,5},{5,6},{6,7},{8,9},{9,10},{10,11},{11... | collective-permute-start | bytes 688136 | tf_op jit(solution)/shard_map/ppermute | solution.py:15
  38.3 1.5 %collective-permute-done.6 = f32[32,1792]{1,0:T(8,128)S(1)} collective-permute-done((f32[32,1792]{1,0:T(8,128)S(1)}, f32[32,1792]{1,0:T(8,128)S(1)}, u32[]{:S(2)}, u32[]{:S(2)}) %collective-permute-start.6) | collective-permute-done | bytes 229408 | tf_op jit(solution)/shard_map/ppermute | solution.py:16
  39.8 0.1 reshape.52
  39.8 1.2 %collective-permute-done.5 = f32[32,1792]{1,0:T(8,128)S(1)} collective-permute-done((f32[32,1792]{1,0:T(8,128)S(1)}, f32[32,1792]{1,0:T(8,128)S(1)}, u32[]{:S(2)}, u32[]{:S(2)}) %collective-permute-start.5) | collective-permute-done | bytes 229408 | tf_op jit(solution)/shard_map/ppermute | solution.py:15
  41.0 0.1 reshape.50
  41.1 0.2 pad_maximum_fusion.1
  41.3 0.2 fusion.7
  41.5 0.4 fusion.6
  41.9 0.6 %pad_subtract_fusion.2 = f32[8,24,1792]{2,1,0:T(8,128)S(1)} fusion(f32[8,24,1791]{2,1,0:T(8,128)S(1)} %fusion.6, f32[8,23,1792]{2,1,0:T(8,128)S(1)} %fusion.7, f32[8,4,1792]{2,1,0:T(4,128)S(1)} %reshape.52, f32[8,16,1792]{2,1,0:T(8,128)S(1)} %broadcast_multiply_fusion, f32[8,4,1792]{2,1,0:T(4,128)S(1)} %reshape.50), kind=kLoop, calls=%fused_computation.37 | loop fusion | flops 2064384 | bytes 5446912 | tf_op jit(solution)/shard_map/sub | solution.py:59
  42.5 0.2 fusion.5
  42.7 0.4 fusion.4
  43.1 0.5 %pad_subtract_fusion.1 = f32[8,24,1792]{2,1,0:T(8,128)S(1)} fusion(f32[8,24,1791]{2,1,0:T(8,128)S(1)} %fusion.4, f32[8,23,1792]{2,1,0:T(8,128)S(1)} %fusion.5, f32[8,24,1792]{2,1,0:T(8,128)S(1)} %pad_subtract_fusion.2), kind=kLoop, calls=%fused_computation.36 | loop fusion | flops 1376256 | bytes 5446912 | tf_op jit(solution)/shard_map/sub | solution.py:59
  43.6 0.2 fusion.3
  43.8 0.4 fusion.2
  44.2 0.5 %pad_subtract_fusion = f32[8,24,1792]{2,1,0:T(8,128)S(1)} fusion(f32[8,24,1791]{2,1,0:T(8,128)S(1)} %fusion.2, f32[8,23,1792]{2,1,0:T(8,128)S(1)} %fusion.3, f32[8,24,1792]{2,1,0:T(8,128)S(1)} %pad_subtract_fusion.1), kind=kLoop, calls=%fused_computation.35 | loop fusion | flops 1376256 | bytes 5446912 | tf_op jit(solution)/shard_map/sub | solution.py:59
  44.7 0.2 fusion.1
  44.9 0.4 fusion
  45.3 1.5 %fusion.16 = f32[8,16,1792]{2,1,0:T(8,128)} fusion(f32[8,16,1792]{2,1,0:T(8,128)S(1)} %copy-done, f32[8,24,1791]{2,1,0:T(8,128)S(1)} %fusion, f32[8,23,1792]{2,1,0:T(8,128)S(1)} %fusion.1, f32[8,24,1792]{2,1,0:T(8,128)S(1)} %pad_subtract_fusion), kind=kLoop, calls=%fused_computation.42 | loop fusion | flops 1146880 | bytes 5446912 | tf_op jit(solution)/shard_map/add | solution.py:86
  (17 shorter events, 0.2 us)
Async XLA Ops:
  1.9 9.7 %copy-start.1 = (bf16[8,4,16,1792]{3,2,1,0:T(8,128)(2,1)S(1)}, bf16[8,4,16,1792]{3,2,1,0:T(8,128)(2,1)}, u32[]{:S(2)}) copy-start(bf16[8,4,16,1792]{3,2,1,0:T(8,128)(2,1)} %param.8) | copy-start | bytes 5505028
  1.9 9.7 %copy-start.2 = (f32[4,16,1792]{2,1,0:T(8,128)S(1)}, f32[4,16,1792]{2,1,0:T(8,128)}, u32[]{:S(2)}) copy-start(f32[4,16,1792]{2,1,0:T(8,128)} %param.9) | copy-start | bytes 1376260
  4.1 9.2 %collective-permute-start.1 = (f32[40,1792]{1,0:T(8,128)}, f32[40,1792]{1,0:T(8,128)}, u32[]{:S(2)}, u32[]{:S(2)}) collective-permute-start(f32[40,1792]{1,0:T(8,128)} %pad_maximum_fusion.4), channel_id=1, source_target_pairs={{1,0},{2,1},{3,2},{4,3},{5,4},{6,5},{7,6},{9,8},{10,9},{11,10},{12... | collective-permute-start | bytes 860168 | tf_op jit(solution)/shard_map/ppermute | solution.py:16
  6.9 9.4 %copy-start.3 = (f32[16,1792]{1,0:T(8,128)S(1)}, f32[16,1792]{1,0:T(8,128)}, u32[]{:S(2)}) copy-start(f32[16,1792]{1,0:T(8,128)} %param.13) | copy-start | bytes 344068
  6.9 8.6 %collective-permute-start = (f32[40,1792]{1,0:T(8,128)}, f32[40,1792]{1,0:T(8,128)}, u32[]{:S(2)}, u32[]{:S(2)}) collective-permute-start(f32[40,1792]{1,0:T(8,128)} %pad_maximum_fusion.3), channel_id=1, source_target_pairs={{0,1},{1,2},{2,3},{3,4},{4,5},{5,6},{6,7},{8,9},{9,10},{10,11},{11... | collective-permute-start | bytes 860168 | tf_op jit(solution)/shard_map/ppermute | solution.py:15
  16.4 2.2 %copy-start = (f32[8,16,1792]{2,1,0:T(8,128)S(1)}, f32[8,16,1792]{2,1,0:T(8,128)}, u32[]{:S(2)}) copy-start(f32[8,16,1792]{2,1,0:T(8,128)} %param.7) | copy-start | bytes 2752516
  22.8 7.6 %copy-start.4 = (f32[16,1792]{1,0:T(8,128)S(1)}, f32[16,1792]{1,0:T(8,128)}, u32[]{:S(2)}) copy-start(f32[16,1792]{1,0:T(8,128)} %param.10) | copy-start | bytes 344068
  22.8 7.6 %copy-start.5 = (s32[16,1792]{1,0:T(8,128)S(1)}, s32[16,1792]{1,0:T(8,128)}, u32[]{:S(2)}) copy-start(s32[16,1792]{1,0:T(8,128)} %param.11) | copy-start | bytes 344068
  23.4 5.0 %collective-permute-start.4 = (f32[16,1792]{1,0:T(8,128)S(1)}, f32[16,1792]{1,0:T(8,128)S(1)}, u32[]{:S(2)}, u32[]{:S(2)}) collective-permute-start(f32[16,1792]{1,0:T(8,128)S(1)} %fusion.18), channel_id=1, source_target_pairs={{0,24},{8,16},{16,8},{24,0},{1,25},{9,17},{17,9},{25,1},{2,26},{10... | collective-permute-start | bytes 344072 | tf_op jit(solution)/shard_map/ppermute | solution.py:34
  25.7 4.2 %collective-permute-start.3 = (f32[16,1792]{1,0:T(8,128)S(1)}, f32[16,1792]{1,0:T(8,128)S(1)}, u32[]{:S(2)}, u32[]{:S(2)}) collective-permute-start(f32[16,1792]{1,0:T(8,128)S(1)} %fusion.18), channel_id=1, source_target_pairs={{0,16},{8,24},{16,0},{24,8},{1,17},{9,25},{17,1},{25,9},{2,18},{10... | collective-permute-start | bytes 344072 | tf_op jit(solution)/shard_map/ppermute | solution.py:34
  25.9 4.5 %collective-permute-start.2 = (f32[16,1792]{1,0:T(8,128)S(1)}, f32[16,1792]{1,0:T(8,128)S(1)}, u32[]{:S(2)}, u32[]{:S(2)}) collective-permute-start(f32[16,1792]{1,0:T(8,128)S(1)} %fusion.18), channel_id=1, source_target_pairs={{0,8},{8,0},{16,24},{24,16},{1,9},{9,1},{17,25},{25,17},{2,10},{10... | collective-permute-start | bytes 344072 | tf_op jit(solution)/shard_map/ppermute | solution.py:34
  30.7 9.1 %collective-permute-start.6 = (f32[32,1792]{1,0:T(8,128)S(1)}, f32[32,1792]{1,0:T(8,128)S(1)}, u32[]{:S(2)}, u32[]{:S(2)}) collective-permute-start(f32[32,1792]{1,0:T(8,128)S(1)} %reshape.51), channel_id=1, source_target_pairs={{1,0},{2,1},{3,2},{4,3},{5,4},{6,5},{7,6},{9,8},{10,9},{11,10},{12... | collective-permute-start | bytes 688136 | tf_op jit(solution)/shard_map/ppermute | solution.py:16
  32.7 8.3 %collective-permute-start.5 = (f32[32,1792]{1,0:T(8,128)S(1)}, f32[32,1792]{1,0:T(8,128)S(1)}, u32[]{:S(2)}, u32[]{:S(2)}) collective-permute-start(f32[32,1792]{1,0:T(8,128)S(1)} %reshape.49), channel_id=1, source_target_pairs={{0,1},{1,2},{2,3},{3,4},{4,5},{5,6},{6,7},{8,9},{9,10},{10,11},{11... | collective-permute-start | bytes 688136 | tf_op jit(solution)/shard_map/ppermute | solution.py:15

commit v11 on v10

--- a/solution.py
+++ b/solution.py
@@ -6,23 +6,13 @@
 STEPS = 4
 
 
-def exchange(parts, width):
+def exchange(part, width):
     count = lax.axis_size("tile")
-    cols = parts[0].shape[-1]
-    sizes = [part[..., :width, :].size // cols for part in parts]
-    head = jnp.concatenate([part[..., :width, :].reshape(-1, cols) for part in parts], 0)
-    tail = jnp.concatenate([part[..., -width:, :].reshape(-1, cols) for part in parts], 0)
+    head = part[..., :width, :]
+    tail = part[..., -width:, :]
     above = lax.ppermute(tail, "tile", [(i, i + 1) for i in range(count - 1)])
     below = lax.ppermute(head, "tile", [(i + 1, i) for i in range(count - 1)])
-    bands = []
-    start = 0
-    for part, size in zip(parts, sizes):
-        shape = part.shape[:-2] + (width, cols)
-        top = above[start : start + size].reshape(shape)
-        bottom = below[start : start + size].reshape(shape)
-        bands.append(jnp.concatenate([top, part, bottom], -2))
-        start += size
-    return bands
+    return jnp.concatenate([above, part, below], -2)
 
 
 def mem_sum(part):
@@ -76,13 +66,15 @@
     row_coef = jnp.where(
         row_index < row_count * lax.axis_size("tile") - 1, row_faces, jnp.zeros_like(row_faces)
     )
-    stacked = jnp.stack([row_coef, col_faces])
-    field, coef_band = exchange([controls, stacked], STEPS)
+    members = controls.shape[0]
+    stacked = jnp.concatenate([controls, row_coef[None], col_faces[None]], 0)
+    band = exchange(stacked, STEPS)
+    field, coef_band = band[:members], band[members:]
     localized = localize(field, coef_band)[:, STEPS : STEPS + row_count]
     mix = jnp.sum(perturbations.astype(jnp.float32) * jacobian[None], axis=1)
     reflect = mem_sum(jnp.sum(mix * localized, 0))
     weighted = radar_mask.astype(jnp.float32) * obs_weight * reflect
-    (sensitivity,) = exchange([mix * weighted[None]], STEPS)
+    sensitivity = exchange(mix * weighted[None], STEPS)
     return controls + localize(sensitivity, coef_band)[:, STEPS : STEPS + row_count]
 
 

time: 47.2 us -> 47 us (level)
  waiting for transfers between devices: 9.59 us -> 17 us
  local copies, waits for them, and re-layouts: 5.83 us -> 0.63 us
  starting transfers between devices: 16.8 us -> 15.5 us
  other arithmetic: 14.2 us -> 13.3 us
    ppermute x2, waiting for transfers between devices: 2.81 us -> 8.68 us  [exchange(): below = lax.ppermute(head, 'tile', [(i + 1, i) for i in range(count - 1)])]
    slice x6 -> x3, local copies, waits for them, and re-layouts: 5.1 us -> 0.22 us  [the longest x2 0.15 us: exchange(): tail = part[..., -width:, :]]
    ppermute x2, waiting for transfers between devices: 2.51 us -> 3.99 us  [exchange(): above = lax.ppermute(tail, 'tile', [(i, i + 1) for i in range(count - 1)])]
    concatenate x5 -> x2, other arithmetic: 1.89 us -> 0.44 us  [exchange(): return jnp.concatenate([above, part, below], -2)]
    ppermute x2, starting transfers between devices: 10.2 us -> 9 us  [exchange(): above = lax.ppermute(tail, 'tile', [(i, i + 1) for i in range(count - 1)])]
    another operation x1 -> x0, other arithmetic: 0.98 us -> none  [per_device(): stacked = jnp.stack([row_coef, col_faces])]
    broadcast_in_dim x0 -> x1, other arithmetic: none -> 0.98 us  [per_device(): stacked = jnp.concatenate([controls, row_coef[None], col_faces[None]], 0)]
    reshape x12 -> x0, local copies, waits for them, and re-layouts: 0.67 us -> none  [the longest x3 0.18 us: exchange(): part[..., :width, :].reshape(-1, cols)]
  transfers between devices with their start and end apart: 7 -> 7, of which waited for: 7 -> 7; matrix products, arithmetic and copies ran while one was open for 5% -> 1% of each run, Pallas kernels for 0% -> 0%
where the time goes in v11:
time: 47 us; the launch traced here: 46.8 us
  waiting for transfers between devices  17 us (36%)
  starting transfers between devices  15.5 us (33%)
  other arithmetic  13.3 us (28%)
  local copies, waits for them, and re-layouts  0.63 us (1%)
    ppermute x2, starting transfers between devices, exchange(): above = lax.ppermute(tail, 'tile', [(i, i + 1) for i in range(count - 1)])  9 us
    ppermute x2, waiting for transfers between devices, exchange(): below = lax.ppermute(head, 'tile', [(i + 1, i) for i in range(count - 1)])  8.68 us
    ppermute x3, waiting for transfers between devices, partner(): return lax.ppermute(part, 'mem', [(i, i ^ stride) for i in range(count)])  4.34 us
    ppermute x2, waiting for transfers between devices, exchange(): above = lax.ppermute(tail, 'tile', [(i, i + 1) for i in range(count - 1)])  3.99 us
    ppermute x2, starting transfers between devices, exchange(): below = lax.ppermute(head, 'tile', [(i + 1, i) for i in range(count - 1)])  3.84 us
    mul x8, other arithmetic, diffuse(): col_coef[..., :, :-1] * (values[..., :, 1:] - values[..., :, :-1])  3.39 us
    sub x6, other arithmetic, diffuse(): values + jnp.concatenate([col_flux, zeros_col], -1)  2.95 us
    ppermute x3, starting transfers between devices, partner(): return lax.ppermute(part, 'mem', [(i, i ^ stride) for i in range(count)])  2.71 us
  transfers between devices with their start and end apart: 7, of which 7 were waited for; matrix products, arithmetic and copies ran while one was open for 1% of the time, Pallas kernels for 0%

profile of v11, /device:TPU:1, one launch (start us, length us, event | category | flops | bytes accessed | tf_op | source)
XLA Modules:
  0.0 46.8 jit_solution(13744343663438634302)
XLA Ops:
  0.0 1.0 %select_bitcast_fusion = f32[1,16,1792]{2,1,0:T(8,128)S(1)} fusion(f32[16,1792]{1,0:T(8,128)} %param.12, pred[16]{0:T(512)(128)(4,1)S(1)} %add_compare_fusion), kind=kLoop, calls=%fused_computation.62 | loop fusion | flops 28672 | bytes 229392 | tf_op jit(solution)/shard_map/broadcast_in_dim | solution.py:70
  1.0 0.0 copy-start.1
  1.0 0.0 copy-start.3
  1.0 1.5 %pad_maximum_fusion.4 = (f32[10,4,1792]{2,1,0:T(4,128)S(1)}, f32[10,4,1792]{2,1,0:T(4,128)S(1)}) fusion(f32[1,16,1792]{2,1,0:T(8,128)} %bitcast.16, f32[1,16,1792]{2,1,0:T(8,128)S(1)} %select_bitcast_fusion, f32[8,16,1792]{2,1,0:T(8,128)} %param.7), kind=kLoop, calls=%fused_computation.58 | loop fusion | flops 286720 | bytes 1720320 | tf_op jit(solution)/shard_map/slice | solution.py:12
  2.5 0.1 copy.11
  2.6 4.6 %collective-permute-start = (f32[10,4,1792]{2,0,1:T(8,128)S(1)}, f32[10,4,1792]{2,0,1:T(8,128)S(1)}, u32[]{:S(2)}, u32[]{:S(2)}) collective-permute-start(f32[10,4,1792]{2,0,1:T(8,128)S(1)} %copy.11), channel_id=1, source_target_pairs={{0,1},{1,2},{2,3},{3,4},{4,5},{5,6},{6,7},{8,9},{9,10},{10,11},{11... | collective-permute-start | bytes 860168 | tf_op jit(solution)/shard_map/ppermute | solution.py:13
  7.2 0.1 copy.12
  7.2 1.9 %collective-permute-start.1 = (f32[10,4,1792]{2,0,1:T(8,128)S(1)}, f32[10,4,1792]{2,0,1:T(8,128)S(1)}, u32[]{:S(2)}, u32[]{:S(2)}) collective-permute-start(f32[10,4,1792]{2,0,1:T(8,128)S(1)} %copy.12), channel_id=1, source_target_pairs={{1,0},{2,1},{3,2},{4,3},{5,4},{6,5},{7,6},{9,8},{10,9},{11,10},{12... | collective-permute-start | bytes 860168 | tf_op jit(solution)/shard_map/ppermute | solution.py:14
  9.2 0.0 copy-done.1
  9.2 0.0 copy-done.3
  9.2 0.4 multiply_reduce_fusion
  9.6 0.0 copy-start
  9.6 0.0 copy-start.2
  9.6 3.0 %collective-permute-done = f32[10,4,1792]{2,0,1:T(8,128)S(1)} collective-permute-done((f32[10,4,1792]{2,0,1:T(8,128)S(1)}, f32[10,4,1792]{2,0,1:T(8,128)S(1)}, u32[]{:S(2)}, u32[]{:S(2)}) %collective-permute-start) | collective-permute-done | bytes 286752 | tf_op jit(solution)/shard_map/ppermute | solution.py:13
  12.6 0.2 copy.13
  12.8 4.3 %collective-permute-done.1 = f32[10,4,1792]{2,0,1:T(8,128)S(1)} collective-permute-done((f32[10,4,1792]{2,0,1:T(8,128)S(1)}, f32[10,4,1792]{2,0,1:T(8,128)S(1)}, u32[]{:S(2)}, u32[]{:S(2)}) %collective-permute-start.1) | collective-permute-done | bytes 286752 | tf_op jit(solution)/shard_map/ppermute | solution.py:14
  17.0 0.2 copy.14
  17.2 0.0 copy-done
  17.2 0.0 copy-done.2
  17.3 0.3 pad_maximum_fusion
  17.6 0.2 fusion.15
  17.8 0.4 fusion.14
  18.2 0.5 %fusion.18 = f32[8,24,1792]{2,1,0:T(8,128)S(1)} fusion(f32[10,24,1792]{2,1,0:T(8,128)S(1)} %pad_maximum_fusion, f32[8,24,1791]{2,1,0:T(8,128)S(1)} %fusion.14, f32[8,23,1792]{2,1,0:T(8,128)S(1)} %fusion.15), kind=kLoop, calls=%fused_computation.37 | loop fusion | flops 1376256 | bytes 5446912 | tf_op jit(solution)/shard_map/sub | solution.py:49
  18.7 0.2 fusion.13
  18.9 0.4 fusion.12
  19.3 0.5 %pad_subtract_fusion.4 = f32[8,24,1792]{2,1,0:T(8,128)S(1)} fusion(f32[8,24,1791]{2,1,0:T(8,128)S(1)} %fusion.12, f32[8,23,1792]{2,1,0:T(8,128)S(1)} %fusion.13, f32[8,24,1792]{2,1,0:T(8,128)S(1)} %fusion.18), kind=kLoop, calls=%fused_computation.43 | loop fusion | flops 1376256 | bytes 5446912 | tf_op jit(solution)/shard_map/sub | solution.py:49
  19.8 0.2 fusion.11
  20.0 0.4 fusion.10
  20.4 0.5 %pad_subtract_fusion.3 = f32[8,24,1792]{2,1,0:T(8,128)S(1)} fusion(f32[8,24,1791]{2,1,0:T(8,128)S(1)} %fusion.10, f32[8,23,1792]{2,1,0:T(8,128)S(1)} %fusion.11, f32[8,24,1792]{2,1,0:T(8,128)S(1)} %pad_subtract_fusion.4), kind=kLoop, calls=%fused_computation.42 | loop fusion | flops 1376256 | bytes 5446912 | tf_op jit(solution)/shard_map/sub | solution.py:49
  20.9 0.2 fusion.9
  21.1 0.4 fusion.8
  21.5 0.0 copy-start.4
  21.5 0.0 copy-start.5
  21.5 0.6 %fusion.21 = f32[16,1792]{1,0:T(8,128)S(1)} fusion(f32[8,16,1792]{2,1,0:T(8,128)S(1)} %multiply_reduce_fusion, f32[8,24,1791]{2,1,0:T(8,128)S(1)} %fusion.8, f32[8,23,1792]{2,1,0:T(8,128)S(1)} %fusion.9, f32[8,24,1792]{2,1,0:T(8,128)S(1)} %pad_subtract_fusion.3), kind=kLoop, calls=%fused_computation.51 | loop fusion | flops 1347584 | bytes 4644096 | tf_op jit(solution)/shard_map/reduce_sum | solution.py:75
  22.1 1.3 %collective-permute-start.2 = (f32[16,1792]{1,0:T(8,128)S(1)}, f32[16,1792]{1,0:T(8,128)S(1)}, u32[]{:S(2)}, u32[]{:S(2)}) collective-permute-start(f32[16,1792]{1,0:T(8,128)S(1)} %fusion.21), channel_id=1, source_target_pairs={{0,8},{8,0},{16,24},{24,16},{1,9},{9,1},{17,25},{25,17},{2,10},{10... | collective-permute-start | bytes 344072 | tf_op jit(solution)/shard_map/ppermute | solution.py:24
  23.4 1.2 %collective-permute-start.3 = (f32[16,1792]{1,0:T(8,128)S(1)}, f32[16,1792]{1,0:T(8,128)S(1)}, u32[]{:S(2)}, u32[]{:S(2)}) collective-permute-start(f32[16,1792]{1,0:T(8,128)S(1)} %fusion.21), channel_id=1, source_target_pairs={{0,16},{8,24},{16,0},{24,8},{1,17},{9,25},{17,1},{25,9},{2,18},{10... | collective-permute-start | bytes 344072 | tf_op jit(solution)/shard_map/ppermute | solution.py:24
  24.6 0.2 collective-permute-start.4
  24.8 1.0 %collective-permute-done.2 = f32[16,1792]{1,0:T(8,128)S(1)} collective-permute-done((f32[16,1792]{1,0:T(8,128)S(1)}, f32[16,1792]{1,0:T(8,128)S(1)}, u32[]{:S(2)}, u32[]{:S(2)}) %collective-permute-start.2) | collective-permute-done | bytes 114720 | tf_op jit(solution)/shard_map/ppermute | solution.py:24
  25.8 1.2 %collective-permute-done.3 = f32[16,1792]{1,0:T(8,128)S(1)} collective-permute-done((f32[16,1792]{1,0:T(8,128)S(1)}, f32[16,1792]{1,0:T(8,128)S(1)}, u32[]{:S(2)}, u32[]{:S(2)}) %collective-permute-start.3) | collective-permute-done | bytes 114720 | tf_op jit(solution)/shard_map/ppermute | solution.py:24
  27.0 2.1 %collective-permute-done.4 = f32[16,1792]{1,0:T(8,128)S(1)} collective-permute-done((f32[16,1792]{1,0:T(8,128)S(1)}, f32[16,1792]{1,0:T(8,128)S(1)}, u32[]{:S(2)}, u32[]{:S(2)}) %collective-permute-start.4) | collective-permute-done | bytes 114720 | tf_op jit(solution)/shard_map/ppermute | solution.py:24
  29.2 0.0 copy-done.4
  29.2 0.0 copy-done.5
  29.2 0.1 broadcast_multiply_fusion
  29.3 0.1 fusion.22
  29.4 4.4 %collective-permute-start.5 = (f32[8,4,1792]{2,1,0:T(4,128)S(1)}, f32[8,4,1792]{2,1,0:T(4,128)S(1)}, u32[]{:S(2)}, u32[]{:S(2)}) collective-permute-start(f32[8,4,1792]{2,1,0:T(4,128)S(1)} %get-tuple-element.7), channel_id=1, source_target_pairs={{0,1},{1,2},{2,3},{3,4},{4,5},{5,6},{6,7},{8,9},{9,10},{10,11},{11... | collective-permute-start | bytes 688136 | tf_op jit(solution)/shard_map/ppermute | solution.py:13
  33.8 1.9 %collective-permute-start.6 = (f32[8,4,1792]{2,1,0:T(4,128)S(1)}, f32[8,4,1792]{2,1,0:T(4,128)S(1)}, u32[]{:S(2)}, u32[]{:S(2)}) collective-permute-start(f32[8,4,1792]{2,1,0:T(4,128)S(1)} %get-tuple-element.8), channel_id=1, source_target_pairs={{1,0},{2,1},{3,2},{4,3},{5,4},{6,5},{7,6},{9,8},{10,9},{11,10},{12... | collective-permute-start | bytes 688136 | tf_op jit(solution)/shard_map/ppermute | solution.py:14
  35.7 1.0 %collective-permute-done.5 = f32[8,4,1792]{2,1,0:T(4,128)S(1)} collective-permute-done((f32[8,4,1792]{2,1,0:T(4,128)S(1)}, f32[8,4,1792]{2,1,0:T(4,128)S(1)}, u32[]{:S(2)}, u32[]{:S(2)}) %collective-permute-start.5) | collective-permute-done | bytes 229408 | tf_op jit(solution)/shard_map/ppermute | solution.py:13
  36.7 4.4 %collective-permute-done.6 = f32[8,4,1792]{2,1,0:T(4,128)S(1)} collective-permute-done((f32[8,4,1792]{2,1,0:T(4,128)S(1)}, f32[8,4,1792]{2,1,0:T(4,128)S(1)}, u32[]{:S(2)}, u32[]{:S(2)}) %collective-permute-start.6) | collective-permute-done | bytes 229408 | tf_op jit(solution)/shard_map/ppermute | solution.py:14
  41.1 0.2 pad_maximum_fusion.1
  41.3 0.2 fusion.7
  41.5 0.4 fusion.6
  41.9 0.6 %pad_subtract_fusion.2 = f32[8,24,1792]{2,1,0:T(8,128)S(1)} fusion(f32[8,24,1791]{2,1,0:T(8,128)S(1)} %fusion.6, f32[8,23,1792]{2,1,0:T(8,128)S(1)} %fusion.7, f32[8,4,1792]{2,1,0:T(4,128)S(1)} %collective-permute-done.6, f32[8,16,1792]{2,1,0:T(8,128)S(1)} %broadcast_multiply_fusion, f32[8,4,1792]{2,1,0:T(4,128)S(1)} %collective-permute-done.5), kind=kLoop, calls=%fused_computation.41 | loop fusion | flops 2064384 | bytes 5446912 | tf_op jit(solution)/shard_map/sub | solution.py:49
  42.5 0.2 fusion.5
  42.7 0.4 fusion.4
  43.1 0.5 %pad_subtract_fusion.1 = f32[8,24,1792]{2,1,0:T(8,128)S(1)} fusion(f32[8,24,1791]{2,1,0:T(8,128)S(1)} %fusion.4, f32[8,23,1792]{2,1,0:T(8,128)S(1)} %fusion.5, f32[8,24,1792]{2,1,0:T(8,128)S(1)} %pad_subtract_fusion.2), kind=kLoop, calls=%fused_computation.40 | loop fusion | flops 1376256 | bytes 5446912 | tf_op jit(solution)/shard_map/sub | solution.py:49
  43.6 0.2 fusion.3
  43.8 0.4 fusion.2
  44.2 0.5 %pad_subtract_fusion = f32[8,24,1792]{2,1,0:T(8,128)S(1)} fusion(f32[8,24,1791]{2,1,0:T(8,128)S(1)} %fusion.2, f32[8,23,1792]{2,1,0:T(8,128)S(1)} %fusion.3, f32[8,24,1792]{2,1,0:T(8,128)S(1)} %pad_subtract_fusion.1), kind=kLoop, calls=%fused_computation.39 | loop fusion | flops 1376256 | bytes 5446912 | tf_op jit(solution)/shard_map/sub | solution.py:49
  44.7 0.2 fusion.1
  44.9 0.4 fusion
  45.3 1.5 %fusion.19 = f32[8,16,1792]{2,1,0:T(8,128)} fusion(f32[8,16,1792]{2,1,0:T(8,128)S(1)} %copy-done, f32[8,24,1791]{2,1,0:T(8,128)S(1)} %fusion, f32[8,23,1792]{2,1,0:T(8,128)S(1)} %fusion.1, f32[8,24,1792]{2,1,0:T(8,128)S(1)} %pad_subtract_fusion), kind=kLoop, calls=%fused_computation.45 | loop fusion | flops 1146880 | bytes 5446912 | tf_op jit(solution)/shard_map/add | solution.py:78
  (4 shorter events, 0.1 us)
Async XLA Ops:
  1.0 8.2 %copy-start.1 = (bf16[8,4,16,1792]{3,2,1,0:T(8,128)(2,1)S(1)}, bf16[8,4,16,1792]{3,2,1,0:T(8,128)(2,1)}, u32[]{:S(2)}) copy-start(bf16[8,4,16,1792]{3,2,1,0:T(8,128)(2,1)} %param.8) | copy-start | bytes 5505028
  1.0 8.2 %copy-start.3 = (f32[4,16,1792]{2,1,0:T(8,128)S(1)}, f32[4,16,1792]{2,1,0:T(8,128)}, u32[]{:S(2)}) copy-start(f32[4,16,1792]{2,1,0:T(8,128)} %param.9) | copy-start | bytes 1376260
  2.6 10.0 %collective-permute-start = (f32[10,4,1792]{2,0,1:T(8,128)S(1)}, f32[10,4,1792]{2,0,1:T(8,128)S(1)}, u32[]{:S(2)}, u32[]{:S(2)}) collective-permute-start(f32[10,4,1792]{2,0,1:T(8,128)S(1)} %copy.11), channel_id=1, source_target_pairs={{0,1},{1,2},{2,3},{3,4},{4,5},{5,6},{6,7},{8,9},{9,10},{10,11},{11... | collective-permute-start | bytes 860168 | tf_op jit(solution)/shard_map/ppermute | solution.py:13
  7.2 9.8 %collective-permute-start.1 = (f32[10,4,1792]{2,0,1:T(8,128)S(1)}, f32[10,4,1792]{2,0,1:T(8,128)S(1)}, u32[]{:S(2)}, u32[]{:S(2)}) collective-permute-start(f32[10,4,1792]{2,0,1:T(8,128)S(1)} %copy.12), channel_id=1, source_target_pairs={{1,0},{2,1},{3,2},{4,3},{5,4},{6,5},{7,6},{9,8},{10,9},{11,10},{12... | collective-permute-start | bytes 860168 | tf_op jit(solution)/shard_map/ppermute | solution.py:14
  9.6 7.7 %copy-start = (f32[8,16,1792]{2,1,0:T(8,128)S(1)}, f32[8,16,1792]{2,1,0:T(8,128)}, u32[]{:S(2)}) copy-start(f32[8,16,1792]{2,1,0:T(8,128)} %param.7) | copy-start | bytes 2752516
  9.6 7.7 %copy-start.2 = (f32[16,1792]{1,0:T(8,128)S(1)}, f32[16,1792]{1,0:T(8,128)}, u32[]{:S(2)}) copy-start(f32[16,1792]{1,0:T(8,128)} %param.13) | copy-start | bytes 344068
  21.5 7.6 %copy-start.4 = (f32[16,1792]{1,0:T(8,128)S(1)}, f32[16,1792]{1,0:T(8,128)}, u32[]{:S(2)}) copy-start(f32[16,1792]{1,0:T(8,128)} %param.10) | copy-start | bytes 344068
  21.5 7.6 %copy-start.5 = (s32[16,1792]{1,0:T(8,128)S(1)}, s32[16,1792]{1,0:T(8,128)}, u32[]{:S(2)}) copy-start(s32[16,1792]{1,0:T(8,128)} %param.11) | copy-start | bytes 344068
  22.1 3.7 %collective-permute-start.2 = (f32[16,1792]{1,0:T(8,128)S(1)}, f32[16,1792]{1,0:T(8,128)S(1)}, u32[]{:S(2)}, u32[]{:S(2)}) collective-permute-start(f32[16,1792]{1,0:T(8,128)S(1)} %fusion.21), channel_id=1, source_target_pairs={{0,8},{8,0},{16,24},{24,16},{1,9},{9,1},{17,25},{25,17},{2,10},{10... | collective-permute-start | bytes 344072 | tf_op jit(solution)/shard_map/ppermute | solution.py:24
  23.4 3.6 %collective-permute-start.3 = (f32[16,1792]{1,0:T(8,128)S(1)}, f32[16,1792]{1,0:T(8,128)S(1)}, u32[]{:S(2)}, u32[]{:S(2)}) collective-permute-start(f32[16,1792]{1,0:T(8,128)S(1)} %fusion.21), channel_id=1, source_target_pairs={{0,16},{8,24},{16,0},{24,8},{1,17},{9,25},{17,1},{25,9},{2,18},{10... | collective-permute-start | bytes 344072 | tf_op jit(solution)/shard_map/ppermute | solution.py:24
  24.6 4.5 %collective-permute-start.4 = (f32[16,1792]{1,0:T(8,128)S(1)}, f32[16,1792]{1,0:T(8,128)S(1)}, u32[]{:S(2)}, u32[]{:S(2)}) collective-permute-start(f32[16,1792]{1,0:T(8,128)S(1)} %fusion.21), channel_id=1, source_target_pairs={{0,24},{8,16},{16,8},{24,0},{1,25},{9,17},{17,9},{25,1},{2,26},{10... | collective-permute-start | bytes 344072 | tf_op jit(solution)/shard_map/ppermute | solution.py:24
  29.4 7.4 %collective-permute-start.5 = (f32[8,4,1792]{2,1,0:T(4,128)S(1)}, f32[8,4,1792]{2,1,0:T(4,128)S(1)}, u32[]{:S(2)}, u32[]{:S(2)}) collective-permute-start(f32[8,4,1792]{2,1,0:T(4,128)S(1)} %get-tuple-element.7), channel_id=1, source_target_pairs={{0,1},{1,2},{2,3},{3,4},{4,5},{5,6},{6,7},{8,9},{9,10},{10,11},{11... | collective-permute-start | bytes 688136 | tf_op jit(solution)/shard_map/ppermute | solution.py:13
  33.8 7.3 %collective-permute-start.6 = (f32[8,4,1792]{2,1,0:T(4,128)S(1)}, f32[8,4,1792]{2,1,0:T(4,128)S(1)}, u32[]{:S(2)}, u32[]{:S(2)}) collective-permute-start(f32[8,4,1792]{2,1,0:T(4,128)S(1)} %get-tuple-element.8), channel_id=1, source_target_pairs={{1,0},{2,1},{3,2},{4,3},{5,4},{6,5},{7,6},{9,8},{10,9},{11,10},{12... | collective-permute-start | bytes 688136 | tf_op jit(solution)/shard_map/ppermute | solution.py:14

commit v12 on v11

--- a/solution.py
+++ b/solution.py
@@ -17,22 +17,13 @@
 
 def mem_sum(part):
     count = lax.axis_size("mem")
-    if count & (count - 1):
+    rows, cols = part.shape
+    if rows % count:
         return lax.psum(part, "mem")
-
-    def partner(stride):
-        return lax.ppermute(part, "mem", [(i, i ^ stride) for i in range(count)])
-
-    stride = 1
-    while stride < count:
-        if stride * 2 < count:
-            near, far, both = partner(stride), partner(2 * stride), partner(3 * stride)
-            part = (part + near) + (far + both)
-            stride *= 4
-        else:
-            part = part + partner(stride)
-            stride *= 2
-    return part
+    chunks = part.reshape(count, rows // count, cols)
+    mine = jnp.sum(lax.all_to_all(chunks, "mem", 0, 0), 0)
+    spread = jnp.broadcast_to(mine[None], chunks.shape)
+    return lax.all_to_all(spread, "mem", 0, 0).reshape(rows, cols)
 
 
 def diffuse(values, row_coef, col_coef):

time: 47 us -> 53.5 us (1.14)
  blocking collectives: 0 us -> 13.3 us
  waiting for transfers between devices: 17 us -> 12.7 us
  starting transfers between devices: 15.5 us -> 12.9 us
    all_to_all x0 -> x2, blocking collectives: none -> 13.3 us  [the longest x1 7.06 us: mem_sum(): mine = jnp.sum(lax.all_to_all(chunks, 'mem', 0, 0), 0)]
    ppermute x3 -> x0, waiting for transfers between devices: 4.34 us -> none  [partner(): return lax.ppermute(part, 'mem', [(i, i ^ stride) for i in range(count)])]
    ppermute x3 -> x0, starting transfers between devices: 2.71 us -> none  [partner(): return lax.ppermute(part, 'mem', [(i, i ^ stride) for i in range(count)])]
  transfers between devices with their start and end apart: 7 -> 4, of which waited for: 7 -> 4; matrix products, arithmetic and copies ran while one was open for 1% -> 1% of each run, Pallas kernels for 0% -> 0%
where the time goes in v12:
time: 53.5 us; the launch traced here: 53.2 us
  other arithmetic  13.3 us (25%)
  blocking collectives  13.3 us (25%)
  starting transfers between devices  12.9 us (24%)
  waiting for transfers between devices  12.7 us (24%)
  local copies, waits for them, and re-layouts  0.72 us (1%)
    ppermute x2, starting transfers between devices, exchange(): above = lax.ppermute(tail, 'tile', [(i, i + 1) for i in range(count - 1)])  9.02 us
    ppermute x2, waiting for transfers between devices, exchange(): below = lax.ppermute(head, 'tile', [(i + 1, i) for i in range(count - 1)])  8.68 us
    all_to_all x1, blocking collectives, mem_sum(): mine = jnp.sum(lax.all_to_all(chunks, 'mem', 0, 0), 0)  7.06 us
    all_to_all x1, blocking collectives, mem_sum(): return lax.all_to_all(spread, 'mem', 0, 0).reshape(rows, cols)  6.21 us
    ppermute x2, waiting for transfers between devices, exchange(): above = lax.ppermute(tail, 'tile', [(i, i + 1) for i in range(count - 1)])  3.99 us
    ppermute x2, starting transfers between devices, exchange(): below = lax.ppermute(head, 'tile', [(i + 1, i) for i in range(count - 1)])  3.84 us
    mul x8, other arithmetic, diffuse(): col_coef[..., :, :-1] * (values[..., :, 1:] - values[..., :, :-1])  3.39 us
    sub x6, other arithmetic, diffuse(): values + jnp.concatenate([col_flux, zeros_col], -1)  2.95 us
  transfers between devices with their start and end apart: 4, of which 4 were waited for; matrix products, arithmetic and copies ran while one was open for 1% of the time, Pallas kernels for 0%

profile of v12, /device:TPU:1, one launch (start us, length us, event | category | flops | bytes accessed | tf_op | source)
XLA Modules:
  0.0 53.2 jit_solution(11784136071399940874)
XLA Ops:
  0.0 1.0 %select_bitcast_fusion = f32[1,16,1792]{2,1,0:T(8,128)S(1)} fusion(f32[16,1792]{1,0:T(8,128)} %param.12, pred[16]{0:T(512)(128)(4,1)S(1)} %add_compare_fusion), kind=kLoop, calls=%fused_computation.61 | loop fusion | flops 28672 | bytes 229392 | tf_op jit(solution)/shard_map/broadcast_in_dim | solution.py:61
  1.0 0.0 copy-start.1
  1.0 0.0 copy-start.3
  1.0 1.5 %pad_maximum_fusion.4 = (f32[10,4,1792]{2,1,0:T(4,128)S(1)}, f32[10,4,1792]{2,1,0:T(4,128)S(1)}) fusion(f32[1,16,1792]{2,1,0:T(8,128)} %bitcast.16, f32[1,16,1792]{2,1,0:T(8,128)S(1)} %select_bitcast_fusion, f32[8,16,1792]{2,1,0:T(8,128)} %param.7), kind=kLoop, calls=%fused_computation.58 | loop fusion | flops 286720 | bytes 1720320 | tf_op jit(solution)/shard_map/slice | solution.py:12
  2.5 0.1 copy.15
  2.6 4.6 %collective-permute-start = (f32[10,4,1792]{2,0,1:T(8,128)S(1)}, f32[10,4,1792]{2,0,1:T(8,128)S(1)}, u32[]{:S(2)}, u32[]{:S(2)}) collective-permute-start(f32[10,4,1792]{2,0,1:T(8,128)S(1)} %copy.15), channel_id=1, source_target_pairs={{0,1},{1,2},{2,3},{3,4},{4,5},{5,6},{6,7},{8,9},{9,10},{10,11},{11... | collective-permute-start | bytes 860168 | tf_op jit(solution)/shard_map/ppermute | solution.py:13
  7.2 0.1 copy.16
  7.2 1.9 %collective-permute-start.1 = (f32[10,4,1792]{2,0,1:T(8,128)S(1)}, f32[10,4,1792]{2,0,1:T(8,128)S(1)}, u32[]{:S(2)}, u32[]{:S(2)}) collective-permute-start(f32[10,4,1792]{2,0,1:T(8,128)S(1)} %copy.16), channel_id=1, source_target_pairs={{1,0},{2,1},{3,2},{4,3},{5,4},{6,5},{7,6},{9,8},{10,9},{11,10},{12... | collective-permute-start | bytes 860168 | tf_op jit(solution)/shard_map/ppermute | solution.py:14
  9.2 0.0 copy-done.1
  9.2 0.0 copy-done.3
  9.2 0.4 multiply_reduce_fusion
  9.6 0.0 copy-start
  9.6 0.0 copy-start.2
  9.6 3.0 %collective-permute-done = f32[10,4,1792]{2,0,1:T(8,128)S(1)} collective-permute-done((f32[10,4,1792]{2,0,1:T(8,128)S(1)}, f32[10,4,1792]{2,0,1:T(8,128)S(1)}, u32[]{:S(2)}, u32[]{:S(2)}) %collective-permute-start) | collective-permute-done | bytes 286752 | tf_op jit(solution)/shard_map/ppermute | solution.py:13
  12.6 0.2 copy.17
  12.8 4.3 %collective-permute-done.1 = f32[10,4,1792]{2,0,1:T(8,128)S(1)} collective-permute-done((f32[10,4,1792]{2,0,1:T(8,128)S(1)}, f32[10,4,1792]{2,0,1:T(8,128)S(1)}, u32[]{:S(2)}, u32[]{:S(2)}) %collective-permute-start.1) | collective-permute-done | bytes 286752 | tf_op jit(solution)/shard_map/ppermute | solution.py:14
  17.0 0.2 copy.18
  17.2 0.0 copy-done
  17.2 0.0 copy-done.2
  17.3 0.3 pad_maximum_fusion
  17.6 0.2 fusion.15
  17.8 0.4 fusion.14
  18.2 0.5 fusion.18
  18.7 0.2 fusion.13
  18.9 0.4 fusion.12
  19.3 0.5 pad_subtract_fusion.4
  19.8 0.2 fusion.11
  20.0 0.4 fusion.10
  20.4 0.5 pad_subtract_fusion.3
  20.9 0.2 fusion.9
  21.1 0.4 fusion.8
  21.5 0.0 copy-start.4
  21.5 0.0 copy-start.5
  21.5 0.6 %fusion.21 = f32[16,1792]{1,0:T(8,128)S(1)} fusion(f32[8,16,1792]{2,1,0:T(8,128)S(1)} %multiply_reduce_fusion, f32[8,24,1791]{2,1,0:T(8,128)S(1)} %fusion.8, f32[8,23,1792]{2,1,0:T(8,128)S(1)} %fusion.9, f32[8,24,1792]{2,1,0:T(8,128)S(1)} %pad_subtract_fusion.3), kind=kLoop, calls=%fused_computation.51 | loop fusion | flops 1347584 | bytes 4644096 | tf_op jit(solution)/shard_map/reduce_sum | solution.py:66
  22.1 7.1 %all_to_all.10 = f32[4,4,1792]{2,1,0:T(4,128)S(1)} all-to-all(f32[4,4,1792]{2,1,0:T(4,128)S(1)} %reshape.12), channel_id=1, replica_groups=mesh['mem'=4,'tile'=8] {'mem'}, dimensions={0} | all-to-all | bytes 229376 | tf_op jit(solution)/shard_map/all_to_all | solution.py:24
  29.3 6.2 %all_to_all.11 = f32[4,4,1792]{2,1,0:T(4,128)S(1)} all-to-all(f32[4,4,1792]{2,1,0:T(4,128)S(1)} %broadcast_in_dim.11), channel_id=1, replica_groups=mesh['mem'=4,'tile'=8] {'mem'}, dimensions={0} | all-to-all | bytes 229376 | tf_op jit(solution)/shard_map/all_to_all | solution.py:26
  35.5 0.0 copy-done.4
  35.5 0.0 copy-done.5
  35.6 0.1 broadcast_multiply_fusion
  35.6 0.1 fusion.22
  35.7 4.4 %collective-permute-start.2 = (f32[8,4,1792]{2,1,0:T(4,128)S(1)}, f32[8,4,1792]{2,1,0:T(4,128)S(1)}, u32[]{:S(2)}, u32[]{:S(2)}) collective-permute-start(f32[8,4,1792]{2,1,0:T(4,128)S(1)} %get-tuple-element.7), channel_id=1, source_target_pairs={{0,1},{1,2},{2,3},{3,4},{4,5},{5,6},{6,7},{8,9},{9,10},{10,11},{11... | collective-permute-start | bytes 688136 | tf_op jit(solution)/shard_map/ppermute | solution.py:13
  40.2 1.9 %collective-permute-start.3 = (f32[8,4,1792]{2,1,0:T(4,128)S(1)}, f32[8,4,1792]{2,1,0:T(4,128)S(1)}, u32[]{:S(2)}, u32[]{:S(2)}) collective-permute-start(f32[8,4,1792]{2,1,0:T(4,128)S(1)} %get-tuple-element.8), channel_id=1, source_target_pairs={{1,0},{2,1},{3,2},{4,3},{5,4},{6,5},{7,6},{9,8},{10,9},{11,10},{12... | collective-permute-start | bytes 688136 | tf_op jit(solution)/shard_map/ppermute | solution.py:14
  42.1 1.0 %collective-permute-done.2 = f32[8,4,1792]{2,1,0:T(4,128)S(1)} collective-permute-done((f32[8,4,1792]{2,1,0:T(4,128)S(1)}, f32[8,4,1792]{2,1,0:T(4,128)S(1)}, u32[]{:S(2)}, u32[]{:S(2)}) %collective-permute-start.2) | collective-permute-done | bytes 229408 | tf_op jit(solution)/shard_map/ppermute | solution.py:13
  43.1 4.4 %collective-permute-done.3 = f32[8,4,1792]{2,1,0:T(4,128)S(1)} collective-permute-done((f32[8,4,1792]{2,1,0:T(4,128)S(1)}, f32[8,4,1792]{2,1,0:T(4,128)S(1)}, u32[]{:S(2)}, u32[]{:S(2)}) %collective-permute-start.3) | collective-permute-done | bytes 229408 | tf_op jit(solution)/shard_map/ppermute | solution.py:14
  47.5 0.2 pad_maximum_fusion.1
  47.7 0.2 fusion.7
  47.9 0.4 fusion.6
  48.3 0.6 %pad_subtract_fusion.2 = f32[8,24,1792]{2,1,0:T(8,128)S(1)} fusion(f32[8,24,1791]{2,1,0:T(8,128)S(1)} %fusion.6, f32[8,23,1792]{2,1,0:T(8,128)S(1)} %fusion.7, f32[8,4,1792]{2,1,0:T(4,128)S(1)} %collective-permute-done.3, f32[8,16,1792]{2,1,0:T(8,128)S(1)} %broadcast_multiply_fusion, f32[8,4,1792]{2,1,0:T(4,128)S(1)} %collective-permute-done.2), kind=kLoop, calls=%fused_computation.41 | loop fusion | flops 2064384 | bytes 5446912 | tf_op jit(solution)/shard_map/sub | solution.py:40
  48.9 0.2 fusion.5
  49.1 0.4 fusion.4
  49.5 0.5 pad_subtract_fusion.1
  50.0 0.2 fusion.3
  50.2 0.4 fusion.2
  50.6 0.5 pad_subtract_fusion
  51.1 0.2 fusion.1
  51.3 0.4 fusion
  51.7 1.5 %fusion.19 = f32[8,16,1792]{2,1,0:T(8,128)} fusion(f32[8,16,1792]{2,1,0:T(8,128)S(1)} %copy-done, f32[8,24,1791]{2,1,0:T(8,128)S(1)} %fusion, f32[8,23,1792]{2,1,0:T(8,128)S(1)} %fusion.1, f32[8,24,1792]{2,1,0:T(8,128)S(1)} %pad_subtract_fusion), kind=kLoop, calls=%fused_computation.45 | loop fusion | flops 1146880 | bytes 5446912 | tf_op jit(solution)/shard_map/add | solution.py:69
  (8 shorter events, 0.2 us)
Async XLA Ops:
  1.0 8.2 %copy-start.1 = (bf16[8,4,16,1792]{3,2,1,0:T(8,128)(2,1)S(1)}, bf16[8,4,16,1792]{3,2,1,0:T(8,128)(2,1)}, u32[]{:S(2)}) copy-start(bf16[8,4,16,1792]{3,2,1,0:T(8,128)(2,1)} %param.8) | copy-start | bytes 5505028
  1.0 8.2 %copy-start.3 = (f32[4,16,1792]{2,1,0:T(8,128)S(1)}, f32[4,16,1792]{2,1,0:T(8,128)}, u32[]{:S(2)}) copy-start(f32[4,16,1792]{2,1,0:T(8,128)} %param.9) | copy-start | bytes 1376260
  2.6 10.0 %collective-permute-start = (f32[10,4,1792]{2,0,1:T(8,128)S(1)}, f32[10,4,1792]{2,0,1:T(8,128)S(1)}, u32[]{:S(2)}, u32[]{:S(2)}) collective-permute-start(f32[10,4,1792]{2,0,1:T(8,128)S(1)} %copy.15), channel_id=1, source_target_pairs={{0,1},{1,2},{2,3},{3,4},{4,5},{5,6},{6,7},{8,9},{9,10},{10,11},{11... | collective-permute-start | bytes 860168 | tf_op jit(solution)/shard_map/ppermute | solution.py:13
  7.2 9.8 %collective-permute-start.1 = (f32[10,4,1792]{2,0,1:T(8,128)S(1)}, f32[10,4,1792]{2,0,1:T(8,128)S(1)}, u32[]{:S(2)}, u32[]{:S(2)}) collective-permute-start(f32[10,4,1792]{2,0,1:T(8,128)S(1)} %copy.16), channel_id=1, source_target_pairs={{1,0},{2,1},{3,2},{4,3},{5,4},{6,5},{7,6},{9,8},{10,9},{11,10},{12... | collective-permute-start | bytes 860168 | tf_op jit(solution)/shard_map/ppermute | solution.py:14
  9.6 7.7 %copy-start = (f32[8,16,1792]{2,1,0:T(8,128)S(1)}, f32[8,16,1792]{2,1,0:T(8,128)}, u32[]{:S(2)}) copy-start(f32[8,16,1792]{2,1,0:T(8,128)} %param.7) | copy-start | bytes 2752516
  9.6 7.7 %copy-start.2 = (f32[16,1792]{1,0:T(8,128)S(1)}, f32[16,1792]{1,0:T(8,128)}, u32[]{:S(2)}) copy-start(f32[16,1792]{1,0:T(8,128)} %param.13) | copy-start | bytes 344068
  21.5 14.0 %copy-start.4 = (f32[16,1792]{1,0:T(8,128)S(1)}, f32[16,1792]{1,0:T(8,128)}, u32[]{:S(2)}) copy-start(f32[16,1792]{1,0:T(8,128)} %param.10) | copy-start | bytes 344068
  21.5 14.0 %copy-start.5 = (s32[16,1792]{1,0:T(8,128)S(1)}, s32[16,1792]{1,0:T(8,128)}, u32[]{:S(2)}) copy-start(s32[16,1792]{1,0:T(8,128)} %param.11) | copy-start | bytes 344068
  35.7 7.4 %collective-permute-start.2 = (f32[8,4,1792]{2,1,0:T(4,128)S(1)}, f32[8,4,1792]{2,1,0:T(4,128)S(1)}, u32[]{:S(2)}, u32[]{:S(2)}) collective-permute-start(f32[8,4,1792]{2,1,0:T(4,128)S(1)} %get-tuple-element.7), channel_id=1, source_target_pairs={{0,1},{1,2},{2,3},{3,4},{4,5},{5,6},{6,7},{8,9},{9,10},{10,11},{11... | collective-permute-start | bytes 688136 | tf_op jit(solution)/shard_map/ppermute | solution.py:13
  40.2 7.3 %collective-permute-start.3 = (f32[8,4,1792]{2,1,0:T(4,128)S(1)}, f32[8,4,1792]{2,1,0:T(4,128)S(1)}, u32[]{:S(2)}, u32[]{:S(2)}) collective-permute-start(f32[8,4,1792]{2,1,0:T(4,128)S(1)} %get-tuple-element.8), channel_id=1, source_target_pairs={{1,0},{2,1},{3,2},{4,3},{5,4},{6,5},{7,6},{9,8},{10,9},{11,10},{12... | collective-permute-start | bytes 688136 | tf_op jit(solution)/shard_map/ppermute | solution.py:14

commit v13 on v11

--- a/solution.py
+++ b/solution.py
@@ -10,8 +10,18 @@
     count = lax.axis_size("tile")
     head = part[..., :width, :]
     tail = part[..., -width:, :]
-    above = lax.ppermute(tail, "tile", [(i, i + 1) for i in range(count - 1)])
-    below = lax.ppermute(head, "tile", [(i + 1, i) for i in range(count - 1)])
+    if count % 2:
+        above = lax.ppermute(tail, "tile", [(i, i + 1) for i in range(count - 1)])
+        below = lax.ppermute(head, "tile", [(i + 1, i) for i in range(count - 1)])
+        return jnp.concatenate([above, part, below], -2)
+    odd = lax.axis_index("tile") % 2 == 1
+    pairs = lambda first: [(i, i + 1) for i in range(first, count - 1, 2)] + [
+        (i + 1, i) for i in range(first, count - 1, 2)
+    ]
+    far = lax.ppermute(jnp.where(odd, tail, head), "tile", pairs(1))
+    near = lax.ppermute(jnp.where(odd, head, tail), "tile", pairs(0))
+    above = jnp.where(odd, near, far)
+    below = jnp.where(odd, far, near)
     return jnp.concatenate([above, part, below], -2)
 
 

time: 47 us -> 41.1 us (0.87)
  waiting for transfers between devices: 17 us -> 13.6 us
  starting transfers between devices: 15.5 us -> 13.1 us
    ppermute x4, waiting for transfers between devices: 12.7 us -> 9.25 us  [the longest x2 9.25 us: exchange(): far = lax.ppermute(jnp.where(odd, tail, head), 'tile', pairs(1))]
    ppermute x4, starting transfers between devices: 12.8 us -> 10.4 us  [the longest x2 10.2 us: exchange(): far = lax.ppermute(jnp.where(odd, tail, head), 'tile', pairs(1))]
    select_n x0 -> x5, other arithmetic: none -> 1.89 us  [the longest x2 1.44 us: exchange(): near = lax.ppermute(jnp.where(odd, head, tail), 'tile', pairs(0))]
    slice x1 -> x0, other arithmetic: 1.48 us -> none  [exchange(): tail = part[..., -width:, :]]
  transfers between devices with their start and end apart: 7 -> 7, of which waited for: 7 -> 5; matrix products, arithmetic and copies ran while one was open for 1% -> 1% of each run, Pallas kernels for 0% -> 0%
where the time goes in v13:
time: 41.1 us; the launch traced here: 40.9 us
  other arithmetic  13.7 us (33%)
  waiting for transfers between devices  13.6 us (33%)
  starting transfers between devices  13.1 us (32%)
    ppermute x2, starting transfers between devices, exchange(): far = lax.ppermute(jnp.where(odd, tail, head), 'tile', pairs(1))  10.2 us
    ppermute x2, waiting for transfers between devices, exchange(): far = lax.ppermute(jnp.where(odd, tail, head), 'tile', pairs(1))  9.25 us
    ppermute x3, waiting for transfers between devices, partner(): return lax.ppermute(part, 'mem', [(i, i ^ stride) for i in range(count)])  4.34 us
    mul x8, other arithmetic, diffuse(): col_coef[..., :, :-1] * (values[..., :, 1:] - values[..., :, :-1])  3.39 us
    sub x6, other arithmetic, diffuse(): values + jnp.concatenate([col_flux, zeros_col], -1)  2.95 us
    ppermute x3, starting transfers between devices, partner(): return lax.ppermute(part, 'mem', [(i, i ^ stride) for i in range(count)])  2.71 us
    mul x9, other arithmetic, diffuse(): row_coef[..., :-1, :] * (values[..., 1:, :] - values[..., :-1, :])  1.5 us
    add x1, other arithmetic, per_device(): controls + localize(sensitivity, coef_band)[:, STEPS:STEPS + row_count]  1.46 us
  transfers between devices with their start and end apart: 7, of which 5 were waited for; matrix products, arithmetic and copies ran while one was open for 1% of the time, Pallas kernels for 0%

profile of v13, /device:TPU:1, one launch (start us, length us, event | category | flops | bytes accessed | tf_op | source)
XLA Modules:
  0.0 40.9 jit_solution(8426027593375398029)
XLA Ops:
  0.0 1.0 %select_bitcast_fusion = f32[1,16,1792]{2,1,0:T(8,128)S(1)} fusion(f32[16,1792]{1,0:T(8,128)} %param.12, pred[16]{0:T(512)(128)(4,1)S(1)} %add_compare_fusion), kind=kLoop, calls=%fused_computation.68 | loop fusion | flops 28672 | bytes 229392 | tf_op jit(solution)/shard_map/broadcast_in_dim | solution.py:80
  1.0 1.4 %broadcast_select_fusion.1 = (f32[10,4,1792]{2,1,0:T(4,128)S(1)}, f32[10,4,1792]{2,1,0:T(4,128)S(1)}, f32[10,4,1792]{2,1,0:T(4,128)S(1)}) fusion(pred[]{:T(512)S(6)} %eq.7, f32[1,16,1792]{2,1,0:T(8,128)} %bitcast.27, f32[1,16,1792]{2,1,0:T(8,128)S(1)} %select_bitcast_fusion, f32[8,16,1792]{2,1,0:T(8,128)} %param.7), kind=kLoop, calls=%fused_computation.66 | loop fusion | flops 358400 | bytes 2007041 | tf_op jit(solution)/shard_map/jit(_where)/select_n | solution.py:22
  2.3 0.0 copy-start.1
  2.4 0.0 copy-start.3
  2.4 0.1 copy.12
  2.5 4.7 %collective-permute-start.1 = (f32[10,4,1792]{2,0,1:T(8,128)S(1)}, f32[10,4,1792]{2,0,1:T(8,128)S(1)}, u32[]{:S(2)}, u32[]{:S(2)}) collective-permute-start(f32[10,4,1792]{2,0,1:T(8,128)S(1)} %copy.12), channel_id=1, source_target_pairs={{1,2},{3,4},{5,6},{2,1},{4,3},{6,5},{9,10},{11,12},{13,14},{10,9},... | collective-permute-start | bytes 860168 | tf_op jit(solution)/shard_map/ppermute | solution.py:21
  7.2 0.1 copy.11
  7.3 0.1 collective-permute-start
  7.4 0.0 copy-done.1
  7.4 0.0 copy-done.3
  7.4 0.4 multiply_reduce_fusion
  7.8 0.0 copy-start
  7.8 0.0 copy-start.2
  7.8 5.6 %collective-permute-done.1 = f32[10,4,1792]{2,0,1:T(8,128)S(1)} collective-permute-done((f32[10,4,1792]{2,0,1:T(8,128)S(1)}, f32[10,4,1792]{2,0,1:T(8,128)S(1)}, u32[]{:S(2)}, u32[]{:S(2)}) %collective-permute-start.1) | collective-permute-done | bytes 286752 | tf_op jit(solution)/shard_map/ppermute | solution.py:21
  13.4 0.0 collective-permute-done
  13.4 0.4 copy_select_fusion.1
  13.7 0.0 copy-done
  13.8 0.0 copy-done.2
  13.8 0.3 pad_maximum_fusion
  14.1 0.2 fusion.15
  14.3 0.4 %fusion.14 = f32[8,24,1791]{2,1,0:T(8,128)S(1)} fusion(f32[10,24,1792]{2,1,0:T(8,128)S(1)} %pad_maximum_fusion, f32[24,1791]{1,0:T(8,128)S(1)} %bitcast.15), kind=kLoop, calls=%fused_computation.31 | loop fusion | flops 687744 | bytes 4298400 | tf_op jit(solution)/shard_map/mul | solution.py:50
  14.7 0.5 %fusion.18 = f32[8,24,1792]{2,1,0:T(8,128)S(1)} fusion(f32[10,24,1792]{2,1,0:T(8,128)S(1)} %pad_maximum_fusion, f32[8,24,1791]{2,1,0:T(8,128)S(1)} %fusion.14, f32[8,23,1792]{2,1,0:T(8,128)S(1)} %fusion.15), kind=kLoop, calls=%fused_computation.37 | loop fusion | flops 1376256 | bytes 5446912 | tf_op jit(solution)/shard_map/sub | solution.py:59
  15.2 0.2 fusion.13
  15.4 0.4 %fusion.12 = f32[8,24,1791]{2,1,0:T(8,128)S(1)} fusion(f32[8,24,1792]{2,1,0:T(8,128)S(1)} %fusion.18, f32[24,1791]{1,0:T(8,128)S(1)} %bitcast.16), kind=kLoop, calls=%fused_computation.27 | loop fusion | flops 687744 | bytes 4298400 | tf_op jit(solution)/shard_map/mul | solution.py:50
  15.8 0.5 %pad_subtract_fusion.4 = f32[8,24,1792]{2,1,0:T(8,128)S(1)} fusion(f32[8,24,1791]{2,1,0:T(8,128)S(1)} %fusion.12, f32[8,23,1792]{2,1,0:T(8,128)S(1)} %fusion.13, f32[8,24,1792]{2,1,0:T(8,128)S(1)} %fusion.18), kind=kLoop, calls=%fused_computation.43 | loop fusion | flops 1376256 | bytes 5446912 | tf_op jit(solution)/shard_map/sub | solution.py:59
  16.3 0.2 fusion.11
  16.5 0.4 %fusion.10 = f32[8,24,1791]{2,1,0:T(8,128)S(1)} fusion(f32[8,24,1792]{2,1,0:T(8,128)S(1)} %pad_subtract_fusion.4, f32[24,1791]{1,0:T(8,128)S(1)} %bitcast.17), kind=kLoop, calls=%fused_computation.23 | loop fusion | flops 687744 | bytes 4298400 | tf_op jit(solution)/shard_map/mul | solution.py:50
  16.9 0.5 %pad_subtract_fusion.3 = f32[8,24,1792]{2,1,0:T(8,128)S(1)} fusion(f32[8,24,1791]{2,1,0:T(8,128)S(1)} %fusion.10, f32[8,23,1792]{2,1,0:T(8,128)S(1)} %fusion.11, f32[8,24,1792]{2,1,0:T(8,128)S(1)} %pad_subtract_fusion.4), kind=kLoop, calls=%fused_computation.42 | loop fusion | flops 1376256 | bytes 5446912 | tf_op jit(solution)/shard_map/sub | solution.py:59
  17.4 0.2 fusion.9
  17.6 0.4 %fusion.8 = f32[8,24,1791]{2,1,0:T(8,128)S(1)} fusion(f32[8,24,1792]{2,1,0:T(8,128)S(1)} %pad_subtract_fusion.3, f32[24,1791]{1,0:T(8,128)S(1)} %bitcast.18), kind=kLoop, calls=%fused_computation.19 | loop fusion | flops 687744 | bytes 4298400 | tf_op jit(solution)/shard_map/mul | solution.py:50
  18.0 0.0 copy-start.4
  18.0 0.0 copy-start.5
  18.1 0.6 %fusion.21 = f32[16,1792]{1,0:T(8,128)S(1)} fusion(f32[8,16,1792]{2,1,0:T(8,128)S(1)} %multiply_reduce_fusion, f32[8,24,1791]{2,1,0:T(8,128)S(1)} %fusion.8, f32[8,23,1792]{2,1,0:T(8,128)S(1)} %fusion.9, f32[8,24,1792]{2,1,0:T(8,128)S(1)} %pad_subtract_fusion.3), kind=kLoop, calls=%fused_computation.51 | loop fusion | flops 1347584 | bytes 4644096 | tf_op jit(solution)/shard_map/reduce_sum | solution.py:85
  18.6 1.3 %collective-permute-start.2 = (f32[16,1792]{1,0:T(8,128)S(1)}, f32[16,1792]{1,0:T(8,128)S(1)}, u32[]{:S(2)}, u32[]{:S(2)}) collective-permute-start(f32[16,1792]{1,0:T(8,128)S(1)} %fusion.21), channel_id=1, source_target_pairs={{0,8},{8,0},{16,24},{24,16},{1,9},{9,1},{17,25},{25,17},{2,10},{10... | collective-permute-start | bytes 344072 | tf_op jit(solution)/shard_map/ppermute | solution.py:34
  19.9 1.2 %collective-permute-start.3 = (f32[16,1792]{1,0:T(8,128)S(1)}, f32[16,1792]{1,0:T(8,128)S(1)}, u32[]{:S(2)}, u32[]{:S(2)}) collective-permute-start(f32[16,1792]{1,0:T(8,128)S(1)} %fusion.21), channel_id=1, source_target_pairs={{0,16},{8,24},{16,0},{24,8},{1,17},{9,25},{17,1},{25,9},{2,18},{10... | collective-permute-start | bytes 344072 | tf_op jit(solution)/shard_map/ppermute | solution.py:34
  21.1 0.2 collective-permute-start.4
  21.3 1.9 %collective-permute-done.2 = f32[16,1792]{1,0:T(8,128)S(1)} collective-permute-done((f32[16,1792]{1,0:T(8,128)S(1)}, f32[16,1792]{1,0:T(8,128)S(1)}, u32[]{:S(2)}, u32[]{:S(2)}) %collective-permute-start.2) | collective-permute-done | bytes 114720 | tf_op jit(solution)/shard_map/ppermute | solution.py:34
  23.2 0.8 %collective-permute-done.3 = f32[16,1792]{1,0:T(8,128)S(1)} collective-permute-done((f32[16,1792]{1,0:T(8,128)S(1)}, f32[16,1792]{1,0:T(8,128)S(1)}, u32[]{:S(2)}, u32[]{:S(2)}) %collective-permute-start.3) | collective-permute-done | bytes 114720 | tf_op jit(solution)/shard_map/ppermute | solution.py:34
  24.0 1.7 %collective-permute-done.4 = f32[16,1792]{1,0:T(8,128)S(1)} collective-permute-done((f32[16,1792]{1,0:T(8,128)S(1)}, f32[16,1792]{1,0:T(8,128)S(1)}, u32[]{:S(2)}, u32[]{:S(2)}) %collective-permute-start.4) | collective-permute-done | bytes 114720 | tf_op jit(solution)/shard_map/ppermute | solution.py:34
  25.7 0.0 copy-done.4
  25.7 0.0 copy-done.5
  25.7 0.1 broadcast_multiply_fusion
  25.8 0.1 slice_select_fusion.1
  25.9 0.1 collective-permute-start.5
  26.0 5.5 %collective-permute-start.6 = (f32[8,4,1792]{2,1,0:T(4,128)S(1)}, f32[8,4,1792]{2,1,0:T(4,128)S(1)}, u32[]{:S(2)}, u32[]{:S(2)}) collective-permute-start(f32[8,4,1792]{2,1,0:T(4,128)S(1)} %get-tuple-element.9), channel_id=1, source_target_pairs={{1,2},{3,4},{5,6},{2,1},{4,3},{6,5},{9,10},{11,12},{13,14},{10,9},... | collective-permute-start | bytes 688136 | tf_op jit(solution)/shard_map/ppermute | solution.py:21
  31.5 0.0 collective-permute-done.5
  31.5 3.7 %collective-permute-done.6 = f32[8,4,1792]{2,1,0:T(4,128)S(1)} collective-permute-done((f32[8,4,1792]{2,1,0:T(4,128)S(1)}, f32[8,4,1792]{2,1,0:T(4,128)S(1)}, u32[]{:S(2)}, u32[]{:S(2)}) %collective-permute-start.6) | collective-permute-done | bytes 229408 | tf_op jit(solution)/shard_map/ppermute | solution.py:21
  35.2 0.2 pad_maximum_fusion.1
  35.4 0.2 fusion.7
  35.6 0.4 %fusion.6 = f32[8,24,1791]{2,1,0:T(8,128)S(1)} fusion(f32[8,24,1792]{2,1,0:T(8,128)S(1)} %pad_maximum_fusion.1, f32[24,1791]{1,0:T(8,128)S(1)} %bitcast.19), kind=kLoop, calls=%fused_computation.15 | loop fusion | flops 687744 | bytes 4298400 | tf_op jit(solution)/shard_map/mul | solution.py:50
  36.0 0.6 %pad_subtract_fusion.2 = f32[8,24,1792]{2,1,0:T(8,128)S(1)} fusion(f32[8,24,1791]{2,1,0:T(8,128)S(1)} %fusion.6, f32[8,23,1792]{2,1,0:T(8,128)S(1)} %fusion.7, f32[8,4,1792]{2,1,0:T(4,128)S(1)} %bitcast.26, f32[8,16,1792]{2,1,0:T(8,128)S(1)} %broadcast_multiply_fusion, f32[8,4,1792]{2,1,0:T(4,128)S(1)} %bitcast.24), kind=kLoop, calls=%fused_computation.41 | loop fusion | flops 2064384 | bytes 5446912 | tf_op jit(solution)/shard_map/sub | solution.py:59
  36.6 0.2 fusion.5
  36.8 0.4 %fusion.4 = f32[8,24,1791]{2,1,0:T(8,128)S(1)} fusion(f32[8,24,1792]{2,1,0:T(8,128)S(1)} %pad_subtract_fusion.2, f32[24,1791]{1,0:T(8,128)S(1)} %bitcast.20), kind=kLoop, calls=%fused_computation.11 | loop fusion | flops 687744 | bytes 4298400 | tf_op jit(solution)/shard_map/mul | solution.py:50
  37.2 0.5 %pad_subtract_fusion.1 = f32[8,24,1792]{2,1,0:T(8,128)S(1)} fusion(f32[8,24,1791]{2,1,0:T(8,128)S(1)} %fusion.4, f32[8,23,1792]{2,1,0:T(8,128)S(1)} %fusion.5, f32[8,24,1792]{2,1,0:T(8,128)S(1)} %pad_subtract_fusion.2), kind=kLoop, calls=%fused_computation.40 | loop fusion | flops 1376256 | bytes 5446912 | tf_op jit(solution)/shard_map/sub | solution.py:59
  37.7 0.2 fusion.3
  37.9 0.4 %fusion.2 = f32[8,24,1791]{2,1,0:T(8,128)S(1)} fusion(f32[8,24,1792]{2,1,0:T(8,128)S(1)} %pad_subtract_fusion.1, f32[24,1791]{1,0:T(8,128)S(1)} %bitcast.21), kind=kLoop, calls=%fused_computation.7 | loop fusion | flops 687744 | bytes 4298400 | tf_op jit(solution)/shard_map/mul | solution.py:50
  38.3 0.5 %pad_subtract_fusion = f32[8,24,1792]{2,1,0:T(8,128)S(1)} fusion(f32[8,24,1791]{2,1,0:T(8,128)S(1)} %fusion.2, f32[8,23,1792]{2,1,0:T(8,128)S(1)} %fusion.3, f32[8,24,1792]{2,1,0:T(8,128)S(1)} %pad_subtract_fusion.1), kind=kLoop, calls=%fused_computation.39 | loop fusion | flops 1376256 | bytes 5446912 | tf_op jit(solution)/shard_map/sub | solution.py:59
  38.8 0.2 fusion.1
  39.0 0.4 %fusion = f32[8,24,1791]{2,1,0:T(8,128)S(1)} fusion(f32[8,24,1792]{2,1,0:T(8,128)S(1)} %pad_subtract_fusion, f32[24,1791]{1,0:T(8,128)S(1)} %bitcast.22), kind=kLoop, calls=%fused_computation.3 | loop fusion | flops 687744 | bytes 4298400 | tf_op jit(solution)/shard_map/mul | solution.py:50
  39.4 1.5 %fusion.19 = f32[8,16,1792]{2,1,0:T(8,128)} fusion(f32[8,16,1792]{2,1,0:T(8,128)S(1)} %copy-done, f32[8,24,1791]{2,1,0:T(8,128)S(1)} %fusion, f32[8,23,1792]{2,1,0:T(8,128)S(1)} %fusion.1, f32[8,24,1792]{2,1,0:T(8,128)S(1)} %pad_subtract_fusion), kind=kLoop, calls=%fused_computation.45 | loop fusion | flops 1146880 | bytes 5446912 | tf_op jit(solution)/shard_map/add | solution.py:88
  (6 shorter events, 0.2 us)
Async XLA Ops:
  2.3 5.0 %copy-start.1 = (bf16[8,4,16,1792]{3,2,1,0:T(8,128)(2,1)S(1)}, bf16[8,4,16,1792]{3,2,1,0:T(8,128)(2,1)}, u32[]{:S(2)}) copy-start(bf16[8,4,16,1792]{3,2,1,0:T(8,128)(2,1)} %param.8) | copy-start | bytes 5505028
  2.4 5.0 %copy-start.3 = (f32[4,16,1792]{2,1,0:T(8,128)S(1)}, f32[4,16,1792]{2,1,0:T(8,128)}, u32[]{:S(2)}) copy-start(f32[4,16,1792]{2,1,0:T(8,128)} %param.9) | copy-start | bytes 1376260
  2.5 10.9 %collective-permute-start.1 = (f32[10,4,1792]{2,0,1:T(8,128)S(1)}, f32[10,4,1792]{2,0,1:T(8,128)S(1)}, u32[]{:S(2)}, u32[]{:S(2)}) collective-permute-start(f32[10,4,1792]{2,0,1:T(8,128)S(1)} %copy.12), channel_id=1, source_target_pairs={{1,2},{3,4},{5,6},{2,1},{4,3},{6,5},{9,10},{11,12},{13,14},{10,9},... | collective-permute-start | bytes 860168 | tf_op jit(solution)/shard_map/ppermute | solution.py:21
  7.3 6.1 %collective-permute-start = (f32[10,4,1792]{2,0,1:T(8,128)S(1)}, f32[10,4,1792]{2,0,1:T(8,128)S(1)}, u32[]{:S(2)}, u32[]{:S(2)}) collective-permute-start(f32[10,4,1792]{2,0,1:T(8,128)S(1)} %copy.11), channel_id=1, source_target_pairs={{0,1},{2,3},{4,5},{6,7},{1,0},{3,2},{5,4},{7,6},{8,9},{10,11},{12,... | collective-permute-start | bytes 860168 | tf_op jit(solution)/shard_map/ppermute | solution.py:22
  7.8 6.0 %copy-start = (f32[8,16,1792]{2,1,0:T(8,128)S(1)}, f32[8,16,1792]{2,1,0:T(8,128)}, u32[]{:S(2)}) copy-start(f32[8,16,1792]{2,1,0:T(8,128)} %param.7) | copy-start | bytes 2752516
  7.8 6.0 %copy-start.2 = (f32[16,1792]{1,0:T(8,128)S(1)}, f32[16,1792]{1,0:T(8,128)}, u32[]{:S(2)}) copy-start(f32[16,1792]{1,0:T(8,128)} %param.13) | copy-start | bytes 344068
  18.0 7.6 %copy-start.4 = (f32[16,1792]{1,0:T(8,128)S(1)}, f32[16,1792]{1,0:T(8,128)}, u32[]{:S(2)}) copy-start(f32[16,1792]{1,0:T(8,128)} %param.10) | copy-start | bytes 344068
  18.0 7.6 %copy-start.5 = (s32[16,1792]{1,0:T(8,128)S(1)}, s32[16,1792]{1,0:T(8,128)}, u32[]{:S(2)}) copy-start(s32[16,1792]{1,0:T(8,128)} %param.11) | copy-start | bytes 344068
  18.6 4.6 %collective-permute-start.2 = (f32[16,1792]{1,0:T(8,128)S(1)}, f32[16,1792]{1,0:T(8,128)S(1)}, u32[]{:S(2)}, u32[]{:S(2)}) collective-permute-start(f32[16,1792]{1,0:T(8,128)S(1)} %fusion.21), channel_id=1, source_target_pairs={{0,8},{8,0},{16,24},{24,16},{1,9},{9,1},{17,25},{25,17},{2,10},{10... | collective-permute-start | bytes 344072 | tf_op jit(solution)/shard_map/ppermute | solution.py:34
  19.9 4.1 %collective-permute-start.3 = (f32[16,1792]{1,0:T(8,128)S(1)}, f32[16,1792]{1,0:T(8,128)S(1)}, u32[]{:S(2)}, u32[]{:S(2)}) collective-permute-start(f32[16,1792]{1,0:T(8,128)S(1)} %fusion.21), channel_id=1, source_target_pairs={{0,16},{8,24},{16,0},{24,8},{1,17},{9,25},{17,1},{25,9},{2,18},{10... | collective-permute-start | bytes 344072 | tf_op jit(solution)/shard_map/ppermute | solution.py:34
  21.1 4.5 %collective-permute-start.4 = (f32[16,1792]{1,0:T(8,128)S(1)}, f32[16,1792]{1,0:T(8,128)S(1)}, u32[]{:S(2)}, u32[]{:S(2)}) collective-permute-start(f32[16,1792]{1,0:T(8,128)S(1)} %fusion.21), channel_id=1, source_target_pairs={{0,24},{8,16},{16,8},{24,0},{1,25},{9,17},{17,9},{25,1},{2,26},{10... | collective-permute-start | bytes 344072 | tf_op jit(solution)/shard_map/ppermute | solution.py:34
  25.9 5.6 %collective-permute-start.5 = (f32[8,4,1792]{2,1,0:T(4,128)S(1)}, f32[8,4,1792]{2,1,0:T(4,128)S(1)}, u32[]{:S(2)}, u32[]{:S(2)}) collective-permute-start(f32[8,4,1792]{2,1,0:T(4,128)S(1)} %get-tuple-element.8), channel_id=1, source_target_pairs={{0,1},{2,3},{4,5},{6,7},{1,0},{3,2},{5,4},{7,6},{8,9},{10,11},{12,... | collective-permute-start | bytes 688136 | tf_op jit(solution)/shard_map/ppermute | solution.py:22
  26.0 9.2 %collective-permute-start.6 = (f32[8,4,1792]{2,1,0:T(4,128)S(1)}, f32[8,4,1792]{2,1,0:T(4,128)S(1)}, u32[]{:S(2)}, u32[]{:S(2)}) collective-permute-start(f32[8,4,1792]{2,1,0:T(4,128)S(1)} %get-tuple-element.9), channel_id=1, source_target_pairs={{1,2},{3,4},{5,6},{2,1},{4,3},{6,5},{9,10},{11,12},{13,14},{10,9},... | collective-permute-start | bytes 688136 | tf_op jit(solution)/shard_map/ppermute | solution.py:21

commit v14 on v13

--- a/solution.py
+++ b/solution.py
@@ -69,22 +69,22 @@
 
 
 def per_device(controls, perturbations, jacobian, obs_weight, radar_mask, row_faces, col_faces):
-    row_count = controls.shape[1]
+    members, row_count = controls.shape[:2]
     row_index = lax.axis_index("tile") * row_count + lax.broadcasted_iota(
         jnp.int32, row_faces.shape, 0
     )
     row_coef = jnp.where(
         row_index < row_count * lax.axis_size("tile") - 1, row_faces, jnp.zeros_like(row_faces)
     )
-    members = controls.shape[0]
-    stacked = jnp.concatenate([controls, row_coef[None], col_faces[None]], 0)
+    mix = jnp.sum(perturbations.astype(jnp.float32) * jacobian[None], axis=1)
+    stacked = jnp.concatenate([controls, row_coef[None], col_faces[None], mix], 0)
     band = exchange(stacked, STEPS)
-    field, coef_band = band[:members], band[members:]
+    field, coef_band, mix_band = band[:members], band[members : members + 2], band[members + 2 :]
     localized = localize(field, coef_band)[:, STEPS : STEPS + row_count]
-    mix = jnp.sum(perturbations.astype(jnp.float32) * jacobian[None], axis=1)
     reflect = mem_sum(jnp.sum(mix * localized, 0))
     weighted = radar_mask.astype(jnp.float32) * obs_weight * reflect
-    sensitivity = exchange(mix * weighted[None], STEPS)
+    weighted_band = exchange(weighted[None], STEPS)
+    sensitivity = mix_band * weighted_band
     return controls + localize(sensitivity, coef_band)[:, STEPS : STEPS + row_count]
 
 

time: 41.1 us -> 42.5 us (1.034)
  other arithmetic: 13.7 us -> 14.3 us
  starting transfers between devices: 13.1 us -> 13.6 us
    reduce_sum x1, other arithmetic: 0.37 us -> 2.11 us  [per_device(): mix = jnp.sum(perturbations.astype(jnp.float32) * jacobian[None], axis=1)]
    select_n x2, other arithmetic: 1.44 us -> 0.24 us  [exchange(): near = lax.ppermute(jnp.where(odd, head, tail), 'tile', pairs(0))]
    ppermute x2, waiting for transfers between devices: 9.25 us -> 10.4 us  [exchange(): far = lax.ppermute(jnp.where(odd, tail, head), 'tile', pairs(1))]
    ppermute x3, waiting for transfers between devices: 4.34 us -> 3.51 us  [partner(): return lax.ppermute(part, 'mem', [(i, i ^ stride) for i in range(count)])]
    broadcast_in_dim x1 -> x2, other arithmetic: 0.98 us -> 1.01 us  [the longest x1 0.98 us: per_device(): row_coef[None]]
  transfers between devices with their start and end apart: 7 -> 7, of which waited for: 5 -> 5; matrix products, arithmetic and copies ran while one was open for 1% -> 0% of each run, Pallas kernels for 0% -> 0%
where the time goes in v14:
time: 42.5 us; the launch traced here: 42.4 us
  other arithmetic  14.3 us (34%)
  waiting for transfers between devices  13.9 us (33%)
  starting transfers between devices  13.6 us (32%)
    ppermute x2, waiting for transfers between devices, exchange(): far = lax.ppermute(jnp.where(odd, tail, head), 'tile', pairs(1))  10.4 us
    ppermute x2, starting transfers between devices, exchange(): far = lax.ppermute(jnp.where(odd, tail, head), 'tile', pairs(1))  10.3 us
    ppermute x3, waiting for transfers between devices, partner(): return lax.ppermute(part, 'mem', [(i, i ^ stride) for i in range(count)])  3.51 us
    mul x8, other arithmetic, diffuse(): col_coef[..., :, :-1] * (values[..., :, 1:] - values[..., :, :-1])  3.38 us
    ppermute x3, starting transfers between devices, partner(): return lax.ppermute(part, 'mem', [(i, i ^ stride) for i in range(count)])  3.13 us
    sub x6, other arithmetic, diffuse(): values + jnp.concatenate([col_flux, zeros_col], -1)  2.88 us
    reduce_sum x1, other arithmetic, per_device(): mix = jnp.sum(perturbations.astype(jnp.float32) * jacobian[None], axis=1)  2.11 us
    mul x9, other arithmetic, diffuse(): row_coef[..., :-1, :] * (values[..., 1:, :] - values[..., :-1, :])  1.56 us
  transfers between devices with their start and end apart: 7, of which 5 were waited for; matrix products, arithmetic and copies ran while one was open for 0% of the time, Pallas kernels for 0%

profile of v14, /device:TPU:1, one launch (start us, length us, event | category | flops | bytes accessed | tf_op | source)
XLA Modules:
  0.0 42.4 jit_solution(5756810274695433044)
XLA Ops:
  0.0 1.0 %select_bitcast_fusion = f32[1,16,1792]{2,1,0:T(8,128)S(1)} fusion(f32[16,1792]{1,0:T(8,128)} %param.12, pred[16]{0:T(512)(128)(4,1)S(1)} %add_compare_fusion), kind=kLoop, calls=%fused_computation.67 | loop fusion | flops 28672 | bytes 229392 | tf_op jit(solution)/shard_map/broadcast_in_dim | solution.py:80
  1.0 0.0 copy-start
  1.0 0.0 copy-start.1
  1.0 2.1 %multiply_reduce_fusion = f32[8,16,1792]{2,1,0:T(8,128)S(1)} fusion(bf16[8,4,16,1792]{3,2,1,0:T(8,128)(2,1)} %param.8, f32[4,16,1792]{2,1,0:T(8,128)} %param.9), kind=kLoop, calls=%fused_computation | loop fusion | flops 2523136 | bytes 3211264 | tf_op jit(solution)/shard_map/reduce_sum | solution.py:79
  3.1 0.0 copy-done
  3.1 0.0 copy-done.1
  3.1 0.2 broadcast_select_fusion.1
  3.4 0.1 copy.11
  3.5 0.1 collective-permute-start
  3.6 0.1 broadcast_select_fusion
  3.7 0.1 copy.12
  3.8 4.6 %collective-permute-start.1 = (f32[18,4,1792]{2,0,1:T(8,128)S(1)}, f32[18,4,1792]{2,0,1:T(8,128)S(1)}, u32[]{:S(2)}, u32[]{:S(2)}) collective-permute-start(f32[18,4,1792]{2,0,1:T(8,128)S(1)} %copy.12), channel_id=1, source_target_pairs={{1,2},{3,4},{5,6},{2,1},{4,3},{6,5},{9,10},{11,12},{13,14},{10,9},... | collective-permute-start | bytes 1548296 | tf_op jit(solution)/shard_map/ppermute | solution.py:21
  8.4 0.0 collective-permute-done
  8.4 8.9 %collective-permute-done.1 = f32[18,4,1792]{2,0,1:T(8,128)S(1)} collective-permute-done((f32[18,4,1792]{2,0,1:T(8,128)S(1)}, f32[18,4,1792]{2,0,1:T(8,128)S(1)}, u32[]{:S(2)}, u32[]{:S(2)}) %collective-permute-start.1) | collective-permute-done | bytes 516128 | tf_op jit(solution)/shard_map/ppermute | solution.py:21
  17.3 0.4 copy_select_fusion.1
  17.7 0.4 %pad_maximum_fusion = f32[18,24,1792]{2,1,0:T(8,128)S(1)} fusion(f32[18,4,1792]{2,1,0:T(4,128)S(1)} %get-tuple-element.9, f32[8,16,1792]{2,1,0:T(8,128)S(1)} %multiply_reduce_fusion, f32[1,16,1792]{2,1,0:T(8,128)S(1)} %bitcast.29, f32[1,16,1792]{2,1,0:T(8,128)S(1)} %select_bitcast_fusion, f32[8,16,1792]{2,1,0:T(8,128)S(1)} %copy-done, ...), kind=kLoop, calls=%fused_computation.1 | loop fusion | flops 3870720 | bytes 6193152 | tf_op jit(solution)/shard_map/concatenate | solution.py:25
  18.2 0.2 fusion.15
  18.4 0.4 fusion.14
  18.8 0.5 %fusion.18 = f32[8,24,1792]{2,1,0:T(8,128)S(1)} fusion(f32[18,24,1792]{2,1,0:T(8,128)S(1)} %pad_maximum_fusion, f32[8,24,1791]{2,1,0:T(8,128)S(1)} %fusion.14, f32[8,23,1792]{2,1,0:T(8,128)S(1)} %fusion.15), kind=kLoop, calls=%fused_computation.37 | loop fusion | flops 1376256 | bytes 5446912 | tf_op jit(solution)/shard_map/sub | solution.py:59
  19.3 0.2 fusion.13
  19.5 0.4 fusion.12
  19.9 0.5 %pad_subtract_fusion.4 = f32[8,24,1792]{2,1,0:T(8,128)S(1)} fusion(f32[8,24,1791]{2,1,0:T(8,128)S(1)} %fusion.12, f32[8,23,1792]{2,1,0:T(8,128)S(1)} %fusion.13, f32[8,24,1792]{2,1,0:T(8,128)S(1)} %fusion.18), kind=kLoop, calls=%fused_computation.43 | loop fusion | flops 1376256 | bytes 5446912 | tf_op jit(solution)/shard_map/sub | solution.py:59
  20.4 0.2 fusion.11
  20.6 0.4 fusion.10
  21.0 0.5 %pad_subtract_fusion.3 = f32[8,24,1792]{2,1,0:T(8,128)S(1)} fusion(f32[8,24,1791]{2,1,0:T(8,128)S(1)} %fusion.10, f32[8,23,1792]{2,1,0:T(8,128)S(1)} %fusion.11, f32[8,24,1792]{2,1,0:T(8,128)S(1)} %pad_subtract_fusion.4), kind=kLoop, calls=%fused_computation.42 | loop fusion | flops 1376256 | bytes 5446912 | tf_op jit(solution)/shard_map/sub | solution.py:59
  21.5 0.2 fusion.9
  21.7 0.4 fusion.8
  22.1 0.0 copy-start.2
  22.1 0.0 copy-start.3
  22.2 0.6 %fusion.21 = f32[16,1792]{1,0:T(8,128)S(1)} fusion(f32[8,16,1792]{2,1,0:T(8,128)S(1)} %multiply_reduce_fusion, f32[8,24,1791]{2,1,0:T(8,128)S(1)} %fusion.8, f32[8,23,1792]{2,1,0:T(8,128)S(1)} %fusion.9, f32[8,24,1792]{2,1,0:T(8,128)S(1)} %pad_subtract_fusion.3), kind=kLoop, calls=%fused_computation.51 | loop fusion | flops 1347584 | bytes 4644096 | tf_op jit(solution)/shard_map/reduce_sum | solution.py:84
  22.7 2.8 %collective-permute-start.4 = (f32[16,1792]{1,0:T(8,128)S(1)}, f32[16,1792]{1,0:T(8,128)S(1)}, u32[]{:S(2)}, u32[]{:S(2)}) collective-permute-start(f32[16,1792]{1,0:T(8,128)S(1)} %fusion.21), channel_id=1, source_target_pairs={{0,24},{8,16},{16,8},{24,0},{1,25},{9,17},{17,9},{25,1},{2,26},{10... | collective-permute-start | bytes 344072 | tf_op jit(solution)/shard_map/ppermute | solution.py:34
  25.5 0.2 collective-permute-start.3
  25.7 0.1 collective-permute-start.2
  25.9 1.8 %collective-permute-done.4 = f32[16,1792]{1,0:T(8,128)S(1)} collective-permute-done((f32[16,1792]{1,0:T(8,128)S(1)}, f32[16,1792]{1,0:T(8,128)S(1)}, u32[]{:S(2)}, u32[]{:S(2)}) %collective-permute-start.4) | collective-permute-done | bytes 114720 | tf_op jit(solution)/shard_map/ppermute | solution.py:34
  27.7 1.5 %collective-permute-done.3 = f32[16,1792]{1,0:T(8,128)S(1)} collective-permute-done((f32[16,1792]{1,0:T(8,128)S(1)}, f32[16,1792]{1,0:T(8,128)S(1)}, u32[]{:S(2)}, u32[]{:S(2)}) %collective-permute-start.3) | collective-permute-done | bytes 114720 | tf_op jit(solution)/shard_map/ppermute | solution.py:34
  29.1 0.2 collective-permute-done.2
  29.4 0.0 copy-done.2
  29.4 0.0 copy-done.3
  29.4 0.1 collective-permute-start.5
  29.5 5.8 %collective-permute-start.6 = (f32[1,4,1792]{2,1,0:T(4,128)S(1)}, f32[1,4,1792]{2,1,0:T(4,128)S(1)}, u32[]{:S(2)}, u32[]{:S(2)}) collective-permute-start(f32[1,4,1792]{2,1,0:T(4,128)S(1)} %get-tuple-element.11), channel_id=1, source_target_pairs={{1,2},{3,4},{5,6},{2,1},{4,3},{6,5},{9,10},{11,12},{13,14},{10,9},... | collective-permute-start | bytes 86024 | tf_op jit(solution)/shard_map/ppermute | solution.py:21
  35.3 0.0 collective-permute-done.5
  35.3 1.5 %collective-permute-done.6 = f32[1,4,1792]{2,1,0:T(4,128)S(1)} collective-permute-done((f32[1,4,1792]{2,1,0:T(4,128)S(1)}, f32[1,4,1792]{2,1,0:T(4,128)S(1)}, u32[]{:S(2)}, u32[]{:S(2)}) %collective-permute-start.6) | collective-permute-done | bytes 28704 | tf_op jit(solution)/shard_map/ppermute | solution.py:21
  36.9 0.1 slice_multiply_fusion
  37.0 0.2 fusion.7
  37.2 0.4 fusion.6
  37.6 0.5 %pad_subtract_fusion.2 = f32[8,24,1792]{2,1,0:T(8,128)S(1)} fusion(f32[8,24,1791]{2,1,0:T(8,128)S(1)} %fusion.6, f32[8,23,1792]{2,1,0:T(8,128)S(1)} %fusion.7, f32[24,1792]{1,0:T(8,128)S(1)} %maximum_bitcast_fusion.2, f32[18,24,1792]{2,1,0:T(8,128)S(1)} %pad_maximum_fusion), kind=kLoop, calls=%fused_computation.41 | loop fusion | flops 1720320 | bytes 5618944 | tf_op jit(solution)/shard_map/sub | solution.py:59
  38.1 0.2 fusion.5
  38.3 0.4 fusion.4
  38.7 0.5 %pad_subtract_fusion.1 = f32[8,24,1792]{2,1,0:T(8,128)S(1)} fusion(f32[8,24,1791]{2,1,0:T(8,128)S(1)} %fusion.4, f32[8,23,1792]{2,1,0:T(8,128)S(1)} %fusion.5, f32[8,24,1792]{2,1,0:T(8,128)S(1)} %pad_subtract_fusion.2), kind=kLoop, calls=%fused_computation.40 | loop fusion | flops 1376256 | bytes 5446912 | tf_op jit(solution)/shard_map/sub | solution.py:59
  39.2 0.2 fusion.3
  39.4 0.4 fusion.2
  39.8 0.5 %pad_subtract_fusion = f32[8,24,1792]{2,1,0:T(8,128)S(1)} fusion(f32[8,24,1791]{2,1,0:T(8,128)S(1)} %fusion.2, f32[8,23,1792]{2,1,0:T(8,128)S(1)} %fusion.3, f32[8,24,1792]{2,1,0:T(8,128)S(1)} %pad_subtract_fusion.1), kind=kLoop, calls=%fused_computation.39 | loop fusion | flops 1376256 | bytes 5446912 | tf_op jit(solution)/shard_map/sub | solution.py:59
  40.3 0.2 fusion.1
  40.5 0.4 fusion
  40.9 1.5 %fusion.19 = f32[8,16,1792]{2,1,0:T(8,128)} fusion(f32[8,16,1792]{2,1,0:T(8,128)S(1)} %copy-done, f32[8,24,1791]{2,1,0:T(8,128)S(1)} %fusion, f32[8,23,1792]{2,1,0:T(8,128)S(1)} %fusion.1, f32[8,24,1792]{2,1,0:T(8,128)S(1)} %pad_subtract_fusion), kind=kLoop, calls=%fused_computation.45 | loop fusion | flops 1146880 | bytes 5446912 | tf_op jit(solution)/shard_map/add | solution.py:88
  (7 shorter events, 0.2 us)
Async XLA Ops:
  1.0 2.1 %copy-start = (f32[8,16,1792]{2,1,0:T(8,128)S(1)}, f32[8,16,1792]{2,1,0:T(8,128)}, u32[]{:S(2)}) copy-start(f32[8,16,1792]{2,1,0:T(8,128)} %param.7) | copy-start | bytes 2752516
  1.0 2.1 %copy-start.1 = (f32[16,1792]{1,0:T(8,128)S(1)}, f32[16,1792]{1,0:T(8,128)}, u32[]{:S(2)}) copy-start(f32[16,1792]{1,0:T(8,128)} %param.13) | copy-start | bytes 344068
  3.5 4.9 %collective-permute-start = (f32[18,4,1792]{2,0,1:T(8,128)S(1)}, f32[18,4,1792]{2,0,1:T(8,128)S(1)}, u32[]{:S(2)}, u32[]{:S(2)}) collective-permute-start(f32[18,4,1792]{2,0,1:T(8,128)S(1)} %copy.11), channel_id=1, source_target_pairs={{0,1},{2,3},{4,5},{6,7},{1,0},{3,2},{5,4},{7,6},{8,9},{10,11},{12,... | collective-permute-start | bytes 1548296 | tf_op jit(solution)/shard_map/ppermute | solution.py:22
  3.8 13.5 %collective-permute-start.1 = (f32[18,4,1792]{2,0,1:T(8,128)S(1)}, f32[18,4,1792]{2,0,1:T(8,128)S(1)}, u32[]{:S(2)}, u32[]{:S(2)}) collective-permute-start(f32[18,4,1792]{2,0,1:T(8,128)S(1)} %copy.12), channel_id=1, source_target_pairs={{1,2},{3,4},{5,6},{2,1},{4,3},{6,5},{9,10},{11,12},{13,14},{10,9},... | collective-permute-start | bytes 1548296 | tf_op jit(solution)/shard_map/ppermute | solution.py:21
  22.1 7.2 %copy-start.2 = (f32[16,1792]{1,0:T(8,128)S(1)}, f32[16,1792]{1,0:T(8,128)}, u32[]{:S(2)}) copy-start(f32[16,1792]{1,0:T(8,128)} %param.10) | copy-start | bytes 344068
  22.1 7.2 %copy-start.3 = (s32[16,1792]{1,0:T(8,128)S(1)}, s32[16,1792]{1,0:T(8,128)}, u32[]{:S(2)}) copy-start(s32[16,1792]{1,0:T(8,128)} %param.11) | copy-start | bytes 344068
  22.7 5.0 %collective-permute-start.4 = (f32[16,1792]{1,0:T(8,128)S(1)}, f32[16,1792]{1,0:T(8,128)S(1)}, u32[]{:S(2)}, u32[]{:S(2)}) collective-permute-start(f32[16,1792]{1,0:T(8,128)S(1)} %fusion.21), channel_id=1, source_target_pairs={{0,24},{8,16},{16,8},{24,0},{1,25},{9,17},{17,9},{25,1},{2,26},{10... | collective-permute-start | bytes 344072 | tf_op jit(solution)/shard_map/ppermute | solution.py:34
  25.5 3.6 %collective-permute-start.3 = (f32[16,1792]{1,0:T(8,128)S(1)}, f32[16,1792]{1,0:T(8,128)S(1)}, u32[]{:S(2)}, u32[]{:S(2)}) collective-permute-start(f32[16,1792]{1,0:T(8,128)S(1)} %fusion.21), channel_id=1, source_target_pairs={{0,16},{8,24},{16,0},{24,8},{1,17},{9,25},{17,1},{25,9},{2,18},{10... | collective-permute-start | bytes 344072 | tf_op jit(solution)/shard_map/ppermute | solution.py:34
  25.7 3.6 %collective-permute-start.2 = (f32[16,1792]{1,0:T(8,128)S(1)}, f32[16,1792]{1,0:T(8,128)S(1)}, u32[]{:S(2)}, u32[]{:S(2)}) collective-permute-start(f32[16,1792]{1,0:T(8,128)S(1)} %fusion.21), channel_id=1, source_target_pairs={{0,8},{8,0},{16,24},{24,16},{1,9},{9,1},{17,25},{25,17},{2,10},{10... | collective-permute-start | bytes 344072 | tf_op jit(solution)/shard_map/ppermute | solution.py:34
  29.4 5.9 %collective-permute-start.5 = (f32[1,4,1792]{2,1,0:T(4,128)S(1)}, f32[1,4,1792]{2,1,0:T(4,128)S(1)}, u32[]{:S(2)}, u32[]{:S(2)}) collective-permute-start(f32[1,4,1792]{2,1,0:T(4,128)S(1)} %get-tuple-element.10), channel_id=1, source_target_pairs={{0,1},{2,3},{4,5},{6,7},{1,0},{3,2},{5,4},{7,6},{8,9},{10,11},{12,... | collective-permute-start | bytes 86024 | tf_op jit(solution)/shard_map/ppermute | solution.py:22
  29.5 7.3 %collective-permute-start.6 = (f32[1,4,1792]{2,1,0:T(4,128)S(1)}, f32[1,4,1792]{2,1,0:T(4,128)S(1)}, u32[]{:S(2)}, u32[]{:S(2)}) collective-permute-start(f32[1,4,1792]{2,1,0:T(4,128)S(1)} %get-tuple-element.11), channel_id=1, source_target_pairs={{1,2},{3,4},{5,6},{2,1},{4,3},{6,5},{9,10},{11,12},{13,14},{10,9},... | collective-permute-start | bytes 86024 | tf_op jit(solution)/shard_map/ppermute | solution.py:21

commit v15 on v13

--- a/solution.py
+++ b/solution.py
@@ -23,6 +23,25 @@
     above = jnp.where(odd, near, far)
     below = jnp.where(odd, far, near)
     return jnp.concatenate([above, part, below], -2)
+
+
+def split_exchange(part, width):
+    count = lax.axis_size("tile")
+    head = part[..., :width, :]
+    tail = part[..., -width:, :]
+    zero = jnp.zeros_like(head)
+    if count % 2:
+        band = exchange(part, width)
+        return band, zero, False
+    odd = lax.axis_index("tile") % 2 == 1
+    pairs = lambda first: [(i, i + 1) for i in range(first, count - 1, 2)] + [
+        (i + 1, i) for i in range(first, count - 1, 2)
+    ]
+    far = lax.ppermute(jnp.where(odd, tail, head), "tile", pairs(1))
+    near = lax.ppermute(jnp.where(odd, head, tail), "tile", pairs(0))
+    above = jnp.where(odd, near, zero)
+    below = jnp.where(odd, zero, near)
+    return jnp.concatenate([above, part, below], -2), far, odd
 
 
 def mem_sum(part):
@@ -84,8 +103,20 @@
     mix = jnp.sum(perturbations.astype(jnp.float32) * jacobian[None], axis=1)
     reflect = mem_sum(jnp.sum(mix * localized, 0))
     weighted = radar_mask.astype(jnp.float32) * obs_weight * reflect
-    sensitivity = exchange(mix * weighted[None], STEPS)
-    return controls + localize(sensitivity, coef_band)[:, STEPS : STEPS + row_count]
+    sensitivity, far, odd = split_exchange(mix * weighted[None], STEPS)
+    spread = localize(sensitivity, coef_band)[:, STEPS : STEPS + row_count]
+    spread, far = lax.optimization_barrier((spread, far))
+    zero = jnp.zeros_like(far)
+    strip = jnp.where(odd, jnp.concatenate([zero, far], 1), jnp.concatenate([far, zero], 1))
+    strip_coef = jnp.where(odd, coef_band[:, row_count:], coef_band[:, : 2 * STEPS])
+    edge = localize(strip, strip_coef)
+    rest = jnp.zeros_like(spread[:, STEPS:])
+    edge = jnp.where(
+        odd,
+        jnp.concatenate([rest, edge[:, :STEPS]], 1),
+        jnp.concatenate([edge[:, STEPS:], rest], 1),
+    )
+    return controls + (spread + edge)
 
 
 def solution(mesh):

time: 41.1 us -> 39.9 us (0.971)
  waiting for transfers between devices: 13.6 us -> 9.85 us
  other arithmetic: 13.7 us -> 15.9 us
    ppermute x0 -> x2, starting transfers between devices: none -> 5.75 us  [the longest x1 5.68 us: split_exchange(): far = lax.ppermute(jnp.where(odd, tail, head), 'tile', pairs(1))]
    ppermute x2 -> x1, starting transfers between devices: 10.2 us -> 4.73 us  [exchange(): far = lax.ppermute(jnp.where(odd, tail, head), 'tile', pairs(1))]
    ppermute x2 -> x1, waiting for transfers between devices: 9.25 us -> 5.56 us  [exchange(): far = lax.ppermute(jnp.where(odd, tail, head), 'tile', pairs(1))]
    sub x6 -> x11, other arithmetic: 2.95 us -> 4.37 us  [diffuse(): values + jnp.concatenate([col_flux, zeros_col], -1)]
    mul x8 -> x12, other arithmetic: 3.39 us -> 4.14 us  [diffuse(): col_coef[..., :, :-1] * (values[..., :, 1:] - values[..., :, :-1])]
    mul x9 -> x13, other arithmetic: 1.5 us -> 1.76 us  [diffuse(): row_coef[..., :-1, :] * (values[..., 1:, :] - values[..., :-1, :])]
    select_n x2 -> x1, other arithmetic: 1.44 us -> 1.35 us  [exchange(): near = lax.ppermute(jnp.where(odd, head, tail), 'tile', pairs(0))]
  transfers between devices with their start and end apart: 7 -> 7, of which waited for: 5 -> 4; matrix products, arithmetic and copies ran while one was open for 1% -> 13% of each run, Pallas kernels for 0% -> 0%
where the time goes in v15:
time: 39.9 us; the launch traced here: 39.7 us
  other arithmetic  15.9 us (40%)
  starting transfers between devices  13.3 us (33%)
  waiting for transfers between devices  9.85 us (25%)
  between operations  0.46 us (1%)
    ppermute x1, starting transfers between devices, split_exchange(): far = lax.ppermute(jnp.where(odd, tail, head), 'tile', pairs(1))  5.68 us
    ppermute x1, waiting for transfers between devices, exchange(): far = lax.ppermute(jnp.where(odd, tail, head), 'tile', pairs(1))  5.56 us
    ppermute x1, starting transfers between devices, exchange(): far = lax.ppermute(jnp.where(odd, tail, head), 'tile', pairs(1))  4.73 us
    sub x11, other arithmetic, diffuse(): values + jnp.concatenate([col_flux, zeros_col], -1)  4.37 us
    ppermute x3, waiting for transfers between devices, partner(): return lax.ppermute(part, 'mem', [(i, i ^ stride) for i in range(count)])  4.28 us
    mul x12, other arithmetic, diffuse(): col_coef[..., :, :-1] * (values[..., :, 1:] - values[..., :, :-1])  4.14 us
    ppermute x3, starting transfers between devices, partner(): return lax.ppermute(part, 'mem', [(i, i ^ stride) for i in range(count)])  2.71 us
    mul x13, other arithmetic, diffuse(): row_coef[..., :-1, :] * (values[..., 1:, :] - values[..., :-1, :])  1.76 us
  transfers between devices with their start and end apart: 7, of which 4 were waited for; matrix products, arithmetic and copies ran while one was open for 13% of the time, Pallas kernels for 0%

profile of v15, /device:TPU:1, one launch (start us, length us, event | category | flops | bytes accessed | tf_op | source)
XLA Modules:
  0.0 39.7 jit_solution(12482125695888295596)
XLA Ops:
  0.0 1.0 %select_bitcast_fusion = f32[1,16,1792]{2,1,0:T(8,128)S(1)} fusion(f32[16,1792]{1,0:T(8,128)} %param.12, pred[16]{0:T(512)(128)(4,1)S(1)} %add_compare_fusion), kind=kLoop, calls=%fused_computation.98 | loop fusion | flops 28672 | bytes 229392 | tf_op jit(solution)/shard_map/broadcast_in_dim | solution.py:99
  1.0 1.4 %broadcast_select_fusion.1 = (f32[10,4,1792]{2,1,0:T(4,128)S(1)}, f32[10,4,1792]{2,1,0:T(4,128)S(1)}, f32[10,4,1792]{2,1,0:T(4,128)S(1)}) fusion(pred[]{:T(512)S(6)} %eq.7, f32[1,16,1792]{2,1,0:T(8,128)} %bitcast.24, f32[1,16,1792]{2,1,0:T(8,128)S(1)} %select_bitcast_fusion, f32[8,16,1792]{2,1,0:T(8,128)} %param.7), kind=kLoop, calls=%fused_computation.87 | loop fusion | flops 358400 | bytes 2007041 | tf_op jit(solution)/shard_map/jit(_where)/select_n | solution.py:22
  2.3 0.0 copy-start.2
  2.4 0.1 copy.12
  2.5 4.7 %collective-permute-start.1 = (f32[10,4,1792]{2,0,1:T(8,128)S(1)}, f32[10,4,1792]{2,0,1:T(8,128)S(1)}, u32[]{:S(2)}, u32[]{:S(2)}) collective-permute-start(f32[10,4,1792]{2,0,1:T(8,128)S(1)} %copy.12), channel_id=1, source_target_pairs={{1,2},{3,4},{5,6},{2,1},{4,3},{6,5},{9,10},{11,12},{13,14},{10,9},... | collective-permute-start | bytes 860168 | tf_op jit(solution)/shard_map/ppermute | solution.py:21
  7.2 0.1 copy.11
  7.3 0.1 collective-permute-start
  7.4 0.4 multiply_reduce_fusion
  7.8 0.0 copy-start.1
  7.8 5.6 %collective-permute-done.1 = f32[10,4,1792]{2,0,1:T(8,128)S(1)} collective-permute-done((f32[10,4,1792]{2,0,1:T(8,128)S(1)}, f32[10,4,1792]{2,0,1:T(8,128)S(1)}, u32[]{:S(2)}, u32[]{:S(2)}) %collective-permute-start.1) | collective-permute-done | bytes 286752 | tf_op jit(solution)/shard_map/ppermute | solution.py:21
  13.4 0.4 copy_select_fusion.1
  13.8 0.2 pad_maximum_fusion
  14.1 0.2 fusion.15
  14.3 0.4 %fusion.14 = f32[8,24,1791]{2,1,0:T(8,128)S(1)} fusion(f32[10,24,1792]{2,1,0:T(8,128)S(1)} %pad_maximum_fusion, f32[24,1791]{1,0:T(8,128)S(1)} %bitcast.16), kind=kLoop, calls=%fused_computation.31 | loop fusion | flops 687744 | bytes 4298400 | tf_op jit(solution)/shard_map/mul | solution.py:69
  14.7 0.5 %fusion.18 = f32[8,24,1792]{2,1,0:T(8,128)S(1)} fusion(f32[10,24,1792]{2,1,0:T(8,128)S(1)} %pad_maximum_fusion, f32[8,24,1791]{2,1,0:T(8,128)S(1)} %fusion.14, f32[8,23,1792]{2,1,0:T(8,128)S(1)} %fusion.15), kind=kLoop, calls=%fused_computation.37 | loop fusion | flops 1376256 | bytes 5446912 | tf_op jit(solution)/shard_map/sub | solution.py:78
  15.2 0.2 fusion.13
  15.4 0.4 %fusion.12 = f32[8,24,1791]{2,1,0:T(8,128)S(1)} fusion(f32[8,24,1792]{2,1,0:T(8,128)S(1)} %fusion.18, f32[24,1791]{1,0:T(8,128)S(1)} %bitcast.17), kind=kLoop, calls=%fused_computation.27 | loop fusion | flops 687744 | bytes 4298400 | tf_op jit(solution)/shard_map/mul | solution.py:69
  15.8 0.5 %pad_subtract_fusion.4 = f32[8,24,1792]{2,1,0:T(8,128)S(1)} fusion(f32[8,24,1791]{2,1,0:T(8,128)S(1)} %fusion.12, f32[8,23,1792]{2,1,0:T(8,128)S(1)} %fusion.13, f32[8,24,1792]{2,1,0:T(8,128)S(1)} %fusion.18), kind=kLoop, calls=%fused_computation.43 | loop fusion | flops 1376256 | bytes 5446912 | tf_op jit(solution)/shard_map/sub | solution.py:78
  16.3 0.2 fusion.11
  16.5 0.4 %fusion.10 = f32[8,24,1791]{2,1,0:T(8,128)S(1)} fusion(f32[8,24,1792]{2,1,0:T(8,128)S(1)} %pad_subtract_fusion.4, f32[24,1791]{1,0:T(8,128)S(1)} %bitcast.18), kind=kLoop, calls=%fused_computation.23 | loop fusion | flops 687744 | bytes 4298400 | tf_op jit(solution)/shard_map/mul | solution.py:69
  16.9 0.5 %pad_subtract_fusion.3 = f32[8,24,1792]{2,1,0:T(8,128)S(1)} fusion(f32[8,24,1791]{2,1,0:T(8,128)S(1)} %fusion.10, f32[8,23,1792]{2,1,0:T(8,128)S(1)} %fusion.11, f32[8,24,1792]{2,1,0:T(8,128)S(1)} %pad_subtract_fusion.4), kind=kLoop, calls=%fused_computation.42 | loop fusion | flops 1376256 | bytes 5446912 | tf_op jit(solution)/shard_map/sub | solution.py:78
  17.4 0.2 fusion.9
  17.6 0.4 %fusion.8 = f32[8,24,1791]{2,1,0:T(8,128)S(1)} fusion(f32[8,24,1792]{2,1,0:T(8,128)S(1)} %pad_subtract_fusion.3, f32[24,1791]{1,0:T(8,128)S(1)} %bitcast.19), kind=kLoop, calls=%fused_computation.19 | loop fusion | flops 687744 | bytes 4298400 | tf_op jit(solution)/shard_map/mul | solution.py:69
  18.0 0.6 %fusion.20 = f32[16,1792]{1,0:T(8,128)S(1)} fusion(f32[8,16,1792]{2,1,0:T(8,128)S(1)} %multiply_reduce_fusion, f32[8,24,1791]{2,1,0:T(8,128)S(1)} %fusion.8, f32[8,23,1792]{2,1,0:T(8,128)S(1)} %fusion.9, f32[8,24,1792]{2,1,0:T(8,128)S(1)} %pad_subtract_fusion.3), kind=kLoop, calls=%fused_computation.50 | loop fusion | flops 1347584 | bytes 4644096 | tf_op jit(solution)/shard_map/reduce_sum | solution.py:104
  18.6 0.0 copy-start.4
  18.6 1.3 %collective-permute-start.2 = (f32[16,1792]{1,0:T(8,128)S(1)}, f32[16,1792]{1,0:T(8,128)S(1)}, u32[]{:S(2)}, u32[]{:S(2)}) collective-permute-start(f32[16,1792]{1,0:T(8,128)S(1)} %fusion.20), channel_id=1, source_target_pairs={{0,8},{8,0},{16,24},{24,16},{1,9},{9,1},{17,25},{25,17},{2,10},{10... | collective-permute-start | bytes 344072 | tf_op jit(solution)/shard_map/ppermute | solution.py:53
  19.9 1.2 %collective-permute-start.3 = (f32[16,1792]{1,0:T(8,128)S(1)}, f32[16,1792]{1,0:T(8,128)S(1)}, u32[]{:S(2)}, u32[]{:S(2)}) collective-permute-start(f32[16,1792]{1,0:T(8,128)S(1)} %fusion.20), channel_id=1, source_target_pairs={{0,16},{8,24},{16,0},{24,8},{1,17},{9,25},{17,1},{25,9},{2,18},{10... | collective-permute-start | bytes 344072 | tf_op jit(solution)/shard_map/ppermute | solution.py:53
  21.1 0.2 collective-permute-start.4
  21.4 1.8 %collective-permute-done.2 = f32[16,1792]{1,0:T(8,128)S(1)} collective-permute-done((f32[16,1792]{1,0:T(8,128)S(1)}, f32[16,1792]{1,0:T(8,128)S(1)}, u32[]{:S(2)}, u32[]{:S(2)}) %collective-permute-start.2) | collective-permute-done | bytes 114720 | tf_op jit(solution)/shard_map/ppermute | solution.py:53
  23.2 0.8 %collective-permute-done.3 = f32[16,1792]{1,0:T(8,128)S(1)} collective-permute-done((f32[16,1792]{1,0:T(8,128)S(1)}, f32[16,1792]{1,0:T(8,128)S(1)}, u32[]{:S(2)}, u32[]{:S(2)}) %collective-permute-start.3) | collective-permute-done | bytes 114720 | tf_op jit(solution)/shard_map/ppermute | solution.py:53
  24.0 1.7 %collective-permute-done.4 = f32[16,1792]{1,0:T(8,128)S(1)} collective-permute-done((f32[16,1792]{1,0:T(8,128)S(1)}, f32[16,1792]{1,0:T(8,128)S(1)}, u32[]{:S(2)}, u32[]{:S(2)}) %collective-permute-start.4) | collective-permute-done | bytes 114720 | tf_op jit(solution)/shard_map/ppermute | solution.py:53
  25.7 0.1 broadcast_multiply_fusion
  25.8 0.1 slice_select_fusion
  25.9 0.1 collective-permute-start.5
  26.0 5.7 %collective-permute-start.6 = (f32[8,4,1792]{2,1,0:T(4,128)S(1)}, f32[8,4,1792]{2,1,0:T(4,128)S(1)}, u32[]{:S(2)}, u32[]{:S(2)}) collective-permute-start(f32[8,4,1792]{2,1,0:T(4,128)S(1)} %get-tuple-element.12), channel_id=1, source_target_pairs={{1,2},{3,4},{5,6},{2,1},{4,3},{6,5},{9,10},{11,12},{13,14},{10,9},... | collective-permute-start | bytes 688136 | tf_op jit(solution)/shard_map/ppermute | solution.py:40
  31.7 0.1 broadcast_select_fusion.3
  31.8 0.2 pad_maximum_fusion.1
  32.0 0.2 fusion.7
  32.1 0.4 %fusion.6 = f32[8,24,1791]{2,1,0:T(8,128)S(1)} fusion(f32[8,24,1792]{2,1,0:T(8,128)S(1)} %pad_maximum_fusion.1, f32[24,1791]{1,0:T(8,128)S(1)} %bitcast.20), kind=kLoop, calls=%fused_computation.15 | loop fusion | flops 687744 | bytes 4298400 | tf_op jit(solution)/shard_map/mul | solution.py:69
  32.6 0.6 %pad_subtract_fusion.2 = f32[8,24,1792]{2,1,0:T(8,128)S(1)} fusion(f32[8,24,1791]{2,1,0:T(8,128)S(1)} %fusion.6, f32[8,23,1792]{2,1,0:T(8,128)S(1)} %fusion.7, f32[8,4,1792]{2,1,0:T(4,128)S(1)} %get-tuple-element.19, f32[8,16,1792]{2,1,0:T(8,128)S(1)} %broadcast_multiply_fusion, f32[8,4,1792]{2,1,0:T(4,128)S(1)} %get-tuple-element.18), kind=kLoop, calls=%fused_computation.41 | loop fusion | flops 2064384 | bytes 5446912 | tf_op jit(solution)/shard_map/sub | solution.py:78
  33.1 0.2 fusion.5
  33.3 0.4 %fusion.4 = f32[8,24,1791]{2,1,0:T(8,128)S(1)} fusion(f32[8,24,1792]{2,1,0:T(8,128)S(1)} %pad_subtract_fusion.2, f32[24,1791]{1,0:T(8,128)S(1)} %bitcast.21), kind=kLoop, calls=%fused_computation.11 | loop fusion | flops 687744 | bytes 4298400 | tf_op jit(solution)/shard_map/mul | solution.py:69
  33.8 0.5 %pad_subtract_fusion.1 = f32[8,24,1792]{2,1,0:T(8,128)S(1)} fusion(f32[8,24,1791]{2,1,0:T(8,128)S(1)} %fusion.4, f32[8,23,1792]{2,1,0:T(8,128)S(1)} %fusion.5, f32[8,24,1792]{2,1,0:T(8,128)S(1)} %pad_subtract_fusion.2), kind=kLoop, calls=%fused_computation.40 | loop fusion | flops 1376256 | bytes 5446912 | tf_op jit(solution)/shard_map/sub | solution.py:78
  34.2 0.2 fusion.3
  34.4 0.4 %fusion.2 = f32[8,24,1791]{2,1,0:T(8,128)S(1)} fusion(f32[8,24,1792]{2,1,0:T(8,128)S(1)} %pad_subtract_fusion.1, f32[24,1791]{1,0:T(8,128)S(1)} %bitcast.22), kind=kLoop, calls=%fused_computation.7 | loop fusion | flops 687744 | bytes 4298400 | tf_op jit(solution)/shard_map/mul | solution.py:69
  34.9 0.5 %pad_subtract_fusion = f32[8,24,1792]{2,1,0:T(8,128)S(1)} fusion(f32[8,24,1791]{2,1,0:T(8,128)S(1)} %fusion.2, f32[8,23,1792]{2,1,0:T(8,128)S(1)} %fusion.3, f32[8,24,1792]{2,1,0:T(8,128)S(1)} %pad_subtract_fusion.1), kind=kLoop, calls=%fused_computation.39 | loop fusion | flops 1376256 | bytes 5446912 | tf_op jit(solution)/shard_map/sub | solution.py:78
  35.4 0.2 fusion.1
  35.5 0.4 %fusion = f32[8,24,1791]{2,1,0:T(8,128)S(1)} fusion(f32[8,24,1792]{2,1,0:T(8,128)S(1)} %pad_subtract_fusion, f32[24,1791]{1,0:T(8,128)S(1)} %bitcast.23), kind=kLoop, calls=%fused_computation.3 | loop fusion | flops 687744 | bytes 4298400 | tf_op jit(solution)/shard_map/mul | solution.py:69
  36.0 0.5 %pad_subtract_fusion.5 = f32[8,16,1792]{2,1,0:T(8,128)S(1)} fusion(f32[8,24,1791]{2,1,0:T(8,128)S(1)} %fusion, f32[8,23,1792]{2,1,0:T(8,128)S(1)} %fusion.1, f32[8,24,1792]{2,1,0:T(8,128)S(1)} %pad_subtract_fusion), kind=kLoop, calls=%fused_computation.44 | loop fusion | flops 917504 | bytes 4529408 | tf_op jit(solution)/shard_map/sub | solution.py:78
  36.5 0.1 pad_select_fusion
  36.6 0.1 fusion.28
  36.7 0.2 fusion.27
  36.9 0.2 pad_subtract_fusion.12
  37.1 0.1 fusion.26
  37.1 0.2 fusion.25
  37.3 0.2 pad_subtract_fusion.11
  37.6 0.1 fusion.24
  37.6 0.2 fusion.23
  37.8 0.2 pad_subtract_fusion.10
  38.1 0.1 fusion.22
  38.1 0.2 fusion.21
  38.3 0.2 pad_subtract_fusion.9
  38.5 0.1 fusion.30
  38.6 1.1 %add_add_fusion = f32[8,16,1792]{2,1,0:T(8,128)} fusion(f32[8,16,1792]{2,1,0:T(8,128)S(1)} %copy-done, f32[8,16,1792]{2,1,0:T(8,128)S(1)} %pad_subtract_fusion.5, f32[8,4,1792]{2,1,0:T(4,128)S(1)} %get-tuple-element.17, f32[8,4,1792]{2,1,0:T(4,128)S(1)} %get-tuple-element.16, pred[]{:T(512)S(6)} %eq.7), kind=kLoop, calls=%fused_computation.54 | loop fusion | flops 688128 | bytes 3211265 | tf_op jit(solution)/shard_map/add | solution.py:119
  (20 shorter events, 0.2 us)
Async XLA Ops:
  2.3 5.0 %copy-start.2 = (bf16[8,4,16,1792]{3,2,1,0:T(8,128)(2,1)S(1)}, bf16[8,4,16,1792]{3,2,1,0:T(8,128)(2,1)}, u32[]{:S(2)}) copy-start(bf16[8,4,16,1792]{3,2,1,0:T(8,128)(2,1)} %param.8) | copy-start | bytes 5505028
  2.4 5.0 %copy-start.3 = (f32[4,16,1792]{2,1,0:T(8,128)S(1)}, f32[4,16,1792]{2,1,0:T(8,128)}, u32[]{:S(2)}) copy-start(f32[4,16,1792]{2,1,0:T(8,128)} %param.9) | copy-start | bytes 1376260
  2.5 10.9 %collective-permute-start.1 = (f32[10,4,1792]{2,0,1:T(8,128)S(1)}, f32[10,4,1792]{2,0,1:T(8,128)S(1)}, u32[]{:S(2)}, u32[]{:S(2)}) collective-permute-start(f32[10,4,1792]{2,0,1:T(8,128)S(1)} %copy.12), channel_id=1, source_target_pairs={{1,2},{3,4},{5,6},{2,1},{4,3},{6,5},{9,10},{11,12},{13,14},{10,9},... | collective-permute-start | bytes 860168 | tf_op jit(solution)/shard_map/ppermute | solution.py:21
  7.3 6.1 %collective-permute-start = (f32[10,4,1792]{2,0,1:T(8,128)S(1)}, f32[10,4,1792]{2,0,1:T(8,128)S(1)}, u32[]{:S(2)}, u32[]{:S(2)}) collective-permute-start(f32[10,4,1792]{2,0,1:T(8,128)S(1)} %copy.11), channel_id=1, source_target_pairs={{0,1},{2,3},{4,5},{6,7},{1,0},{3,2},{5,4},{7,6},{8,9},{10,11},{12,... | collective-permute-start | bytes 860168 | tf_op jit(solution)/shard_map/ppermute | solution.py:22
  7.8 6.0 %copy-start = (f32[8,16,1792]{2,1,0:T(8,128)S(1)}, f32[8,16,1792]{2,1,0:T(8,128)}, u32[]{:S(2)}) copy-start(f32[8,16,1792]{2,1,0:T(8,128)} %param.7) | copy-start | bytes 2752516
  7.8 6.0 %copy-start.1 = (f32[16,1792]{1,0:T(8,128)S(1)}, f32[16,1792]{1,0:T(8,128)}, u32[]{:S(2)}) copy-start(f32[16,1792]{1,0:T(8,128)} %param.13) | copy-start | bytes 344068
  18.6 7.1 %copy-start.4 = (f32[16,1792]{1,0:T(8,128)S(1)}, f32[16,1792]{1,0:T(8,128)}, u32[]{:S(2)}) copy-start(f32[16,1792]{1,0:T(8,128)} %param.10) | copy-start | bytes 344068
  18.6 7.1 %copy-start.5 = (s32[16,1792]{1,0:T(8,128)S(1)}, s32[16,1792]{1,0:T(8,128)}, u32[]{:S(2)}) copy-start(s32[16,1792]{1,0:T(8,128)} %param.11) | copy-start | bytes 344068
  18.6 4.6 %collective-permute-start.2 = (f32[16,1792]{1,0:T(8,128)S(1)}, f32[16,1792]{1,0:T(8,128)S(1)}, u32[]{:S(2)}, u32[]{:S(2)}) collective-permute-start(f32[16,1792]{1,0:T(8,128)S(1)} %fusion.20), channel_id=1, source_target_pairs={{0,8},{8,0},{16,24},{24,16},{1,9},{9,1},{17,25},{25,17},{2,10},{10... | collective-permute-start | bytes 344072 | tf_op jit(solution)/shard_map/ppermute | solution.py:53
  19.9 4.1 %collective-permute-start.3 = (f32[16,1792]{1,0:T(8,128)S(1)}, f32[16,1792]{1,0:T(8,128)S(1)}, u32[]{:S(2)}, u32[]{:S(2)}) collective-permute-start(f32[16,1792]{1,0:T(8,128)S(1)} %fusion.20), channel_id=1, source_target_pairs={{0,16},{8,24},{16,0},{24,8},{1,17},{9,25},{17,1},{25,9},{2,18},{10... | collective-permute-start | bytes 344072 | tf_op jit(solution)/shard_map/ppermute | solution.py:53
  21.1 4.5 %collective-permute-start.4 = (f32[16,1792]{1,0:T(8,128)S(1)}, f32[16,1792]{1,0:T(8,128)S(1)}, u32[]{:S(2)}, u32[]{:S(2)}) collective-permute-start(f32[16,1792]{1,0:T(8,128)S(1)} %fusion.20), channel_id=1, source_target_pairs={{0,24},{8,16},{16,8},{24,0},{1,25},{9,17},{17,9},{25,1},{2,26},{10... | collective-permute-start | bytes 344072 | tf_op jit(solution)/shard_map/ppermute | solution.py:53
  25.9 5.8 %collective-permute-start.5 = (f32[8,4,1792]{2,1,0:T(4,128)S(1)}, f32[8,4,1792]{2,1,0:T(4,128)S(1)}, u32[]{:S(2)}, u32[]{:S(2)}) collective-permute-start(f32[8,4,1792]{2,1,0:T(4,128)S(1)} %get-tuple-element.13), channel_id=1, source_target_pairs={{0,1},{2,3},{4,5},{6,7},{1,0},{3,2},{5,4},{7,6},{8,9},{10,11},{12,... | collective-permute-start | bytes 688136 | tf_op jit(solution)/shard_map/ppermute | solution.py:41
  26.0 10.5 %collective-permute-start.6 = (f32[8,4,1792]{2,1,0:T(4,128)S(1)}, f32[8,4,1792]{2,1,0:T(4,128)S(1)}, u32[]{:S(2)}, u32[]{:S(2)}) collective-permute-start(f32[8,4,1792]{2,1,0:T(4,128)S(1)} %get-tuple-element.12), channel_id=1, source_target_pairs={{1,2},{3,4},{5,6},{2,1},{4,3},{6,5},{9,10},{11,12},{13,14},{10,9},... | collective-permute-start | bytes 688136 | tf_op jit(solution)/shard_map/ppermute | solution.py:40

commit v16 on v13

--- a/solution.py
+++ b/solution.py
@@ -23,6 +23,13 @@
     above = jnp.where(odd, near, far)
     below = jnp.where(odd, far, near)
     return jnp.concatenate([above, part, below], -2)
+
+
+def tile_pairs(first):
+    count = lax.axis_size("tile")
+    return [(i, i + 1) for i in range(first, count - 1, 2)] + [
+        (i + 1, i) for i in range(first, count - 1, 2)
+    ]
 
 
 def mem_sum(part):
@@ -84,8 +91,30 @@
     mix = jnp.sum(perturbations.astype(jnp.float32) * jacobian[None], axis=1)
     reflect = mem_sum(jnp.sum(mix * localized, 0))
     weighted = radar_mask.astype(jnp.float32) * obs_weight * reflect
-    sensitivity = exchange(mix * weighted[None], STEPS)
-    return controls + localize(sensitivity, coef_band)[:, STEPS : STEPS + row_count]
+    sensitivity = mix * weighted[None]
+    head = sensitivity[:, :STEPS]
+    tail = sensitivity[:, -STEPS:]
+    zero = jnp.zeros_like(head)
+    if lax.axis_size("tile") % 2:
+        spread = localize(exchange(sensitivity, STEPS), coef_band)[:, STEPS : STEPS + row_count]
+        return controls + spread
+    odd = lax.axis_index("tile") % 2 == 1
+    near = lax.ppermute(jnp.where(odd, head, tail), "tile", tile_pairs(0))
+    band = jnp.concatenate([jnp.where(odd, near, zero), sensitivity, jnp.where(odd, zero, near)], 1)
+    spread = localize(band, coef_band)[:, STEPS : STEPS + row_count]
+    spread, outgoing = lax.optimization_barrier((spread, jnp.where(odd, tail, head)))
+    far = lax.ppermute(outgoing, "tile", tile_pairs(1))
+    zero = jnp.zeros_like(far)
+    strip = jnp.where(odd, jnp.concatenate([zero, far], 1), jnp.concatenate([far, zero], 1))
+    strip_coef = jnp.where(odd, coef_band[:, row_count:], coef_band[:, : 2 * STEPS])
+    edge = localize(strip, strip_coef)
+    rest = jnp.zeros_like(spread[:, STEPS:])
+    edge = jnp.where(
+        odd,
+        jnp.concatenate([rest, edge[:, :STEPS]], 1),
+        jnp.concatenate([edge[:, STEPS:], rest], 1),
+    )
+    return controls + (spread + edge)
 
 
 def solution(mesh):

time: 41.1 us -> 44.9 us (1.092)
  other arithmetic: 13.7 us -> 15.9 us
  waiting for transfers between devices: 13.6 us -> 15 us
    ppermute x0 -> x2, starting transfers between devices: none -> 5.57 us  [the longest x1 5.5 us: per_device(): far = lax.ppermute(outgoing, 'tile', tile_pairs(1))]
    ppermute x2 -> x1, starting transfers between devices: 10.2 us -> 4.73 us  [exchange(): far = lax.ppermute(jnp.where(odd, tail, head), 'tile', pairs(1))]
    ppermute x0 -> x2, waiting for transfers between devices: none -> 5.14 us  [the longest x1 3.68 us: per_device(): far = lax.ppermute(outgoing, 'tile', tile_pairs(1))]
    ppermute x2 -> x1, waiting for transfers between devices: 9.25 us -> 5.56 us  [exchange(): far = lax.ppermute(jnp.where(odd, tail, head), 'tile', pairs(1))]
    sub x6 -> x11, other arithmetic: 2.95 us -> 4.37 us  [diffuse(): values + jnp.concatenate([col_flux, zeros_col], -1)]
    mul x8 -> x12, other arithmetic: 3.39 us -> 4.14 us  [diffuse(): col_coef[..., :, :-1] * (values[..., :, 1:] - values[..., :, :-1])]
    mul x9 -> x13, other arithmetic: 1.5 us -> 1.76 us  [diffuse(): row_coef[..., :-1, :] * (values[..., 1:, :] - values[..., :-1, :])]
    select_n x2 -> x1, other arithmetic: 1.44 us -> 1.35 us  [exchange(): near = lax.ppermute(jnp.where(odd, head, tail), 'tile', pairs(0))]
  transfers between devices with their start and end apart: 7 -> 7, of which waited for: 5 -> 6; matrix products, arithmetic and copies ran while one was open for 1% -> 1% of each run, Pallas kernels for 0% -> 0%
where the time goes in v16:
time: 44.9 us; the launch traced here: 44.7 us
  other arithmetic  15.9 us (35%)
  waiting for transfers between devices  15 us (33%)
  starting transfers between devices  13.1 us (29%)
    ppermute x1, waiting for transfers between devices, exchange(): far = lax.ppermute(jnp.where(odd, tail, head), 'tile', pairs(1))  5.56 us
    ppermute x1, starting transfers between devices, per_device(): far = lax.ppermute(outgoing, 'tile', tile_pairs(1))  5.5 us
    ppermute x1, starting transfers between devices, exchange(): far = lax.ppermute(jnp.where(odd, tail, head), 'tile', pairs(1))  4.73 us
    sub x11, other arithmetic, diffuse(): values + jnp.concatenate([col_flux, zeros_col], -1)  4.37 us
    ppermute x3, waiting for transfers between devices, partner(): return lax.ppermute(part, 'mem', [(i, i ^ stride) for i in range(count)])  4.29 us
    mul x12, other arithmetic, diffuse(): col_coef[..., :, :-1] * (values[..., :, 1:] - values[..., :, :-1])  4.14 us
    ppermute x1, waiting for transfers between devices, per_device(): far = lax.ppermute(outgoing, 'tile', tile_pairs(1))  3.68 us
    ppermute x3, starting transfers between devices, partner(): return lax.ppermute(part, 'mem', [(i, i ^ stride) for i in range(count)])  2.71 us
  transfers between devices with their start and end apart: 7, of which 6 were waited for; matrix products, arithmetic and copies ran while one was open for 1% of the time, Pallas kernels for 0%

profile of v16, /device:TPU:1, one launch (start us, length us, event | category | flops | bytes accessed | tf_op | source)
XLA Modules:
  0.0 44.7 jit_solution(18055429462788667298)
XLA Ops:
  0.0 1.0 %select_bitcast_fusion = f32[1,16,1792]{2,1,0:T(8,128)S(1)} fusion(f32[16,1792]{1,0:T(8,128)} %param.12, pred[16]{0:T(512)(128)(4,1)S(1)} %add_compare_fusion), kind=kLoop, calls=%fused_computation.98 | loop fusion | flops 28672 | bytes 229392 | tf_op jit(solution)/shard_map/broadcast_in_dim | solution.py:87
  1.0 1.4 %broadcast_select_fusion.1 = (f32[10,4,1792]{2,1,0:T(4,128)S(1)}, f32[10,4,1792]{2,1,0:T(4,128)S(1)}, f32[10,4,1792]{2,1,0:T(4,128)S(1)}) fusion(pred[]{:T(512)S(6)} %eq.7, f32[1,16,1792]{2,1,0:T(8,128)} %bitcast.24, f32[1,16,1792]{2,1,0:T(8,128)S(1)} %select_bitcast_fusion, f32[8,16,1792]{2,1,0:T(8,128)} %param.7), kind=kLoop, calls=%fused_computation.87 | loop fusion | flops 358400 | bytes 2007041 | tf_op jit(solution)/shard_map/jit(_where)/select_n | solution.py:22
  2.3 0.0 copy-start.2
  2.4 0.1 copy.12
  2.5 4.7 %collective-permute-start.1 = (f32[10,4,1792]{2,0,1:T(8,128)S(1)}, f32[10,4,1792]{2,0,1:T(8,128)S(1)}, u32[]{:S(2)}, u32[]{:S(2)}) collective-permute-start(f32[10,4,1792]{2,0,1:T(8,128)S(1)} %copy.12), channel_id=1, source_target_pairs={{1,2},{3,4},{5,6},{2,1},{4,3},{6,5},{9,10},{11,12},{13,14},{10,9},... | collective-permute-start | bytes 860168 | tf_op jit(solution)/shard_map/ppermute | solution.py:21
  7.2 0.1 copy.11
  7.3 0.1 collective-permute-start
  7.4 0.4 multiply_reduce_fusion
  7.8 5.6 %collective-permute-done.1 = f32[10,4,1792]{2,0,1:T(8,128)S(1)} collective-permute-done((f32[10,4,1792]{2,0,1:T(8,128)S(1)}, f32[10,4,1792]{2,0,1:T(8,128)S(1)}, u32[]{:S(2)}, u32[]{:S(2)}) %collective-permute-start.1) | collective-permute-done | bytes 286752 | tf_op jit(solution)/shard_map/ppermute | solution.py:21
  13.4 0.4 copy_select_fusion.1
  13.8 0.2 pad_maximum_fusion
  14.1 0.2 fusion.15
  14.3 0.4 fusion.14
  14.7 0.5 %fusion.18 = f32[8,24,1792]{2,1,0:T(8,128)S(1)} fusion(f32[10,24,1792]{2,1,0:T(8,128)S(1)} %pad_maximum_fusion, f32[8,24,1791]{2,1,0:T(8,128)S(1)} %fusion.14, f32[8,23,1792]{2,1,0:T(8,128)S(1)} %fusion.15), kind=kLoop, calls=%fused_computation.37 | loop fusion | flops 1376256 | bytes 5446912 | tf_op jit(solution)/shard_map/sub | solution.py:66
  15.2 0.2 fusion.13
  15.4 0.4 fusion.12
  15.8 0.5 %pad_subtract_fusion.4 = f32[8,24,1792]{2,1,0:T(8,128)S(1)} fusion(f32[8,24,1791]{2,1,0:T(8,128)S(1)} %fusion.12, f32[8,23,1792]{2,1,0:T(8,128)S(1)} %fusion.13, f32[8,24,1792]{2,1,0:T(8,128)S(1)} %fusion.18), kind=kLoop, calls=%fused_computation.43 | loop fusion | flops 1376256 | bytes 5446912 | tf_op jit(solution)/shard_map/sub | solution.py:66
  16.3 0.2 fusion.11
  16.5 0.4 fusion.10
  16.9 0.5 %pad_subtract_fusion.3 = f32[8,24,1792]{2,1,0:T(8,128)S(1)} fusion(f32[8,24,1791]{2,1,0:T(8,128)S(1)} %fusion.10, f32[8,23,1792]{2,1,0:T(8,128)S(1)} %fusion.11, f32[8,24,1792]{2,1,0:T(8,128)S(1)} %pad_subtract_fusion.4), kind=kLoop, calls=%fused_computation.42 | loop fusion | flops 1376256 | bytes 5446912 | tf_op jit(solution)/shard_map/sub | solution.py:66
  17.4 0.2 fusion.9
  17.6 0.4 fusion.8
  18.0 0.6 %fusion.20 = f32[16,1792]{1,0:T(8,128)S(1)} fusion(f32[8,16,1792]{2,1,0:T(8,128)S(1)} %multiply_reduce_fusion, f32[8,24,1791]{2,1,0:T(8,128)S(1)} %fusion.8, f32[8,23,1792]{2,1,0:T(8,128)S(1)} %fusion.9, f32[8,24,1792]{2,1,0:T(8,128)S(1)} %pad_subtract_fusion.3), kind=kLoop, calls=%fused_computation.50 | loop fusion | flops 1347584 | bytes 4644096 | tf_op jit(solution)/shard_map/reduce_sum | solution.py:92
  18.6 1.3 %collective-permute-start.2 = (f32[16,1792]{1,0:T(8,128)S(1)}, f32[16,1792]{1,0:T(8,128)S(1)}, u32[]{:S(2)}, u32[]{:S(2)}) collective-permute-start(f32[16,1792]{1,0:T(8,128)S(1)} %fusion.20), channel_id=1, source_target_pairs={{0,8},{8,0},{16,24},{24,16},{1,9},{9,1},{17,25},{25,17},{2,10},{10... | collective-permute-start | bytes 344072 | tf_op jit(solution)/shard_map/ppermute | solution.py:41
  19.9 1.2 %collective-permute-start.3 = (f32[16,1792]{1,0:T(8,128)S(1)}, f32[16,1792]{1,0:T(8,128)S(1)}, u32[]{:S(2)}, u32[]{:S(2)}) collective-permute-start(f32[16,1792]{1,0:T(8,128)S(1)} %fusion.20), channel_id=1, source_target_pairs={{0,16},{8,24},{16,0},{24,8},{1,17},{9,25},{17,1},{25,9},{2,18},{10... | collective-permute-start | bytes 344072 | tf_op jit(solution)/shard_map/ppermute | solution.py:41
  21.1 0.2 collective-permute-start.4
  21.4 1.8 %collective-permute-done.2 = f32[16,1792]{1,0:T(8,128)S(1)} collective-permute-done((f32[16,1792]{1,0:T(8,128)S(1)}, f32[16,1792]{1,0:T(8,128)S(1)}, u32[]{:S(2)}, u32[]{:S(2)}) %collective-permute-start.2) | collective-permute-done | bytes 114720 | tf_op jit(solution)/shard_map/ppermute | solution.py:41
  23.2 0.8 %collective-permute-done.3 = f32[16,1792]{1,0:T(8,128)S(1)} collective-permute-done((f32[16,1792]{1,0:T(8,128)S(1)}, f32[16,1792]{1,0:T(8,128)S(1)}, u32[]{:S(2)}, u32[]{:S(2)}) %collective-permute-start.3) | collective-permute-done | bytes 114720 | tf_op jit(solution)/shard_map/ppermute | solution.py:41
  24.0 1.7 %collective-permute-done.4 = f32[16,1792]{1,0:T(8,128)S(1)} collective-permute-done((f32[16,1792]{1,0:T(8,128)S(1)}, f32[16,1792]{1,0:T(8,128)S(1)}, u32[]{:S(2)}, u32[]{:S(2)}) %collective-permute-start.4) | collective-permute-done | bytes 114720 | tf_op jit(solution)/shard_map/ppermute | solution.py:41
  25.7 0.1 broadcast_multiply_fusion
  25.8 0.1 slice_select_fusion
  25.9 0.1 collective-permute-start.5
  26.0 1.5 %collective-permute-done.5 = f32[8,4,1792]{2,1,0:T(4,128)S(1)} collective-permute-done((f32[8,4,1792]{2,1,0:T(4,128)S(1)}, f32[8,4,1792]{2,1,0:T(4,128)S(1)}, u32[]{:S(2)}, u32[]{:S(2)}) %collective-permute-start.5) | collective-permute-done | bytes 229408 | tf_op jit(solution)/shard_map/ppermute | solution.py:102
  27.4 0.1 broadcast_select_fusion.3
  27.5 0.2 pad_maximum_fusion.1
  27.7 0.2 fusion.7
  27.9 0.4 fusion.6
  28.3 0.6 %pad_subtract_fusion.2 = f32[8,24,1792]{2,1,0:T(8,128)S(1)} fusion(f32[8,24,1791]{2,1,0:T(8,128)S(1)} %fusion.6, f32[8,23,1792]{2,1,0:T(8,128)S(1)} %fusion.7, f32[8,4,1792]{2,1,0:T(4,128)S(1)} %get-tuple-element.19, f32[8,16,1792]{2,1,0:T(8,128)S(1)} %broadcast_multiply_fusion, f32[8,4,1792]{2,1,0:T(4,128)S(1)} %get-tuple-element.18), kind=kLoop, calls=%fused_computation.41 | loop fusion | flops 2064384 | bytes 5446912 | tf_op jit(solution)/shard_map/sub | solution.py:66
  28.9 0.2 fusion.5
  29.1 0.4 fusion.4
  29.5 0.5 %pad_subtract_fusion.1 = f32[8,24,1792]{2,1,0:T(8,128)S(1)} fusion(f32[8,24,1791]{2,1,0:T(8,128)S(1)} %fusion.4, f32[8,23,1792]{2,1,0:T(8,128)S(1)} %fusion.5, f32[8,24,1792]{2,1,0:T(8,128)S(1)} %pad_subtract_fusion.2), kind=kLoop, calls=%fused_computation.40 | loop fusion | flops 1376256 | bytes 5446912 | tf_op jit(solution)/shard_map/sub | solution.py:66
  30.0 0.2 fusion.3
  30.2 0.4 fusion.2
  30.6 0.5 %pad_subtract_fusion = f32[8,24,1792]{2,1,0:T(8,128)S(1)} fusion(f32[8,24,1791]{2,1,0:T(8,128)S(1)} %fusion.2, f32[8,23,1792]{2,1,0:T(8,128)S(1)} %fusion.3, f32[8,24,1792]{2,1,0:T(8,128)S(1)} %pad_subtract_fusion.1), kind=kLoop, calls=%fused_computation.39 | loop fusion | flops 1376256 | bytes 5446912 | tf_op jit(solution)/shard_map/sub | solution.py:66
  31.1 0.2 fusion.1
  31.3 0.4 fusion
  31.7 0.5 %pad_subtract_fusion.5 = f32[8,16,1792]{2,1,0:T(8,128)S(1)} fusion(f32[8,24,1791]{2,1,0:T(8,128)S(1)} %fusion, f32[8,23,1792]{2,1,0:T(8,128)S(1)} %fusion.1, f32[8,24,1792]{2,1,0:T(8,128)S(1)} %pad_subtract_fusion), kind=kLoop, calls=%fused_computation.44 | loop fusion | flops 917504 | bytes 4529408 | tf_op jit(solution)/shard_map/sub | solution.py:66
  32.3 5.5 %collective-permute-start.6 = (f32[8,4,1792]{2,1,0:T(4,128)S(1)}, f32[8,4,1792]{2,1,0:T(4,128)S(1)}, u32[]{:S(2)}, u32[]{:S(2)}) collective-permute-start(f32[8,4,1792]{2,1,0:T(4,128)S(1)} %get-tuple-element.8), channel_id=1, source_target_pairs={{1,2},{3,4},{5,6},{2,1},{4,3},{6,5},{9,10},{11,12},{13,14},{10,9},... | collective-permute-start | bytes 688136 | tf_op jit(solution)/shard_map/ppermute | solution.py:106
  37.8 3.7 %collective-permute-done.6 = f32[8,4,1792]{2,1,0:T(4,128)S(1)} collective-permute-done((f32[8,4,1792]{2,1,0:T(4,128)S(1)}, f32[8,4,1792]{2,1,0:T(4,128)S(1)}, u32[]{:S(2)}, u32[]{:S(2)}) %collective-permute-start.6) | collective-permute-done | bytes 229408 | tf_op jit(solution)/shard_map/ppermute | solution.py:106
  41.5 0.1 pad_select_fusion
  41.5 0.1 fusion.28
  41.6 0.2 fusion.27
  41.8 0.2 pad_subtract_fusion.12
  42.0 0.1 fusion.26
  42.1 0.2 fusion.25
  42.3 0.2 pad_subtract_fusion.11
  42.5 0.1 fusion.24
  42.6 0.2 fusion.23
  42.8 0.2 pad_subtract_fusion.10
  43.0 0.1 fusion.22
  43.1 0.2 fusion.21
  43.3 0.2 pad_subtract_fusion.9
  43.5 0.1 fusion.30
  43.6 1.1 %add_add_fusion = f32[8,16,1792]{2,1,0:T(8,128)} fusion(f32[8,16,1792]{2,1,0:T(8,128)S(1)} %copy-done, f32[8,16,1792]{2,1,0:T(8,128)S(1)} %pad_subtract_fusion.5, f32[8,4,1792]{2,1,0:T(4,128)S(1)} %get-tuple-element.17, f32[8,4,1792]{2,1,0:T(4,128)S(1)} %get-tuple-element.16, pred[]{:T(512)S(6)} %eq.7), kind=kLoop, calls=%fused_computation.54 | loop fusion | flops 688128 | bytes 3211265 | tf_op jit(solution)/shard_map/add | solution.py:117
  (20 shorter events, 0.2 us)
Async XLA Ops:
  2.3 5.0 %copy-start.2 = (bf16[8,4,16,1792]{3,2,1,0:T(8,128)(2,1)S(1)}, bf16[8,4,16,1792]{3,2,1,0:T(8,128)(2,1)}, u32[]{:S(2)}) copy-start(bf16[8,4,16,1792]{3,2,1,0:T(8,128)(2,1)} %param.8) | copy-start | bytes 5505028
  2.4 5.0 %copy-start.3 = (f32[4,16,1792]{2,1,0:T(8,128)S(1)}, f32[4,16,1792]{2,1,0:T(8,128)}, u32[]{:S(2)}) copy-start(f32[4,16,1792]{2,1,0:T(8,128)} %param.9) | copy-start | bytes 1376260
  2.5 10.9 %collective-permute-start.1 = (f32[10,4,1792]{2,0,1:T(8,128)S(1)}, f32[10,4,1792]{2,0,1:T(8,128)S(1)}, u32[]{:S(2)}, u32[]{:S(2)}) collective-permute-start(f32[10,4,1792]{2,0,1:T(8,128)S(1)} %copy.12), channel_id=1, source_target_pairs={{1,2},{3,4},{5,6},{2,1},{4,3},{6,5},{9,10},{11,12},{13,14},{10,9},... | collective-permute-start | bytes 860168 | tf_op jit(solution)/shard_map/ppermute | solution.py:21
  7.3 6.1 %collective-permute-start = (f32[10,4,1792]{2,0,1:T(8,128)S(1)}, f32[10,4,1792]{2,0,1:T(8,128)S(1)}, u32[]{:S(2)}, u32[]{:S(2)}) collective-permute-start(f32[10,4,1792]{2,0,1:T(8,128)S(1)} %copy.11), channel_id=1, source_target_pairs={{0,1},{2,3},{4,5},{6,7},{1,0},{3,2},{5,4},{7,6},{8,9},{10,11},{12,... | collective-permute-start | bytes 860168 | tf_op jit(solution)/shard_map/ppermute | solution.py:22
  7.8 6.0 %copy-start = (f32[8,16,1792]{2,1,0:T(8,128)S(1)}, f32[8,16,1792]{2,1,0:T(8,128)}, u32[]{:S(2)}) copy-start(f32[8,16,1792]{2,1,0:T(8,128)} %param.7) | copy-start | bytes 2752516
  7.8 6.0 %copy-start.1 = (f32[16,1792]{1,0:T(8,128)S(1)}, f32[16,1792]{1,0:T(8,128)}, u32[]{:S(2)}) copy-start(f32[16,1792]{1,0:T(8,128)} %param.13) | copy-start | bytes 344068
  18.6 7.1 %copy-start.4 = (f32[16,1792]{1,0:T(8,128)S(1)}, f32[16,1792]{1,0:T(8,128)}, u32[]{:S(2)}) copy-start(f32[16,1792]{1,0:T(8,128)} %param.10) | copy-start | bytes 344068
  18.6 7.1 %copy-start.5 = (s32[16,1792]{1,0:T(8,128)S(1)}, s32[16,1792]{1,0:T(8,128)}, u32[]{:S(2)}) copy-start(s32[16,1792]{1,0:T(8,128)} %param.11) | copy-start | bytes 344068
  18.6 4.6 %collective-permute-start.2 = (f32[16,1792]{1,0:T(8,128)S(1)}, f32[16,1792]{1,0:T(8,128)S(1)}, u32[]{:S(2)}, u32[]{:S(2)}) collective-permute-start(f32[16,1792]{1,0:T(8,128)S(1)} %fusion.20), channel_id=1, source_target_pairs={{0,8},{8,0},{16,24},{24,16},{1,9},{9,1},{17,25},{25,17},{2,10},{10... | collective-permute-start | bytes 344072 | tf_op jit(solution)/shard_map/ppermute | solution.py:41
  19.9 4.1 %collective-permute-start.3 = (f32[16,1792]{1,0:T(8,128)S(1)}, f32[16,1792]{1,0:T(8,128)S(1)}, u32[]{:S(2)}, u32[]{:S(2)}) collective-permute-start(f32[16,1792]{1,0:T(8,128)S(1)} %fusion.20), channel_id=1, source_target_pairs={{0,16},{8,24},{16,0},{24,8},{1,17},{9,25},{17,1},{25,9},{2,18},{10... | collective-permute-start | bytes 344072 | tf_op jit(solution)/shard_map/ppermute | solution.py:41
  21.1 4.5 %collective-permute-start.4 = (f32[16,1792]{1,0:T(8,128)S(1)}, f32[16,1792]{1,0:T(8,128)S(1)}, u32[]{:S(2)}, u32[]{:S(2)}) collective-permute-start(f32[16,1792]{1,0:T(8,128)S(1)} %fusion.20), channel_id=1, source_target_pairs={{0,24},{8,16},{16,8},{24,0},{1,25},{9,17},{17,9},{25,1},{2,26},{10... | collective-permute-start | bytes 344072 | tf_op jit(solution)/shard_map/ppermute | solution.py:41
  25.9 1.6 %collective-permute-start.5 = (f32[8,4,1792]{2,1,0:T(4,128)S(1)}, f32[8,4,1792]{2,1,0:T(4,128)S(1)}, u32[]{:S(2)}, u32[]{:S(2)}) collective-permute-start(f32[8,4,1792]{2,1,0:T(4,128)S(1)} %get-tuple-element.13), channel_id=1, source_target_pairs={{0,1},{2,3},{4,5},{6,7},{1,0},{3,2},{5,4},{7,6},{8,9},{10,11},{12,... | collective-permute-start | bytes 688136 | tf_op jit(solution)/shard_map/ppermute | solution.py:102
  32.3 9.2 %collective-permute-start.6 = (f32[8,4,1792]{2,1,0:T(4,128)S(1)}, f32[8,4,1792]{2,1,0:T(4,128)S(1)}, u32[]{:S(2)}, u32[]{:S(2)}) collective-permute-start(f32[8,4,1792]{2,1,0:T(4,128)S(1)} %get-tuple-element.8), channel_id=1, source_target_pairs={{1,2},{3,4},{5,6},{2,1},{4,3},{6,5},{9,10},{11,12},{13,14},{10,9},... | collective-permute-start | bytes 688136 | tf_op jit(solution)/shard_map/ppermute | solution.py:106

commit v17 on v15

--- a/solution.py
+++ b/solution.py
@@ -29,19 +29,22 @@
     count = lax.axis_size("tile")
     head = part[..., :width, :]
     tail = part[..., -width:, :]
-    zero = jnp.zeros_like(head)
-    if count % 2:
-        band = exchange(part, width)
-        return band, zero, False
     odd = lax.axis_index("tile") % 2 == 1
     pairs = lambda first: [(i, i + 1) for i in range(first, count - 1, 2)] + [
         (i + 1, i) for i in range(first, count - 1, 2)
     ]
     far = lax.ppermute(jnp.where(odd, tail, head), "tile", pairs(1))
     near = lax.ppermute(jnp.where(odd, head, tail), "tile", pairs(0))
-    above = jnp.where(odd, near, zero)
-    below = jnp.where(odd, zero, near)
-    return jnp.concatenate([above, part, below], -2), far, odd
+    return near, far, odd
+
+
+def near_band(part, near, odd):
+    zero = jnp.zeros_like(near)
+    return jnp.concatenate([jnp.where(odd, near, zero), part, jnp.where(odd, zero, near)], -2)
+
+
+def full_band(part, near, far, odd):
+    return jnp.concatenate([jnp.where(odd, near, far), part, jnp.where(odd, far, near)], -2)
 
 
 def mem_sum(part):
@@ -88,23 +91,41 @@
 
 
 def per_device(controls, perturbations, jacobian, obs_weight, radar_mask, row_faces, col_faces):
-    row_count = controls.shape[1]
+    members, row_count = controls.shape[:2]
     row_index = lax.axis_index("tile") * row_count + lax.broadcasted_iota(
         jnp.int32, row_faces.shape, 0
     )
     row_coef = jnp.where(
         row_index < row_count * lax.axis_size("tile") - 1, row_faces, jnp.zeros_like(row_faces)
     )
-    members = controls.shape[0]
+    mix = jnp.sum(perturbations.astype(jnp.float32) * jacobian[None], axis=1)
     stacked = jnp.concatenate([controls, row_coef[None], col_faces[None]], 0)
-    band = exchange(stacked, STEPS)
-    field, coef_band = band[:members], band[members:]
-    localized = localize(field, coef_band)[:, STEPS : STEPS + row_count]
-    mix = jnp.sum(perturbations.astype(jnp.float32) * jacobian[None], axis=1)
+    if lax.axis_size("tile") % 2:
+        band = exchange(stacked, STEPS)
+        field, coef_band = band[:members], band[members:]
+        localized = localize(field, coef_band)[:, STEPS : STEPS + row_count]
+        reflect = mem_sum(jnp.sum(mix * localized, 0))
+        weighted = radar_mask.astype(jnp.float32) * obs_weight * reflect
+        sensitivity = exchange(mix * weighted[None], STEPS)
+        return controls + localize(sensitivity, coef_band)[:, STEPS : STEPS + row_count]
+    near, far, odd = split_exchange(stacked, STEPS)
+    partial = near_band(stacked, near, odd)
+    main = localize(partial[:members], partial[members:])[:, STEPS : STEPS + row_count]
+    main, far = lax.optimization_barrier((main, far))
+    band = full_band(stacked, near, far, odd)
+    coef_band = band[members:]
+    strip = jnp.where(odd, band[:, row_count - STEPS :], band[:, : 3 * STEPS])
+    edge = localize(strip[:members], strip[members:])[:, STEPS : 2 * STEPS]
+    localized = jnp.where(
+        odd,
+        jnp.concatenate([main[:, : row_count - STEPS], edge], 1),
+        jnp.concatenate([edge, main[:, STEPS:]], 1),
+    )
     reflect = mem_sum(jnp.sum(mix * localized, 0))
     weighted = radar_mask.astype(jnp.float32) * obs_weight * reflect
-    sensitivity, far, odd = split_exchange(mix * weighted[None], STEPS)
-    spread = localize(sensitivity, coef_band)[:, STEPS : STEPS + row_count]
+    near, far, odd = split_exchange(mix * weighted[None], STEPS)
+    spread = localize(near_band(mix * weighted[None], near, odd), coef_band)
+    spread = spread[:, STEPS : STEPS + row_count]
     spread, far = lax.optimization_barrier((spread, far))
     zero = jnp.zeros_like(far)
     strip = jnp.where(odd, jnp.concatenate([zero, far], 1), jnp.concatenate([far, zero], 1))

time: 39.9 us -> 39.8 us (level)
  waiting for transfers between devices: 9.85 us -> 4.17 us
  other arithmetic: 15.9 us -> 20.3 us
  starting transfers between devices: 13.3 us -> 14.1 us
    ppermute x2 -> x0, waiting for transfers between devices: 5.56 us -> none  [the longest x1 5.56 us: exchange(): far = lax.ppermute(jnp.where(odd, tail, head), 'tile', pairs(1))]
    ppermute x1 -> x2, starting transfers between devices: 5.68 us -> 10.9 us  [split_exchange(): far = lax.ppermute(jnp.where(odd, tail, head), 'tile', pairs(1))]
    ppermute x2 -> x0, starting transfers between devices: 4.8 us -> none  [the longest x1 4.73 us: exchange(): far = lax.ppermute(jnp.where(odd, tail, head), 'tile', pairs(1))]
    sub x11 -> x16, other arithmetic: 4.37 us -> 6.55 us  [diffuse(): values + jnp.concatenate([col_flux, zeros_col], -1)]
    select_n x1 -> x2, other arithmetic: 0.08 us -> 1.43 us  [split_exchange(): far = lax.ppermute(jnp.where(odd, tail, head), 'tile', pairs(1))]
    mul x12 -> x16, other arithmetic: 4.14 us -> 5.35 us  [diffuse(): col_coef[..., :, :-1] * (values[..., :, 1:] - values[..., :, :-1])]
    select_n x4 -> x5, other arithmetic: 1.85 us -> 0.86 us  [the longest x1 0.37 us: full_band(): jnp.where(odd, far, near)]
    ppermute x3, waiting for transfers between devices: 4.28 us -> 3.47 us  [partner(): return lax.ppermute(part, 'mem', [(i, i ^ stride) for i in range(count)])]
  transfers between devices with their start and end apart: 7 -> 7, of which waited for: 4 -> 4; matrix products, arithmetic and copies ran while one was open for 13% -> 26% of each run, Pallas kernels for 0% -> 0%
where the time goes in v17:
time: 39.8 us; the launch traced here: 39.7 us
  other arithmetic  20.3 us (51%)
  starting transfers between devices  14.1 us (35%)
  waiting for transfers between devices  4.17 us (10%)
  between operations  0.56 us (1%)
  local copies, waits for them, and re-layouts  0.46 us (1%)
    ppermute x2, starting transfers between devices, split_exchange(): far = lax.ppermute(jnp.where(odd, tail, head), 'tile', pairs(1))  10.9 us
    sub x16, other arithmetic, diffuse(): values + jnp.concatenate([col_flux, zeros_col], -1)  6.55 us
    mul x16, other arithmetic, diffuse(): col_coef[..., :, :-1] * (values[..., :, 1:] - values[..., :, :-1])  5.35 us
    ppermute x3, waiting for transfers between devices, partner(): return lax.ppermute(part, 'mem', [(i, i ^ stride) for i in range(count)])  3.47 us
    ppermute x3, starting transfers between devices, partner(): return lax.ppermute(part, 'mem', [(i, i ^ stride) for i in range(count)])  3.1 us
    mul x16, other arithmetic, diffuse(): row_coef[..., :-1, :] * (values[..., 1:, :] - values[..., :-1, :])  2.24 us
    select_n x2, other arithmetic, split_exchange(): far = lax.ppermute(jnp.where(odd, tail, head), 'tile', pairs(1))  1.43 us
    add x1, other arithmetic, per_device(): return controls + (spread + edge)  1.12 us
  transfers between devices with their start and end apart: 7, of which 4 were waited for; matrix products, arithmetic and copies ran while one was open for 26% of the time, Pallas kernels for 0%

profile of v17, /device:TPU:1, one launch (start us, length us, event | category | flops | bytes accessed | tf_op | source)
XLA Modules:
  0.0 39.7 jit_solution(984363925460738809)
XLA Ops:
  0.0 1.0 %select_bitcast_fusion = f32[1,16,1792]{2,1,0:T(8,128)S(1)} fusion(f32[16,1792]{1,0:T(8,128)} %param.12, pred[16]{0:T(512)(128)(4,1)S(1)} %add_compare_fusion), kind=kLoop, calls=%fused_computation.130 | loop fusion | flops 28672 | bytes 229392 | tf_op jit(solution)/shard_map/broadcast_in_dim | solution.py:102
  1.0 1.4 %broadcast_select_fusion.2 = (f32[10,4,1792]{2,1,0:T(4,128)S(1)}, f32[10,4,1792]{2,1,0:T(4,128)S(1)}, f32[10,4,1792]{2,1,0:T(4,128)S(1)}) fusion(pred[]{:T(512)S(6)} %eq.7, f32[1,16,1792]{2,1,0:T(8,128)} %bitcast.38, f32[1,16,1792]{2,1,0:T(8,128)S(1)} %select_bitcast_fusion, f32[8,16,1792]{2,1,0:T(8,128)} %param.7), kind=kLoop, calls=%fused_computation.122 | loop fusion | flops 358400 | bytes 2007041 | tf_op jit(solution)/shard_map/jit(_where)/select_n | solution.py:36
  2.7 4.7 %collective-permute-start.1 = (f32[10,4,1792]{2,0,1:T(8,128)S(1)}, f32[10,4,1792]{2,0,1:T(8,128)S(1)}, u32[]{:S(2)}, u32[]{:S(2)}) collective-permute-start(f32[10,4,1792]{2,0,1:T(8,128)S(1)} %copy.14), channel_id=1, source_target_pairs={{1,2},{3,4},{5,6},{2,1},{4,3},{6,5},{9,10},{11,12},{13,14},{10,9},... | collective-permute-start | bytes 860168 | tf_op jit(solution)/shard_map/ppermute | solution.py:36
  7.4 0.4 multiply_reduce_fusion
  7.8 0.2 broadcast_select_fusion.1
  8.1 0.2 pad_maximum_fusion
  8.4 0.4 %fusion.14 = f32[8,24,1791]{2,1,0:T(8,128)S(1)} fusion(f32[10,24,1792]{2,1,0:T(8,128)S(1)} %pad_maximum_fusion, f32[24,1791]{1,0:T(8,128)S(1)} %bitcast.30), kind=kLoop, calls=%fused_computation.35 | loop fusion | flops 687744 | bytes 4298400 | tf_op jit(solution)/shard_map/mul | solution.py:72
  8.8 0.2 fusion.15
  9.0 0.5 %fusion.18 = f32[8,24,1792]{2,1,0:T(8,128)S(1)} fusion(f32[10,24,1792]{2,1,0:T(8,128)S(1)} %pad_maximum_fusion, f32[8,24,1791]{2,1,0:T(8,128)S(1)} %fusion.14, f32[8,23,1792]{2,1,0:T(8,128)S(1)} %fusion.15), kind=kLoop, calls=%fused_computation.41 | loop fusion | flops 1376256 | bytes 5446912 | tf_op jit(solution)/shard_map/sub | solution.py:81
  9.5 0.4 %fusion.12 = f32[8,24,1791]{2,1,0:T(8,128)S(1)} fusion(f32[8,24,1792]{2,1,0:T(8,128)S(1)} %fusion.18, f32[24,1791]{1,0:T(8,128)S(1)} %bitcast.31), kind=kLoop, calls=%fused_computation.31 | loop fusion | flops 687744 | bytes 4298400 | tf_op jit(solution)/shard_map/mul | solution.py:72
  9.9 0.2 fusion.13
  10.1 0.5 %pad_subtract_fusion.4 = f32[8,24,1792]{2,1,0:T(8,128)S(1)} fusion(f32[8,24,1791]{2,1,0:T(8,128)S(1)} %fusion.12, f32[8,23,1792]{2,1,0:T(8,128)S(1)} %fusion.13, f32[8,24,1792]{2,1,0:T(8,128)S(1)} %fusion.18), kind=kLoop, calls=%fused_computation.47 | loop fusion | flops 1376256 | bytes 5446912 | tf_op jit(solution)/shard_map/sub | solution.py:81
  10.6 0.4 %fusion.10 = f32[8,24,1791]{2,1,0:T(8,128)S(1)} fusion(f32[8,24,1792]{2,1,0:T(8,128)S(1)} %pad_subtract_fusion.4, f32[24,1791]{1,0:T(8,128)S(1)} %bitcast.32), kind=kLoop, calls=%fused_computation.27 | loop fusion | flops 687744 | bytes 4298400 | tf_op jit(solution)/shard_map/mul | solution.py:72
  11.0 0.2 fusion.11
  11.2 0.5 %pad_subtract_fusion.3 = f32[8,24,1792]{2,1,0:T(8,128)S(1)} fusion(f32[8,24,1791]{2,1,0:T(8,128)S(1)} %fusion.10, f32[8,23,1792]{2,1,0:T(8,128)S(1)} %fusion.11, f32[8,24,1792]{2,1,0:T(8,128)S(1)} %pad_subtract_fusion.4), kind=kLoop, calls=%fused_computation.46 | loop fusion | flops 1376256 | bytes 5446912 | tf_op jit(solution)/shard_map/sub | solution.py:81
  11.7 0.4 %fusion.8 = f32[8,24,1791]{2,1,0:T(8,128)S(1)} fusion(f32[8,24,1792]{2,1,0:T(8,128)S(1)} %pad_subtract_fusion.3, f32[24,1791]{1,0:T(8,128)S(1)} %bitcast.33), kind=kLoop, calls=%fused_computation.23 | loop fusion | flops 687744 | bytes 4298400 | tf_op jit(solution)/shard_map/mul | solution.py:72
  12.1 0.2 fusion.9
  12.3 0.5 %pad_subtract_fusion.7 = f32[8,16,1792]{2,1,0:T(8,128)S(1)} fusion(f32[8,24,1791]{2,1,0:T(8,128)S(1)} %fusion.8, f32[8,23,1792]{2,1,0:T(8,128)S(1)} %fusion.9, f32[8,24,1792]{2,1,0:T(8,128)S(1)} %pad_subtract_fusion.3), kind=kLoop, calls=%fused_computation.73 | loop fusion | flops 917504 | bytes 4529408 | tf_op jit(solution)/shard_map/sub | solution.py:81
  12.9 0.7 %collective-permute-done.1 = f32[10,4,1792]{2,0,1:T(8,128)S(1)} collective-permute-done((f32[10,4,1792]{2,0,1:T(8,128)S(1)}, f32[10,4,1792]{2,0,1:T(8,128)S(1)}, u32[]{:S(2)}, u32[]{:S(2)}) %collective-permute-start.1) | collective-permute-done | bytes 286752 | tf_op jit(solution)/shard_map/ppermute | solution.py:36
  13.5 0.4 copy_select_fusion.1
  13.9 0.2 pad_maximum_fusion.2
  14.3 0.3 fusion.25
  14.6 0.1 fusion.26
  14.8 0.5 %fusion.29 = f32[8,12,1792]{2,1,0:T(8,128)S(1)} fusion(f32[10,12,1792]{2,1,0:T(8,128)S(1)} %slice_select_fusion, f32[8,12,1791]{2,1,0:T(8,128)S(1)} %fusion.25, f32[8,11,1792]{2,1,0:T(8,128)S(1)} %fusion.26), kind=kLoop, calls=%fused_computation.72 | loop fusion | flops 688128 | bytes 2694784 | tf_op jit(solution)/shard_map/sub | solution.py:81
  15.2 0.3 fusion.23
  15.5 0.1 fusion.24
  15.7 0.5 %pad_subtract_fusion.10 = f32[8,12,1792]{2,1,0:T(8,128)S(1)} fusion(f32[8,12,1791]{2,1,0:T(8,128)S(1)} %fusion.23, f32[8,11,1792]{2,1,0:T(8,128)S(1)} %fusion.24, f32[8,12,1792]{2,1,0:T(8,128)S(1)} %fusion.29), kind=kLoop, calls=%fused_computation.82 | loop fusion | flops 688128 | bytes 2694784 | tf_op jit(solution)/shard_map/sub | solution.py:81
  16.1 0.3 fusion.21
  16.4 0.1 fusion.22
  16.6 0.5 %pad_subtract_fusion.9 = f32[8,12,1792]{2,1,0:T(8,128)S(1)} fusion(f32[8,12,1791]{2,1,0:T(8,128)S(1)} %fusion.21, f32[8,11,1792]{2,1,0:T(8,128)S(1)} %fusion.22, f32[8,12,1792]{2,1,0:T(8,128)S(1)} %pad_subtract_fusion.10), kind=kLoop, calls=%fused_computation.81 | loop fusion | flops 688128 | bytes 2694784 | tf_op jit(solution)/shard_map/sub | solution.py:81
  17.0 0.3 fusion.19
  17.3 0.1 fusion.20
  17.5 0.1 fusion.40
  17.6 0.3 pad_subtract_fusion.15
  17.9 0.3 fusion.31
  18.2 1.8 %collective-permute-start.3 = (f32[16,1792]{1,0:T(8,128)S(1)}, f32[16,1792]{1,0:T(8,128)S(1)}, u32[]{:S(2)}, u32[]{:S(2)}) collective-permute-start(f32[16,1792]{1,0:T(8,128)S(1)} %fusion.31), channel_id=1, source_target_pairs={{0,16},{8,24},{16,0},{24,8},{1,17},{9,25},{17,1},{25,9},{2,18},{10... | collective-permute-start | bytes 344072 | tf_op jit(solution)/shard_map/ppermute | solution.py:56
  20.0 1.2 %collective-permute-start.4 = (f32[16,1792]{1,0:T(8,128)S(1)}, f32[16,1792]{1,0:T(8,128)S(1)}, u32[]{:S(2)}, u32[]{:S(2)}) collective-permute-start(f32[16,1792]{1,0:T(8,128)S(1)} %fusion.31), channel_id=1, source_target_pairs={{0,24},{8,16},{16,8},{24,0},{1,25},{9,17},{17,9},{25,1},{2,26},{10... | collective-permute-start | bytes 344072 | tf_op jit(solution)/shard_map/ppermute | solution.py:56
  21.3 0.2 pad_maximum_fusion.3
  21.7 1.8 %collective-permute-done.3 = f32[16,1792]{1,0:T(8,128)S(1)} collective-permute-done((f32[16,1792]{1,0:T(8,128)S(1)}, f32[16,1792]{1,0:T(8,128)S(1)}, u32[]{:S(2)}, u32[]{:S(2)}) %collective-permute-start.3) | collective-permute-done | bytes 114720 | tf_op jit(solution)/shard_map/ppermute | solution.py:56
  23.4 1.4 %collective-permute-done.4 = f32[16,1792]{1,0:T(8,128)S(1)} collective-permute-done((f32[16,1792]{1,0:T(8,128)S(1)}, f32[16,1792]{1,0:T(8,128)S(1)}, u32[]{:S(2)}, u32[]{:S(2)}) %collective-permute-start.4) | collective-permute-done | bytes 114720 | tf_op jit(solution)/shard_map/ppermute | solution.py:56
  24.9 0.3 collective-permute-done.2
  25.4 6.2 %collective-permute-start.6 = (f32[8,4,1792]{2,1,0:T(4,128)S(1)}, f32[8,4,1792]{2,1,0:T(4,128)S(1)}, u32[]{:S(2)}, u32[]{:S(2)}) collective-permute-start(f32[8,4,1792]{2,1,0:T(4,128)S(1)} %get-tuple-element.18), channel_id=1, source_target_pairs={{1,2},{3,4},{5,6},{2,1},{4,3},{6,5},{9,10},{11,12},{13,14},{10,9},... | collective-permute-start | bytes 688136 | tf_op jit(solution)/shard_map/ppermute | solution.py:36
  31.7 0.2 pad_maximum_fusion.4
  31.9 0.4 %fusion.6 = f32[8,24,1791]{2,1,0:T(8,128)S(1)} fusion(f32[8,24,1792]{2,1,0:T(8,128)S(1)} %pad_maximum_fusion.4, f32[24,1791]{1,0:T(8,128)S(1)} %bitcast.26), kind=kLoop, calls=%fused_computation.19 | loop fusion | flops 687744 | bytes 4298400 | tf_op jit(solution)/shard_map/mul | solution.py:72
  32.3 0.2 fusion.7
  32.5 0.6 %pad_subtract_fusion.2 = f32[8,24,1792]{2,1,0:T(8,128)S(1)} fusion(f32[8,24,1791]{2,1,0:T(8,128)S(1)} %fusion.6, f32[8,23,1792]{2,1,0:T(8,128)S(1)} %fusion.7, f32[8,4,1792]{2,1,0:T(4,128)S(1)} %get-tuple-element.29, f32[8,16,1792]{2,1,0:T(8,128)S(1)} %broadcast_multiply_fusion, f32[8,4,1792]{2,1,0:T(4,128)S(1)} %get-tuple-element.28), kind=kLoop, calls=%fused_computation.45 | loop fusion | flops 2064384 | bytes 5446912 | tf_op jit(solution)/shard_map/sub | solution.py:81
  33.1 0.4 %fusion.4 = f32[8,24,1791]{2,1,0:T(8,128)S(1)} fusion(f32[8,24,1792]{2,1,0:T(8,128)S(1)} %pad_subtract_fusion.2, f32[24,1791]{1,0:T(8,128)S(1)} %bitcast.27), kind=kLoop, calls=%fused_computation.15 | loop fusion | flops 687744 | bytes 4298400 | tf_op jit(solution)/shard_map/mul | solution.py:72
  33.5 0.2 fusion.5
  33.7 0.5 %pad_subtract_fusion.1 = f32[8,24,1792]{2,1,0:T(8,128)S(1)} fusion(f32[8,24,1791]{2,1,0:T(8,128)S(1)} %fusion.4, f32[8,23,1792]{2,1,0:T(8,128)S(1)} %fusion.5, f32[8,24,1792]{2,1,0:T(8,128)S(1)} %pad_subtract_fusion.2), kind=kLoop, calls=%fused_computation.44 | loop fusion | flops 1376256 | bytes 5446912 | tf_op jit(solution)/shard_map/sub | solution.py:81
  34.2 0.4 %fusion.2 = f32[8,24,1791]{2,1,0:T(8,128)S(1)} fusion(f32[8,24,1792]{2,1,0:T(8,128)S(1)} %pad_subtract_fusion.1, f32[24,1791]{1,0:T(8,128)S(1)} %bitcast.28), kind=kLoop, calls=%fused_computation.11 | loop fusion | flops 687744 | bytes 4298400 | tf_op jit(solution)/shard_map/mul | solution.py:72
  34.6 0.2 fusion.3
  34.8 0.5 %pad_subtract_fusion = f32[8,24,1792]{2,1,0:T(8,128)S(1)} fusion(f32[8,24,1791]{2,1,0:T(8,128)S(1)} %fusion.2, f32[8,23,1792]{2,1,0:T(8,128)S(1)} %fusion.3, f32[8,24,1792]{2,1,0:T(8,128)S(1)} %pad_subtract_fusion.1), kind=kLoop, calls=%fused_computation.43 | loop fusion | flops 1376256 | bytes 5446912 | tf_op jit(solution)/shard_map/sub | solution.py:81
  35.3 0.4 %fusion = f32[8,24,1791]{2,1,0:T(8,128)S(1)} fusion(f32[8,24,1792]{2,1,0:T(8,128)S(1)} %pad_subtract_fusion, f32[24,1791]{1,0:T(8,128)S(1)} %bitcast.29), kind=kLoop, calls=%fused_computation.7 | loop fusion | flops 687744 | bytes 4298400 | tf_op jit(solution)/shard_map/mul | solution.py:72
  35.7 0.2 fusion.1
  35.9 0.5 %pad_subtract_fusion.5 = f32[8,16,1792]{2,1,0:T(8,128)S(1)} fusion(f32[8,24,1791]{2,1,0:T(8,128)S(1)} %fusion, f32[8,23,1792]{2,1,0:T(8,128)S(1)} %fusion.1, f32[8,24,1792]{2,1,0:T(8,128)S(1)} %pad_subtract_fusion), kind=kLoop, calls=%fused_computation.49 | loop fusion | flops 917504 | bytes 4529408 | tf_op jit(solution)/shard_map/sub | solution.py:81
  36.5 0.2 fusion.38
  36.8 0.2 pad_subtract_fusion.14
  37.0 0.2 fusion.36
  37.3 0.2 pad_subtract_fusion.13
  37.5 0.2 fusion.34
  37.8 0.2 pad_subtract_fusion.12
  38.0 0.2 fusion.32
  38.2 0.2 pad_subtract_fusion.11
  38.6 1.1 %add_add_fusion = f32[8,16,1792]{2,1,0:T(8,128)} fusion(f32[8,16,1792]{2,1,0:T(8,128)S(1)} %copy-done, f32[8,16,1792]{2,1,0:T(8,128)S(1)} %pad_subtract_fusion.5, f32[8,4,1792]{2,1,0:T(4,128)S(1)} %get-tuple-element.25, f32[8,4,1792]{2,1,0:T(4,128)S(1)} %get-tuple-element.24, pred[]{:T(512)S(6)} %eq.7), kind=kLoop, calls=%fused_computation.80 | loop fusion | flops 688128 | bytes 3211265 | tf_op jit(solution)/shard_map/add | solution.py:140
  (42 shorter events, 1.4 us)
Async XLA Ops:
  2.3 5.1 %copy-start.2 = (bf16[8,4,16,1792]{3,2,1,0:T(8,128)(2,1)S(1)}, bf16[8,4,16,1792]{3,2,1,0:T(8,128)(2,1)}, u32[]{:S(2)}) copy-start(bf16[8,4,16,1792]{3,2,1,0:T(8,128)(2,1)} %param.8) | copy-start | bytes 5505028
  2.4 5.1 %copy-start.3 = (f32[4,16,1792]{2,1,0:T(8,128)S(1)}, f32[4,16,1792]{2,1,0:T(8,128)}, u32[]{:S(2)}) copy-start(f32[4,16,1792]{2,1,0:T(8,128)} %param.9) | copy-start | bytes 1376260
  2.5 5.3 %collective-permute-start = (f32[10,4,1792]{2,0,1:T(8,128)S(1)}, f32[10,4,1792]{2,0,1:T(8,128)S(1)}, u32[]{:S(2)}, u32[]{:S(2)}) collective-permute-start(f32[10,4,1792]{2,0,1:T(8,128)S(1)} %copy.11), channel_id=1, source_target_pairs={{0,1},{2,3},{4,5},{6,7},{1,0},{3,2},{5,4},{7,6},{8,9},{10,11},{12,... | collective-permute-start | bytes 860168 | tf_op jit(solution)/shard_map/ppermute | solution.py:37
  2.7 5.4 %copy-start = (f32[8,16,1792]{2,1,0:T(8,128)S(1)}, f32[8,16,1792]{2,1,0:T(8,128)}, u32[]{:S(2)}) copy-start(f32[8,16,1792]{2,1,0:T(8,128)} %param.7) | copy-start | bytes 2752516
  2.7 5.4 %copy-start.1 = (f32[16,1792]{1,0:T(8,128)S(1)}, f32[16,1792]{1,0:T(8,128)}, u32[]{:S(2)}) copy-start(f32[16,1792]{1,0:T(8,128)} %param.13) | copy-start | bytes 344068
  2.7 10.8 %collective-permute-start.1 = (f32[10,4,1792]{2,0,1:T(8,128)S(1)}, f32[10,4,1792]{2,0,1:T(8,128)S(1)}, u32[]{:S(2)}, u32[]{:S(2)}) collective-permute-start(f32[10,4,1792]{2,0,1:T(8,128)S(1)} %copy.14), channel_id=1, source_target_pairs={{1,2},{3,4},{5,6},{2,1},{4,3},{6,5},{9,10},{11,12},{13,14},{10,9},... | collective-permute-start | bytes 860168 | tf_op jit(solution)/shard_map/ppermute | solution.py:36
  18.2 5.3 %collective-permute-start.3 = (f32[16,1792]{1,0:T(8,128)S(1)}, f32[16,1792]{1,0:T(8,128)S(1)}, u32[]{:S(2)}, u32[]{:S(2)}) collective-permute-start(f32[16,1792]{1,0:T(8,128)S(1)} %fusion.31), channel_id=1, source_target_pairs={{0,16},{8,24},{16,0},{24,8},{1,17},{9,25},{17,1},{25,9},{2,18},{10... | collective-permute-start | bytes 344072 | tf_op jit(solution)/shard_map/ppermute | solution.py:56
  20.0 4.8 %collective-permute-start.4 = (f32[16,1792]{1,0:T(8,128)S(1)}, f32[16,1792]{1,0:T(8,128)S(1)}, u32[]{:S(2)}, u32[]{:S(2)}) collective-permute-start(f32[16,1792]{1,0:T(8,128)S(1)} %fusion.31), channel_id=1, source_target_pairs={{0,24},{8,16},{16,8},{24,0},{1,25},{9,17},{17,9},{25,1},{2,26},{10... | collective-permute-start | bytes 344072 | tf_op jit(solution)/shard_map/ppermute | solution.py:56
  21.2 4.0 %collective-permute-start.2 = (f32[16,1792]{1,0:T(8,128)S(1)}, f32[16,1792]{1,0:T(8,128)S(1)}, u32[]{:S(2)}, u32[]{:S(2)}) collective-permute-start(f32[16,1792]{1,0:T(8,128)S(1)} %fusion.31), channel_id=1, source_target_pairs={{0,8},{8,0},{16,24},{24,16},{1,9},{9,1},{17,25},{25,17},{2,10},{10... | collective-permute-start | bytes 344072 | tf_op jit(solution)/shard_map/ppermute | solution.py:56
  21.5 3.6 %copy-start.4 = (f32[16,1792]{1,0:T(8,128)S(1)}, f32[16,1792]{1,0:T(8,128)}, u32[]{:S(2)}) copy-start(f32[16,1792]{1,0:T(8,128)} %param.10) | copy-start | bytes 344068
  21.5 3.6 %copy-start.5 = (s32[16,1792]{1,0:T(8,128)S(1)}, s32[16,1792]{1,0:T(8,128)}, u32[]{:S(2)}) copy-start(s32[16,1792]{1,0:T(8,128)} %param.11) | copy-start | bytes 344068
  25.3 6.3 %collective-permute-start.5 = (f32[8,4,1792]{2,1,0:T(4,128)S(1)}, f32[8,4,1792]{2,1,0:T(4,128)S(1)}, u32[]{:S(2)}, u32[]{:S(2)}) collective-permute-start(f32[8,4,1792]{2,1,0:T(4,128)S(1)} %get-tuple-element.19), channel_id=1, source_target_pairs={{0,1},{2,3},{4,5},{6,7},{1,0},{3,2},{5,4},{7,6},{8,9},{10,11},{12,... | collective-permute-start | bytes 688136 | tf_op jit(solution)/shard_map/ppermute | solution.py:37
  25.4 11.0 %collective-permute-start.6 = (f32[8,4,1792]{2,1,0:T(4,128)S(1)}, f32[8,4,1792]{2,1,0:T(4,128)S(1)}, u32[]{:S(2)}, u32[]{:S(2)}) collective-permute-start(f32[8,4,1792]{2,1,0:T(4,128)S(1)} %get-tuple-element.18), channel_id=1, source_target_pairs={{1,2},{3,4},{5,6},{2,1},{4,3},{6,5},{9,10},{11,12},{13,14},{10,9},... | collective-permute-start | bytes 688136 | tf_op jit(solution)/shard_map/ppermute | solution.py:36

commit v18 on v17

--- a/solution.py
+++ b/solution.py
@@ -27,14 +27,17 @@
 
 def split_exchange(part, width):
     count = lax.axis_size("tile")
-    head = part[..., :width, :]
-    tail = part[..., -width:, :]
+    rows = part.shape[-2]
     odd = lax.axis_index("tile") % 2 == 1
     pairs = lambda first: [(i, i + 1) for i in range(first, count - 1, 2)] + [
         (i + 1, i) for i in range(first, count - 1, 2)
     ]
-    far = lax.ppermute(jnp.where(odd, tail, head), "tile", pairs(1))
-    near = lax.ppermute(jnp.where(odd, head, tail), "tile", pairs(0))
+    far_start = jnp.where(odd, rows - width, 0)
+    near_start = jnp.where(odd, 0, rows - width)
+    outgoing = lax.dynamic_slice_in_dim(part, far_start, width, axis=part.ndim - 2)
+    far = lax.ppermute(outgoing, "tile", pairs(1))
+    outgoing = lax.dynamic_slice_in_dim(part, near_start, width, axis=part.ndim - 2)
+    near = lax.ppermute(outgoing, "tile", pairs(0))
     return near, far, odd
 
 
@@ -92,17 +95,19 @@
 
 def per_device(controls, perturbations, jacobian, obs_weight, radar_mask, row_faces, col_faces):
     members, row_count = controls.shape[:2]
-    row_index = lax.axis_index("tile") * row_count + lax.broadcasted_iota(
-        jnp.int32, row_faces.shape, 0
-    )
-    row_coef = jnp.where(
-        row_index < row_count * lax.axis_size("tile") - 1, row_faces, jnp.zeros_like(row_faces)
-    )
+    last_row = row_count * lax.axis_size("tile") - 1 - lax.axis_index("tile") * row_count
+
+    def masked(coefs, first):
+        band_row = first + lax.broadcasted_iota(jnp.int32, coefs.shape, 1)
+        keep = (band_row != last_row) | (lax.broadcasted_iota(jnp.int32, coefs.shape, 0) > 0)
+        return jnp.where(keep, coefs, jnp.zeros_like(coefs))
+
+    row_coef = row_faces
     mix = jnp.sum(perturbations.astype(jnp.float32) * jacobian[None], axis=1)
     stacked = jnp.concatenate([controls, row_coef[None], col_faces[None]], 0)
     if lax.axis_size("tile") % 2:
         band = exchange(stacked, STEPS)
-        field, coef_band = band[:members], band[members:]
+        field, coef_band = band[:members], masked(band[members:], -STEPS)
         localized = localize(field, coef_band)[:, STEPS : STEPS + row_count]
         reflect = mem_sum(jnp.sum(mix * localized, 0))
         weighted = radar_mask.astype(jnp.float32) * obs_weight * reflect
@@ -110,9 +115,11 @@
         return controls + localize(sensitivity, coef_band)[:, STEPS : STEPS + row_count]
     near, far, odd = split_exchange(stacked, STEPS)
     partial = near_band(stacked, near, odd)
-    main = localize(partial[:members], partial[members:])[:, STEPS : STEPS + row_count]
+    main = localize(partial[:members], masked(partial[members:], -STEPS))
+    main = main[:, STEPS : STEPS + row_count]
     main, far = lax.optimization_barrier((main, far))
     band = full_band(stacked, near, far, odd)
+    band = jnp.concatenate([band[:members], masked(band[members:], -STEPS)], 0)
     coef_band = band[members:]
     strip = jnp.where(odd, band[:, row_count - STEPS :], band[:, : 3 * STEPS])
     edge = localize(strip[:members], strip[members:])[:, STEPS : 2 * STEPS]

time: 39.8 us -> 41 us (1.030)
  local copies, waits for them, and re-layouts: 0.46 us -> 2.05 us
  starting transfers between devices: 14.1 us -> 12.9 us
  waiting for transfers between devices: 4.17 us -> 4.89 us
    concatenate x0 -> x1, other arithmetic: none -> 1.39 us  [per_device(): stacked = jnp.concatenate([controls, row_coef[None], col_faces[None]], 0)]
    ppermute x3, waiting for transfers between devices: 3.47 us -> 4.77 us  [partner(): return lax.ppermute(part, 'mem', [(i, i ^ stride) for i in range(count)])]
    ppermute x4, starting transfers between devices: 11 us -> 9.86 us  [the longest x2 9.73 us: split_exchange(): far = lax.ppermute(outgoing, 'tile', pairs(1))]
    dynamic_slice x0 -> x4, local copies, waits for them, and re-layouts: none -> 1.11 us  [the longest x1 0.83 us: split_exchange(): lax.dynamic_slice_in_dim(part, near_start, width, axis=part.ndim - 2)]
    broadcast_in_dim x1 -> x0, other arithmetic: 0.98 us -> none  [per_device(): stacked = jnp.concatenate([controls, row_coef[None], col_faces[None]], 0)]
    ppermute x4, waiting for transfers between devices: 0.7 us -> 0.12 us  [the longest x2 0.11 us: split_exchange(): far = lax.ppermute(outgoing, 'tile', pairs(1))]
    unnamed x12 -> x14, local copies, waits for them, and re-layouts: 0.04 us -> 0.57 us
    select_n x4 -> x3, other arithmetic: 1.85 us -> 1.58 us  [the longest x1 1.39 us: full_band(): jnp.where(odd, near, far)]
  transfers between devices with their start and end apart: 7 -> 7, of which waited for: 4 -> 3; matrix products, arithmetic and copies ran while one was open for 26% -> 25% of each run, Pallas kernels for 0% -> 0%
where the time goes in v18:
time: 41 us; the launch traced here: 40.7 us
  other arithmetic  20.3 us (50%)
  starting transfers between devices  12.9 us (31%)
  waiting for transfers between devices  4.89 us (12%)
  local copies, waits for them, and re-layouts  2.05 us (5%)
  between operations  0.55 us (1%)
    ppermute x2, starting transfers between devices, split_exchange(): far = lax.ppermute(outgoing, 'tile', pairs(1))  9.73 us
    sub x16, other arithmetic, diffuse(): values + jnp.concatenate([col_flux, zeros_col], -1)  6.57 us
    mul x16, other arithmetic, diffuse(): col_coef[..., :, :-1] * (values[..., :, 1:] - values[..., :, :-1])  5.35 us
    ppermute x3, waiting for transfers between devices, partner(): return lax.ppermute(part, 'mem', [(i, i ^ stride) for i in range(count)])  4.77 us
    ppermute x3, starting transfers between devices, partner(): return lax.ppermute(part, 'mem', [(i, i ^ stride) for i in range(count)])  3.09 us
    mul x16, other arithmetic, diffuse(): row_coef[..., :-1, :] * (values[..., 1:, :] - values[..., :-1, :])  2.3 us
    select_n x1, other arithmetic, full_band(): jnp.where(odd, near, far)  1.39 us
    concatenate x1, other arithmetic, per_device(): stacked = jnp.concatenate([controls, row_coef[None], col_faces[None]], 0)  1.39 us
  transfers between devices with their start and end apart: 7, of which 3 were waited for; matrix products, arithmetic and copies ran while one was open for 25% of the time, Pallas kernels for 0%

profile of v18, /device:TPU:1, one launch (start us, length us, event | category | flops | bytes accessed | tf_op | source)
XLA Modules:
  0.0 40.7 jit_solution(11298971724559895126)
XLA Ops:
  0.0 1.4 %pad_maximum_fusion.5 = f32[10,16,1792]{2,1,0:T(8,128)S(1)} fusion(f32[1,16,1792]{2,1,0:T(8,128)} %bitcast.38, f32[1,16,1792]{2,1,0:T(8,128)} %bitcast.41, f32[8,16,1792]{2,1,0:T(8,128)} %param.7), kind=kLoop, calls=%fused_computation.51 | loop fusion | flops 573440 | bytes 2293760 | tf_op jit(solution)/shard_map/concatenate | solution.py:107
  1.5 0.8 %copy.11 = f32[10,4,1792]{2,0,1:T(8,128)} copy(f32[10,4,1792]{2,1,0:T(4,128)S(1)} %get-tuple-element.14) | data formatting | bytes 573440 | tf_op jit(solution)/shard_map/dynamic_slice | solution.py:39
  2.5 4.5 %collective-permute-start.1 = (f32[10,4,1792]{2,0,1:T(8,128)S(1)}, f32[10,4,1792]{2,0,1:T(8,128)}, u32[]{:S(2)}, u32[]{:S(2)}) collective-permute-start(f32[10,4,1792]{2,0,1:T(8,128)S(1)} %copy.14), channel_id=1, source_target_pairs={{1,2},{3,4},{5,6},{2,1},{4,3},{6,5},{9,10},{11,12},{13,14},{10,9},... | collective-permute-start | bytes 860168 | tf_op jit(solution)/shard_map/ppermute | solution.py:38
  7.1 0.4 multiply_reduce_fusion
  7.5 0.2 broadcast_select_fusion.1
  7.8 0.5 %copy-done = f32[8,16,1792]{2,1,0:T(8,128)S(1)} copy-done((f32[8,16,1792]{2,1,0:T(8,128)S(1)}, f32[8,16,1792]{2,1,0:T(8,128)}, u32[]{:S(2)}) %copy-start) | copy-done | bytes 917528
  8.3 0.3 pad_maximum_fusion
  8.7 0.2 fusion.15
  8.9 0.4 %fusion.14 = f32[8,24,1791]{2,1,0:T(8,128)S(1)} fusion(f32[10,24,1792]{2,1,0:T(8,128)S(1)} %pad_maximum_fusion, f32[24,1791]{1,0:T(8,128)S(1)} %bitcast.26), kind=kLoop, calls=%fused_computation.35 | loop fusion | flops 687744 | bytes 4298400 | tf_op jit(solution)/shard_map/mul | solution.py:75
  9.3 0.5 %fusion.18 = f32[8,24,1792]{2,1,0:T(8,128)S(1)} fusion(f32[10,24,1792]{2,1,0:T(8,128)S(1)} %pad_maximum_fusion, f32[8,24,1791]{2,1,0:T(8,128)S(1)} %fusion.14, f32[8,23,1792]{2,1,0:T(8,128)S(1)} %fusion.15), kind=kLoop, calls=%fused_computation.41 | loop fusion | flops 1376256 | bytes 5446912 | tf_op jit(solution)/shard_map/sub | solution.py:84
  9.8 0.2 fusion.13
  10.0 0.4 %fusion.12 = f32[8,24,1791]{2,1,0:T(8,128)S(1)} fusion(f32[8,24,1792]{2,1,0:T(8,128)S(1)} %fusion.18, f32[24,1791]{1,0:T(8,128)S(1)} %bitcast.27), kind=kLoop, calls=%fused_computation.31 | loop fusion | flops 687744 | bytes 4298400 | tf_op jit(solution)/shard_map/mul | solution.py:75
  10.4 0.5 %pad_subtract_fusion.4 = f32[8,24,1792]{2,1,0:T(8,128)S(1)} fusion(f32[8,24,1791]{2,1,0:T(8,128)S(1)} %fusion.12, f32[8,23,1792]{2,1,0:T(8,128)S(1)} %fusion.13, f32[8,24,1792]{2,1,0:T(8,128)S(1)} %fusion.18), kind=kLoop, calls=%fused_computation.47 | loop fusion | flops 1376256 | bytes 5446912 | tf_op jit(solution)/shard_map/sub | solution.py:84
  10.9 0.2 fusion.11
  11.1 0.4 %fusion.10 = f32[8,24,1791]{2,1,0:T(8,128)S(1)} fusion(f32[8,24,1792]{2,1,0:T(8,128)S(1)} %pad_subtract_fusion.4, f32[24,1791]{1,0:T(8,128)S(1)} %bitcast.28), kind=kLoop, calls=%fused_computation.27 | loop fusion | flops 687744 | bytes 4298400 | tf_op jit(solution)/shard_map/mul | solution.py:75
  11.5 0.5 %pad_subtract_fusion.3 = f32[8,24,1792]{2,1,0:T(8,128)S(1)} fusion(f32[8,24,1791]{2,1,0:T(8,128)S(1)} %fusion.10, f32[8,23,1792]{2,1,0:T(8,128)S(1)} %fusion.11, f32[8,24,1792]{2,1,0:T(8,128)S(1)} %pad_subtract_fusion.4), kind=kLoop, calls=%fused_computation.46 | loop fusion | flops 1376256 | bytes 5446912 | tf_op jit(solution)/shard_map/sub | solution.py:84
  12.0 0.2 fusion.9
  12.2 0.4 %fusion.8 = f32[8,24,1791]{2,1,0:T(8,128)S(1)} fusion(f32[8,24,1792]{2,1,0:T(8,128)S(1)} %pad_subtract_fusion.3, f32[24,1791]{1,0:T(8,128)S(1)} %bitcast.29), kind=kLoop, calls=%fused_computation.23 | loop fusion | flops 687744 | bytes 4298400 | tf_op jit(solution)/shard_map/mul | solution.py:75
  12.6 0.5 %pad_subtract_fusion.7 = f32[8,16,1792]{2,1,0:T(8,128)S(1)} fusion(f32[8,24,1791]{2,1,0:T(8,128)S(1)} %fusion.8, f32[8,23,1792]{2,1,0:T(8,128)S(1)} %fusion.9, f32[8,24,1792]{2,1,0:T(8,128)S(1)} %pad_subtract_fusion.3), kind=kLoop, calls=%fused_computation.76 | loop fusion | flops 917504 | bytes 4529408 | tf_op jit(solution)/shard_map/sub | solution.py:84
  13.2 0.1 collective-permute-done.1
  13.3 1.4 %copy_select_fusion.1 = (f32[10,4,1792]{2,1,0:T(4,128)S(1)}, f32[10,4,1792]{2,1,0:T(4,128)S(1)}) fusion(f32[10,4,1792]{2,0,1:T(8,128)} %collective-permute-done.1, pred[]{:T(512)S(6)} %eq.7, f32[10,4,1792]{2,0,1:T(8,128)S(1)} %collective-permute-done), kind=kLoop, calls=%fused_computation.119 | loop fusion | flops 143360 | bytes 1146881 | tf_op jit(solution)/shard_map/jit(_where)/select_n | solution.py:50
  14.7 0.2 pad_maximum_fusion.2
  15.1 0.1 fusion.20
  15.3 0.1 fusion.28
  15.5 0.3 fusion.27
  15.8 0.5 %fusion.31 = f32[8,12,1792]{2,1,0:T(8,128)S(1)} fusion(f32[10,12,1792]{2,1,0:T(8,128)S(1)} %fusion.20, f32[8,12,1791]{2,1,0:T(8,128)S(1)} %fusion.27, f32[8,11,1792]{2,1,0:T(8,128)S(1)} %fusion.28), kind=kLoop, calls=%fused_computation.75 | loop fusion | flops 688128 | bytes 2694784 | tf_op jit(solution)/shard_map/sub | solution.py:84
  16.2 0.1 fusion.26
  16.4 0.3 fusion.25
  16.7 0.5 %pad_subtract_fusion.10 = f32[8,12,1792]{2,1,0:T(8,128)S(1)} fusion(f32[8,12,1791]{2,1,0:T(8,128)S(1)} %fusion.25, f32[8,11,1792]{2,1,0:T(8,128)S(1)} %fusion.26, f32[8,12,1792]{2,1,0:T(8,128)S(1)} %fusion.31), kind=kLoop, calls=%fused_computation.85 | loop fusion | flops 688128 | bytes 2694784 | tf_op jit(solution)/shard_map/sub | solution.py:84
  17.1 0.1 fusion.24
  17.3 0.3 fusion.23
  17.6 0.5 %pad_subtract_fusion.9 = f32[8,12,1792]{2,1,0:T(8,128)S(1)} fusion(f32[8,12,1791]{2,1,0:T(8,128)S(1)} %fusion.23, f32[8,11,1792]{2,1,0:T(8,128)S(1)} %fusion.24, f32[8,12,1792]{2,1,0:T(8,128)S(1)} %pad_subtract_fusion.10), kind=kLoop, calls=%fused_computation.84 | loop fusion | flops 688128 | bytes 2694784 | tf_op jit(solution)/shard_map/sub | solution.py:84
  18.0 0.1 fusion.22
  18.2 0.3 fusion.21
  18.5 0.1 fusion.42
  18.6 0.3 pad_subtract_fusion.15
  18.9 0.3 fusion.33
  19.2 1.8 %collective-permute-start.2 = (f32[16,1792]{1,0:T(8,128)S(1)}, f32[16,1792]{1,0:T(8,128)S(1)}, u32[]{:S(2)}, u32[]{:S(2)}) collective-permute-start(f32[16,1792]{1,0:T(8,128)S(1)} %fusion.33), channel_id=1, source_target_pairs={{0,8},{8,0},{16,24},{24,16},{1,9},{9,1},{17,25},{25,17},{2,10},{10... | collective-permute-start | bytes 344072 | tf_op jit(solution)/shard_map/ppermute | solution.py:59
  21.0 1.2 %collective-permute-start.3 = (f32[16,1792]{1,0:T(8,128)S(1)}, f32[16,1792]{1,0:T(8,128)S(1)}, u32[]{:S(2)}, u32[]{:S(2)}) collective-permute-start(f32[16,1792]{1,0:T(8,128)S(1)} %fusion.33), channel_id=1, source_target_pairs={{0,16},{8,24},{16,0},{24,8},{1,17},{9,25},{17,1},{25,9},{2,18},{10... | collective-permute-start | bytes 344072 | tf_op jit(solution)/shard_map/ppermute | solution.py:59
  22.4 1.3 %collective-permute-done.2 = f32[16,1792]{1,0:T(8,128)S(1)} collective-permute-done((f32[16,1792]{1,0:T(8,128)S(1)}, f32[16,1792]{1,0:T(8,128)S(1)}, u32[]{:S(2)}, u32[]{:S(2)}) %collective-permute-start.2) | collective-permute-done | bytes 114720 | tf_op jit(solution)/shard_map/ppermute | solution.py:59
  23.7 3.5 %collective-permute-done.3 = f32[16,1792]{1,0:T(8,128)S(1)} collective-permute-done((f32[16,1792]{1,0:T(8,128)S(1)}, f32[16,1792]{1,0:T(8,128)S(1)}, u32[]{:S(2)}, u32[]{:S(2)}) %collective-permute-start.3) | collective-permute-done | bytes 114720 | tf_op jit(solution)/shard_map/ppermute | solution.py:59
  27.5 5.2 %collective-permute-start.6 = (f32[8,4,1792]{2,1,0:T(4,128)S(1)}, f32[8,4,1792]{2,1,0:T(4,128)S(1)}, u32[]{:S(2)}, u32[]{:S(2)}) collective-permute-start(f32[8,4,1792]{2,1,0:T(4,128)S(1)} %get-tuple-element.15), channel_id=1, source_target_pairs={{1,2},{3,4},{5,6},{2,1},{4,3},{6,5},{9,10},{11,12},{13,14},{10,9},... | collective-permute-start | bytes 688136 | tf_op jit(solution)/shard_map/ppermute | solution.py:38
  32.8 0.2 pad_maximum_fusion.3
  32.9 0.2 fusion.7
  33.1 0.4 %fusion.6 = f32[8,24,1791]{2,1,0:T(8,128)S(1)} fusion(f32[8,24,1792]{2,1,0:T(8,128)S(1)} %pad_maximum_fusion.3, f32[24,1791]{1,0:T(8,128)S(1)} %bitcast.22), kind=kLoop, calls=%fused_computation.19 | loop fusion | flops 687744 | bytes 4298400 | tf_op jit(solution)/shard_map/mul | solution.py:75
  33.6 0.6 %pad_subtract_fusion.2 = f32[8,24,1792]{2,1,0:T(8,128)S(1)} fusion(f32[8,24,1791]{2,1,0:T(8,128)S(1)} %fusion.6, f32[8,23,1792]{2,1,0:T(8,128)S(1)} %fusion.7, f32[8,4,1792]{2,1,0:T(4,128)S(1)} %get-tuple-element.26, f32[8,16,1792]{2,1,0:T(8,128)S(1)} %broadcast_multiply_fusion, f32[8,4,1792]{2,1,0:T(4,128)S(1)} %get-tuple-element.25), kind=kLoop, calls=%fused_computation.45 | loop fusion | flops 2064384 | bytes 5446912 | tf_op jit(solution)/shard_map/sub | solution.py:84
  34.1 0.2 fusion.5
  34.3 0.4 %fusion.4 = f32[8,24,1791]{2,1,0:T(8,128)S(1)} fusion(f32[8,24,1792]{2,1,0:T(8,128)S(1)} %pad_subtract_fusion.2, f32[24,1791]{1,0:T(8,128)S(1)} %bitcast.23), kind=kLoop, calls=%fused_computation.15 | loop fusion | flops 687744 | bytes 4298400 | tf_op jit(solution)/shard_map/mul | solution.py:75
  34.8 0.5 %pad_subtract_fusion.1 = f32[8,24,1792]{2,1,0:T(8,128)S(1)} fusion(f32[8,24,1791]{2,1,0:T(8,128)S(1)} %fusion.4, f32[8,23,1792]{2,1,0:T(8,128)S(1)} %fusion.5, f32[8,24,1792]{2,1,0:T(8,128)S(1)} %pad_subtract_fusion.2), kind=kLoop, calls=%fused_computation.44 | loop fusion | flops 1376256 | bytes 5446912 | tf_op jit(solution)/shard_map/sub | solution.py:84
  35.2 0.2 fusion.3
  35.4 0.4 %fusion.2 = f32[8,24,1791]{2,1,0:T(8,128)S(1)} fusion(f32[8,24,1792]{2,1,0:T(8,128)S(1)} %pad_subtract_fusion.1, f32[24,1791]{1,0:T(8,128)S(1)} %bitcast.24), kind=kLoop, calls=%fused_computation.11 | loop fusion | flops 687744 | bytes 4298400 | tf_op jit(solution)/shard_map/mul | solution.py:75
  35.9 0.5 %pad_subtract_fusion = f32[8,24,1792]{2,1,0:T(8,128)S(1)} fusion(f32[8,24,1791]{2,1,0:T(8,128)S(1)} %fusion.2, f32[8,23,1792]{2,1,0:T(8,128)S(1)} %fusion.3, f32[8,24,1792]{2,1,0:T(8,128)S(1)} %pad_subtract_fusion.1), kind=kLoop, calls=%fused_computation.43 | loop fusion | flops 1376256 | bytes 5446912 | tf_op jit(solution)/shard_map/sub | solution.py:84
  36.3 0.2 fusion.1
  36.5 0.4 %fusion = f32[8,24,1791]{2,1,0:T(8,128)S(1)} fusion(f32[8,24,1792]{2,1,0:T(8,128)S(1)} %pad_subtract_fusion, f32[24,1791]{1,0:T(8,128)S(1)} %bitcast.25), kind=kLoop, calls=%fused_computation.7 | loop fusion | flops 687744 | bytes 4298400 | tf_op jit(solution)/shard_map/mul | solution.py:75
  37.0 0.5 %pad_subtract_fusion.5 = f32[8,16,1792]{2,1,0:T(8,128)S(1)} fusion(f32[8,24,1791]{2,1,0:T(8,128)S(1)} %fusion, f32[8,23,1792]{2,1,0:T(8,128)S(1)} %fusion.1, f32[8,24,1792]{2,1,0:T(8,128)S(1)} %pad_subtract_fusion), kind=kLoop, calls=%fused_computation.52 | loop fusion | flops 917504 | bytes 4529408 | tf_op jit(solution)/shard_map/sub | solution.py:84
  37.7 0.2 fusion.40
  37.9 0.2 pad_subtract_fusion.14
  38.1 0.2 fusion.38
  38.3 0.2 pad_subtract_fusion.13
  38.6 0.2 fusion.36
  38.8 0.2 pad_subtract_fusion.12
  39.1 0.2 fusion.34
  39.3 0.2 pad_subtract_fusion.11
  39.6 1.1 %add_add_fusion = f32[8,16,1792]{2,1,0:T(8,128)} fusion(f32[8,16,1792]{2,1,0:T(8,128)S(1)} %copy-done, f32[8,16,1792]{2,1,0:T(8,128)S(1)} %pad_subtract_fusion.5, f32[8,4,1792]{2,1,0:T(4,128)S(1)} %get-tuple-element.22, f32[8,4,1792]{2,1,0:T(4,128)S(1)} %get-tuple-element.21, pred[]{:T(512)S(6)} %eq.7), kind=kLoop, calls=%fused_computation.83 | loop fusion | flops 688128 | bytes 3211265 | tf_op jit(solution)/shard_map/add | solution.py:147
  (46 shorter events, 1.5 us)
Async XLA Ops:
  1.4 5.7 %copy-start.1 = (bf16[8,4,16,1792]{3,2,1,0:T(8,128)(2,1)S(1)}, bf16[8,4,16,1792]{3,2,1,0:T(8,128)(2,1)}, u32[]{:S(2)}) copy-start(bf16[8,4,16,1792]{3,2,1,0:T(8,128)(2,1)} %param.8) | copy-start | bytes 5505028
  1.4 5.7 %copy-start.4 = (f32[4,16,1792]{2,1,0:T(8,128)S(1)}, f32[4,16,1792]{2,1,0:T(8,128)}, u32[]{:S(2)}) copy-start(f32[4,16,1792]{2,1,0:T(8,128)} %param.9) | copy-start | bytes 1376260
  2.4 5.1 %collective-permute-start = (f32[10,4,1792]{2,0,1:T(8,128)}, f32[10,4,1792]{2,0,1:T(8,128)S(1)}, u32[]{:S(2)}, u32[]{:S(2)}) collective-permute-start(f32[10,4,1792]{2,0,1:T(8,128)} %copy.11), channel_id=1, source_target_pairs={{0,1},{2,3},{4,5},{6,7},{1,0},{3,2},{5,4},{7,6},{8,9},{10,11},{12,... | collective-permute-start | bytes 860168 | tf_op jit(solution)/shard_map/ppermute | solution.py:40
  2.5 10.8 %collective-permute-start.1 = (f32[10,4,1792]{2,0,1:T(8,128)S(1)}, f32[10,4,1792]{2,0,1:T(8,128)}, u32[]{:S(2)}, u32[]{:S(2)}) collective-permute-start(f32[10,4,1792]{2,0,1:T(8,128)S(1)} %copy.14), channel_id=1, source_target_pairs={{1,2},{3,4},{5,6},{2,1},{4,3},{6,5},{9,10},{11,12},{13,14},{10,9},... | collective-permute-start | bytes 860168 | tf_op jit(solution)/shard_map/ppermute | solution.py:38
  7.1 1.2 %copy-start = (f32[8,16,1792]{2,1,0:T(8,128)S(1)}, f32[8,16,1792]{2,1,0:T(8,128)}, u32[]{:S(2)}) copy-start(f32[8,16,1792]{2,1,0:T(8,128)} %param.7) | copy-start | bytes 2752516
  7.1 1.2 %copy-start.2 = (f32[16,1792]{1,0:T(8,128)S(1)}, f32[16,1792]{1,0:T(8,128)}, u32[]{:S(2)}) copy-start(f32[16,1792]{1,0:T(8,128)} %param.13) | copy-start | bytes 344068
  7.1 1.2 %copy-start.3 = (f32[16,1792]{1,0:T(8,128)S(1)}, f32[16,1792]{1,0:T(8,128)}, u32[]{:S(2)}) copy-start(f32[16,1792]{1,0:T(8,128)} %param.12) | copy-start | bytes 344068
  18.9 8.2 %copy-start.5 = (f32[16,1792]{1,0:T(8,128)S(1)}, f32[16,1792]{1,0:T(8,128)}, u32[]{:S(2)}) copy-start(f32[16,1792]{1,0:T(8,128)} %param.10) | copy-start | bytes 344068
  18.9 8.2 %copy-start.6 = (s32[16,1792]{1,0:T(8,128)S(1)}, s32[16,1792]{1,0:T(8,128)}, u32[]{:S(2)}) copy-start(s32[16,1792]{1,0:T(8,128)} %param.11) | copy-start | bytes 344068
  19.2 4.5 %collective-permute-start.2 = (f32[16,1792]{1,0:T(8,128)S(1)}, f32[16,1792]{1,0:T(8,128)S(1)}, u32[]{:S(2)}, u32[]{:S(2)}) collective-permute-start(f32[16,1792]{1,0:T(8,128)S(1)} %fusion.33), channel_id=1, source_target_pairs={{0,8},{8,0},{16,24},{24,16},{1,9},{9,1},{17,25},{25,17},{2,10},{10... | collective-permute-start | bytes 344072 | tf_op jit(solution)/shard_map/ppermute | solution.py:59
  21.0 6.1 %collective-permute-start.3 = (f32[16,1792]{1,0:T(8,128)S(1)}, f32[16,1792]{1,0:T(8,128)S(1)}, u32[]{:S(2)}, u32[]{:S(2)}) collective-permute-start(f32[16,1792]{1,0:T(8,128)S(1)} %fusion.33), channel_id=1, source_target_pairs={{0,16},{8,24},{16,0},{24,8},{1,17},{9,25},{17,1},{25,9},{2,18},{10... | collective-permute-start | bytes 344072 | tf_op jit(solution)/shard_map/ppermute | solution.py:59
  22.3 4.9 %collective-permute-start.4 = (f32[16,1792]{1,0:T(8,128)S(1)}, f32[16,1792]{1,0:T(8,128)S(1)}, u32[]{:S(2)}, u32[]{:S(2)}) collective-permute-start(f32[16,1792]{1,0:T(8,128)S(1)} %fusion.33), channel_id=1, source_target_pairs={{0,24},{8,16},{16,8},{24,0},{1,25},{9,17},{17,9},{25,1},{2,26},{10... | collective-permute-start | bytes 344072 | tf_op jit(solution)/shard_map/ppermute | solution.py:59
  27.4 5.3 %collective-permute-start.5 = (f32[8,4,1792]{2,1,0:T(4,128)S(1)}, f32[8,4,1792]{2,1,0:T(4,128)S(1)}, u32[]{:S(2)}, u32[]{:S(2)}) collective-permute-start(f32[8,4,1792]{2,1,0:T(4,128)S(1)} %get-tuple-element.16), channel_id=1, source_target_pairs={{0,1},{2,3},{4,5},{6,7},{1,0},{3,2},{5,4},{7,6},{8,9},{10,11},{12,... | collective-permute-start | bytes 688136 | tf_op jit(solution)/shard_map/ppermute | solution.py:40
  27.5 10.1 %collective-permute-start.6 = (f32[8,4,1792]{2,1,0:T(4,128)S(1)}, f32[8,4,1792]{2,1,0:T(4,128)S(1)}, u32[]{:S(2)}, u32[]{:S(2)}) collective-permute-start(f32[8,4,1792]{2,1,0:T(4,128)S(1)} %get-tuple-element.15), channel_id=1, source_target_pairs={{1,2},{3,4},{5,6},{2,1},{4,3},{6,5},{9,10},{11,12},{13,14},{10,9},... | collective-permute-start | bytes 688136 | tf_op jit(solution)/shard_map/ppermute | solution.py:38

commit v19 on v13

--- a/solution.py
+++ b/solution.py
@@ -19,7 +19,8 @@
         (i + 1, i) for i in range(first, count - 1, 2)
     ]
     far = lax.ppermute(jnp.where(odd, tail, head), "tile", pairs(1))
-    near = lax.ppermute(jnp.where(odd, head, tail), "tile", pairs(0))
+    far, outgoing = lax.optimization_barrier((far, jnp.where(odd, head, tail)))
+    near = lax.ppermute(outgoing, "tile", pairs(0))
     above = jnp.where(odd, near, far)
     below = jnp.where(odd, far, near)
     return jnp.concatenate([above, part, below], -2)

time: 41.1 us -> 44.5 us (1.083)
  waiting for transfers between devices: 13.6 us -> 17.6 us
  starting transfers between devices: 13.1 us -> 12.5 us
    ppermute x2, waiting for transfers between devices: 0.01 us -> 2.86 us  [exchange(): near = lax.ppermute(outgoing, 'tile', pairs(0))]
    ppermute x2, waiting for transfers between devices: 9.25 us -> 9.84 us  [exchange(): far = lax.ppermute(jnp.where(odd, tail, head), 'tile', pairs(1))]
    ppermute x3, waiting for transfers between devices: 4.34 us -> 4.89 us  [partner(): return lax.ppermute(part, 'mem', [(i, i ^ stride) for i in range(count)])]
    ppermute x2, starting transfers between devices: 10.2 us -> 9.7 us  [exchange(): far = lax.ppermute(jnp.where(odd, tail, head), 'tile', pairs(1))]
  transfers between devices with their start and end apart: 7 -> 7, of which waited for: 5 -> 7; matrix products, arithmetic and copies ran while one was open for 1% -> 1% of each run, Pallas kernels for 0% -> 0%
where the time goes in v19:
time: 44.5 us; the launch traced here: 44.3 us
  waiting for transfers between devices  17.6 us (40%)
  other arithmetic  13.7 us (31%)
  starting transfers between devices  12.5 us (28%)
    ppermute x2, waiting for transfers between devices, exchange(): far = lax.ppermute(jnp.where(odd, tail, head), 'tile', pairs(1))  9.84 us
    ppermute x2, starting transfers between devices, exchange(): far = lax.ppermute(jnp.where(odd, tail, head), 'tile', pairs(1))  9.7 us
    ppermute x3, waiting for transfers between devices, partner(): return lax.ppermute(part, 'mem', [(i, i ^ stride) for i in range(count)])  4.89 us
    mul x8, other arithmetic, diffuse(): col_coef[..., :, :-1] * (values[..., :, 1:] - values[..., :, :-1])  3.39 us
    sub x6, other arithmetic, diffuse(): values + jnp.concatenate([col_flux, zeros_col], -1)  2.95 us
    ppermute x2, waiting for transfers between devices, exchange(): near = lax.ppermute(outgoing, 'tile', pairs(0))  2.86 us
    ppermute x3, starting transfers between devices, partner(): return lax.ppermute(part, 'mem', [(i, i ^ stride) for i in range(count)])  2.71 us
    mul x9, other arithmetic, diffuse(): row_coef[..., :-1, :] * (values[..., 1:, :] - values[..., :-1, :])  1.5 us
  transfers between devices with their start and end apart: 7, of which 7 were waited for; matrix products, arithmetic and copies ran while one was open for 1% of the time, Pallas kernels for 0%

profile of v19, /device:TPU:1, one launch (start us, length us, event | category | flops | bytes accessed | tf_op | source)
XLA Modules:
  0.0 44.3 jit_solution(6298089379649066112)
XLA Ops:
  0.0 1.0 %select_bitcast_fusion = f32[1,16,1792]{2,1,0:T(8,128)S(1)} fusion(f32[16,1792]{1,0:T(8,128)} %param.12, pred[16]{0:T(512)(128)(4,1)S(1)} %add_compare_fusion), kind=kLoop, calls=%fused_computation.68 | loop fusion | flops 28672 | bytes 229392 | tf_op jit(solution)/shard_map/broadcast_in_dim | solution.py:81
  1.0 1.4 %broadcast_select_fusion = (f32[10,4,1792]{2,1,0:T(4,128)S(1)}, f32[10,4,1792]{2,1,0:T(4,128)S(1)}, f32[10,4,1792]{2,1,0:T(4,128)S(1)}) fusion(pred[]{:T(512)S(6)} %eq.7, f32[1,16,1792]{2,1,0:T(8,128)} %bitcast.27, f32[1,16,1792]{2,1,0:T(8,128)S(1)} %select_bitcast_fusion, f32[8,16,1792]{2,1,0:T(8,128)} %param.7), kind=kLoop, calls=%fused_computation.65 | loop fusion | flops 358400 | bytes 2007041 | tf_op jit(solution)/shard_map/jit(_where)/select_n | solution.py:22
  2.3 0.0 copy-start.1
  2.4 0.0 copy-start.3
  2.4 0.1 copy.11
  2.5 4.7 %collective-permute-start = (f32[10,4,1792]{2,0,1:T(8,128)S(1)}, f32[10,4,1792]{2,0,1:T(8,128)S(1)}, u32[]{:S(2)}, u32[]{:S(2)}) collective-permute-start(f32[10,4,1792]{2,0,1:T(8,128)S(1)} %copy.11), channel_id=1, source_target_pairs={{1,2},{3,4},{5,6},{2,1},{4,3},{6,5},{9,10},{11,12},{13,14},{10,9},... | collective-permute-start | bytes 860168 | tf_op jit(solution)/shard_map/ppermute | solution.py:21
  7.2 6.1 %collective-permute-done = f32[10,4,1792]{2,0,1:T(8,128)S(1)} collective-permute-done((f32[10,4,1792]{2,0,1:T(8,128)S(1)}, f32[10,4,1792]{2,0,1:T(8,128)S(1)}, u32[]{:S(2)}, u32[]{:S(2)}) %collective-permute-start) | collective-permute-done | bytes 286752 | tf_op jit(solution)/shard_map/ppermute | solution.py:21
  13.4 0.1 copy.12
  13.4 0.1 collective-permute-start.1
  13.5 0.0 copy-done.1
  13.5 0.0 copy-done.3
  13.5 0.4 multiply_reduce_fusion
  13.9 0.0 copy-start
  13.9 0.0 copy-start.2
  13.9 1.4 %collective-permute-done.1 = f32[10,4,1792]{2,0,1:T(8,128)S(1)} collective-permute-done((f32[10,4,1792]{2,0,1:T(8,128)S(1)}, f32[10,4,1792]{2,0,1:T(8,128)S(1)}, u32[]{:S(2)}, u32[]{:S(2)}) %collective-permute-start.1) | collective-permute-done | bytes 286752 | tf_op jit(solution)/shard_map/ppermute | solution.py:23
  15.3 0.4 copy_select_fusion.1
  15.7 0.0 copy-done
  15.7 0.0 copy-done.2
  15.8 0.3 pad_maximum_fusion
  16.0 0.2 fusion.15
  16.2 0.4 fusion.14
  16.7 0.5 %fusion.18 = f32[8,24,1792]{2,1,0:T(8,128)S(1)} fusion(f32[10,24,1792]{2,1,0:T(8,128)S(1)} %pad_maximum_fusion, f32[8,24,1791]{2,1,0:T(8,128)S(1)} %fusion.14, f32[8,23,1792]{2,1,0:T(8,128)S(1)} %fusion.15), kind=kLoop, calls=%fused_computation.37 | loop fusion | flops 1376256 | bytes 5446912 | tf_op jit(solution)/shard_map/sub | solution.py:60
  17.2 0.2 fusion.13
  17.3 0.4 fusion.12
  17.8 0.5 %pad_subtract_fusion.4 = f32[8,24,1792]{2,1,0:T(8,128)S(1)} fusion(f32[8,24,1791]{2,1,0:T(8,128)S(1)} %fusion.12, f32[8,23,1792]{2,1,0:T(8,128)S(1)} %fusion.13, f32[8,24,1792]{2,1,0:T(8,128)S(1)} %fusion.18), kind=kLoop, calls=%fused_computation.43 | loop fusion | flops 1376256 | bytes 5446912 | tf_op jit(solution)/shard_map/sub | solution.py:60
  18.3 0.2 fusion.11
  18.4 0.4 fusion.10
  18.9 0.5 %pad_subtract_fusion.3 = f32[8,24,1792]{2,1,0:T(8,128)S(1)} fusion(f32[8,24,1791]{2,1,0:T(8,128)S(1)} %fusion.10, f32[8,23,1792]{2,1,0:T(8,128)S(1)} %fusion.11, f32[8,24,1792]{2,1,0:T(8,128)S(1)} %pad_subtract_fusion.4), kind=kLoop, calls=%fused_computation.42 | loop fusion | flops 1376256 | bytes 5446912 | tf_op jit(solution)/shard_map/sub | solution.py:60
  19.4 0.2 fusion.9
  19.6 0.4 fusion.8
  20.0 0.0 copy-start.4
  20.0 0.0 copy-start.5
  20.0 0.6 %fusion.21 = f32[16,1792]{1,0:T(8,128)S(1)} fusion(f32[8,16,1792]{2,1,0:T(8,128)S(1)} %multiply_reduce_fusion, f32[8,24,1791]{2,1,0:T(8,128)S(1)} %fusion.8, f32[8,23,1792]{2,1,0:T(8,128)S(1)} %fusion.9, f32[8,24,1792]{2,1,0:T(8,128)S(1)} %pad_subtract_fusion.3), kind=kLoop, calls=%fused_computation.51 | loop fusion | flops 1347584 | bytes 4644096 | tf_op jit(solution)/shard_map/reduce_sum | solution.py:86
  20.6 1.3 %collective-permute-start.2 = (f32[16,1792]{1,0:T(8,128)S(1)}, f32[16,1792]{1,0:T(8,128)S(1)}, u32[]{:S(2)}, u32[]{:S(2)}) collective-permute-start(f32[16,1792]{1,0:T(8,128)S(1)} %fusion.21), channel_id=1, source_target_pairs={{0,8},{8,0},{16,24},{24,16},{1,9},{9,1},{17,25},{25,17},{2,10},{10... | collective-permute-start | bytes 344072 | tf_op jit(solution)/shard_map/ppermute | solution.py:35
  21.8 1.2 %collective-permute-start.3 = (f32[16,1792]{1,0:T(8,128)S(1)}, f32[16,1792]{1,0:T(8,128)S(1)}, u32[]{:S(2)}, u32[]{:S(2)}) collective-permute-start(f32[16,1792]{1,0:T(8,128)S(1)} %fusion.21), channel_id=1, source_target_pairs={{0,16},{8,24},{16,0},{24,8},{1,17},{9,25},{17,1},{25,9},{2,18},{10... | collective-permute-start | bytes 344072 | tf_op jit(solution)/shard_map/ppermute | solution.py:35
  23.1 0.2 collective-permute-start.4
  23.3 2.0 %collective-permute-done.2 = f32[16,1792]{1,0:T(8,128)S(1)} collective-permute-done((f32[16,1792]{1,0:T(8,128)S(1)}, f32[16,1792]{1,0:T(8,128)S(1)}, u32[]{:S(2)}, u32[]{:S(2)}) %collective-permute-start.2) | collective-permute-done | bytes 114720 | tf_op jit(solution)/shard_map/ppermute | solution.py:35
  25.2 0.9 %collective-permute-done.3 = f32[16,1792]{1,0:T(8,128)S(1)} collective-permute-done((f32[16,1792]{1,0:T(8,128)S(1)}, f32[16,1792]{1,0:T(8,128)S(1)}, u32[]{:S(2)}, u32[]{:S(2)}) %collective-permute-start.3) | collective-permute-done | bytes 114720 | tf_op jit(solution)/shard_map/ppermute | solution.py:35
  26.1 2.0 %collective-permute-done.4 = f32[16,1792]{1,0:T(8,128)S(1)} collective-permute-done((f32[16,1792]{1,0:T(8,128)S(1)}, f32[16,1792]{1,0:T(8,128)S(1)}, u32[]{:S(2)}, u32[]{:S(2)}) %collective-permute-start.4) | collective-permute-done | bytes 114720 | tf_op jit(solution)/shard_map/ppermute | solution.py:35
  28.2 0.0 copy-done.4
  28.2 0.0 copy-done.5
  28.2 0.1 broadcast_multiply_fusion
  28.3 0.1 slice_select_fusion
  28.4 5.0 %collective-permute-start.5 = (f32[8,4,1792]{2,1,0:T(4,128)S(1)}, f32[8,4,1792]{2,1,0:T(4,128)S(1)}, u32[]{:S(2)}, u32[]{:S(2)}) collective-permute-start(f32[8,4,1792]{2,1,0:T(4,128)S(1)} %get-tuple-element.17), channel_id=1, source_target_pairs={{1,2},{3,4},{5,6},{2,1},{4,3},{6,5},{9,10},{11,12},{13,14},{10,9},... | collective-permute-start | bytes 688136 | tf_op jit(solution)/shard_map/ppermute | solution.py:21
  33.4 3.7 %collective-permute-done.5 = f32[8,4,1792]{2,1,0:T(4,128)S(1)} collective-permute-done((f32[8,4,1792]{2,1,0:T(4,128)S(1)}, f32[8,4,1792]{2,1,0:T(4,128)S(1)}, u32[]{:S(2)}, u32[]{:S(2)}) %collective-permute-start.5) | collective-permute-done | bytes 229408 | tf_op jit(solution)/shard_map/ppermute | solution.py:21
  37.1 0.0 collective-permute-start.6
  37.1 1.5 %collective-permute-done.6 = f32[8,4,1792]{2,1,0:T(4,128)S(1)} collective-permute-done((f32[8,4,1792]{2,1,0:T(4,128)S(1)}, f32[8,4,1792]{2,1,0:T(4,128)S(1)}, u32[]{:S(2)}, u32[]{:S(2)}) %collective-permute-start.6) | collective-permute-done | bytes 229408 | tf_op jit(solution)/shard_map/ppermute | solution.py:23
  38.6 0.2 pad_maximum_fusion.1
  38.8 0.2 fusion.7
  39.0 0.4 fusion.6
  39.4 0.6 %pad_subtract_fusion.2 = f32[8,24,1792]{2,1,0:T(8,128)S(1)} fusion(f32[8,24,1791]{2,1,0:T(8,128)S(1)} %fusion.6, f32[8,23,1792]{2,1,0:T(8,128)S(1)} %fusion.7, f32[8,4,1792]{2,1,0:T(4,128)S(1)} %bitcast.26, f32[8,16,1792]{2,1,0:T(8,128)S(1)} %broadcast_multiply_fusion, f32[8,4,1792]{2,1,0:T(4,128)S(1)} %bitcast.24), kind=kLoop, calls=%fused_computation.41 | loop fusion | flops 2064384 | bytes 5446912 | tf_op jit(solution)/shard_map/sub | solution.py:60
  40.0 0.2 fusion.5
  40.2 0.4 fusion.4
  40.6 0.5 %pad_subtract_fusion.1 = f32[8,24,1792]{2,1,0:T(8,128)S(1)} fusion(f32[8,24,1791]{2,1,0:T(8,128)S(1)} %fusion.4, f32[8,23,1792]{2,1,0:T(8,128)S(1)} %fusion.5, f32[8,24,1792]{2,1,0:T(8,128)S(1)} %pad_subtract_fusion.2), kind=kLoop, calls=%fused_computation.40 | loop fusion | flops 1376256 | bytes 5446912 | tf_op jit(solution)/shard_map/sub | solution.py:60
  41.1 0.2 fusion.3
  41.3 0.4 fusion.2
  41.7 0.5 %pad_subtract_fusion = f32[8,24,1792]{2,1,0:T(8,128)S(1)} fusion(f32[8,24,1791]{2,1,0:T(8,128)S(1)} %fusion.2, f32[8,23,1792]{2,1,0:T(8,128)S(1)} %fusion.3, f32[8,24,1792]{2,1,0:T(8,128)S(1)} %pad_subtract_fusion.1), kind=kLoop, calls=%fused_computation.39 | loop fusion | flops 1376256 | bytes 5446912 | tf_op jit(solution)/shard_map/sub | solution.py:60
  42.2 0.2 fusion.1
  42.4 0.4 fusion
  42.8 1.5 %fusion.19 = f32[8,16,1792]{2,1,0:T(8,128)} fusion(f32[8,16,1792]{2,1,0:T(8,128)S(1)} %copy-done, f32[8,24,1791]{2,1,0:T(8,128)S(1)} %fusion, f32[8,23,1792]{2,1,0:T(8,128)S(1)} %fusion.1, f32[8,24,1792]{2,1,0:T(8,128)S(1)} %pad_subtract_fusion), kind=kLoop, calls=%fused_computation.45 | loop fusion | flops 1146880 | bytes 5446912 | tf_op jit(solution)/shard_map/add | solution.py:89
  (6 shorter events, 0.2 us)
Async XLA Ops:
  2.3 11.2 %copy-start.1 = (bf16[8,4,16,1792]{3,2,1,0:T(8,128)(2,1)S(1)}, bf16[8,4,16,1792]{3,2,1,0:T(8,128)(2,1)}, u32[]{:S(2)}) copy-start(bf16[8,4,16,1792]{3,2,1,0:T(8,128)(2,1)} %param.8) | copy-start | bytes 5505028
  2.4 11.2 %copy-start.3 = (f32[4,16,1792]{2,1,0:T(8,128)S(1)}, f32[4,16,1792]{2,1,0:T(8,128)}, u32[]{:S(2)}) copy-start(f32[4,16,1792]{2,1,0:T(8,128)} %param.9) | copy-start | bytes 1376260
  2.5 10.9 %collective-permute-start = (f32[10,4,1792]{2,0,1:T(8,128)S(1)}, f32[10,4,1792]{2,0,1:T(8,128)S(1)}, u32[]{:S(2)}, u32[]{:S(2)}) collective-permute-start(f32[10,4,1792]{2,0,1:T(8,128)S(1)} %copy.11), channel_id=1, source_target_pairs={{1,2},{3,4},{5,6},{2,1},{4,3},{6,5},{9,10},{11,12},{13,14},{10,9},... | collective-permute-start | bytes 860168 | tf_op jit(solution)/shard_map/ppermute | solution.py:21
  13.4 1.9 %collective-permute-start.1 = (f32[10,4,1792]{2,0,1:T(8,128)S(1)}, f32[10,4,1792]{2,0,1:T(8,128)S(1)}, u32[]{:S(2)}, u32[]{:S(2)}) collective-permute-start(f32[10,4,1792]{2,0,1:T(8,128)S(1)} %copy.12), channel_id=1, source_target_pairs={{0,1},{2,3},{4,5},{6,7},{1,0},{3,2},{5,4},{7,6},{8,9},{10,11},{12,... | collective-permute-start | bytes 860168 | tf_op jit(solution)/shard_map/ppermute | solution.py:23
  13.9 1.8 %copy-start = (f32[8,16,1792]{2,1,0:T(8,128)S(1)}, f32[8,16,1792]{2,1,0:T(8,128)}, u32[]{:S(2)}) copy-start(f32[8,16,1792]{2,1,0:T(8,128)} %param.7) | copy-start | bytes 2752516
  13.9 1.8 %copy-start.2 = (f32[16,1792]{1,0:T(8,128)S(1)}, f32[16,1792]{1,0:T(8,128)}, u32[]{:S(2)}) copy-start(f32[16,1792]{1,0:T(8,128)} %param.13) | copy-start | bytes 344068
  20.0 8.2 %copy-start.4 = (f32[16,1792]{1,0:T(8,128)S(1)}, f32[16,1792]{1,0:T(8,128)}, u32[]{:S(2)}) copy-start(f32[16,1792]{1,0:T(8,128)} %param.10) | copy-start | bytes 344068
  20.0 8.2 %copy-start.5 = (s32[16,1792]{1,0:T(8,128)S(1)}, s32[16,1792]{1,0:T(8,128)}, u32[]{:S(2)}) copy-start(s32[16,1792]{1,0:T(8,128)} %param.11) | copy-start | bytes 344068
  20.6 4.7 %collective-permute-start.2 = (f32[16,1792]{1,0:T(8,128)S(1)}, f32[16,1792]{1,0:T(8,128)S(1)}, u32[]{:S(2)}, u32[]{:S(2)}) collective-permute-start(f32[16,1792]{1,0:T(8,128)S(1)} %fusion.21), channel_id=1, source_target_pairs={{0,8},{8,0},{16,24},{24,16},{1,9},{9,1},{17,25},{25,17},{2,10},{10... | collective-permute-start | bytes 344072 | tf_op jit(solution)/shard_map/ppermute | solution.py:35
  21.8 4.3 %collective-permute-start.3 = (f32[16,1792]{1,0:T(8,128)S(1)}, f32[16,1792]{1,0:T(8,128)S(1)}, u32[]{:S(2)}, u32[]{:S(2)}) collective-permute-start(f32[16,1792]{1,0:T(8,128)S(1)} %fusion.21), channel_id=1, source_target_pairs={{0,16},{8,24},{16,0},{24,8},{1,17},{9,25},{17,1},{25,9},{2,18},{10... | collective-permute-start | bytes 344072 | tf_op jit(solution)/shard_map/ppermute | solution.py:35
  23.1 5.1 %collective-permute-start.4 = (f32[16,1792]{1,0:T(8,128)S(1)}, f32[16,1792]{1,0:T(8,128)S(1)}, u32[]{:S(2)}, u32[]{:S(2)}) collective-permute-start(f32[16,1792]{1,0:T(8,128)S(1)} %fusion.21), channel_id=1, source_target_pairs={{0,24},{8,16},{16,8},{24,0},{1,25},{9,17},{17,9},{25,1},{2,26},{10... | collective-permute-start | bytes 344072 | tf_op jit(solution)/shard_map/ppermute | solution.py:35
  28.4 8.7 %collective-permute-start.5 = (f32[8,4,1792]{2,1,0:T(4,128)S(1)}, f32[8,4,1792]{2,1,0:T(4,128)S(1)}, u32[]{:S(2)}, u32[]{:S(2)}) collective-permute-start(f32[8,4,1792]{2,1,0:T(4,128)S(1)} %get-tuple-element.17), channel_id=1, source_target_pairs={{1,2},{3,4},{5,6},{2,1},{4,3},{6,5},{9,10},{11,12},{13,14},{10,9},... | collective-permute-start | bytes 688136 | tf_op jit(solution)/shard_map/ppermute | solution.py:21
  37.1 1.5 %collective-permute-start.6 = (f32[8,4,1792]{2,1,0:T(4,128)S(1)}, f32[8,4,1792]{2,1,0:T(4,128)S(1)}, u32[]{:S(2)}, u32[]{:S(2)}) collective-permute-start(f32[8,4,1792]{2,1,0:T(4,128)S(1)} %get-tuple-element.11), channel_id=1, source_target_pairs={{0,1},{2,3},{4,5},{6,7},{1,0},{3,2},{5,4},{7,6},{8,9},{10,11},{12,... | collective-permute-start | bytes 688136 | tf_op jit(solution)/shard_map/ppermute | solution.py:23

commit v20 on v17

--- a/solution.py
+++ b/solution.py
@@ -58,7 +58,8 @@
     stride = 1
     while stride < count:
         if stride * 2 < count:
-            near, far, both = partner(stride), partner(2 * stride), partner(3 * stride)
+            both = partner(3 * stride)
+            near, far = partner(stride), partner(2 * stride)
             part = (part + near) + (far + both)
             stride *= 4
         else:

time: 39.8 us -> 39.8 us (level)
  no operation moved by 1% of the time
where the time goes in v20:
time: 39.8 us; the launch traced here: 39.7 us
  other arithmetic  20.3 us (51%)
  starting transfers between devices  14.1 us (35%)
  waiting for transfers between devices  4.17 us (10%)
  between operations  0.56 us (1%)
  local copies, waits for them, and re-layouts  0.46 us (1%)
    ppermute x2, starting transfers between devices, split_exchange(): far = lax.ppermute(jnp.where(odd, tail, head), 'tile', pairs(1))  10.9 us
    sub x16, other arithmetic, diffuse(): values + jnp.concatenate([col_flux, zeros_col], -1)  6.55 us
    mul x16, other arithmetic, diffuse(): col_coef[..., :, :-1] * (values[..., :, 1:] - values[..., :, :-1])  5.35 us
    ppermute x3, waiting for transfers between devices, partner(): return lax.ppermute(part, 'mem', [(i, i ^ stride) for i in range(count)])  3.47 us
    ppermute x3, starting transfers between devices, partner(): return lax.ppermute(part, 'mem', [(i, i ^ stride) for i in range(count)])  3.1 us
    mul x16, other arithmetic, diffuse(): row_coef[..., :-1, :] * (values[..., 1:, :] - values[..., :-1, :])  2.24 us
    select_n x2, other arithmetic, split_exchange(): far = lax.ppermute(jnp.where(odd, tail, head), 'tile', pairs(1))  1.43 us
    add x1, other arithmetic, per_device(): return controls + (spread + edge)  1.12 us
  transfers between devices with their start and end apart: 7, of which 4 were waited for; matrix products, arithmetic and copies ran while one was open for 26% of the time, Pallas kernels for 0%

profile of v20, /device:TPU:1, one launch (start us, length us, event | category | flops | bytes accessed | tf_op | source)
XLA Modules:
  0.0 39.7 jit_solution(984363925460738809)
XLA Ops:
  0.0 1.0 %select_bitcast_fusion = f32[1,16,1792]{2,1,0:T(8,128)S(1)} fusion(f32[16,1792]{1,0:T(8,128)} %param.12, pred[16]{0:T(512)(128)(4,1)S(1)} %add_compare_fusion), kind=kLoop, calls=%fused_computation.130 | loop fusion | flops 28672 | bytes 229392 | tf_op jit(solution)/shard_map/broadcast_in_dim | solution.py:103
  1.0 1.4 %broadcast_select_fusion.2 = (f32[10,4,1792]{2,1,0:T(4,128)S(1)}, f32[10,4,1792]{2,1,0:T(4,128)S(1)}, f32[10,4,1792]{2,1,0:T(4,128)S(1)}) fusion(pred[]{:T(512)S(6)} %eq.7, f32[1,16,1792]{2,1,0:T(8,128)} %bitcast.38, f32[1,16,1792]{2,1,0:T(8,128)S(1)} %select_bitcast_fusion, f32[8,16,1792]{2,1,0:T(8,128)} %param.7), kind=kLoop, calls=%fused_computation.122 | loop fusion | flops 358400 | bytes 2007041 | tf_op jit(solution)/shard_map/jit(_where)/select_n | solution.py:36
  2.7 4.7 %collective-permute-start.1 = (f32[10,4,1792]{2,0,1:T(8,128)S(1)}, f32[10,4,1792]{2,0,1:T(8,128)S(1)}, u32[]{:S(2)}, u32[]{:S(2)}) collective-permute-start(f32[10,4,1792]{2,0,1:T(8,128)S(1)} %copy.14), channel_id=1, source_target_pairs={{1,2},{3,4},{5,6},{2,1},{4,3},{6,5},{9,10},{11,12},{13,14},{10,9},... | collective-permute-start | bytes 860168 | tf_op jit(solution)/shard_map/ppermute | solution.py:36
  7.4 0.4 multiply_reduce_fusion
  7.8 0.2 broadcast_select_fusion.1
  8.1 0.2 pad_maximum_fusion
  8.4 0.4 %fusion.14 = f32[8,24,1791]{2,1,0:T(8,128)S(1)} fusion(f32[10,24,1792]{2,1,0:T(8,128)S(1)} %pad_maximum_fusion, f32[24,1791]{1,0:T(8,128)S(1)} %bitcast.30), kind=kLoop, calls=%fused_computation.35 | loop fusion | flops 687744 | bytes 4298400 | tf_op jit(solution)/shard_map/mul | solution.py:73
  8.8 0.2 fusion.15
  9.0 0.5 %fusion.18 = f32[8,24,1792]{2,1,0:T(8,128)S(1)} fusion(f32[10,24,1792]{2,1,0:T(8,128)S(1)} %pad_maximum_fusion, f32[8,24,1791]{2,1,0:T(8,128)S(1)} %fusion.14, f32[8,23,1792]{2,1,0:T(8,128)S(1)} %fusion.15), kind=kLoop, calls=%fused_computation.41 | loop fusion | flops 1376256 | bytes 5446912 | tf_op jit(solution)/shard_map/sub | solution.py:82
  9.5 0.4 %fusion.12 = f32[8,24,1791]{2,1,0:T(8,128)S(1)} fusion(f32[8,24,1792]{2,1,0:T(8,128)S(1)} %fusion.18, f32[24,1791]{1,0:T(8,128)S(1)} %bitcast.31), kind=kLoop, calls=%fused_computation.31 | loop fusion | flops 687744 | bytes 4298400 | tf_op jit(solution)/shard_map/mul | solution.py:73
  9.9 0.2 fusion.13
  10.1 0.5 %pad_subtract_fusion.4 = f32[8,24,1792]{2,1,0:T(8,128)S(1)} fusion(f32[8,24,1791]{2,1,0:T(8,128)S(1)} %fusion.12, f32[8,23,1792]{2,1,0:T(8,128)S(1)} %fusion.13, f32[8,24,1792]{2,1,0:T(8,128)S(1)} %fusion.18), kind=kLoop, calls=%fused_computation.47 | loop fusion | flops 1376256 | bytes 5446912 | tf_op jit(solution)/shard_map/sub | solution.py:82
  10.6 0.4 %fusion.10 = f32[8,24,1791]{2,1,0:T(8,128)S(1)} fusion(f32[8,24,1792]{2,1,0:T(8,128)S(1)} %pad_subtract_fusion.4, f32[24,1791]{1,0:T(8,128)S(1)} %bitcast.32), kind=kLoop, calls=%fused_computation.27 | loop fusion | flops 687744 | bytes 4298400 | tf_op jit(solution)/shard_map/mul | solution.py:73
  11.0 0.2 fusion.11
  11.2 0.5 %pad_subtract_fusion.3 = f32[8,24,1792]{2,1,0:T(8,128)S(1)} fusion(f32[8,24,1791]{2,1,0:T(8,128)S(1)} %fusion.10, f32[8,23,1792]{2,1,0:T(8,128)S(1)} %fusion.11, f32[8,24,1792]{2,1,0:T(8,128)S(1)} %pad_subtract_fusion.4), kind=kLoop, calls=%fused_computation.46 | loop fusion | flops 1376256 | bytes 5446912 | tf_op jit(solution)/shard_map/sub | solution.py:82
  11.7 0.4 %fusion.8 = f32[8,24,1791]{2,1,0:T(8,128)S(1)} fusion(f32[8,24,1792]{2,1,0:T(8,128)S(1)} %pad_subtract_fusion.3, f32[24,1791]{1,0:T(8,128)S(1)} %bitcast.33), kind=kLoop, calls=%fused_computation.23 | loop fusion | flops 687744 | bytes 4298400 | tf_op jit(solution)/shard_map/mul | solution.py:73
  12.1 0.2 fusion.9
  12.3 0.5 %pad_subtract_fusion.7 = f32[8,16,1792]{2,1,0:T(8,128)S(1)} fusion(f32[8,24,1791]{2,1,0:T(8,128)S(1)} %fusion.8, f32[8,23,1792]{2,1,0:T(8,128)S(1)} %fusion.9, f32[8,24,1792]{2,1,0:T(8,128)S(1)} %pad_subtract_fusion.3), kind=kLoop, calls=%fused_computation.73 | loop fusion | flops 917504 | bytes 4529408 | tf_op jit(solution)/shard_map/sub | solution.py:82
  12.9 0.7 %collective-permute-done.1 = f32[10,4,1792]{2,0,1:T(8,128)S(1)} collective-permute-done((f32[10,4,1792]{2,0,1:T(8,128)S(1)}, f32[10,4,1792]{2,0,1:T(8,128)S(1)}, u32[]{:S(2)}, u32[]{:S(2)}) %collective-permute-start.1) | collective-permute-done | bytes 286752 | tf_op jit(solution)/shard_map/ppermute | solution.py:36
  13.5 0.4 copy_select_fusion.1
  13.9 0.2 pad_maximum_fusion.2
  14.3 0.3 fusion.25
  14.6 0.1 fusion.26
  14.8 0.5 %fusion.29 = f32[8,12,1792]{2,1,0:T(8,128)S(1)} fusion(f32[10,12,1792]{2,1,0:T(8,128)S(1)} %slice_select_fusion, f32[8,12,1791]{2,1,0:T(8,128)S(1)} %fusion.25, f32[8,11,1792]{2,1,0:T(8,128)S(1)} %fusion.26), kind=kLoop, calls=%fused_computation.72 | loop fusion | flops 688128 | bytes 2694784 | tf_op jit(solution)/shard_map/sub | solution.py:82
  15.2 0.3 fusion.23
  15.5 0.1 fusion.24
  15.7 0.5 %pad_subtract_fusion.10 = f32[8,12,1792]{2,1,0:T(8,128)S(1)} fusion(f32[8,12,1791]{2,1,0:T(8,128)S(1)} %fusion.23, f32[8,11,1792]{2,1,0:T(8,128)S(1)} %fusion.24, f32[8,12,1792]{2,1,0:T(8,128)S(1)} %fusion.29), kind=kLoop, calls=%fused_computation.82 | loop fusion | flops 688128 | bytes 2694784 | tf_op jit(solution)/shard_map/sub | solution.py:82
  16.1 0.3 fusion.21
  16.4 0.1 fusion.22
  16.6 0.5 %pad_subtract_fusion.9 = f32[8,12,1792]{2,1,0:T(8,128)S(1)} fusion(f32[8,12,1791]{2,1,0:T(8,128)S(1)} %fusion.21, f32[8,11,1792]{2,1,0:T(8,128)S(1)} %fusion.22, f32[8,12,1792]{2,1,0:T(8,128)S(1)} %pad_subtract_fusion.10), kind=kLoop, calls=%fused_computation.81 | loop fusion | flops 688128 | bytes 2694784 | tf_op jit(solution)/shard_map/sub | solution.py:82
  17.0 0.3 fusion.19
  17.3 0.1 fusion.20
  17.5 0.1 fusion.40
  17.6 0.3 pad_subtract_fusion.15
  17.9 0.3 fusion.31
  18.2 1.8 %collective-permute-start.3 = (f32[16,1792]{1,0:T(8,128)S(1)}, f32[16,1792]{1,0:T(8,128)S(1)}, u32[]{:S(2)}, u32[]{:S(2)}) collective-permute-start(f32[16,1792]{1,0:T(8,128)S(1)} %fusion.31), channel_id=1, source_target_pairs={{0,16},{8,24},{16,0},{24,8},{1,17},{9,25},{17,1},{25,9},{2,18},{10... | collective-permute-start | bytes 344072 | tf_op jit(solution)/shard_map/ppermute | solution.py:56
  20.0 1.2 %collective-permute-start.4 = (f32[16,1792]{1,0:T(8,128)S(1)}, f32[16,1792]{1,0:T(8,128)S(1)}, u32[]{:S(2)}, u32[]{:S(2)}) collective-permute-start(f32[16,1792]{1,0:T(8,128)S(1)} %fusion.31), channel_id=1, source_target_pairs={{0,24},{8,16},{16,8},{24,0},{1,25},{9,17},{17,9},{25,1},{2,26},{10... | collective-permute-start | bytes 344072 | tf_op jit(solution)/shard_map/ppermute | solution.py:56
  21.3 0.2 pad_maximum_fusion.3
  21.7 1.8 %collective-permute-done.3 = f32[16,1792]{1,0:T(8,128)S(1)} collective-permute-done((f32[16,1792]{1,0:T(8,128)S(1)}, f32[16,1792]{1,0:T(8,128)S(1)}, u32[]{:S(2)}, u32[]{:S(2)}) %collective-permute-start.3) | collective-permute-done | bytes 114720 | tf_op jit(solution)/shard_map/ppermute | solution.py:56
  23.4 1.4 %collective-permute-done.4 = f32[16,1792]{1,0:T(8,128)S(1)} collective-permute-done((f32[16,1792]{1,0:T(8,128)S(1)}, f32[16,1792]{1,0:T(8,128)S(1)}, u32[]{:S(2)}, u32[]{:S(2)}) %collective-permute-start.4) | collective-permute-done | bytes 114720 | tf_op jit(solution)/shard_map/ppermute | solution.py:56
  24.9 0.3 collective-permute-done.2
  25.4 6.2 %collective-permute-start.6 = (f32[8,4,1792]{2,1,0:T(4,128)S(1)}, f32[8,4,1792]{2,1,0:T(4,128)S(1)}, u32[]{:S(2)}, u32[]{:S(2)}) collective-permute-start(f32[8,4,1792]{2,1,0:T(4,128)S(1)} %get-tuple-element.18), channel_id=1, source_target_pairs={{1,2},{3,4},{5,6},{2,1},{4,3},{6,5},{9,10},{11,12},{13,14},{10,9},... | collective-permute-start | bytes 688136 | tf_op jit(solution)/shard_map/ppermute | solution.py:36
  31.7 0.2 pad_maximum_fusion.4
  31.9 0.4 %fusion.6 = f32[8,24,1791]{2,1,0:T(8,128)S(1)} fusion(f32[8,24,1792]{2,1,0:T(8,128)S(1)} %pad_maximum_fusion.4, f32[24,1791]{1,0:T(8,128)S(1)} %bitcast.26), kind=kLoop, calls=%fused_computation.19 | loop fusion | flops 687744 | bytes 4298400 | tf_op jit(solution)/shard_map/mul | solution.py:73
  32.3 0.2 fusion.7
  32.5 0.6 %pad_subtract_fusion.2 = f32[8,24,1792]{2,1,0:T(8,128)S(1)} fusion(f32[8,24,1791]{2,1,0:T(8,128)S(1)} %fusion.6, f32[8,23,1792]{2,1,0:T(8,128)S(1)} %fusion.7, f32[8,4,1792]{2,1,0:T(4,128)S(1)} %get-tuple-element.29, f32[8,16,1792]{2,1,0:T(8,128)S(1)} %broadcast_multiply_fusion, f32[8,4,1792]{2,1,0:T(4,128)S(1)} %get-tuple-element.28), kind=kLoop, calls=%fused_computation.45 | loop fusion | flops 2064384 | bytes 5446912 | tf_op jit(solution)/shard_map/sub | solution.py:82
  33.1 0.4 %fusion.4 = f32[8,24,1791]{2,1,0:T(8,128)S(1)} fusion(f32[8,24,1792]{2,1,0:T(8,128)S(1)} %pad_subtract_fusion.2, f32[24,1791]{1,0:T(8,128)S(1)} %bitcast.27), kind=kLoop, calls=%fused_computation.15 | loop fusion | flops 687744 | bytes 4298400 | tf_op jit(solution)/shard_map/mul | solution.py:73
  33.5 0.2 fusion.5
  33.7 0.5 %pad_subtract_fusion.1 = f32[8,24,1792]{2,1,0:T(8,128)S(1)} fusion(f32[8,24,1791]{2,1,0:T(8,128)S(1)} %fusion.4, f32[8,23,1792]{2,1,0:T(8,128)S(1)} %fusion.5, f32[8,24,1792]{2,1,0:T(8,128)S(1)} %pad_subtract_fusion.2), kind=kLoop, calls=%fused_computation.44 | loop fusion | flops 1376256 | bytes 5446912 | tf_op jit(solution)/shard_map/sub | solution.py:82
  34.2 0.4 %fusion.2 = f32[8,24,1791]{2,1,0:T(8,128)S(1)} fusion(f32[8,24,1792]{2,1,0:T(8,128)S(1)} %pad_subtract_fusion.1, f32[24,1791]{1,0:T(8,128)S(1)} %bitcast.28), kind=kLoop, calls=%fused_computation.11 | loop fusion | flops 687744 | bytes 4298400 | tf_op jit(solution)/shard_map/mul | solution.py:73
  34.6 0.2 fusion.3
  34.8 0.5 %pad_subtract_fusion = f32[8,24,1792]{2,1,0:T(8,128)S(1)} fusion(f32[8,24,1791]{2,1,0:T(8,128)S(1)} %fusion.2, f32[8,23,1792]{2,1,0:T(8,128)S(1)} %fusion.3, f32[8,24,1792]{2,1,0:T(8,128)S(1)} %pad_subtract_fusion.1), kind=kLoop, calls=%fused_computation.43 | loop fusion | flops 1376256 | bytes 5446912 | tf_op jit(solution)/shard_map/sub | solution.py:82
  35.3 0.4 %fusion = f32[8,24,1791]{2,1,0:T(8,128)S(1)} fusion(f32[8,24,1792]{2,1,0:T(8,128)S(1)} %pad_subtract_fusion, f32[24,1791]{1,0:T(8,128)S(1)} %bitcast.29), kind=kLoop, calls=%fused_computation.7 | loop fusion | flops 687744 | bytes 4298400 | tf_op jit(solution)/shard_map/mul | solution.py:73
  35.7 0.2 fusion.1
  35.9 0.5 %pad_subtract_fusion.5 = f32[8,16,1792]{2,1,0:T(8,128)S(1)} fusion(f32[8,24,1791]{2,1,0:T(8,128)S(1)} %fusion, f32[8,23,1792]{2,1,0:T(8,128)S(1)} %fusion.1, f32[8,24,1792]{2,1,0:T(8,128)S(1)} %pad_subtract_fusion), kind=kLoop, calls=%fused_computation.49 | loop fusion | flops 917504 | bytes 4529408 | tf_op jit(solution)/shard_map/sub | solution.py:82
  36.5 0.2 fusion.38
  36.8 0.2 pad_subtract_fusion.14
  37.0 0.2 fusion.36
  37.3 0.2 pad_subtract_fusion.13
  37.5 0.2 fusion.34
  37.8 0.2 pad_subtract_fusion.12
  38.0 0.2 fusion.32
  38.2 0.2 pad_subtract_fusion.11
  38.6 1.1 %add_add_fusion = f32[8,16,1792]{2,1,0:T(8,128)} fusion(f32[8,16,1792]{2,1,0:T(8,128)S(1)} %copy-done, f32[8,16,1792]{2,1,0:T(8,128)S(1)} %pad_subtract_fusion.5, f32[8,4,1792]{2,1,0:T(4,128)S(1)} %get-tuple-element.25, f32[8,4,1792]{2,1,0:T(4,128)S(1)} %get-tuple-element.24, pred[]{:T(512)S(6)} %eq.7), kind=kLoop, calls=%fused_computation.80 | loop fusion | flops 688128 | bytes 3211265 | tf_op jit(solution)/shard_map/add | solution.py:141
  (42 shorter events, 1.4 us)
Async XLA Ops:
  2.3 5.1 %copy-start.2 = (bf16[8,4,16,1792]{3,2,1,0:T(8,128)(2,1)S(1)}, bf16[8,4,16,1792]{3,2,1,0:T(8,128)(2,1)}, u32[]{:S(2)}) copy-start(bf16[8,4,16,1792]{3,2,1,0:T(8,128)(2,1)} %param.8) | copy-start | bytes 5505028
  2.4 5.1 %copy-start.3 = (f32[4,16,1792]{2,1,0:T(8,128)S(1)}, f32[4,16,1792]{2,1,0:T(8,128)}, u32[]{:S(2)}) copy-start(f32[4,16,1792]{2,1,0:T(8,128)} %param.9) | copy-start | bytes 1376260
  2.5 5.3 %collective-permute-start = (f32[10,4,1792]{2,0,1:T(8,128)S(1)}, f32[10,4,1792]{2,0,1:T(8,128)S(1)}, u32[]{:S(2)}, u32[]{:S(2)}) collective-permute-start(f32[10,4,1792]{2,0,1:T(8,128)S(1)} %copy.11), channel_id=1, source_target_pairs={{0,1},{2,3},{4,5},{6,7},{1,0},{3,2},{5,4},{7,6},{8,9},{10,11},{12,... | collective-permute-start | bytes 860168 | tf_op jit(solution)/shard_map/ppermute | solution.py:37
  2.7 5.4 %copy-start = (f32[8,16,1792]{2,1,0:T(8,128)S(1)}, f32[8,16,1792]{2,1,0:T(8,128)}, u32[]{:S(2)}) copy-start(f32[8,16,1792]{2,1,0:T(8,128)} %param.7) | copy-start | bytes 2752516
  2.7 5.4 %copy-start.1 = (f32[16,1792]{1,0:T(8,128)S(1)}, f32[16,1792]{1,0:T(8,128)}, u32[]{:S(2)}) copy-start(f32[16,1792]{1,0:T(8,128)} %param.13) | copy-start | bytes 344068
  2.7 10.8 %collective-permute-start.1 = (f32[10,4,1792]{2,0,1:T(8,128)S(1)}, f32[10,4,1792]{2,0,1:T(8,128)S(1)}, u32[]{:S(2)}, u32[]{:S(2)}) collective-permute-start(f32[10,4,1792]{2,0,1:T(8,128)S(1)} %copy.14), channel_id=1, source_target_pairs={{1,2},{3,4},{5,6},{2,1},{4,3},{6,5},{9,10},{11,12},{13,14},{10,9},... | collective-permute-start | bytes 860168 | tf_op jit(solution)/shard_map/ppermute | solution.py:36
  18.2 5.3 %collective-permute-start.3 = (f32[16,1792]{1,0:T(8,128)S(1)}, f32[16,1792]{1,0:T(8,128)S(1)}, u32[]{:S(2)}, u32[]{:S(2)}) collective-permute-start(f32[16,1792]{1,0:T(8,128)S(1)} %fusion.31), channel_id=1, source_target_pairs={{0,16},{8,24},{16,0},{24,8},{1,17},{9,25},{17,1},{25,9},{2,18},{10... | collective-permute-start | bytes 344072 | tf_op jit(solution)/shard_map/ppermute | solution.py:56
  20.0 4.8 %collective-permute-start.4 = (f32[16,1792]{1,0:T(8,128)S(1)}, f32[16,1792]{1,0:T(8,128)S(1)}, u32[]{:S(2)}, u32[]{:S(2)}) collective-permute-start(f32[16,1792]{1,0:T(8,128)S(1)} %fusion.31), channel_id=1, source_target_pairs={{0,24},{8,16},{16,8},{24,0},{1,25},{9,17},{17,9},{25,1},{2,26},{10... | collective-permute-start | bytes 344072 | tf_op jit(solution)/shard_map/ppermute | solution.py:56
  21.2 4.0 %collective-permute-start.2 = (f32[16,1792]{1,0:T(8,128)S(1)}, f32[16,1792]{1,0:T(8,128)S(1)}, u32[]{:S(2)}, u32[]{:S(2)}) collective-permute-start(f32[16,1792]{1,0:T(8,128)S(1)} %fusion.31), channel_id=1, source_target_pairs={{0,8},{8,0},{16,24},{24,16},{1,9},{9,1},{17,25},{25,17},{2,10},{10... | collective-permute-start | bytes 344072 | tf_op jit(solution)/shard_map/ppermute | solution.py:56
  21.5 3.6 %copy-start.4 = (f32[16,1792]{1,0:T(8,128)S(1)}, f32[16,1792]{1,0:T(8,128)}, u32[]{:S(2)}) copy-start(f32[16,1792]{1,0:T(8,128)} %param.10) | copy-start | bytes 344068
  21.5 3.6 %copy-start.5 = (s32[16,1792]{1,0:T(8,128)S(1)}, s32[16,1792]{1,0:T(8,128)}, u32[]{:S(2)}) copy-start(s32[16,1792]{1,0:T(8,128)} %param.11) | copy-start | bytes 344068
  25.3 6.3 %collective-permute-start.5 = (f32[8,4,1792]{2,1,0:T(4,128)S(1)}, f32[8,4,1792]{2,1,0:T(4,128)S(1)}, u32[]{:S(2)}, u32[]{:S(2)}) collective-permute-start(f32[8,4,1792]{2,1,0:T(4,128)S(1)} %get-tuple-element.19), channel_id=1, source_target_pairs={{0,1},{2,3},{4,5},{6,7},{1,0},{3,2},{5,4},{7,6},{8,9},{10,11},{12,... | collective-permute-start | bytes 688136 | tf_op jit(solution)/shard_map/ppermute | solution.py:37
  25.4 11.0 %collective-permute-start.6 = (f32[8,4,1792]{2,1,0:T(4,128)S(1)}, f32[8,4,1792]{2,1,0:T(4,128)S(1)}, u32[]{:S(2)}, u32[]{:S(2)}) collective-permute-start(f32[8,4,1792]{2,1,0:T(4,128)S(1)} %get-tuple-element.18), channel_id=1, source_target_pairs={{1,2},{3,4},{5,6},{2,1},{4,3},{6,5},{9,10},{11,12},{13,14},{10,9},... | collective-permute-start | bytes 688136 | tf_op jit(solution)/shard_map/ppermute | solution.py:36

commit v21 on v17

--- a/solution.py
+++ b/solution.py
@@ -125,19 +125,16 @@
     weighted = radar_mask.astype(jnp.float32) * obs_weight * reflect
     near, far, odd = split_exchange(mix * weighted[None], STEPS)
     spread = localize(near_band(mix * weighted[None], near, odd), coef_band)
-    spread = spread[:, STEPS : STEPS + row_count]
-    spread, far = lax.optimization_barrier((spread, far))
+    base = controls + spread[:, STEPS : STEPS + row_count]
+    base, far = lax.optimization_barrier((base, far))
     zero = jnp.zeros_like(far)
     strip = jnp.where(odd, jnp.concatenate([zero, far], 1), jnp.concatenate([far, zero], 1))
     strip_coef = jnp.where(odd, coef_band[:, row_count:], coef_band[:, : 2 * STEPS])
     edge = localize(strip, strip_coef)
-    rest = jnp.zeros_like(spread[:, STEPS:])
-    edge = jnp.where(
-        odd,
-        jnp.concatenate([rest, edge[:, :STEPS]], 1),
-        jnp.concatenate([edge[:, STEPS:], rest], 1),
-    )
-    return controls + (spread + edge)
+    edge = jnp.where(odd, edge[:, :STEPS], edge[:, STEPS:])
+    first = jnp.where(odd, row_count - STEPS, 0)
+    current = lax.dynamic_slice_in_dim(base, first, STEPS, axis=1)
+    return lax.dynamic_update_slice_in_dim(base, current + edge, first, axis=1)
 
 
 def solution(mesh):

time: 39.8 us -> 43.1 us (1.083)
  other arithmetic: 20.3 us -> 22.9 us
  local copies, waits for them, and re-layouts: 0.46 us -> 1.67 us
  starting transfers between devices: 14.1 us -> 13.3 us
    dynamic_update_slice x0 -> x1, other arithmetic: none -> 1.81 us  [per_device(): return lax.dynamic_update_slice_in_dim(base, current + edge, first, axis=1)]
    select_n x1, other arithmetic: 0.37 us -> 1.39 us  [full_band(): jnp.where(odd, far, near)]
    ppermute x2, starting transfers between devices: 10.9 us -> 10 us  [split_exchange(): far = lax.ppermute(jnp.where(odd, tail, head), 'tile', pairs(1))]
    select_n x1, local copies, waits for them, and re-layouts: 0.07 us -> 0.83 us  [split_exchange(): near = lax.ppermute(jnp.where(odd, head, tail), 'tile', pairs(0))]
    ppermute x3, waiting for transfers between devices: 3.47 us -> 4.13 us  [partner(): return lax.ppermute(part, 'mem', [(i, i ^ stride) for i in range(count)])]
    sub x16 -> x15, other arithmetic: 6.55 us -> 5.98 us  [diffuse(): values + jnp.concatenate([col_flux, zeros_col], -1)]
    unnamed x12, local copies, waits for them, and re-layouts: 0.04 us -> 0.55 us
  transfers between devices with their start and end apart: 7 -> 7, of which waited for: 4 -> 4; matrix products, arithmetic and copies ran while one was open for 26% -> 27% of each run, Pallas kernels for 0% -> 0%
where the time goes in v21:
time: 43.1 us; the launch traced here: 42.8 us
  other arithmetic  22.9 us (53%)
  starting transfers between devices  13.3 us (31%)
  waiting for transfers between devices  4.42 us (10%)
  local copies, waits for them, and re-layouts  1.67 us (4%)
  between operations  0.53 us (1%)
    ppermute x2, starting transfers between devices, split_exchange(): far = lax.ppermute(jnp.where(odd, tail, head), 'tile', pairs(1))  10 us
    sub x15, other arithmetic, diffuse(): values + jnp.concatenate([col_flux, zeros_col], -1)  5.98 us
    mul x16, other arithmetic, diffuse(): col_coef[..., :, :-1] * (values[..., :, 1:] - values[..., :, :-1])  5.35 us
    ppermute x3, waiting for transfers between devices, partner(): return lax.ppermute(part, 'mem', [(i, i ^ stride) for i in range(count)])  4.13 us
    ppermute x3, starting transfers between devices, partner(): return lax.ppermute(part, 'mem', [(i, i ^ stride) for i in range(count)])  3.11 us
    mul x16, other arithmetic, diffuse(): row_coef[..., :-1, :] * (values[..., 1:, :] - values[..., :-1, :])  2.24 us
    dynamic_update_slice x1, other arithmetic, per_device(): return lax.dynamic_update_slice_in_dim(base, current + edge, first, axis=1)  1.81 us
    add x1, other arithmetic, per_device(): base = controls + spread[:, STEPS:STEPS + row_count]  1.46 us
  transfers between devices with their start and end apart: 7, of which 4 were waited for; matrix products, arithmetic and copies ran while one was open for 27% of the time, Pallas kernels for 0%

profile of v21, /device:TPU:1, one launch (start us, length us, event | category | flops | bytes accessed | tf_op | source)
XLA Modules:
  0.0 42.8 jit_solution(16497345837646314116)
XLA Ops:
  0.0 1.0 %select_bitcast_fusion = f32[1,16,1792]{2,1,0:T(8,128)S(1)} fusion(f32[16,1792]{1,0:T(8,128)} %param.12, pred[16]{0:T(512)(128)(4,1)S(1)} %add_compare_fusion), kind=kLoop, calls=%fused_computation.133 | loop fusion | flops 28672 | bytes 229392 | tf_op jit(solution)/shard_map/broadcast_in_dim | solution.py:102
  1.0 1.4 %broadcast_select_fusion.2 = (f32[10,4,1792]{2,1,0:T(4,128)S(1)}, f32[10,4,1792]{2,1,0:T(4,128)S(1)}, f32[10,4,1792]{2,1,0:T(4,128)S(1)}) fusion(pred[]{:T(512)S(6)} %eq.7, f32[1,16,1792]{2,1,0:T(8,128)} %bitcast.38, f32[1,16,1792]{2,1,0:T(8,128)S(1)} %select_bitcast_fusion, f32[8,16,1792]{2,1,0:T(8,128)} %param.7), kind=kLoop, calls=%fused_computation.125 | loop fusion | flops 358400 | bytes 2007041 | tf_op jit(solution)/shard_map/jit(_where)/select_n | solution.py:36
  2.4 0.8 %copy.11 = f32[10,4,1792]{2,0,1:T(8,128)} copy(f32[10,4,1792]{2,1,0:T(4,128)S(1)} %bitcast.47) | data formatting | bytes 573440 | tf_op jit(solution)/shard_map/jit(_where)/select_n | solution.py:37
  3.4 4.5 %collective-permute-start.1 = (f32[10,4,1792]{2,0,1:T(8,128)S(1)}, f32[10,4,1792]{2,0,1:T(8,128)}, u32[]{:S(2)}, u32[]{:S(2)}) collective-permute-start(f32[10,4,1792]{2,0,1:T(8,128)S(1)} %copy.14), channel_id=1, source_target_pairs={{1,2},{3,4},{5,6},{2,1},{4,3},{6,5},{9,10},{11,12},{13,14},{10,9},... | collective-permute-start | bytes 860168 | tf_op jit(solution)/shard_map/ppermute | solution.py:36
  8.0 0.4 multiply_reduce_fusion
  8.4 0.2 broadcast_select_fusion.1
  8.6 0.5 %copy-done = f32[8,16,1792]{2,1,0:T(8,128)S(1)} copy-done((f32[8,16,1792]{2,1,0:T(8,128)S(1)}, f32[8,16,1792]{2,1,0:T(8,128)}, u32[]{:S(2)}) %copy-start) | copy-done | bytes 917528
  9.1 0.2 pad_maximum_fusion
  9.4 0.4 fusion.14
  9.8 0.2 fusion.15
  10.0 0.5 %fusion.18 = f32[8,24,1792]{2,1,0:T(8,128)S(1)} fusion(f32[10,24,1792]{2,1,0:T(8,128)S(1)} %pad_maximum_fusion, f32[8,24,1791]{2,1,0:T(8,128)S(1)} %fusion.14, f32[8,23,1792]{2,1,0:T(8,128)S(1)} %fusion.15), kind=kLoop, calls=%fused_computation.41 | loop fusion | flops 1376256 | bytes 5446912 | tf_op jit(solution)/shard_map/sub | solution.py:81
  10.5 0.4 fusion.12
  11.0 0.2 fusion.13
  11.1 0.5 %pad_subtract_fusion.4 = f32[8,24,1792]{2,1,0:T(8,128)S(1)} fusion(f32[8,24,1791]{2,1,0:T(8,128)S(1)} %fusion.12, f32[8,23,1792]{2,1,0:T(8,128)S(1)} %fusion.13, f32[8,24,1792]{2,1,0:T(8,128)S(1)} %fusion.18), kind=kLoop, calls=%fused_computation.47 | loop fusion | flops 1376256 | bytes 5446912 | tf_op jit(solution)/shard_map/sub | solution.py:81
  11.6 0.4 fusion.10
  12.1 0.2 fusion.11
  12.2 0.5 %pad_subtract_fusion.3 = f32[8,24,1792]{2,1,0:T(8,128)S(1)} fusion(f32[8,24,1791]{2,1,0:T(8,128)S(1)} %fusion.10, f32[8,23,1792]{2,1,0:T(8,128)S(1)} %fusion.11, f32[8,24,1792]{2,1,0:T(8,128)S(1)} %pad_subtract_fusion.4), kind=kLoop, calls=%fused_computation.46 | loop fusion | flops 1376256 | bytes 5446912 | tf_op jit(solution)/shard_map/sub | solution.py:81
  12.7 0.4 fusion.8
  13.2 0.2 fusion.9
  13.4 0.5 %pad_subtract_fusion.7 = f32[8,16,1792]{2,1,0:T(8,128)S(1)} fusion(f32[8,24,1791]{2,1,0:T(8,128)S(1)} %fusion.8, f32[8,23,1792]{2,1,0:T(8,128)S(1)} %fusion.9, f32[8,24,1792]{2,1,0:T(8,128)S(1)} %pad_subtract_fusion.3), kind=kLoop, calls=%fused_computation.74 | loop fusion | flops 917504 | bytes 4529408 | tf_op jit(solution)/shard_map/sub | solution.py:81
  13.9 0.3 collective-permute-done.1
  14.2 1.4 %copy_select_fusion.1 = (f32[10,4,1792]{2,1,0:T(4,128)S(1)}, f32[10,4,1792]{2,1,0:T(4,128)S(1)}) fusion(f32[10,4,1792]{2,0,1:T(8,128)} %collective-permute-done.1, pred[]{:T(512)S(6)} %eq.7, f32[10,4,1792]{2,0,1:T(8,128)S(1)} %collective-permute-done), kind=kLoop, calls=%fused_computation.122 | loop fusion | flops 143360 | bytes 1146881 | tf_op jit(solution)/shard_map/jit(_where)/select_n | solution.py:47
  15.6 0.2 pad_maximum_fusion.2
  16.0 0.3 fusion.26
  16.4 0.5 %fusion.30 = f32[8,12,1792]{2,1,0:T(8,128)S(1)} fusion(f32[10,12,1792]{2,1,0:T(8,128)S(1)} %slice_select_fusion, f32[8,12,1791]{2,1,0:T(8,128)S(1)} %fusion.26, f32[8,11,1792]{2,1,0:T(8,128)S(1)} %fusion.27), kind=kLoop, calls=%fused_computation.73 | loop fusion | flops 688128 | bytes 2694784 | tf_op jit(solution)/shard_map/sub | solution.py:81
  16.9 0.3 fusion.24
  17.2 0.1 fusion.25
  17.3 0.5 %pad_subtract_fusion.10 = f32[8,12,1792]{2,1,0:T(8,128)S(1)} fusion(f32[8,12,1791]{2,1,0:T(8,128)S(1)} %fusion.24, f32[8,11,1792]{2,1,0:T(8,128)S(1)} %fusion.25, f32[8,12,1792]{2,1,0:T(8,128)S(1)} %fusion.30), kind=kLoop, calls=%fused_computation.82 | loop fusion | flops 688128 | bytes 2694784 | tf_op jit(solution)/shard_map/sub | solution.py:81
  17.8 0.3 fusion.22
  18.1 0.1 fusion.23
  18.2 0.5 %pad_subtract_fusion.9 = f32[8,12,1792]{2,1,0:T(8,128)S(1)} fusion(f32[8,12,1791]{2,1,0:T(8,128)S(1)} %fusion.22, f32[8,11,1792]{2,1,0:T(8,128)S(1)} %fusion.23, f32[8,12,1792]{2,1,0:T(8,128)S(1)} %pad_subtract_fusion.10), kind=kLoop, calls=%fused_computation.81 | loop fusion | flops 688128 | bytes 2694784 | tf_op jit(solution)/shard_map/sub | solution.py:81
  18.7 0.3 fusion.20
  19.1 0.1 fusion.43
  19.3 0.3 pad_subtract_fusion.15
  19.5 0.3 fusion.32
  19.8 1.9 %collective-permute-start.3 = (f32[16,1792]{1,0:T(8,128)S(1)}, f32[16,1792]{1,0:T(8,128)S(1)}, u32[]{:S(2)}, u32[]{:S(2)}) collective-permute-start(f32[16,1792]{1,0:T(8,128)S(1)} %fusion.32), channel_id=1, source_target_pairs={{0,16},{8,24},{16,0},{24,8},{1,17},{9,25},{17,1},{25,9},{2,18},{10... | collective-permute-start | bytes 344072 | tf_op jit(solution)/shard_map/ppermute | solution.py:56
  21.7 1.2 %collective-permute-start.4 = (f32[16,1792]{1,0:T(8,128)S(1)}, f32[16,1792]{1,0:T(8,128)S(1)}, u32[]{:S(2)}, u32[]{:S(2)}) collective-permute-start(f32[16,1792]{1,0:T(8,128)S(1)} %fusion.32), channel_id=1, source_target_pairs={{0,24},{8,16},{16,8},{24,0},{1,25},{9,17},{17,9},{25,1},{2,26},{10... | collective-permute-start | bytes 344072 | tf_op jit(solution)/shard_map/ppermute | solution.py:56
  23.0 0.2 pad_maximum_fusion.3
  23.3 2.1 %collective-permute-done.3 = f32[16,1792]{1,0:T(8,128)S(1)} collective-permute-done((f32[16,1792]{1,0:T(8,128)S(1)}, f32[16,1792]{1,0:T(8,128)S(1)}, u32[]{:S(2)}, u32[]{:S(2)}) %collective-permute-start.3) | collective-permute-done | bytes 114720 | tf_op jit(solution)/shard_map/ppermute | solution.py:56
  25.5 1.7 %collective-permute-done.4 = f32[16,1792]{1,0:T(8,128)S(1)} collective-permute-done((f32[16,1792]{1,0:T(8,128)S(1)}, f32[16,1792]{1,0:T(8,128)S(1)}, u32[]{:S(2)}, u32[]{:S(2)}) %collective-permute-start.4) | collective-permute-done | bytes 114720 | tf_op jit(solution)/shard_map/ppermute | solution.py:56
  27.2 0.3 collective-permute-done.2
  27.8 5.5 %collective-permute-start.6 = (f32[8,4,1792]{2,1,0:T(4,128)S(1)}, f32[8,4,1792]{2,1,0:T(4,128)S(1)}, u32[]{:S(2)}, u32[]{:S(2)}) collective-permute-start(f32[8,4,1792]{2,1,0:T(4,128)S(1)} %get-tuple-element.18), channel_id=1, source_target_pairs={{1,2},{3,4},{5,6},{2,1},{4,3},{6,5},{9,10},{11,12},{13,14},{10,9},... | collective-permute-start | bytes 688136 | tf_op jit(solution)/shard_map/ppermute | solution.py:36
  33.4 0.2 pad_maximum_fusion.4
  33.6 0.4 fusion.6
  34.0 0.2 fusion.7
  34.2 0.6 %pad_subtract_fusion.2 = f32[8,24,1792]{2,1,0:T(8,128)S(1)} fusion(f32[8,24,1791]{2,1,0:T(8,128)S(1)} %fusion.6, f32[8,23,1792]{2,1,0:T(8,128)S(1)} %fusion.7, f32[8,4,1792]{2,1,0:T(4,128)S(1)} %get-tuple-element.27, f32[8,16,1792]{2,1,0:T(8,128)S(1)} %broadcast_multiply_fusion, f32[8,4,1792]{2,1,0:T(4,128)S(1)} %get-tuple-element.26), kind=kLoop, calls=%fused_computation.45 | loop fusion | flops 2064384 | bytes 5446912 | tf_op jit(solution)/shard_map/sub | solution.py:81
  34.8 0.4 fusion.4
  35.2 0.2 fusion.5
  35.4 0.5 %pad_subtract_fusion.1 = f32[8,24,1792]{2,1,0:T(8,128)S(1)} fusion(f32[8,24,1791]{2,1,0:T(8,128)S(1)} %fusion.4, f32[8,23,1792]{2,1,0:T(8,128)S(1)} %fusion.5, f32[8,24,1792]{2,1,0:T(8,128)S(1)} %pad_subtract_fusion.2), kind=kLoop, calls=%fused_computation.44 | loop fusion | flops 1376256 | bytes 5446912 | tf_op jit(solution)/shard_map/sub | solution.py:81
  35.9 0.4 fusion.2
  36.3 0.2 fusion.3
  36.5 0.5 %pad_subtract_fusion = f32[8,24,1792]{2,1,0:T(8,128)S(1)} fusion(f32[8,24,1791]{2,1,0:T(8,128)S(1)} %fusion.2, f32[8,23,1792]{2,1,0:T(8,128)S(1)} %fusion.3, f32[8,24,1792]{2,1,0:T(8,128)S(1)} %pad_subtract_fusion.1), kind=kLoop, calls=%fused_computation.43 | loop fusion | flops 1376256 | bytes 5446912 | tf_op jit(solution)/shard_map/sub | solution.py:81
  37.0 0.4 fusion
  37.4 0.2 fusion.1
  37.6 1.5 %fusion.19 = f32[8,16,1792]{2,1,0:T(8,128)} fusion(f32[8,16,1792]{2,1,0:T(8,128)S(1)} %copy-done, f32[8,24,1791]{2,1,0:T(8,128)S(1)} %fusion, f32[8,23,1792]{2,1,0:T(8,128)S(1)} %fusion.1, f32[8,24,1792]{2,1,0:T(8,128)S(1)} %pad_subtract_fusion), kind=kLoop, calls=%fused_computation.50 | loop fusion | flops 1146880 | bytes 5446912 | tf_op jit(solution)/shard_map/add | solution.py:128
  39.1 0.2 fusion.39
  39.4 0.2 pad_subtract_fusion.14
  39.6 0.2 fusion.37
  39.9 0.2 pad_subtract_fusion.13
  40.1 0.2 fusion.35
  40.3 0.2 pad_subtract_fusion.12
  40.5 0.2 fusion.33
  40.8 0.2 pad_subtract_fusion.11
  41.0 1.8 %fusion.42 = f32[8,16,1792]{2,1,0:T(8,128)} fusion(f32[8,16,1792]{2,1,0:T(8,128)} %fusion.19, s32[]{:T(128)S(6)} %select_n.121, f32[8,8,1792]{2,1,0:T(8,128)S(1)} %pad_subtract_fusion.11, pred[]{:T(512)S(6)} %eq.7), kind=kLoop, calls=%fused_computation.110 | loop fusion | flops 114688 | bytes 917509 | tf_op jit(solution)/shard_map/dynamic_update_slice | solution.py:137
  (41 shorter events, 1.5 us)
Async XLA Ops:
  2.3 5.6 %copy-start.2 = (bf16[8,4,16,1792]{3,2,1,0:T(8,128)(2,1)S(1)}, bf16[8,4,16,1792]{3,2,1,0:T(8,128)(2,1)}, u32[]{:S(2)}) copy-start(bf16[8,4,16,1792]{3,2,1,0:T(8,128)(2,1)} %param.8) | copy-start | bytes 5505028
  2.4 5.6 %copy-start.3 = (f32[4,16,1792]{2,1,0:T(8,128)S(1)}, f32[4,16,1792]{2,1,0:T(8,128)}, u32[]{:S(2)}) copy-start(f32[4,16,1792]{2,1,0:T(8,128)} %param.9) | copy-start | bytes 1376260
  3.2 5.1 %collective-permute-start = (f32[10,4,1792]{2,0,1:T(8,128)}, f32[10,4,1792]{2,0,1:T(8,128)S(1)}, u32[]{:S(2)}, u32[]{:S(2)}) collective-permute-start(f32[10,4,1792]{2,0,1:T(8,128)} %copy.11), channel_id=1, source_target_pairs={{0,1},{2,3},{4,5},{6,7},{1,0},{3,2},{5,4},{7,6},{8,9},{10,11},{12,... | collective-permute-start | bytes 860168 | tf_op jit(solution)/shard_map/ppermute | solution.py:37
  3.4 10.8 %collective-permute-start.1 = (f32[10,4,1792]{2,0,1:T(8,128)S(1)}, f32[10,4,1792]{2,0,1:T(8,128)}, u32[]{:S(2)}, u32[]{:S(2)}) collective-permute-start(f32[10,4,1792]{2,0,1:T(8,128)S(1)} %copy.14), channel_id=1, source_target_pairs={{1,2},{3,4},{5,6},{2,1},{4,3},{6,5},{9,10},{11,12},{13,14},{10,9},... | collective-permute-start | bytes 860168 | tf_op jit(solution)/shard_map/ppermute | solution.py:36
  7.9 1.2 %copy-start = (f32[8,16,1792]{2,1,0:T(8,128)S(1)}, f32[8,16,1792]{2,1,0:T(8,128)}, u32[]{:S(2)}) copy-start(f32[8,16,1792]{2,1,0:T(8,128)} %param.7) | copy-start | bytes 2752516
  8.0 1.2 %copy-start.1 = (f32[16,1792]{1,0:T(8,128)S(1)}, f32[16,1792]{1,0:T(8,128)}, u32[]{:S(2)}) copy-start(f32[16,1792]{1,0:T(8,128)} %param.13) | copy-start | bytes 344068
  19.8 5.6 %collective-permute-start.3 = (f32[16,1792]{1,0:T(8,128)S(1)}, f32[16,1792]{1,0:T(8,128)S(1)}, u32[]{:S(2)}, u32[]{:S(2)}) collective-permute-start(f32[16,1792]{1,0:T(8,128)S(1)} %fusion.32), channel_id=1, source_target_pairs={{0,16},{8,24},{16,0},{24,8},{1,17},{9,25},{17,1},{25,9},{2,18},{10... | collective-permute-start | bytes 344072 | tf_op jit(solution)/shard_map/ppermute | solution.py:56
  21.7 5.5 %collective-permute-start.4 = (f32[16,1792]{1,0:T(8,128)S(1)}, f32[16,1792]{1,0:T(8,128)S(1)}, u32[]{:S(2)}, u32[]{:S(2)}) collective-permute-start(f32[16,1792]{1,0:T(8,128)S(1)} %fusion.32), channel_id=1, source_target_pairs={{0,24},{8,16},{16,8},{24,0},{1,25},{9,17},{17,9},{25,1},{2,26},{10... | collective-permute-start | bytes 344072 | tf_op jit(solution)/shard_map/ppermute | solution.py:56
  22.8 4.6 %collective-permute-start.2 = (f32[16,1792]{1,0:T(8,128)S(1)}, f32[16,1792]{1,0:T(8,128)S(1)}, u32[]{:S(2)}, u32[]{:S(2)}) collective-permute-start(f32[16,1792]{1,0:T(8,128)S(1)} %fusion.32), channel_id=1, source_target_pairs={{0,8},{8,0},{16,24},{24,16},{1,9},{9,1},{17,25},{25,17},{2,10},{10... | collective-permute-start | bytes 344072 | tf_op jit(solution)/shard_map/ppermute | solution.py:56
  23.2 4.3 %copy-start.4 = (f32[16,1792]{1,0:T(8,128)S(1)}, f32[16,1792]{1,0:T(8,128)}, u32[]{:S(2)}) copy-start(f32[16,1792]{1,0:T(8,128)} %param.10) | copy-start | bytes 344068
  23.2 4.3 %copy-start.5 = (s32[16,1792]{1,0:T(8,128)S(1)}, s32[16,1792]{1,0:T(8,128)}, u32[]{:S(2)}) copy-start(s32[16,1792]{1,0:T(8,128)} %param.11) | copy-start | bytes 344068
  27.7 5.6 %collective-permute-start.5 = (f32[8,4,1792]{2,1,0:T(4,128)S(1)}, f32[8,4,1792]{2,1,0:T(4,128)S(1)}, u32[]{:S(2)}, u32[]{:S(2)}) collective-permute-start(f32[8,4,1792]{2,1,0:T(4,128)S(1)} %get-tuple-element.19), channel_id=1, source_target_pairs={{0,1},{2,3},{4,5},{6,7},{1,0},{3,2},{5,4},{7,6},{8,9},{10,11},{12,... | collective-permute-start | bytes 688136 | tf_op jit(solution)/shard_map/ppermute | solution.py:37
  27.8 11.3 %collective-permute-start.6 = (f32[8,4,1792]{2,1,0:T(4,128)S(1)}, f32[8,4,1792]{2,1,0:T(4,128)S(1)}, u32[]{:S(2)}, u32[]{:S(2)}) collective-permute-start(f32[8,4,1792]{2,1,0:T(4,128)S(1)} %get-tuple-element.18), channel_id=1, source_target_pairs={{1,2},{3,4},{5,6},{2,1},{4,3},{6,5},{9,10},{11,12},{13,14},{10,9},... | collective-permute-start | bytes 688136 | tf_op jit(solution)/shard_map/ppermute | solution.py:36

commit v22 on v17

--- a/solution.py
+++ b/solution.py
@@ -90,6 +90,13 @@
     return field
 
 
+def localize_inner(field, coef_band):
+    for repeat in range(STEPS):
+        field = diffuse(field, coef_band[0], coef_band[1])[..., 1:-1, :]
+        coef_band = coef_band[..., 1:-1, :]
+    return field
+
+
 def per_device(controls, perturbations, jacobian, obs_weight, radar_mask, row_faces, col_faces):
     members, row_count = controls.shape[:2]
     row_index = lax.axis_index("tile") * row_count + lax.broadcasted_iota(
@@ -115,7 +122,7 @@
     band = full_band(stacked, near, far, odd)
     coef_band = band[members:]
     strip = jnp.where(odd, band[:, row_count - STEPS :], band[:, : 3 * STEPS])
-    edge = localize(strip[:members], strip[members:])[:, STEPS : 2 * STEPS]
+    edge = localize_inner(strip[:members], strip[members:])
     localized = jnp.where(
         odd,
         jnp.concatenate([main[:, : row_count - STEPS], edge], 1),

time: 39.8 us -> 39.5 us (level)
  other arithmetic: 20.3 us -> 19.8 us
  transfers between devices with their start and end apart: 7 -> 7, of which waited for: 4 -> 4; matrix products, arithmetic and copies ran while one was open for 26% -> 27% of each run, Pallas kernels for 0% -> 0%
where the time goes in v22:
time: 39.5 us; the launch traced here: 39.3 us
  other arithmetic  19.8 us (50%)
  starting transfers between devices  14.1 us (36%)
  waiting for transfers between devices  4.17 us (11%)
  between operations  0.64 us (2%)
  local copies, waits for them, and re-layouts  0.56 us (1%)
    ppermute x2, starting transfers between devices, split_exchange(): far = lax.ppermute(jnp.where(odd, tail, head), 'tile', pairs(1))  10.9 us
    sub x16, other arithmetic, diffuse(): values + jnp.concatenate([col_flux, zeros_col], -1)  6.23 us
    mul x16, other arithmetic, diffuse(): col_coef[..., :, :-1] * (values[..., :, 1:] - values[..., :, :-1])  5.12 us
    ppermute x3, waiting for transfers between devices, partner(): return lax.ppermute(part, 'mem', [(i, i ^ stride) for i in range(count)])  3.47 us
    ppermute x3, starting transfers between devices, partner(): return lax.ppermute(part, 'mem', [(i, i ^ stride) for i in range(count)])  3.1 us
    mul x16, other arithmetic, diffuse(): row_coef[..., :-1, :] * (values[..., 1:, :] - values[..., :-1, :])  2.24 us
    select_n x2, other arithmetic, split_exchange(): far = lax.ppermute(jnp.where(odd, tail, head), 'tile', pairs(1))  1.43 us
    add x1, other arithmetic, per_device(): return controls + (spread + edge)  1.12 us
  transfers between devices with their start and end apart: 7, of which 4 were waited for; matrix products, arithmetic and copies ran while one was open for 27% of the time, Pallas kernels for 0%

profile of v22, /device:TPU:1, one launch (start us, length us, event | category | flops | bytes accessed | tf_op | source)
XLA Modules:
  0.0 39.3 jit_solution(16799294430396485962)
XLA Ops:
  0.0 1.0 %select_bitcast_fusion = f32[1,16,1792]{2,1,0:T(8,128)S(1)} fusion(f32[16,1792]{1,0:T(8,128)} %param.12, pred[16]{0:T(512)(128)(4,1)S(1)} %add_compare_fusion), kind=kLoop, calls=%fused_computation.138 | loop fusion | flops 28672 | bytes 229392 | tf_op jit(solution)/shard_map/broadcast_in_dim | solution.py:109
  1.0 1.4 %broadcast_select_fusion.2 = (f32[10,4,1792]{2,1,0:T(4,128)S(1)}, f32[10,4,1792]{2,1,0:T(4,128)S(1)}, f32[10,4,1792]{2,1,0:T(4,128)S(1)}) fusion(pred[]{:T(512)S(6)} %eq.7, f32[1,16,1792]{2,1,0:T(8,128)} %bitcast.49, f32[1,16,1792]{2,1,0:T(8,128)S(1)} %select_bitcast_fusion, f32[8,16,1792]{2,1,0:T(8,128)} %param.7), kind=kLoop, calls=%fused_computation.128 | loop fusion | flops 358400 | bytes 2007041 | tf_op jit(solution)/shard_map/jit(_where)/select_n | solution.py:36
  2.5 0.1 collective-permute-start
  2.7 4.7 %collective-permute-start.1 = (f32[10,4,1792]{2,0,1:T(8,128)S(1)}, f32[10,4,1792]{2,0,1:T(8,128)S(1)}, u32[]{:S(2)}, u32[]{:S(2)}) collective-permute-start(f32[10,4,1792]{2,0,1:T(8,128)S(1)} %copy.14), channel_id=1, source_target_pairs={{1,2},{3,4},{5,6},{2,1},{4,3},{6,5},{9,10},{11,12},{13,14},{10,9},... | collective-permute-start | bytes 860168 | tf_op jit(solution)/shard_map/ppermute | solution.py:36
  7.4 0.4 multiply_reduce_fusion
  7.8 0.2 broadcast_select_fusion.1
  8.1 0.2 pad_maximum_fusion
  8.4 0.4 %fusion.14 = f32[8,24,1791]{2,1,0:T(8,128)S(1)} fusion(f32[10,24,1792]{2,1,0:T(8,128)S(1)} %pad_maximum_fusion, f32[24,1791]{1,0:T(8,128)S(1)} %bitcast.45), kind=kLoop, calls=%fused_computation.35 | loop fusion | flops 687744 | bytes 4298400 | tf_op jit(solution)/shard_map/mul | solution.py:72
  8.8 0.2 fusion.15
  9.0 0.5 %fusion.18 = f32[8,24,1792]{2,1,0:T(8,128)S(1)} fusion(f32[10,24,1792]{2,1,0:T(8,128)S(1)} %pad_maximum_fusion, f32[8,24,1791]{2,1,0:T(8,128)S(1)} %fusion.14, f32[8,23,1792]{2,1,0:T(8,128)S(1)} %fusion.15), kind=kLoop, calls=%fused_computation.41 | loop fusion | flops 1376256 | bytes 5446912 | tf_op jit(solution)/shard_map/sub | solution.py:81
  9.5 0.4 %fusion.12 = f32[8,24,1791]{2,1,0:T(8,128)S(1)} fusion(f32[8,24,1792]{2,1,0:T(8,128)S(1)} %fusion.18, f32[24,1791]{1,0:T(8,128)S(1)} %bitcast.46), kind=kLoop, calls=%fused_computation.31 | loop fusion | flops 687744 | bytes 4298400 | tf_op jit(solution)/shard_map/mul | solution.py:72
  9.9 0.2 fusion.13
  10.1 0.5 %pad_subtract_fusion.4 = f32[8,24,1792]{2,1,0:T(8,128)S(1)} fusion(f32[8,24,1791]{2,1,0:T(8,128)S(1)} %fusion.12, f32[8,23,1792]{2,1,0:T(8,128)S(1)} %fusion.13, f32[8,24,1792]{2,1,0:T(8,128)S(1)} %fusion.18), kind=kLoop, calls=%fused_computation.47 | loop fusion | flops 1376256 | bytes 5446912 | tf_op jit(solution)/shard_map/sub | solution.py:81
  10.6 0.4 %fusion.10 = f32[8,24,1791]{2,1,0:T(8,128)S(1)} fusion(f32[8,24,1792]{2,1,0:T(8,128)S(1)} %pad_subtract_fusion.4, f32[24,1791]{1,0:T(8,128)S(1)} %bitcast.47), kind=kLoop, calls=%fused_computation.27 | loop fusion | flops 687744 | bytes 4298400 | tf_op jit(solution)/shard_map/mul | solution.py:72
  11.0 0.2 fusion.11
  11.2 0.5 %pad_subtract_fusion.3 = f32[8,24,1792]{2,1,0:T(8,128)S(1)} fusion(f32[8,24,1791]{2,1,0:T(8,128)S(1)} %fusion.10, f32[8,23,1792]{2,1,0:T(8,128)S(1)} %fusion.11, f32[8,24,1792]{2,1,0:T(8,128)S(1)} %pad_subtract_fusion.4), kind=kLoop, calls=%fused_computation.46 | loop fusion | flops 1376256 | bytes 5446912 | tf_op jit(solution)/shard_map/sub | solution.py:81
  11.7 0.4 %fusion.8 = f32[8,24,1791]{2,1,0:T(8,128)S(1)} fusion(f32[8,24,1792]{2,1,0:T(8,128)S(1)} %pad_subtract_fusion.3, f32[24,1791]{1,0:T(8,128)S(1)} %bitcast.48), kind=kLoop, calls=%fused_computation.23 | loop fusion | flops 687744 | bytes 4298400 | tf_op jit(solution)/shard_map/mul | solution.py:72
  12.1 0.2 fusion.9
  12.3 0.5 %pad_subtract_fusion.7 = f32[8,16,1792]{2,1,0:T(8,128)S(1)} fusion(f32[8,24,1791]{2,1,0:T(8,128)S(1)} %fusion.8, f32[8,23,1792]{2,1,0:T(8,128)S(1)} %fusion.9, f32[8,24,1792]{2,1,0:T(8,128)S(1)} %pad_subtract_fusion.3), kind=kLoop, calls=%fused_computation.69 | loop fusion | flops 917504 | bytes 4529408 | tf_op jit(solution)/shard_map/sub | solution.py:81
  12.9 0.7 %collective-permute-done.1 = f32[10,4,1792]{2,0,1:T(8,128)S(1)} collective-permute-done((f32[10,4,1792]{2,0,1:T(8,128)S(1)}, f32[10,4,1792]{2,0,1:T(8,128)S(1)}, u32[]{:S(2)}, u32[]{:S(2)}) %collective-permute-start.1) | collective-permute-done | bytes 286752 | tf_op jit(solution)/shard_map/ppermute | solution.py:36
  13.5 0.4 copy_select_fusion.1
  13.9 0.2 pad_maximum_fusion.2
  14.2 0.1 slice_select_fusion
  14.4 0.3 fusion.24
  14.7 0.1 fusion.25
  14.9 0.5 %fusion.28 = f32[8,12,1792]{2,1,0:T(8,128)S(1)} fusion(f32[10,12,1792]{2,1,0:T(8,128)S(1)} %slice_select_fusion, f32[8,12,1791]{2,1,0:T(8,128)S(1)} %fusion.24, f32[8,11,1792]{2,1,0:T(8,128)S(1)} %fusion.25), kind=kLoop, calls=%fused_computation.68 | loop fusion | flops 688128 | bytes 2694784 | tf_op jit(solution)/shard_map/sub | solution.py:81
  15.3 0.3 fusion.19
  15.6 0.2 fusion.20
  15.8 0.4 %fusion.23 = f32[8,10,1792]{2,1,0:T(8,128)S(1)} fusion(f32[8,12,1792]{2,1,0:T(8,128)S(1)} %fusion.28, f32[8,10,1791]{2,1,0:T(8,128)S(1)} %fusion.19, f32[8,9,1792]{2,1,0:T(8,128)S(1)} %fusion.20), kind=kLoop, calls=%fused_computation.60 | loop fusion | flops 573440 | bytes 2236096 | tf_op jit(solution)/shard_map/sub | solution.py:81
  16.3 0.2 fusion.41
  16.6 0.2 fusion.45
  16.9 0.2 fusion.39
  17.2 0.1 fusion.46
  17.3 0.2 pad_subtract_fusion.13
  17.5 0.3 fusion.30
  17.8 1.8 %collective-permute-start.3 = (f32[16,1792]{1,0:T(8,128)S(1)}, f32[16,1792]{1,0:T(8,128)S(1)}, u32[]{:S(2)}, u32[]{:S(2)}) collective-permute-start(f32[16,1792]{1,0:T(8,128)S(1)} %fusion.30), channel_id=1, source_target_pairs={{0,16},{8,24},{16,0},{24,8},{1,17},{9,25},{17,1},{25,9},{2,18},{10... | collective-permute-start | bytes 344072 | tf_op jit(solution)/shard_map/ppermute | solution.py:56
  19.6 1.2 %collective-permute-start.4 = (f32[16,1792]{1,0:T(8,128)S(1)}, f32[16,1792]{1,0:T(8,128)S(1)}, u32[]{:S(2)}, u32[]{:S(2)}) collective-permute-start(f32[16,1792]{1,0:T(8,128)S(1)} %fusion.30), channel_id=1, source_target_pairs={{0,24},{8,16},{16,8},{24,0},{1,25},{9,17},{17,9},{25,1},{2,26},{10... | collective-permute-start | bytes 344072 | tf_op jit(solution)/shard_map/ppermute | solution.py:56
  20.9 0.2 pad_maximum_fusion.3
  21.3 1.8 %collective-permute-done.3 = f32[16,1792]{1,0:T(8,128)S(1)} collective-permute-done((f32[16,1792]{1,0:T(8,128)S(1)}, f32[16,1792]{1,0:T(8,128)S(1)}, u32[]{:S(2)}, u32[]{:S(2)}) %collective-permute-start.3) | collective-permute-done | bytes 114720 | tf_op jit(solution)/shard_map/ppermute | solution.py:56
  23.1 1.4 %collective-permute-done.4 = f32[16,1792]{1,0:T(8,128)S(1)} collective-permute-done((f32[16,1792]{1,0:T(8,128)S(1)}, f32[16,1792]{1,0:T(8,128)S(1)}, u32[]{:S(2)}, u32[]{:S(2)}) %collective-permute-start.4) | collective-permute-done | bytes 114720 | tf_op jit(solution)/shard_map/ppermute | solution.py:56
  24.5 0.3 collective-permute-done.2
  25.1 6.2 %collective-permute-start.6 = (f32[8,4,1792]{2,1,0:T(4,128)S(1)}, f32[8,4,1792]{2,1,0:T(4,128)S(1)}, u32[]{:S(2)}, u32[]{:S(2)}) collective-permute-start(f32[8,4,1792]{2,1,0:T(4,128)S(1)} %get-tuple-element.18), channel_id=1, source_target_pairs={{1,2},{3,4},{5,6},{2,1},{4,3},{6,5},{9,10},{11,12},{13,14},{10,9},... | collective-permute-start | bytes 688136 | tf_op jit(solution)/shard_map/ppermute | solution.py:36
  31.3 0.2 pad_maximum_fusion.4
  31.5 0.4 %fusion.6 = f32[8,24,1791]{2,1,0:T(8,128)S(1)} fusion(f32[8,24,1792]{2,1,0:T(8,128)S(1)} %pad_maximum_fusion.4, f32[24,1791]{1,0:T(8,128)S(1)} %bitcast.41), kind=kLoop, calls=%fused_computation.19 | loop fusion | flops 687744 | bytes 4298400 | tf_op jit(solution)/shard_map/mul | solution.py:72
  32.0 0.2 fusion.7
  32.1 0.6 %pad_subtract_fusion.2 = f32[8,24,1792]{2,1,0:T(8,128)S(1)} fusion(f32[8,24,1791]{2,1,0:T(8,128)S(1)} %fusion.6, f32[8,23,1792]{2,1,0:T(8,128)S(1)} %fusion.7, f32[8,4,1792]{2,1,0:T(4,128)S(1)} %get-tuple-element.29, f32[8,16,1792]{2,1,0:T(8,128)S(1)} %broadcast_multiply_fusion, f32[8,4,1792]{2,1,0:T(4,128)S(1)} %get-tuple-element.28), kind=kLoop, calls=%fused_computation.45 | loop fusion | flops 2064384 | bytes 5446912 | tf_op jit(solution)/shard_map/sub | solution.py:81
  32.7 0.4 %fusion.4 = f32[8,24,1791]{2,1,0:T(8,128)S(1)} fusion(f32[8,24,1792]{2,1,0:T(8,128)S(1)} %pad_subtract_fusion.2, f32[24,1791]{1,0:T(8,128)S(1)} %bitcast.42), kind=kLoop, calls=%fused_computation.15 | loop fusion | flops 687744 | bytes 4298400 | tf_op jit(solution)/shard_map/mul | solution.py:72
  33.1 0.2 fusion.5
  33.3 0.5 %pad_subtract_fusion.1 = f32[8,24,1792]{2,1,0:T(8,128)S(1)} fusion(f32[8,24,1791]{2,1,0:T(8,128)S(1)} %fusion.4, f32[8,23,1792]{2,1,0:T(8,128)S(1)} %fusion.5, f32[8,24,1792]{2,1,0:T(8,128)S(1)} %pad_subtract_fusion.2), kind=kLoop, calls=%fused_computation.44 | loop fusion | flops 1376256 | bytes 5446912 | tf_op jit(solution)/shard_map/sub | solution.py:81
  33.8 0.4 %fusion.2 = f32[8,24,1791]{2,1,0:T(8,128)S(1)} fusion(f32[8,24,1792]{2,1,0:T(8,128)S(1)} %pad_subtract_fusion.1, f32[24,1791]{1,0:T(8,128)S(1)} %bitcast.43), kind=kLoop, calls=%fused_computation.11 | loop fusion | flops 687744 | bytes 4298400 | tf_op jit(solution)/shard_map/mul | solution.py:72
  34.2 0.2 fusion.3
  34.4 0.5 %pad_subtract_fusion = f32[8,24,1792]{2,1,0:T(8,128)S(1)} fusion(f32[8,24,1791]{2,1,0:T(8,128)S(1)} %fusion.2, f32[8,23,1792]{2,1,0:T(8,128)S(1)} %fusion.3, f32[8,24,1792]{2,1,0:T(8,128)S(1)} %pad_subtract_fusion.1), kind=kLoop, calls=%fused_computation.43 | loop fusion | flops 1376256 | bytes 5446912 | tf_op jit(solution)/shard_map/sub | solution.py:81
  34.9 0.4 %fusion = f32[8,24,1791]{2,1,0:T(8,128)S(1)} fusion(f32[8,24,1792]{2,1,0:T(8,128)S(1)} %pad_subtract_fusion, f32[24,1791]{1,0:T(8,128)S(1)} %bitcast.44), kind=kLoop, calls=%fused_computation.7 | loop fusion | flops 687744 | bytes 4298400 | tf_op jit(solution)/shard_map/mul | solution.py:72
  35.3 0.2 fusion.1
  35.5 0.5 %pad_subtract_fusion.5 = f32[8,16,1792]{2,1,0:T(8,128)S(1)} fusion(f32[8,24,1791]{2,1,0:T(8,128)S(1)} %fusion, f32[8,23,1792]{2,1,0:T(8,128)S(1)} %fusion.1, f32[8,24,1792]{2,1,0:T(8,128)S(1)} %pad_subtract_fusion), kind=kLoop, calls=%fused_computation.49 | loop fusion | flops 917504 | bytes 4529408 | tf_op jit(solution)/shard_map/sub | solution.py:81
  36.1 0.2 fusion.37
  36.4 0.2 pad_subtract_fusion.12
  36.6 0.2 fusion.35
  36.9 0.2 pad_subtract_fusion.11
  37.1 0.2 fusion.33
  37.4 0.2 pad_subtract_fusion.10
  37.6 0.2 fusion.31
  37.9 0.2 pad_subtract_fusion.9
  38.2 1.1 %add_add_fusion = f32[8,16,1792]{2,1,0:T(8,128)} fusion(f32[8,16,1792]{2,1,0:T(8,128)S(1)} %copy-done, f32[8,16,1792]{2,1,0:T(8,128)S(1)} %pad_subtract_fusion.5, f32[8,4,1792]{2,1,0:T(4,128)S(1)} %get-tuple-element.25, f32[8,4,1792]{2,1,0:T(4,128)S(1)} %get-tuple-element.24, pred[]{:T(512)S(6)} %eq.7), kind=kLoop, calls=%fused_computation.76 | loop fusion | flops 688128 | bytes 3211265 | tf_op jit(solution)/shard_map/add | solution.py:147
  (49 shorter events, 1.5 us)
Async XLA Ops:
  2.3 5.1 %copy-start.2 = (bf16[8,4,16,1792]{3,2,1,0:T(8,128)(2,1)S(1)}, bf16[8,4,16,1792]{3,2,1,0:T(8,128)(2,1)}, u32[]{:S(2)}) copy-start(bf16[8,4,16,1792]{3,2,1,0:T(8,128)(2,1)} %param.8) | copy-start | bytes 5505028
  2.4 5.1 %copy-start.3 = (f32[4,16,1792]{2,1,0:T(8,128)S(1)}, f32[4,16,1792]{2,1,0:T(8,128)}, u32[]{:S(2)}) copy-start(f32[4,16,1792]{2,1,0:T(8,128)} %param.9) | copy-start | bytes 1376260
  2.5 5.3 %collective-permute-start = (f32[10,4,1792]{2,0,1:T(8,128)S(1)}, f32[10,4,1792]{2,0,1:T(8,128)S(1)}, u32[]{:S(2)}, u32[]{:S(2)}) collective-permute-start(f32[10,4,1792]{2,0,1:T(8,128)S(1)} %copy.11), channel_id=1, source_target_pairs={{0,1},{2,3},{4,5},{6,7},{1,0},{3,2},{5,4},{7,6},{8,9},{10,11},{12,... | collective-permute-start | bytes 860168 | tf_op jit(solution)/shard_map/ppermute | solution.py:37
  2.7 5.4 %copy-start = (f32[8,16,1792]{2,1,0:T(8,128)S(1)}, f32[8,16,1792]{2,1,0:T(8,128)}, u32[]{:S(2)}) copy-start(f32[8,16,1792]{2,1,0:T(8,128)} %param.7) | copy-start | bytes 2752516
  2.7 5.4 %copy-start.1 = (f32[16,1792]{1,0:T(8,128)S(1)}, f32[16,1792]{1,0:T(8,128)}, u32[]{:S(2)}) copy-start(f32[16,1792]{1,0:T(8,128)} %param.13) | copy-start | bytes 344068
  2.7 10.8 %collective-permute-start.1 = (f32[10,4,1792]{2,0,1:T(8,128)S(1)}, f32[10,4,1792]{2,0,1:T(8,128)S(1)}, u32[]{:S(2)}, u32[]{:S(2)}) collective-permute-start(f32[10,4,1792]{2,0,1:T(8,128)S(1)} %copy.14), channel_id=1, source_target_pairs={{1,2},{3,4},{5,6},{2,1},{4,3},{6,5},{9,10},{11,12},{13,14},{10,9},... | collective-permute-start | bytes 860168 | tf_op jit(solution)/shard_map/ppermute | solution.py:36
  17.8 5.3 %collective-permute-start.3 = (f32[16,1792]{1,0:T(8,128)S(1)}, f32[16,1792]{1,0:T(8,128)S(1)}, u32[]{:S(2)}, u32[]{:S(2)}) collective-permute-start(f32[16,1792]{1,0:T(8,128)S(1)} %fusion.30), channel_id=1, source_target_pairs={{0,16},{8,24},{16,0},{24,8},{1,17},{9,25},{17,1},{25,9},{2,18},{10... | collective-permute-start | bytes 344072 | tf_op jit(solution)/shard_map/ppermute | solution.py:56
  19.6 4.8 %collective-permute-start.4 = (f32[16,1792]{1,0:T(8,128)S(1)}, f32[16,1792]{1,0:T(8,128)S(1)}, u32[]{:S(2)}, u32[]{:S(2)}) collective-permute-start(f32[16,1792]{1,0:T(8,128)S(1)} %fusion.30), channel_id=1, source_target_pairs={{0,24},{8,16},{16,8},{24,0},{1,25},{9,17},{17,9},{25,1},{2,26},{10... | collective-permute-start | bytes 344072 | tf_op jit(solution)/shard_map/ppermute | solution.py:56
  20.8 4.0 %collective-permute-start.2 = (f32[16,1792]{1,0:T(8,128)S(1)}, f32[16,1792]{1,0:T(8,128)S(1)}, u32[]{:S(2)}, u32[]{:S(2)}) collective-permute-start(f32[16,1792]{1,0:T(8,128)S(1)} %fusion.30), channel_id=1, source_target_pairs={{0,8},{8,0},{16,24},{24,16},{1,9},{9,1},{17,25},{25,17},{2,10},{10... | collective-permute-start | bytes 344072 | tf_op jit(solution)/shard_map/ppermute | solution.py:56
  21.1 3.6 %copy-start.4 = (f32[16,1792]{1,0:T(8,128)S(1)}, f32[16,1792]{1,0:T(8,128)}, u32[]{:S(2)}) copy-start(f32[16,1792]{1,0:T(8,128)} %param.10) | copy-start | bytes 344068
  21.2 3.6 %copy-start.5 = (s32[16,1792]{1,0:T(8,128)S(1)}, s32[16,1792]{1,0:T(8,128)}, u32[]{:S(2)}) copy-start(s32[16,1792]{1,0:T(8,128)} %param.11) | copy-start | bytes 344068
  25.0 6.3 %collective-permute-start.5 = (f32[8,4,1792]{2,1,0:T(4,128)S(1)}, f32[8,4,1792]{2,1,0:T(4,128)S(1)}, u32[]{:S(2)}, u32[]{:S(2)}) collective-permute-start(f32[8,4,1792]{2,1,0:T(4,128)S(1)} %get-tuple-element.19), channel_id=1, source_target_pairs={{0,1},{2,3},{4,5},{6,7},{1,0},{3,2},{5,4},{7,6},{8,9},{10,11},{12,... | collective-permute-start | bytes 688136 | tf_op jit(solution)/shard_map/ppermute | solution.py:37
  25.1 11.0 %collective-permute-start.6 = (f32[8,4,1792]{2,1,0:T(4,128)S(1)}, f32[8,4,1792]{2,1,0:T(4,128)S(1)}, u32[]{:S(2)}, u32[]{:S(2)}) collective-permute-start(f32[8,4,1792]{2,1,0:T(4,128)S(1)} %get-tuple-element.18), channel_id=1, source_target_pairs={{1,2},{3,4},{5,6},{2,1},{4,3},{6,5},{9,10},{11,12},{13,14},{10,9},... | collective-permute-start | bytes 688136 | tf_op jit(solution)/shard_map/ppermute | solution.py:36

commit v23 on v22

--- a/solution.py
+++ b/solution.py
@@ -117,7 +117,7 @@
         return controls + localize(sensitivity, coef_band)[:, STEPS : STEPS + row_count]
     near, far, odd = split_exchange(stacked, STEPS)
     partial = near_band(stacked, near, odd)
-    main = localize(partial[:members], partial[members:])[:, STEPS : STEPS + row_count]
+    main = localize_inner(partial[:members], partial[members:])
     main, far = lax.optimization_barrier((main, far))
     band = full_band(stacked, near, far, odd)
     coef_band = band[members:]
@@ -131,8 +131,7 @@
     reflect = mem_sum(jnp.sum(mix * localized, 0))
     weighted = radar_mask.astype(jnp.float32) * obs_weight * reflect
     near, far, odd = split_exchange(mix * weighted[None], STEPS)
-    spread = localize(near_band(mix * weighted[None], near, odd), coef_band)
-    spread = spread[:, STEPS : STEPS + row_count]
+    spread = localize_inner(near_band(mix * weighted[None], near, odd), coef_band)
     spread, far = lax.optimization_barrier((spread, far))
     zero = jnp.zeros_like(far)
     strip = jnp.where(odd, jnp.concatenate([zero, far], 1), jnp.concatenate([far, zero], 1))

time: 39.5 us -> 41 us (1.038)
  starting transfers between devices: 14.1 us -> 11.4 us
  waiting for transfers between devices: 4.17 us -> 6.38 us
  local copies, waits for them, and re-layouts: 0.56 us -> 1.61 us
  other arithmetic: 19.8 us -> 20.7 us
    ppermute x2, starting transfers between devices: 10.9 us -> 8.02 us  [split_exchange(): far = lax.ppermute(jnp.where(odd, tail, head), 'tile', pairs(1))]
    ppermute x3, waiting for transfers between devices: 3.47 us -> 5.78 us  [partner(): return lax.ppermute(part, 'mem', [(i, i ^ stride) for i in range(count)])]
    ppermute x2, waiting for transfers between devices: 0.7 us -> 0.01 us  [split_exchange(): far = lax.ppermute(jnp.where(odd, tail, head), 'tile', pairs(1))]
    unnamed x12, local copies, waits for them, and re-layouts: 0.04 us -> 0.71 us
    mul x16 -> x17, other arithmetic: 2.24 us -> 2.83 us  [diffuse(): row_coef[..., :-1, :] * (values[..., 1:, :] - values[..., :-1, :])]
    ppermute x2, waiting for transfers between devices: 0.01 us -> 0.59 us  [split_exchange(): near = lax.ppermute(jnp.where(odd, head, tail), 'tile', pairs(0))]
    ppermute x2, starting transfers between devices: 0.19 us -> 0.68 us  [split_exchange(): near = lax.ppermute(jnp.where(odd, head, tail), 'tile', pairs(0))]
  transfers between devices with their start and end apart: 7 -> 7, of which waited for: 4 -> 3; matrix products, arithmetic and copies ran while one was open for 27% -> 28% of each run, Pallas kernels for 0% -> 0%
where the time goes in v23:
time: 41 us; the launch traced here: 40.8 us
  other arithmetic  20.7 us (50%)
  starting transfers between devices  11.4 us (28%)
  waiting for transfers between devices  6.38 us (16%)
  local copies, waits for them, and re-layouts  1.61 us (4%)
  between operations  0.72 us (2%)
    ppermute x2, starting transfers between devices, split_exchange(): far = lax.ppermute(jnp.where(odd, tail, head), 'tile', pairs(1))  8.02 us
    sub x16, other arithmetic, diffuse(): values + jnp.concatenate([col_flux, zeros_col], -1)  6.3 us
    ppermute x3, waiting for transfers between devices, partner(): return lax.ppermute(part, 'mem', [(i, i ^ stride) for i in range(count)])  5.78 us
    mul x16, other arithmetic, diffuse(): col_coef[..., :, :-1] * (values[..., :, 1:] - values[..., :, :-1])  5.19 us
    mul x17, other arithmetic, diffuse(): row_coef[..., :-1, :] * (values[..., 1:, :] - values[..., :-1, :])  2.83 us
    ppermute x3, starting transfers between devices, partner(): return lax.ppermute(part, 'mem', [(i, i ^ stride) for i in range(count)])  2.71 us
    select_n x2, other arithmetic, split_exchange(): far = lax.ppermute(jnp.where(odd, tail, head), 'tile', pairs(1))  1.43 us
    add x1, other arithmetic, per_device(): return controls + (spread + edge)  1.12 us
  transfers between devices with their start and end apart: 7, of which 3 were waited for; matrix products, arithmetic and copies ran while one was open for 28% of the time, Pallas kernels for 0%

profile of v23, /device:TPU:1, one launch (start us, length us, event | category | flops | bytes accessed | tf_op | source)
XLA Modules:
  0.0 40.8 jit_solution(12852835328492649594)
XLA Ops:
  0.0 1.0 %select_bitcast_fusion = f32[1,16,1792]{2,1,0:T(8,128)S(1)} fusion(f32[16,1792]{1,0:T(8,128)} %param.12, pred[16]{0:T(512)(128)(4,1)S(1)} %add_compare_fusion), kind=kLoop, calls=%fused_computation.164 | loop fusion | flops 28672 | bytes 229392 | tf_op jit(solution)/shard_map/broadcast_in_dim | solution.py:109
  1.0 1.4 %broadcast_select_fusion.2 = (f32[10,4,1792]{2,1,0:T(4,128)S(1)}, f32[10,4,1792]{2,1,0:T(4,128)S(1)}, f32[10,4,1792]{2,1,0:T(4,128)S(1)}) fusion(pred[]{:T(512)S(6)} %eq.7, f32[1,16,1792]{2,1,0:T(8,128)} %bitcast.71, f32[1,16,1792]{2,1,0:T(8,128)S(1)} %select_bitcast_fusion, f32[8,16,1792]{2,1,0:T(8,128)} %param.7), kind=kLoop, calls=%fused_computation.154 | loop fusion | flops 358400 | bytes 2007041 | tf_op jit(solution)/shard_map/jit(_where)/select_n | solution.py:36
  2.4 4.7 %collective-permute-start.1 = (f32[10,4,1792]{2,0,1:T(8,128)S(1)}, f32[10,4,1792]{2,0,1:T(8,128)S(1)}, u32[]{:S(2)}, u32[]{:S(2)}) collective-permute-start(f32[10,4,1792]{2,0,1:T(8,128)S(1)} %copy.14), channel_id=1, source_target_pairs={{1,2},{3,4},{5,6},{2,1},{4,3},{6,5},{9,10},{11,12},{13,14},{10,9},... | collective-permute-start | bytes 860168 | tf_op jit(solution)/shard_map/ppermute | solution.py:36
  7.4 0.4 multiply_reduce_fusion
  7.8 0.7 %copy-done = f32[8,16,1792]{2,1,0:T(8,128)S(1)} copy-done((f32[8,16,1792]{2,1,0:T(8,128)S(1)}, f32[8,16,1792]{2,1,0:T(8,128)}, u32[]{:S(2)}) %copy-start) | copy-done | bytes 917528
  8.5 0.1 pad_maximum_fusion.2
  8.6 0.6 %collective-permute-done = f32[10,4,1792]{2,0,1:T(8,128)S(1)} collective-permute-done((f32[10,4,1792]{2,0,1:T(8,128)S(1)}, f32[10,4,1792]{2,0,1:T(8,128)S(1)}, u32[]{:S(2)}, u32[]{:S(2)}) %collective-permute-start) | collective-permute-done | bytes 286752 | tf_op jit(solution)/shard_map/ppermute | solution.py:37
  9.2 0.2 broadcast_select_fusion.1
  9.4 0.2 pad_maximum_fusion
  9.8 0.2 fusion.27
  10.0 0.4 %fusion.26 = f32[8,24,1791]{2,1,0:T(8,128)S(1)} fusion(f32[10,24,1792]{2,1,0:T(8,128)S(1)} %pad_maximum_fusion, f32[24,1791]{1,0:T(8,128)S(1)} %bitcast.91), kind=kLoop, calls=%fused_computation.52 | loop fusion | flops 687744 | bytes 4298400 | tf_op jit(solution)/shard_map/mul | solution.py:72
  10.5 0.5 %fusion.30 = f32[8,24,1792]{2,1,0:T(8,128)S(1)} fusion(f32[10,24,1792]{2,1,0:T(8,128)S(1)} %pad_maximum_fusion, f32[8,24,1791]{2,1,0:T(8,128)S(1)} %fusion.26, f32[8,23,1792]{2,1,0:T(8,128)S(1)} %fusion.27), kind=kLoop, calls=%fused_computation.58 | loop fusion | flops 1376256 | bytes 5446912 | tf_op jit(solution)/shard_map/sub | solution.py:81
  11.0 0.3 fusion.22
  11.2 0.4 %fusion.21 = f32[8,22,1791]{2,1,0:T(8,128)S(1)} fusion(f32[8,24,1792]{2,1,0:T(8,128)S(1)} %fusion.30, f32[22,1791]{1,0:T(8,128)S(1)} %bitcast.90), kind=kLoop, calls=%fused_computation.44 | loop fusion | flops 630432 | bytes 3940200 | tf_op jit(solution)/shard_map/mul | solution.py:72
  11.7 0.5 %fusion.25 = f32[8,22,1792]{2,1,0:T(8,128)S(1)} fusion(f32[8,24,1792]{2,1,0:T(8,128)S(1)} %fusion.30, f32[8,22,1791]{2,1,0:T(8,128)S(1)} %fusion.21, f32[8,21,1792]{2,1,0:T(8,128)S(1)} %fusion.22), kind=kLoop, calls=%fused_computation.50 | loop fusion | flops 1261568 | bytes 4988224 | tf_op jit(solution)/shard_map/sub | solution.py:81
  12.2 0.3 fusion.17
  12.5 0.4 %fusion.16 = f32[8,20,1791]{2,1,0:T(8,128)S(1)} fusion(f32[8,22,1792]{2,1,0:T(8,128)S(1)} %fusion.25, f32[20,1791]{1,0:T(8,128)S(1)} %bitcast.89), kind=kLoop, calls=%fused_computation.36 | loop fusion | flops 573120 | bytes 3582000 | tf_op jit(solution)/shard_map/mul | solution.py:72
  12.9 0.5 %fusion.20 = f32[8,20,1792]{2,1,0:T(8,128)S(1)} fusion(f32[8,22,1792]{2,1,0:T(8,128)S(1)} %fusion.25, f32[8,20,1791]{2,1,0:T(8,128)S(1)} %fusion.16, f32[8,19,1792]{2,1,0:T(8,128)S(1)} %fusion.17), kind=kLoop, calls=%fused_computation.42 | loop fusion | flops 1146880 | bytes 4529536 | tf_op jit(solution)/shard_map/sub | solution.py:81
  13.5 0.4 %fusion.14 = f32[8,18,1791]{2,1,0:T(8,128)S(1)} fusion(f32[8,20,1792]{2,1,0:T(8,128)S(1)} %fusion.20, f32[18,1791]{1,0:T(8,128)S(1)} %bitcast.88), kind=kLoop, calls=%fused_computation.32 | loop fusion | flops 515808 | bytes 3223800 | tf_op jit(solution)/shard_map/mul | solution.py:72
  14.0 0.3 fusion.15
  14.3 0.5 %pad_subtract_fusion.3 = f32[8,16,1792]{2,1,0:T(8,128)S(1)} fusion(f32[8,18,1791]{2,1,0:T(8,128)S(1)} %fusion.14, f32[8,17,1792]{2,1,0:T(8,128)S(1)} %fusion.15, f32[8,18,1792]{2,1,0:T(8,128)S(1)} %slice.688), kind=kLoop, calls=%fused_computation.82 | loop fusion | flops 917504 | bytes 3841472 | tf_op jit(solution)/shard_map/sub | solution.py:81
  14.8 0.4 copy_select_fusion.1
  15.2 0.3 pad_maximum_fusion.5
  15.6 0.3 pad_maximum_fusion.3
  16.2 0.1 fusion.59
  16.5 0.3 fusion.36
  16.8 0.5 %fusion.40 = f32[8,12,1792]{2,1,0:T(8,128)S(1)} fusion(f32[10,12,1792]{2,1,0:T(8,128)S(1)} %slice_select_fusion, f32[8,12,1791]{2,1,0:T(8,128)S(1)} %fusion.36, f32[8,11,1792]{2,1,0:T(8,128)S(1)} %fusion.37), kind=kLoop, calls=%fused_computation.81 | loop fusion | flops 688128 | bytes 2694784 | tf_op jit(solution)/shard_map/sub | solution.py:81
  17.3 0.2 fusion.32
  17.5 0.3 fusion.31
  17.8 0.4 %fusion.35 = f32[8,10,1792]{2,1,0:T(8,128)S(1)} fusion(f32[8,12,1792]{2,1,0:T(8,128)S(1)} %fusion.40, f32[8,10,1791]{2,1,0:T(8,128)S(1)} %fusion.31, f32[8,9,1792]{2,1,0:T(8,128)S(1)} %fusion.32), kind=kLoop, calls=%fused_computation.73 | loop fusion | flops 573440 | bytes 2236096 | tf_op jit(solution)/shard_map/sub | solution.py:81
  18.3 0.2 fusion.53
  18.5 0.2 fusion.57
  18.9 0.2 fusion.51
  19.1 0.2 pad_subtract_fusion.9
  19.3 0.3 fusion.42
  19.7 2.2 %collective-permute-start.4 = (f32[16,1792]{1,0:T(8,128)S(1)}, f32[16,1792]{1,0:T(8,128)S(1)}, u32[]{:S(2)}, u32[]{:S(2)}) collective-permute-start(f32[16,1792]{1,0:T(8,128)S(1)} %fusion.42), channel_id=1, source_target_pairs={{0,24},{8,16},{16,8},{24,0},{1,25},{9,17},{17,9},{25,1},{2,26},{10... | collective-permute-start | bytes 344072 | tf_op jit(solution)/shard_map/ppermute | solution.py:56
  21.9 0.2 collective-permute-start.3
  22.1 0.3 collective-permute-start.2
  22.4 2.9 %collective-permute-done.4 = f32[16,1792]{1,0:T(8,128)S(1)} collective-permute-done((f32[16,1792]{1,0:T(8,128)S(1)}, f32[16,1792]{1,0:T(8,128)S(1)}, u32[]{:S(2)}, u32[]{:S(2)}) %collective-permute-start.4) | collective-permute-done | bytes 114720 | tf_op jit(solution)/shard_map/ppermute | solution.py:56
  25.2 2.9 %collective-permute-done.3 = f32[16,1792]{1,0:T(8,128)S(1)} collective-permute-done((f32[16,1792]{1,0:T(8,128)S(1)}, f32[16,1792]{1,0:T(8,128)S(1)}, u32[]{:S(2)}, u32[]{:S(2)}) %collective-permute-start.3) | collective-permute-done | bytes 114720 | tf_op jit(solution)/shard_map/ppermute | solution.py:56
  28.4 0.6 %collective-permute-start.5 = (f32[8,4,1792]{2,1,0:T(4,128)S(1)}, f32[8,4,1792]{2,1,0:T(4,128)S(1)}, u32[]{:S(2)}, u32[]{:S(2)}) collective-permute-start(f32[8,4,1792]{2,1,0:T(4,128)S(1)} %get-tuple-element.19), channel_id=1, source_target_pairs={{0,1},{2,3},{4,5},{6,7},{1,0},{3,2},{5,4},{7,6},{8,9},{10,11},{12,... | collective-permute-start | bytes 688136 | tf_op jit(solution)/shard_map/ppermute | solution.py:37
  29.0 3.3 %collective-permute-start.6 = (f32[8,4,1792]{2,1,0:T(4,128)S(1)}, f32[8,4,1792]{2,1,0:T(4,128)S(1)}, u32[]{:S(2)}, u32[]{:S(2)}) collective-permute-start(f32[8,4,1792]{2,1,0:T(4,128)S(1)} %get-tuple-element.18), channel_id=1, source_target_pairs={{1,2},{3,4},{5,6},{2,1},{4,3},{6,5},{9,10},{11,12},{13,14},{10,9},... | collective-permute-start | bytes 688136 | tf_op jit(solution)/shard_map/ppermute | solution.py:36
  32.4 0.2 pad_maximum_fusion.6
  32.6 0.2 fusion.13
  32.8 0.4 %fusion.12 = f32[8,24,1791]{2,1,0:T(8,128)S(1)} fusion(f32[8,24,1792]{2,1,0:T(8,128)S(1)} %pad_maximum_fusion.6, f32[24,1791]{1,0:T(8,128)S(1)} %bitcast.87), kind=kLoop, calls=%fused_computation.28 | loop fusion | flops 687744 | bytes 4298400 | tf_op jit(solution)/shard_map/mul | solution.py:72
  33.2 0.6 %pad_subtract_fusion = f32[8,24,1792]{2,1,0:T(8,128)S(1)} fusion(f32[8,24,1791]{2,1,0:T(8,128)S(1)} %fusion.12, f32[8,23,1792]{2,1,0:T(8,128)S(1)} %fusion.13, f32[8,4,1792]{2,1,0:T(4,128)S(1)} %get-tuple-element.29, f32[8,16,1792]{2,1,0:T(8,128)S(1)} %broadcast_multiply_fusion, f32[8,4,1792]{2,1,0:T(4,128)S(1)} %get-tuple-element.28), kind=kLoop, calls=%fused_computation.60 | loop fusion | flops 2064384 | bytes 5446912 | tf_op jit(solution)/shard_map/sub | solution.py:81
  33.8 0.3 fusion.8
  34.1 0.4 %fusion.7 = f32[8,22,1791]{2,1,0:T(8,128)S(1)} fusion(f32[8,24,1792]{2,1,0:T(8,128)S(1)} %pad_subtract_fusion, f32[22,1791]{1,0:T(8,128)S(1)} %bitcast.86), kind=kLoop, calls=%fused_computation.20 | loop fusion | flops 630432 | bytes 3940200 | tf_op jit(solution)/shard_map/mul | solution.py:72
  34.5 0.5 %fusion.11 = f32[8,22,1792]{2,1,0:T(8,128)S(1)} fusion(f32[8,24,1792]{2,1,0:T(8,128)S(1)} %pad_subtract_fusion, f32[8,22,1791]{2,1,0:T(8,128)S(1)} %fusion.7, f32[8,21,1792]{2,1,0:T(8,128)S(1)} %fusion.8), kind=kLoop, calls=%fused_computation.26 | loop fusion | flops 1261568 | bytes 4988224 | tf_op jit(solution)/shard_map/sub | solution.py:81
  35.0 0.3 fusion.3
  35.3 0.4 %fusion.2 = f32[8,20,1791]{2,1,0:T(8,128)S(1)} fusion(f32[8,22,1792]{2,1,0:T(8,128)S(1)} %fusion.11, f32[20,1791]{1,0:T(8,128)S(1)} %bitcast.85), kind=kLoop, calls=%fused_computation.12 | loop fusion | flops 573120 | bytes 3582000 | tf_op jit(solution)/shard_map/mul | solution.py:72
  35.7 0.5 %fusion.6 = f32[8,20,1792]{2,1,0:T(8,128)S(1)} fusion(f32[8,22,1792]{2,1,0:T(8,128)S(1)} %fusion.11, f32[8,20,1791]{2,1,0:T(8,128)S(1)} %fusion.2, f32[8,19,1792]{2,1,0:T(8,128)S(1)} %fusion.3), kind=kLoop, calls=%fused_computation.18 | loop fusion | flops 1146880 | bytes 4529536 | tf_op jit(solution)/shard_map/sub | solution.py:81
  36.4 0.3 fusion.1
  36.6 0.4 %fusion = f32[8,18,1791]{2,1,0:T(8,128)S(1)} fusion(f32[8,20,1792]{2,1,0:T(8,128)S(1)} %fusion.6, f32[18,1791]{1,0:T(8,128)S(1)} %bitcast.84), kind=kLoop, calls=%fused_computation.8 | loop fusion | flops 515808 | bytes 3223800 | tf_op jit(solution)/shard_map/mul | solution.py:72
  37.1 0.5 %pad_subtract_fusion.1 = f32[8,16,1792]{2,1,0:T(8,128)S(1)} fusion(f32[8,18,1791]{2,1,0:T(8,128)S(1)} %fusion, f32[8,17,1792]{2,1,0:T(8,128)S(1)} %fusion.1, f32[8,18,1792]{2,1,0:T(8,128)S(1)} %slice.757), kind=kLoop, calls=%fused_computation.62 | loop fusion | flops 917504 | bytes 3841472 | tf_op jit(solution)/shard_map/sub | solution.py:81
  37.7 0.2 fusion.49
  37.9 0.2 pad_subtract_fusion.8
  38.2 0.2 fusion.47
  38.4 0.2 pad_subtract_fusion.7
  38.7 0.2 fusion.45
  38.9 0.2 pad_subtract_fusion.6
  39.2 0.2 fusion.43
  39.4 0.2 pad_subtract_fusion.5
  39.7 1.1 %add_add_fusion = f32[8,16,1792]{2,1,0:T(8,128)} fusion(f32[8,16,1792]{2,1,0:T(8,128)S(1)} %copy-done, f32[8,16,1792]{2,1,0:T(8,128)S(1)} %pad_subtract_fusion.1, f32[8,4,1792]{2,1,0:T(4,128)S(1)} %get-tuple-element.25, f32[8,4,1792]{2,1,0:T(4,128)S(1)} %get-tuple-element.24, pred[]{:T(512)S(6)} %eq.7), kind=kLoop, calls=%fused_computation.89 | loop fusion | flops 688128 | bytes 3211265 | tf_op jit(solution)/shard_map/add | solution.py:146
  (64 shorter events, 2.0 us)
Async XLA Ops:
  2.3 5.1 %copy-start.2 = (bf16[8,4,16,1792]{3,2,1,0:T(8,128)(2,1)S(1)}, bf16[8,4,16,1792]{3,2,1,0:T(8,128)(2,1)}, u32[]{:S(2)}) copy-start(bf16[8,4,16,1792]{3,2,1,0:T(8,128)(2,1)} %param.8) | copy-start | bytes 5505028
  2.4 5.1 %copy-start.3 = (f32[4,16,1792]{2,1,0:T(8,128)S(1)}, f32[4,16,1792]{2,1,0:T(8,128)}, u32[]{:S(2)}) copy-start(f32[4,16,1792]{2,1,0:T(8,128)} %param.9) | copy-start | bytes 1376260
  2.4 12.4 %collective-permute-start.1 = (f32[10,4,1792]{2,0,1:T(8,128)S(1)}, f32[10,4,1792]{2,0,1:T(8,128)S(1)}, u32[]{:S(2)}, u32[]{:S(2)}) collective-permute-start(f32[10,4,1792]{2,0,1:T(8,128)S(1)} %copy.14), channel_id=1, source_target_pairs={{1,2},{3,4},{5,6},{2,1},{4,3},{6,5},{9,10},{11,12},{13,14},{10,9},... | collective-permute-start | bytes 860168 | tf_op jit(solution)/shard_map/ppermute | solution.py:36
  7.3 1.2 %copy-start = (f32[8,16,1792]{2,1,0:T(8,128)S(1)}, f32[8,16,1792]{2,1,0:T(8,128)}, u32[]{:S(2)}) copy-start(f32[8,16,1792]{2,1,0:T(8,128)} %param.7) | copy-start | bytes 2752516
  7.3 1.2 %copy-start.1 = (f32[16,1792]{1,0:T(8,128)S(1)}, f32[16,1792]{1,0:T(8,128)}, u32[]{:S(2)}) copy-start(f32[16,1792]{1,0:T(8,128)} %param.13) | copy-start | bytes 344068
  7.3 1.9 %collective-permute-start = (f32[10,4,1792]{2,0,1:T(8,128)S(1)}, f32[10,4,1792]{2,0,1:T(8,128)S(1)}, u32[]{:S(2)}, u32[]{:S(2)}) collective-permute-start(f32[10,4,1792]{2,0,1:T(8,128)S(1)} %copy.11), channel_id=1, source_target_pairs={{0,1},{2,3},{4,5},{6,7},{1,0},{3,2},{5,4},{7,6},{8,9},{10,11},{12,... | collective-permute-start | bytes 860168 | tf_op jit(solution)/shard_map/ppermute | solution.py:37
  19.3 8.8 %copy-start.4 = (f32[16,1792]{1,0:T(8,128)S(1)}, f32[16,1792]{1,0:T(8,128)}, u32[]{:S(2)}) copy-start(f32[16,1792]{1,0:T(8,128)} %param.10) | copy-start | bytes 344068
  19.3 8.8 %copy-start.5 = (s32[16,1792]{1,0:T(8,128)S(1)}, s32[16,1792]{1,0:T(8,128)}, u32[]{:S(2)}) copy-start(s32[16,1792]{1,0:T(8,128)} %param.11) | copy-start | bytes 344068
  19.7 5.6 %collective-permute-start.4 = (f32[16,1792]{1,0:T(8,128)S(1)}, f32[16,1792]{1,0:T(8,128)S(1)}, u32[]{:S(2)}, u32[]{:S(2)}) collective-permute-start(f32[16,1792]{1,0:T(8,128)S(1)} %fusion.42), channel_id=1, source_target_pairs={{0,24},{8,16},{16,8},{24,0},{1,25},{9,17},{17,9},{25,1},{2,26},{10... | collective-permute-start | bytes 344072 | tf_op jit(solution)/shard_map/ppermute | solution.py:56
  21.9 6.3 %collective-permute-start.3 = (f32[16,1792]{1,0:T(8,128)S(1)}, f32[16,1792]{1,0:T(8,128)S(1)}, u32[]{:S(2)}, u32[]{:S(2)}) collective-permute-start(f32[16,1792]{1,0:T(8,128)S(1)} %fusion.42), channel_id=1, source_target_pairs={{0,16},{8,24},{16,0},{24,8},{1,17},{9,25},{17,1},{25,9},{2,18},{10... | collective-permute-start | bytes 344072 | tf_op jit(solution)/shard_map/ppermute | solution.py:56
  22.1 6.0 %collective-permute-start.2 = (f32[16,1792]{1,0:T(8,128)S(1)}, f32[16,1792]{1,0:T(8,128)S(1)}, u32[]{:S(2)}, u32[]{:S(2)}) collective-permute-start(f32[16,1792]{1,0:T(8,128)S(1)} %fusion.42), channel_id=1, source_target_pairs={{0,8},{8,0},{16,24},{24,16},{1,9},{9,1},{17,25},{25,17},{2,10},{10... | collective-permute-start | bytes 344072 | tf_op jit(solution)/shard_map/ppermute | solution.py:56
  28.4 3.9 %collective-permute-start.5 = (f32[8,4,1792]{2,1,0:T(4,128)S(1)}, f32[8,4,1792]{2,1,0:T(4,128)S(1)}, u32[]{:S(2)}, u32[]{:S(2)}) collective-permute-start(f32[8,4,1792]{2,1,0:T(4,128)S(1)} %get-tuple-element.19), channel_id=1, source_target_pairs={{0,1},{2,3},{4,5},{6,7},{1,0},{3,2},{5,4},{7,6},{8,9},{10,11},{12,... | collective-permute-start | bytes 688136 | tf_op jit(solution)/shard_map/ppermute | solution.py:37
  29.0 8.6 %collective-permute-start.6 = (f32[8,4,1792]{2,1,0:T(4,128)S(1)}, f32[8,4,1792]{2,1,0:T(4,128)S(1)}, u32[]{:S(2)}, u32[]{:S(2)}) collective-permute-start(f32[8,4,1792]{2,1,0:T(4,128)S(1)} %get-tuple-element.18), channel_id=1, source_target_pairs={{1,2},{3,4},{5,6},{2,1},{4,3},{6,5},{9,10},{11,12},{13,14},{10,9},... | collective-permute-start | bytes 688136 | tf_op jit(solution)/shard_map/ppermute | solution.py:36

commit v24 on v22

--- a/solution.py
+++ b/solution.py
@@ -117,7 +117,7 @@
         return controls + localize(sensitivity, coef_band)[:, STEPS : STEPS + row_count]
     near, far, odd = split_exchange(stacked, STEPS)
     partial = near_band(stacked, near, odd)
-    main = localize(partial[:members], partial[members:])[:, STEPS : STEPS + row_count]
+    main = localize_inner(partial[:members], partial[members:])
     main, far = lax.optimization_barrier((main, far))
     band = full_band(stacked, near, far, odd)
     coef_band = band[members:]

time: 39.5 us -> 40.4 us (1.023)
  starting transfers between devices: 14.1 us -> 11.4 us
  waiting for transfers between devices: 4.17 us -> 6.38 us
  local copies, waits for them, and re-layouts: 0.56 us -> 1.41 us
  other arithmetic: 19.8 us -> 20.3 us
    ppermute x2, starting transfers between devices: 10.9 us -> 8.02 us  [split_exchange(): far = lax.ppermute(jnp.where(odd, tail, head), 'tile', pairs(1))]
    ppermute x3, waiting for transfers between devices: 3.47 us -> 5.78 us  [partner(): return lax.ppermute(part, 'mem', [(i, i ^ stride) for i in range(count)])]
    ppermute x2, waiting for transfers between devices: 0.7 us -> 0.01 us  [split_exchange(): far = lax.ppermute(jnp.where(odd, tail, head), 'tile', pairs(1))]
    unnamed x12, local copies, waits for them, and re-layouts: 0.04 us -> 0.71 us
    ppermute x2, waiting for transfers between devices: 0.01 us -> 0.59 us  [split_exchange(): near = lax.ppermute(jnp.where(odd, head, tail), 'tile', pairs(0))]
    ppermute x2, starting transfers between devices: 0.19 us -> 0.68 us  [split_exchange(): near = lax.ppermute(jnp.where(odd, head, tail), 'tile', pairs(0))]
    mul x16 -> x17, other arithmetic: 2.24 us -> 2.56 us  [diffuse(): row_coef[..., :-1, :] * (values[..., 1:, :] - values[..., :-1, :])]
  transfers between devices with their start and end apart: 7 -> 7, of which waited for: 4 -> 3; matrix products, arithmetic and copies ran while one was open for 27% -> 27% of each run, Pallas kernels for 0% -> 0%
where the time goes in v24:
time: 40.4 us; the launch traced here: 40.2 us
  other arithmetic  20.3 us (50%)
  starting transfers between devices  11.4 us (28%)
  waiting for transfers between devices  6.38 us (16%)
  local copies, waits for them, and re-layouts  1.41 us (3%)
  between operations  0.67 us (2%)
    ppermute x2, starting transfers between devices, split_exchange(): far = lax.ppermute(jnp.where(odd, tail, head), 'tile', pairs(1))  8.02 us
    sub x16, other arithmetic, diffuse(): values + jnp.concatenate([col_flux, zeros_col], -1)  6.27 us
    ppermute x3, waiting for transfers between devices, partner(): return lax.ppermute(part, 'mem', [(i, i ^ stride) for i in range(count)])  5.78 us
    mul x16, other arithmetic, diffuse(): col_coef[..., :, :-1] * (values[..., :, 1:] - values[..., :, :-1])  5.16 us
    ppermute x3, starting transfers between devices, partner(): return lax.ppermute(part, 'mem', [(i, i ^ stride) for i in range(count)])  2.71 us
    mul x17, other arithmetic, diffuse(): row_coef[..., :-1, :] * (values[..., 1:, :] - values[..., :-1, :])  2.56 us
    select_n x2, other arithmetic, split_exchange(): far = lax.ppermute(jnp.where(odd, tail, head), 'tile', pairs(1))  1.43 us
    add x1, other arithmetic, per_device(): return controls + (spread + edge)  1.12 us
  transfers between devices with their start and end apart: 7, of which 3 were waited for; matrix products, arithmetic and copies ran while one was open for 27% of the time, Pallas kernels for 0%

profile of v24, /device:TPU:1, one launch (start us, length us, event | category | flops | bytes accessed | tf_op | source)
XLA Modules:
  0.0 40.2 jit_solution(8164698677701253361)
XLA Ops:
  0.0 1.0 %select_bitcast_fusion = f32[1,16,1792]{2,1,0:T(8,128)S(1)} fusion(f32[16,1792]{1,0:T(8,128)} %param.12, pred[16]{0:T(512)(128)(4,1)S(1)} %add_compare_fusion), kind=kLoop, calls=%fused_computation.152 | loop fusion | flops 28672 | bytes 229392 | tf_op jit(solution)/shard_map/broadcast_in_dim | solution.py:109
  1.0 1.4 %broadcast_select_fusion.2 = (f32[10,4,1792]{2,1,0:T(4,128)S(1)}, f32[10,4,1792]{2,1,0:T(4,128)S(1)}, f32[10,4,1792]{2,1,0:T(4,128)S(1)}) fusion(pred[]{:T(512)S(6)} %eq.7, f32[1,16,1792]{2,1,0:T(8,128)} %bitcast.60, f32[1,16,1792]{2,1,0:T(8,128)S(1)} %select_bitcast_fusion, f32[8,16,1792]{2,1,0:T(8,128)} %param.7), kind=kLoop, calls=%fused_computation.142 | loop fusion | flops 358400 | bytes 2007041 | tf_op jit(solution)/shard_map/jit(_where)/select_n | solution.py:36
  2.4 4.7 %collective-permute-start.1 = (f32[10,4,1792]{2,0,1:T(8,128)S(1)}, f32[10,4,1792]{2,0,1:T(8,128)S(1)}, u32[]{:S(2)}, u32[]{:S(2)}) collective-permute-start(f32[10,4,1792]{2,0,1:T(8,128)S(1)} %copy.14), channel_id=1, source_target_pairs={{1,2},{3,4},{5,6},{2,1},{4,3},{6,5},{9,10},{11,12},{13,14},{10,9},... | collective-permute-start | bytes 860168 | tf_op jit(solution)/shard_map/ppermute | solution.py:36
  7.4 0.4 multiply_reduce_fusion
  7.8 0.7 %copy-done = f32[8,16,1792]{2,1,0:T(8,128)S(1)} copy-done((f32[8,16,1792]{2,1,0:T(8,128)S(1)}, f32[8,16,1792]{2,1,0:T(8,128)}, u32[]{:S(2)}) %copy-start) | copy-done | bytes 917528
  8.5 0.1 pad_maximum_fusion.2
  8.6 0.6 %collective-permute-done = f32[10,4,1792]{2,0,1:T(8,128)S(1)} collective-permute-done((f32[10,4,1792]{2,0,1:T(8,128)S(1)}, f32[10,4,1792]{2,0,1:T(8,128)S(1)}, u32[]{:S(2)}, u32[]{:S(2)}) %collective-permute-start) | collective-permute-done | bytes 286752 | tf_op jit(solution)/shard_map/ppermute | solution.py:37
  9.2 0.2 broadcast_select_fusion.1
  9.4 0.2 pad_maximum_fusion
  9.8 0.2 fusion.21
  10.0 0.4 %fusion.20 = f32[8,24,1791]{2,1,0:T(8,128)S(1)} fusion(f32[10,24,1792]{2,1,0:T(8,128)S(1)} %pad_maximum_fusion, f32[24,1791]{1,0:T(8,128)S(1)} %bitcast.76), kind=kLoop, calls=%fused_computation.44 | loop fusion | flops 687744 | bytes 4298400 | tf_op jit(solution)/shard_map/mul | solution.py:72
  10.5 0.5 %fusion.24 = f32[8,24,1792]{2,1,0:T(8,128)S(1)} fusion(f32[10,24,1792]{2,1,0:T(8,128)S(1)} %pad_maximum_fusion, f32[8,24,1791]{2,1,0:T(8,128)S(1)} %fusion.20, f32[8,23,1792]{2,1,0:T(8,128)S(1)} %fusion.21), kind=kLoop, calls=%fused_computation.50 | loop fusion | flops 1376256 | bytes 5446912 | tf_op jit(solution)/shard_map/sub | solution.py:81
  11.0 0.3 fusion.16
  11.2 0.4 %fusion.15 = f32[8,22,1791]{2,1,0:T(8,128)S(1)} fusion(f32[8,24,1792]{2,1,0:T(8,128)S(1)} %fusion.24, f32[22,1791]{1,0:T(8,128)S(1)} %bitcast.75), kind=kLoop, calls=%fused_computation.36 | loop fusion | flops 630432 | bytes 3940200 | tf_op jit(solution)/shard_map/mul | solution.py:72
  11.7 0.5 %fusion.19 = f32[8,22,1792]{2,1,0:T(8,128)S(1)} fusion(f32[8,24,1792]{2,1,0:T(8,128)S(1)} %fusion.24, f32[8,22,1791]{2,1,0:T(8,128)S(1)} %fusion.15, f32[8,21,1792]{2,1,0:T(8,128)S(1)} %fusion.16), kind=kLoop, calls=%fused_computation.42 | loop fusion | flops 1261568 | bytes 4988224 | tf_op jit(solution)/shard_map/sub | solution.py:81
  12.2 0.3 fusion.11
  12.5 0.4 %fusion.10 = f32[8,20,1791]{2,1,0:T(8,128)S(1)} fusion(f32[8,22,1792]{2,1,0:T(8,128)S(1)} %fusion.19, f32[20,1791]{1,0:T(8,128)S(1)} %bitcast.74), kind=kLoop, calls=%fused_computation.28 | loop fusion | flops 573120 | bytes 3582000 | tf_op jit(solution)/shard_map/mul | solution.py:72
  12.9 0.5 %fusion.14 = f32[8,20,1792]{2,1,0:T(8,128)S(1)} fusion(f32[8,22,1792]{2,1,0:T(8,128)S(1)} %fusion.19, f32[8,20,1791]{2,1,0:T(8,128)S(1)} %fusion.10, f32[8,19,1792]{2,1,0:T(8,128)S(1)} %fusion.11), kind=kLoop, calls=%fused_computation.34 | loop fusion | flops 1146880 | bytes 4529536 | tf_op jit(solution)/shard_map/sub | solution.py:81
  13.5 0.4 %fusion.8 = f32[8,18,1791]{2,1,0:T(8,128)S(1)} fusion(f32[8,20,1792]{2,1,0:T(8,128)S(1)} %fusion.14, f32[18,1791]{1,0:T(8,128)S(1)} %bitcast.73), kind=kLoop, calls=%fused_computation.24 | loop fusion | flops 515808 | bytes 3223800 | tf_op jit(solution)/shard_map/mul | solution.py:72
  14.0 0.3 fusion.9
  14.3 0.5 %pad_subtract_fusion.5 = f32[8,16,1792]{2,1,0:T(8,128)S(1)} fusion(f32[8,18,1791]{2,1,0:T(8,128)S(1)} %fusion.8, f32[8,17,1792]{2,1,0:T(8,128)S(1)} %fusion.9, f32[8,18,1792]{2,1,0:T(8,128)S(1)} %slice.618), kind=kLoop, calls=%fused_computation.76 | loop fusion | flops 917504 | bytes 3841472 | tf_op jit(solution)/shard_map/sub | solution.py:81
  14.8 0.4 copy_select_fusion.1
  15.2 0.3 pad_maximum_fusion.5
  15.5 0.3 pad_maximum_fusion.3
  16.1 0.1 fusion.53
  16.3 0.3 fusion.30
  16.6 0.5 %fusion.34 = f32[8,12,1792]{2,1,0:T(8,128)S(1)} fusion(f32[10,12,1792]{2,1,0:T(8,128)S(1)} %slice_select_fusion, f32[8,12,1791]{2,1,0:T(8,128)S(1)} %fusion.30, f32[8,11,1792]{2,1,0:T(8,128)S(1)} %fusion.31), kind=kLoop, calls=%fused_computation.75 | loop fusion | flops 688128 | bytes 2694784 | tf_op jit(solution)/shard_map/sub | solution.py:81
  17.1 0.2 fusion.26
  17.3 0.3 fusion.25
  17.6 0.4 %fusion.29 = f32[8,10,1792]{2,1,0:T(8,128)S(1)} fusion(f32[8,12,1792]{2,1,0:T(8,128)S(1)} %fusion.34, f32[8,10,1791]{2,1,0:T(8,128)S(1)} %fusion.25, f32[8,9,1792]{2,1,0:T(8,128)S(1)} %fusion.26), kind=kLoop, calls=%fused_computation.67 | loop fusion | flops 573440 | bytes 2236096 | tf_op jit(solution)/shard_map/sub | solution.py:81
  18.2 0.2 fusion.47
  18.4 0.2 fusion.51
  18.7 0.2 fusion.45
  18.9 0.2 pad_subtract_fusion.11
  19.2 0.3 fusion.36
  19.5 2.2 %collective-permute-start.4 = (f32[16,1792]{1,0:T(8,128)S(1)}, f32[16,1792]{1,0:T(8,128)S(1)}, u32[]{:S(2)}, u32[]{:S(2)}) collective-permute-start(f32[16,1792]{1,0:T(8,128)S(1)} %fusion.36), channel_id=1, source_target_pairs={{0,24},{8,16},{16,8},{24,0},{1,25},{9,17},{17,9},{25,1},{2,26},{10... | collective-permute-start | bytes 344072 | tf_op jit(solution)/shard_map/ppermute | solution.py:56
  21.7 0.2 collective-permute-start.3
  22.0 0.3 collective-permute-start.2
  22.2 2.9 %collective-permute-done.4 = f32[16,1792]{1,0:T(8,128)S(1)} collective-permute-done((f32[16,1792]{1,0:T(8,128)S(1)}, f32[16,1792]{1,0:T(8,128)S(1)}, u32[]{:S(2)}, u32[]{:S(2)}) %collective-permute-start.4) | collective-permute-done | bytes 114720 | tf_op jit(solution)/shard_map/ppermute | solution.py:56
  25.1 2.9 %collective-permute-done.3 = f32[16,1792]{1,0:T(8,128)S(1)} collective-permute-done((f32[16,1792]{1,0:T(8,128)S(1)}, f32[16,1792]{1,0:T(8,128)S(1)}, u32[]{:S(2)}, u32[]{:S(2)}) %collective-permute-start.3) | collective-permute-done | bytes 114720 | tf_op jit(solution)/shard_map/ppermute | solution.py:56
  28.2 0.6 %collective-permute-start.5 = (f32[8,4,1792]{2,1,0:T(4,128)S(1)}, f32[8,4,1792]{2,1,0:T(4,128)S(1)}, u32[]{:S(2)}, u32[]{:S(2)}) collective-permute-start(f32[8,4,1792]{2,1,0:T(4,128)S(1)} %get-tuple-element.19), channel_id=1, source_target_pairs={{0,1},{2,3},{4,5},{6,7},{1,0},{3,2},{5,4},{7,6},{8,9},{10,11},{12,... | collective-permute-start | bytes 688136 | tf_op jit(solution)/shard_map/ppermute | solution.py:37
  28.9 3.3 %collective-permute-start.6 = (f32[8,4,1792]{2,1,0:T(4,128)S(1)}, f32[8,4,1792]{2,1,0:T(4,128)S(1)}, u32[]{:S(2)}, u32[]{:S(2)}) collective-permute-start(f32[8,4,1792]{2,1,0:T(4,128)S(1)} %get-tuple-element.18), channel_id=1, source_target_pairs={{1,2},{3,4},{5,6},{2,1},{4,3},{6,5},{9,10},{11,12},{13,14},{10,9},... | collective-permute-start | bytes 688136 | tf_op jit(solution)/shard_map/ppermute | solution.py:36
  32.3 0.2 pad_maximum_fusion.6
  32.4 0.2 fusion.7
  32.6 0.4 %fusion.6 = f32[8,24,1791]{2,1,0:T(8,128)S(1)} fusion(f32[8,24,1792]{2,1,0:T(8,128)S(1)} %pad_maximum_fusion.6, f32[24,1791]{1,0:T(8,128)S(1)} %bitcast.56), kind=kLoop, calls=%fused_computation.20 | loop fusion | flops 687744 | bytes 4298400 | tf_op jit(solution)/shard_map/mul | solution.py:72
  33.1 0.6 %pad_subtract_fusion.2 = f32[8,24,1792]{2,1,0:T(8,128)S(1)} fusion(f32[8,24,1791]{2,1,0:T(8,128)S(1)} %fusion.6, f32[8,23,1792]{2,1,0:T(8,128)S(1)} %fusion.7, f32[8,4,1792]{2,1,0:T(4,128)S(1)} %get-tuple-element.29, f32[8,16,1792]{2,1,0:T(8,128)S(1)} %broadcast_multiply_fusion, f32[8,4,1792]{2,1,0:T(4,128)S(1)} %get-tuple-element.28), kind=kLoop, calls=%fused_computation.54 | loop fusion | flops 2064384 | bytes 5446912 | tf_op jit(solution)/shard_map/sub | solution.py:81
  33.6 0.2 fusion.5
  33.8 0.4 %fusion.4 = f32[8,24,1791]{2,1,0:T(8,128)S(1)} fusion(f32[8,24,1792]{2,1,0:T(8,128)S(1)} %pad_subtract_fusion.2, f32[24,1791]{1,0:T(8,128)S(1)} %bitcast.57), kind=kLoop, calls=%fused_computation.16 | loop fusion | flops 687744 | bytes 4298400 | tf_op jit(solution)/shard_map/mul | solution.py:72
  34.3 0.5 %pad_subtract_fusion.1 = f32[8,24,1792]{2,1,0:T(8,128)S(1)} fusion(f32[8,24,1791]{2,1,0:T(8,128)S(1)} %fusion.4, f32[8,23,1792]{2,1,0:T(8,128)S(1)} %fusion.5, f32[8,24,1792]{2,1,0:T(8,128)S(1)} %pad_subtract_fusion.2), kind=kLoop, calls=%fused_computation.53 | loop fusion | flops 1376256 | bytes 5446912 | tf_op jit(solution)/shard_map/sub | solution.py:81
  34.7 0.2 fusion.3
  34.9 0.4 %fusion.2 = f32[8,24,1791]{2,1,0:T(8,128)S(1)} fusion(f32[8,24,1792]{2,1,0:T(8,128)S(1)} %pad_subtract_fusion.1, f32[24,1791]{1,0:T(8,128)S(1)} %bitcast.58), kind=kLoop, calls=%fused_computation.12 | loop fusion | flops 687744 | bytes 4298400 | tf_op jit(solution)/shard_map/mul | solution.py:72
  35.4 0.5 %pad_subtract_fusion = f32[8,24,1792]{2,1,0:T(8,128)S(1)} fusion(f32[8,24,1791]{2,1,0:T(8,128)S(1)} %fusion.2, f32[8,23,1792]{2,1,0:T(8,128)S(1)} %fusion.3, f32[8,24,1792]{2,1,0:T(8,128)S(1)} %pad_subtract_fusion.1), kind=kLoop, calls=%fused_computation.52 | loop fusion | flops 1376256 | bytes 5446912 | tf_op jit(solution)/shard_map/sub | solution.py:81
  35.8 0.2 fusion.1
  36.0 0.4 %fusion = f32[8,24,1791]{2,1,0:T(8,128)S(1)} fusion(f32[8,24,1792]{2,1,0:T(8,128)S(1)} %pad_subtract_fusion, f32[24,1791]{1,0:T(8,128)S(1)} %bitcast.59), kind=kLoop, calls=%fused_computation.8 | loop fusion | flops 687744 | bytes 4298400 | tf_op jit(solution)/shard_map/mul | solution.py:72
  36.5 0.5 %pad_subtract_fusion.3 = f32[8,16,1792]{2,1,0:T(8,128)S(1)} fusion(f32[8,24,1791]{2,1,0:T(8,128)S(1)} %fusion, f32[8,23,1792]{2,1,0:T(8,128)S(1)} %fusion.1, f32[8,24,1792]{2,1,0:T(8,128)S(1)} %pad_subtract_fusion), kind=kLoop, calls=%fused_computation.56 | loop fusion | flops 917504 | bytes 4529408 | tf_op jit(solution)/shard_map/sub | solution.py:81
  37.1 0.2 fusion.43
  37.3 0.2 pad_subtract_fusion.10
  37.6 0.2 fusion.41
  37.8 0.2 pad_subtract_fusion.9
  38.1 0.2 fusion.39
  38.3 0.2 pad_subtract_fusion.8
  38.6 0.2 fusion.37
  38.8 0.2 pad_subtract_fusion.7
  39.1 1.1 %add_add_fusion = f32[8,16,1792]{2,1,0:T(8,128)} fusion(f32[8,16,1792]{2,1,0:T(8,128)S(1)} %copy-done, f32[8,16,1792]{2,1,0:T(8,128)S(1)} %pad_subtract_fusion.3, f32[8,4,1792]{2,1,0:T(4,128)S(1)} %get-tuple-element.25, f32[8,4,1792]{2,1,0:T(4,128)S(1)} %get-tuple-element.24, pred[]{:T(512)S(6)} %eq.7), kind=kLoop, calls=%fused_computation.83 | loop fusion | flops 688128 | bytes 3211265 | tf_op jit(solution)/shard_map/add | solution.py:147
  (57 shorter events, 1.8 us)
Async XLA Ops:
  2.3 5.1 %copy-start.2 = (bf16[8,4,16,1792]{3,2,1,0:T(8,128)(2,1)S(1)}, bf16[8,4,16,1792]{3,2,1,0:T(8,128)(2,1)}, u32[]{:S(2)}) copy-start(bf16[8,4,16,1792]{3,2,1,0:T(8,128)(2,1)} %param.8) | copy-start | bytes 5505028
  2.4 5.1 %copy-start.3 = (f32[4,16,1792]{2,1,0:T(8,128)S(1)}, f32[4,16,1792]{2,1,0:T(8,128)}, u32[]{:S(2)}) copy-start(f32[4,16,1792]{2,1,0:T(8,128)} %param.9) | copy-start | bytes 1376260
  2.4 12.4 %collective-permute-start.1 = (f32[10,4,1792]{2,0,1:T(8,128)S(1)}, f32[10,4,1792]{2,0,1:T(8,128)S(1)}, u32[]{:S(2)}, u32[]{:S(2)}) collective-permute-start(f32[10,4,1792]{2,0,1:T(8,128)S(1)} %copy.14), channel_id=1, source_target_pairs={{1,2},{3,4},{5,6},{2,1},{4,3},{6,5},{9,10},{11,12},{13,14},{10,9},... | collective-permute-start | bytes 860168 | tf_op jit(solution)/shard_map/ppermute | solution.py:36
  7.3 1.2 %copy-start = (f32[8,16,1792]{2,1,0:T(8,128)S(1)}, f32[8,16,1792]{2,1,0:T(8,128)}, u32[]{:S(2)}) copy-start(f32[8,16,1792]{2,1,0:T(8,128)} %param.7) | copy-start | bytes 2752516
  7.3 1.2 %copy-start.1 = (f32[16,1792]{1,0:T(8,128)S(1)}, f32[16,1792]{1,0:T(8,128)}, u32[]{:S(2)}) copy-start(f32[16,1792]{1,0:T(8,128)} %param.13) | copy-start | bytes 344068
  7.3 1.9 %collective-permute-start = (f32[10,4,1792]{2,0,1:T(8,128)S(1)}, f32[10,4,1792]{2,0,1:T(8,128)S(1)}, u32[]{:S(2)}, u32[]{:S(2)}) collective-permute-start(f32[10,4,1792]{2,0,1:T(8,128)S(1)} %copy.11), channel_id=1, source_target_pairs={{0,1},{2,3},{4,5},{6,7},{1,0},{3,2},{5,4},{7,6},{8,9},{10,11},{12,... | collective-permute-start | bytes 860168 | tf_op jit(solution)/shard_map/ppermute | solution.py:37
  19.2 8.8 %copy-start.4 = (f32[16,1792]{1,0:T(8,128)S(1)}, f32[16,1792]{1,0:T(8,128)}, u32[]{:S(2)}) copy-start(f32[16,1792]{1,0:T(8,128)} %param.10) | copy-start | bytes 344068
  19.2 8.8 %copy-start.5 = (s32[16,1792]{1,0:T(8,128)S(1)}, s32[16,1792]{1,0:T(8,128)}, u32[]{:S(2)}) copy-start(s32[16,1792]{1,0:T(8,128)} %param.11) | copy-start | bytes 344068
  19.5 5.6 %collective-permute-start.4 = (f32[16,1792]{1,0:T(8,128)S(1)}, f32[16,1792]{1,0:T(8,128)S(1)}, u32[]{:S(2)}, u32[]{:S(2)}) collective-permute-start(f32[16,1792]{1,0:T(8,128)S(1)} %fusion.36), channel_id=1, source_target_pairs={{0,24},{8,16},{16,8},{24,0},{1,25},{9,17},{17,9},{25,1},{2,26},{10... | collective-permute-start | bytes 344072 | tf_op jit(solution)/shard_map/ppermute | solution.py:56
  21.7 6.3 %collective-permute-start.3 = (f32[16,1792]{1,0:T(8,128)S(1)}, f32[16,1792]{1,0:T(8,128)S(1)}, u32[]{:S(2)}, u32[]{:S(2)}) collective-permute-start(f32[16,1792]{1,0:T(8,128)S(1)} %fusion.36), channel_id=1, source_target_pairs={{0,16},{8,24},{16,0},{24,8},{1,17},{9,25},{17,1},{25,9},{2,18},{10... | collective-permute-start | bytes 344072 | tf_op jit(solution)/shard_map/ppermute | solution.py:56
  22.0 6.0 %collective-permute-start.2 = (f32[16,1792]{1,0:T(8,128)S(1)}, f32[16,1792]{1,0:T(8,128)S(1)}, u32[]{:S(2)}, u32[]{:S(2)}) collective-permute-start(f32[16,1792]{1,0:T(8,128)S(1)} %fusion.36), channel_id=1, source_target_pairs={{0,8},{8,0},{16,24},{24,16},{1,9},{9,1},{17,25},{25,17},{2,10},{10... | collective-permute-start | bytes 344072 | tf_op jit(solution)/shard_map/ppermute | solution.py:56
  28.2 3.9 %collective-permute-start.5 = (f32[8,4,1792]{2,1,0:T(4,128)S(1)}, f32[8,4,1792]{2,1,0:T(4,128)S(1)}, u32[]{:S(2)}, u32[]{:S(2)}) collective-permute-start(f32[8,4,1792]{2,1,0:T(4,128)S(1)} %get-tuple-element.19), channel_id=1, source_target_pairs={{0,1},{2,3},{4,5},{6,7},{1,0},{3,2},{5,4},{7,6},{8,9},{10,11},{12,... | collective-permute-start | bytes 688136 | tf_op jit(solution)/shard_map/ppermute | solution.py:37
  28.9 8.1 %collective-permute-start.6 = (f32[8,4,1792]{2,1,0:T(4,128)S(1)}, f32[8,4,1792]{2,1,0:T(4,128)S(1)}, u32[]{:S(2)}, u32[]{:S(2)}) collective-permute-start(f32[8,4,1792]{2,1,0:T(4,128)S(1)} %get-tuple-element.18), channel_id=1, source_target_pairs={{1,2},{3,4},{5,6},{2,1},{4,3},{6,5},{9,10},{11,12},{13,14},{10,9},... | collective-permute-start | bytes 688136 | tf_op jit(solution)/shard_map/ppermute | solution.py:36

commit v25 on v24

--- a/solution.py
+++ b/solution.py
@@ -99,17 +99,19 @@
 
 def per_device(controls, perturbations, jacobian, obs_weight, radar_mask, row_faces, col_faces):
     members, row_count = controls.shape[:2]
-    row_index = lax.axis_index("tile") * row_count + lax.broadcasted_iota(
-        jnp.int32, row_faces.shape, 0
-    )
-    row_coef = jnp.where(
-        row_index < row_count * lax.axis_size("tile") - 1, row_faces, jnp.zeros_like(row_faces)
-    )
+    last_row = row_count * lax.axis_size("tile") - 1 - lax.axis_index("tile") * row_count
+
+    def masked(coefs):
+        band_row = lax.broadcasted_iota(jnp.int32, coefs.shape, 1) - STEPS
+        keep = (band_row != last_row) | (lax.broadcasted_iota(jnp.int32, coefs.shape, 0) > 0)
+        return jnp.where(keep, coefs, jnp.zeros_like(coefs))
+
+    row_coef = row_faces
     mix = jnp.sum(perturbations.astype(jnp.float32) * jacobian[None], axis=1)
     stacked = jnp.concatenate([controls, row_coef[None], col_faces[None]], 0)
     if lax.axis_size("tile") % 2:
         band = exchange(stacked, STEPS)
-        field, coef_band = band[:members], band[members:]
+        field, coef_band = band[:members], masked(band[members:])
         localized = localize(field, coef_band)[:, STEPS : STEPS + row_count]
         reflect = mem_sum(jnp.sum(mix * localized, 0))
         weighted = radar_mask.astype(jnp.float32) * obs_weight * reflect
@@ -117,9 +119,10 @@
         return controls + localize(sensitivity, coef_band)[:, STEPS : STEPS + row_count]
     near, far, odd = split_exchange(stacked, STEPS)
     partial = near_band(stacked, near, odd)
-    main = localize_inner(partial[:members], partial[members:])
+    main = localize(partial[:members], masked(partial[members:]))[:, STEPS : STEPS + row_count]
     main, far = lax.optimization_barrier((main, far))
     band = full_band(stacked, near, far, odd)
+    band = jnp.concatenate([band[:members], masked(band[members:])], 0)
     coef_band = band[members:]
     strip = jnp.where(odd, band[:, row_count - STEPS :], band[:, : 3 * STEPS])
     edge = localize_inner(strip[:members], strip[members:])

time: 40.4 us -> 40.5 us (level)
  starting transfers between devices: 11.4 us -> 12.9 us
  waiting for transfers between devices: 6.38 us -> 4.89 us
  local copies, waits for them, and re-layouts: 1.41 us -> 1.95 us
    ppermute x2, starting transfers between devices: 8.02 us -> 9.73 us  [split_exchange(): far = lax.ppermute(jnp.where(odd, tail, head), 'tile', pairs(1))]
    select_n x1 -> x3, other arithmetic: 0.37 us -> 1.58 us  [the longest x1 1.39 us: full_band(): jnp.where(odd, near, far)]
    ppermute x3, waiting for transfers between devices: 5.78 us -> 4.77 us  [partner(): return lax.ppermute(part, 'mem', [(i, i ^ stride) for i in range(count)])]
    broadcast_in_dim x1 -> x0, other arithmetic: 0.98 us -> none  [per_device(): stacked = jnp.concatenate([controls, row_coef[None], col_faces[None]], 0)]
    select_n x1, local copies, waits for them, and re-layouts: 0.07 us -> 0.83 us  [split_exchange(): near = lax.ppermute(jnp.where(odd, head, tail), 'tile', pairs(0))]
    ppermute x2, waiting for transfers between devices: 0.59 us -> 0.01 us  [split_exchange(): near = lax.ppermute(jnp.where(odd, head, tail), 'tile', pairs(0))]
    ppermute x2, starting transfers between devices: 0.68 us -> 0.13 us  [split_exchange(): near = lax.ppermute(jnp.where(odd, head, tail), 'tile', pairs(0))]
    mul x17 -> x16, other arithmetic: 2.56 us -> 2.3 us  [diffuse(): row_coef[..., :-1, :] * (values[..., 1:, :] - values[..., :-1, :])]
  transfers between devices with their start and end apart: 7 -> 7, of which waited for: 3 -> 3; matrix products, arithmetic and copies ran while one was open for 27% -> 26% of each run, Pallas kernels for 0% -> 0%
where the time goes in v25:
time: 40.5 us; the launch traced here: 40.3 us
  other arithmetic  19.9 us (49%)
  starting transfers between devices  12.9 us (32%)
  waiting for transfers between devices  4.89 us (12%)
  local copies, waits for them, and re-layouts  1.95 us (5%)
  between operations  0.62 us (2%)
    ppermute x2, starting transfers between devices, split_exchange(): far = lax.ppermute(jnp.where(odd, tail, head), 'tile', pairs(1))  9.73 us
    sub x16, other arithmetic, diffuse(): values + jnp.concatenate([col_flux, zeros_col], -1)  6.24 us
    mul x16, other arithmetic, diffuse(): col_coef[..., :, :-1] * (values[..., :, 1:] - values[..., :, :-1])  5.12 us
    ppermute x3, waiting for transfers between devices, partner(): return lax.ppermute(part, 'mem', [(i, i ^ stride) for i in range(count)])  4.77 us
    ppermute x3, starting transfers between devices, partner(): return lax.ppermute(part, 'mem', [(i, i ^ stride) for i in range(count)])  3.09 us
    mul x16, other arithmetic, diffuse(): row_coef[..., :-1, :] * (values[..., 1:, :] - values[..., :-1, :])  2.3 us
    select_n x2, other arithmetic, split_exchange(): far = lax.ppermute(jnp.where(odd, tail, head), 'tile', pairs(1))  1.5 us
    select_n x1, other arithmetic, full_band(): jnp.where(odd, near, far)  1.39 us
  transfers between devices with their start and end apart: 7, of which 3 were waited for; matrix products, arithmetic and copies ran while one was open for 26% of the time, Pallas kernels for 0%

profile of v25, /device:TPU:1, one launch (start us, length us, event | category | flops | bytes accessed | tf_op | source)
XLA Modules:
  0.0 40.3 jit_solution(6716461759401651906)
XLA Ops:
  0.0 1.4 %broadcast_select_fusion.2 = (f32[10,4,1792]{2,1,0:T(4,128)S(1)}, f32[10,4,1792]{2,1,0:T(4,128)S(1)}, f32[10,4,1792]{2,1,0:T(4,128)S(1)}) fusion(pred[]{:T(512)S(6)} %eq.7, f32[1,16,1792]{2,1,0:T(8,128)} %bitcast.55, f32[1,16,1792]{2,1,0:T(8,128)} %bitcast.58, f32[8,16,1792]{2,1,0:T(8,128)} %param.7), kind=kLoop, calls=%fused_computation.132 | loop fusion | flops 358400 | bytes 2007041 | tf_op jit(solution)/shard_map/jit(_where)/select_n | solution.py:36
  1.5 0.8 %copy.11 = f32[10,4,1792]{2,0,1:T(8,128)} copy(f32[10,4,1792]{2,1,0:T(4,128)S(1)} %bitcast.52) | data formatting | bytes 573440 | tf_op jit(solution)/shard_map/jit(_where)/select_n | solution.py:37
  2.5 4.5 %collective-permute-start.1 = (f32[10,4,1792]{2,0,1:T(8,128)S(1)}, f32[10,4,1792]{2,0,1:T(8,128)}, u32[]{:S(2)}, u32[]{:S(2)}) collective-permute-start(f32[10,4,1792]{2,0,1:T(8,128)S(1)} %copy.14), channel_id=1, source_target_pairs={{1,2},{3,4},{5,6},{2,1},{4,3},{6,5},{9,10},{11,12},{13,14},{10,9},... | collective-permute-start | bytes 860168 | tf_op jit(solution)/shard_map/ppermute | solution.py:36
  7.1 0.4 multiply_reduce_fusion
  7.5 0.2 broadcast_select_fusion.1
  7.7 0.5 %copy-done = f32[8,16,1792]{2,1,0:T(8,128)S(1)} copy-done((f32[8,16,1792]{2,1,0:T(8,128)S(1)}, f32[8,16,1792]{2,1,0:T(8,128)}, u32[]{:S(2)}) %copy-start) | copy-done | bytes 917528
  8.3 0.3 pad_maximum_fusion
  8.7 0.2 fusion.15
  8.9 0.4 %fusion.14 = f32[8,24,1791]{2,1,0:T(8,128)S(1)} fusion(f32[10,24,1792]{2,1,0:T(8,128)S(1)} %pad_maximum_fusion, f32[24,1791]{1,0:T(8,128)S(1)} %bitcast.44), kind=kLoop, calls=%fused_computation.35 | loop fusion | flops 687744 | bytes 4298400 | tf_op jit(solution)/shard_map/mul | solution.py:72
  9.3 0.5 %fusion.18 = f32[8,24,1792]{2,1,0:T(8,128)S(1)} fusion(f32[10,24,1792]{2,1,0:T(8,128)S(1)} %pad_maximum_fusion, f32[8,24,1791]{2,1,0:T(8,128)S(1)} %fusion.14, f32[8,23,1792]{2,1,0:T(8,128)S(1)} %fusion.15), kind=kLoop, calls=%fused_computation.41 | loop fusion | flops 1376256 | bytes 5446912 | tf_op jit(solution)/shard_map/sub | solution.py:81
  9.8 0.2 fusion.13
  10.0 0.4 %fusion.12 = f32[8,24,1791]{2,1,0:T(8,128)S(1)} fusion(f32[8,24,1792]{2,1,0:T(8,128)S(1)} %fusion.18, f32[24,1791]{1,0:T(8,128)S(1)} %bitcast.45), kind=kLoop, calls=%fused_computation.31 | loop fusion | flops 687744 | bytes 4298400 | tf_op jit(solution)/shard_map/mul | solution.py:72
  10.4 0.5 %pad_subtract_fusion.4 = f32[8,24,1792]{2,1,0:T(8,128)S(1)} fusion(f32[8,24,1791]{2,1,0:T(8,128)S(1)} %fusion.12, f32[8,23,1792]{2,1,0:T(8,128)S(1)} %fusion.13, f32[8,24,1792]{2,1,0:T(8,128)S(1)} %fusion.18), kind=kLoop, calls=%fused_computation.47 | loop fusion | flops 1376256 | bytes 5446912 | tf_op jit(solution)/shard_map/sub | solution.py:81
  10.9 0.2 fusion.11
  11.1 0.4 %fusion.10 = f32[8,24,1791]{2,1,0:T(8,128)S(1)} fusion(f32[8,24,1792]{2,1,0:T(8,128)S(1)} %pad_subtract_fusion.4, f32[24,1791]{1,0:T(8,128)S(1)} %bitcast.46), kind=kLoop, calls=%fused_computation.27 | loop fusion | flops 687744 | bytes 4298400 | tf_op jit(solution)/shard_map/mul | solution.py:72
  11.5 0.5 %pad_subtract_fusion.3 = f32[8,24,1792]{2,1,0:T(8,128)S(1)} fusion(f32[8,24,1791]{2,1,0:T(8,128)S(1)} %fusion.10, f32[8,23,1792]{2,1,0:T(8,128)S(1)} %fusion.11, f32[8,24,1792]{2,1,0:T(8,128)S(1)} %pad_subtract_fusion.4), kind=kLoop, calls=%fused_computation.46 | loop fusion | flops 1376256 | bytes 5446912 | tf_op jit(solution)/shard_map/sub | solution.py:81
  12.0 0.2 fusion.9
  12.2 0.4 %fusion.8 = f32[8,24,1791]{2,1,0:T(8,128)S(1)} fusion(f32[8,24,1792]{2,1,0:T(8,128)S(1)} %pad_subtract_fusion.3, f32[24,1791]{1,0:T(8,128)S(1)} %bitcast.47), kind=kLoop, calls=%fused_computation.23 | loop fusion | flops 687744 | bytes 4298400 | tf_op jit(solution)/shard_map/mul | solution.py:72
  12.6 0.5 %pad_subtract_fusion.7 = f32[8,16,1792]{2,1,0:T(8,128)S(1)} fusion(f32[8,24,1791]{2,1,0:T(8,128)S(1)} %fusion.8, f32[8,23,1792]{2,1,0:T(8,128)S(1)} %fusion.9, f32[8,24,1792]{2,1,0:T(8,128)S(1)} %pad_subtract_fusion.3), kind=kLoop, calls=%fused_computation.71 | loop fusion | flops 917504 | bytes 4529408 | tf_op jit(solution)/shard_map/sub | solution.py:81
  13.1 0.1 collective-permute-done.1
  13.3 1.4 %copy_select_fusion.1 = (f32[10,4,1792]{2,1,0:T(4,128)S(1)}, f32[10,4,1792]{2,1,0:T(4,128)S(1)}) fusion(f32[10,4,1792]{2,0,1:T(8,128)} %collective-permute-done.1, pred[]{:T(512)S(6)} %eq.7, f32[10,4,1792]{2,0,1:T(8,128)S(1)} %collective-permute-done), kind=kLoop, calls=%fused_computation.129 | loop fusion | flops 143360 | bytes 1146881 | tf_op jit(solution)/shard_map/jit(_where)/select_n | solution.py:47
  14.6 0.2 pad_maximum_fusion.2
  15.0 0.1 or_select_fusion
  15.1 0.1 fusion.20
  15.4 0.1 fusion.27
  15.5 0.3 fusion.26
  15.8 0.5 %fusion.30 = f32[8,12,1792]{2,1,0:T(8,128)S(1)} fusion(f32[10,12,1792]{2,1,0:T(8,128)S(1)} %fusion.20, f32[8,12,1791]{2,1,0:T(8,128)S(1)} %fusion.26, f32[8,11,1792]{2,1,0:T(8,128)S(1)} %fusion.27), kind=kLoop, calls=%fused_computation.70 | loop fusion | flops 688128 | bytes 2694784 | tf_op jit(solution)/shard_map/sub | solution.py:81
  16.3 0.2 fusion.22
  16.5 0.3 fusion.21
  16.8 0.4 fusion.25
  17.2 0.1 fusion.44
  17.3 0.2 fusion.43
  17.5 0.2 fusion.47
  17.9 0.2 fusion.41
  18.1 0.1 fusion.48
  18.2 0.2 pad_subtract_fusion.13
  18.5 0.3 fusion.32
  18.8 1.8 %collective-permute-start.2 = (f32[16,1792]{1,0:T(8,128)S(1)}, f32[16,1792]{1,0:T(8,128)S(1)}, u32[]{:S(2)}, u32[]{:S(2)}) collective-permute-start(f32[16,1792]{1,0:T(8,128)S(1)} %fusion.32), channel_id=1, source_target_pairs={{0,8},{8,0},{16,24},{24,16},{1,9},{9,1},{17,25},{25,17},{2,10},{10... | collective-permute-start | bytes 344072 | tf_op jit(solution)/shard_map/ppermute | solution.py:56
  20.6 1.2 %collective-permute-start.3 = (f32[16,1792]{1,0:T(8,128)S(1)}, f32[16,1792]{1,0:T(8,128)S(1)}, u32[]{:S(2)}, u32[]{:S(2)}) collective-permute-start(f32[16,1792]{1,0:T(8,128)S(1)} %fusion.32), channel_id=1, source_target_pairs={{0,16},{8,24},{16,0},{24,8},{1,17},{9,25},{17,1},{25,9},{2,18},{10... | collective-permute-start | bytes 344072 | tf_op jit(solution)/shard_map/ppermute | solution.py:56
  21.9 1.3 %collective-permute-done.2 = f32[16,1792]{1,0:T(8,128)S(1)} collective-permute-done((f32[16,1792]{1,0:T(8,128)S(1)}, f32[16,1792]{1,0:T(8,128)S(1)}, u32[]{:S(2)}, u32[]{:S(2)}) %collective-permute-start.2) | collective-permute-done | bytes 114720 | tf_op jit(solution)/shard_map/ppermute | solution.py:56
  23.2 3.5 %collective-permute-done.3 = f32[16,1792]{1,0:T(8,128)S(1)} collective-permute-done((f32[16,1792]{1,0:T(8,128)S(1)}, f32[16,1792]{1,0:T(8,128)S(1)}, u32[]{:S(2)}, u32[]{:S(2)}) %collective-permute-start.3) | collective-permute-done | bytes 114720 | tf_op jit(solution)/shard_map/ppermute | solution.py:56
  27.0 5.2 %collective-permute-start.6 = (f32[8,4,1792]{2,1,0:T(4,128)S(1)}, f32[8,4,1792]{2,1,0:T(4,128)S(1)}, u32[]{:S(2)}, u32[]{:S(2)}) collective-permute-start(f32[8,4,1792]{2,1,0:T(4,128)S(1)} %get-tuple-element.16), channel_id=1, source_target_pairs={{1,2},{3,4},{5,6},{2,1},{4,3},{6,5},{9,10},{11,12},{13,14},{10,9},... | collective-permute-start | bytes 688136 | tf_op jit(solution)/shard_map/ppermute | solution.py:36
  32.3 0.2 pad_maximum_fusion.3
  32.5 0.2 fusion.7
  32.7 0.4 %fusion.6 = f32[8,24,1791]{2,1,0:T(8,128)S(1)} fusion(f32[8,24,1792]{2,1,0:T(8,128)S(1)} %pad_maximum_fusion.3, f32[24,1791]{1,0:T(8,128)S(1)} %bitcast.40), kind=kLoop, calls=%fused_computation.19 | loop fusion | flops 687744 | bytes 4298400 | tf_op jit(solution)/shard_map/mul | solution.py:72
  33.1 0.6 %pad_subtract_fusion.2 = f32[8,24,1792]{2,1,0:T(8,128)S(1)} fusion(f32[8,24,1791]{2,1,0:T(8,128)S(1)} %fusion.6, f32[8,23,1792]{2,1,0:T(8,128)S(1)} %fusion.7, f32[8,4,1792]{2,1,0:T(4,128)S(1)} %get-tuple-element.27, f32[8,16,1792]{2,1,0:T(8,128)S(1)} %broadcast_multiply_fusion, f32[8,4,1792]{2,1,0:T(4,128)S(1)} %get-tuple-element.26), kind=kLoop, calls=%fused_computation.45 | loop fusion | flops 2064384 | bytes 5446912 | tf_op jit(solution)/shard_map/sub | solution.py:81
  33.7 0.2 fusion.5
  33.9 0.4 %fusion.4 = f32[8,24,1791]{2,1,0:T(8,128)S(1)} fusion(f32[8,24,1792]{2,1,0:T(8,128)S(1)} %pad_subtract_fusion.2, f32[24,1791]{1,0:T(8,128)S(1)} %bitcast.41), kind=kLoop, calls=%fused_computation.15 | loop fusion | flops 687744 | bytes 4298400 | tf_op jit(solution)/shard_map/mul | solution.py:72
  34.3 0.5 %pad_subtract_fusion.1 = f32[8,24,1792]{2,1,0:T(8,128)S(1)} fusion(f32[8,24,1791]{2,1,0:T(8,128)S(1)} %fusion.4, f32[8,23,1792]{2,1,0:T(8,128)S(1)} %fusion.5, f32[8,24,1792]{2,1,0:T(8,128)S(1)} %pad_subtract_fusion.2), kind=kLoop, calls=%fused_computation.44 | loop fusion | flops 1376256 | bytes 5446912 | tf_op jit(solution)/shard_map/sub | solution.py:81
  34.8 0.2 fusion.3
  35.0 0.4 %fusion.2 = f32[8,24,1791]{2,1,0:T(8,128)S(1)} fusion(f32[8,24,1792]{2,1,0:T(8,128)S(1)} %pad_subtract_fusion.1, f32[24,1791]{1,0:T(8,128)S(1)} %bitcast.42), kind=kLoop, calls=%fused_computation.11 | loop fusion | flops 687744 | bytes 4298400 | tf_op jit(solution)/shard_map/mul | solution.py:72
  35.4 0.5 %pad_subtract_fusion = f32[8,24,1792]{2,1,0:T(8,128)S(1)} fusion(f32[8,24,1791]{2,1,0:T(8,128)S(1)} %fusion.2, f32[8,23,1792]{2,1,0:T(8,128)S(1)} %fusion.3, f32[8,24,1792]{2,1,0:T(8,128)S(1)} %pad_subtract_fusion.1), kind=kLoop, calls=%fused_computation.43 | loop fusion | flops 1376256 | bytes 5446912 | tf_op jit(solution)/shard_map/sub | solution.py:81
  35.9 0.2 fusion.1
  36.1 0.4 %fusion = f32[8,24,1791]{2,1,0:T(8,128)S(1)} fusion(f32[8,24,1792]{2,1,0:T(8,128)S(1)} %pad_subtract_fusion, f32[24,1791]{1,0:T(8,128)S(1)} %bitcast.43), kind=kLoop, calls=%fused_computation.7 | loop fusion | flops 687744 | bytes 4298400 | tf_op jit(solution)/shard_map/mul | solution.py:72
  36.5 0.5 %pad_subtract_fusion.5 = f32[8,16,1792]{2,1,0:T(8,128)S(1)} fusion(f32[8,24,1791]{2,1,0:T(8,128)S(1)} %fusion, f32[8,23,1792]{2,1,0:T(8,128)S(1)} %fusion.1, f32[8,24,1792]{2,1,0:T(8,128)S(1)} %pad_subtract_fusion), kind=kLoop, calls=%fused_computation.51 | loop fusion | flops 917504 | bytes 4529408 | tf_op jit(solution)/shard_map/sub | solution.py:81
  37.2 0.2 fusion.39
  37.4 0.2 pad_subtract_fusion.12
  37.7 0.2 fusion.37
  37.9 0.2 pad_subtract_fusion.11
  38.2 0.2 fusion.35
  38.4 0.2 pad_subtract_fusion.10
  38.7 0.2 fusion.33
  38.9 0.2 pad_subtract_fusion.9
  39.2 1.1 %add_add_fusion = f32[8,16,1792]{2,1,0:T(8,128)} fusion(f32[8,16,1792]{2,1,0:T(8,128)S(1)} %copy-done, f32[8,16,1792]{2,1,0:T(8,128)S(1)} %pad_subtract_fusion.5, f32[8,4,1792]{2,1,0:T(4,128)S(1)} %get-tuple-element.23, f32[8,4,1792]{2,1,0:T(4,128)S(1)} %get-tuple-element.22, pred[]{:T(512)S(6)} %eq.7), kind=kLoop, calls=%fused_computation.78 | loop fusion | flops 688128 | bytes 3211265 | tf_op jit(solution)/shard_map/add | solution.py:150
  (53 shorter events, 1.5 us)
Async XLA Ops:
  1.4 5.6 %copy-start.1 = (bf16[8,4,16,1792]{3,2,1,0:T(8,128)(2,1)S(1)}, bf16[8,4,16,1792]{3,2,1,0:T(8,128)(2,1)}, u32[]{:S(2)}) copy-start(bf16[8,4,16,1792]{3,2,1,0:T(8,128)(2,1)} %param.8) | copy-start | bytes 5505028
  1.4 5.6 %copy-start.4 = (f32[4,16,1792]{2,1,0:T(8,128)S(1)}, f32[4,16,1792]{2,1,0:T(8,128)}, u32[]{:S(2)}) copy-start(f32[4,16,1792]{2,1,0:T(8,128)} %param.9) | copy-start | bytes 1376260
  2.3 5.1 %collective-permute-start = (f32[10,4,1792]{2,0,1:T(8,128)}, f32[10,4,1792]{2,0,1:T(8,128)S(1)}, u32[]{:S(2)}, u32[]{:S(2)}) collective-permute-start(f32[10,4,1792]{2,0,1:T(8,128)} %copy.11), channel_id=1, source_target_pairs={{0,1},{2,3},{4,5},{6,7},{1,0},{3,2},{5,4},{7,6},{8,9},{10,11},{12,... | collective-permute-start | bytes 860168 | tf_op jit(solution)/shard_map/ppermute | solution.py:37
  2.5 10.8 %collective-permute-start.1 = (f32[10,4,1792]{2,0,1:T(8,128)S(1)}, f32[10,4,1792]{2,0,1:T(8,128)}, u32[]{:S(2)}, u32[]{:S(2)}) collective-permute-start(f32[10,4,1792]{2,0,1:T(8,128)S(1)} %copy.14), channel_id=1, source_target_pairs={{1,2},{3,4},{5,6},{2,1},{4,3},{6,5},{9,10},{11,12},{13,14},{10,9},... | collective-permute-start | bytes 860168 | tf_op jit(solution)/shard_map/ppermute | solution.py:36
  7.1 1.2 %copy-start = (f32[8,16,1792]{2,1,0:T(8,128)S(1)}, f32[8,16,1792]{2,1,0:T(8,128)}, u32[]{:S(2)}) copy-start(f32[8,16,1792]{2,1,0:T(8,128)} %param.7) | copy-start | bytes 2752516
  7.1 1.2 %copy-start.2 = (f32[16,1792]{1,0:T(8,128)S(1)}, f32[16,1792]{1,0:T(8,128)}, u32[]{:S(2)}) copy-start(f32[16,1792]{1,0:T(8,128)} %param.13) | copy-start | bytes 344068
  7.1 1.2 %copy-start.3 = (f32[16,1792]{1,0:T(8,128)S(1)}, f32[16,1792]{1,0:T(8,128)}, u32[]{:S(2)}) copy-start(f32[16,1792]{1,0:T(8,128)} %param.12) | copy-start | bytes 344068
  18.5 8.2 %copy-start.5 = (f32[16,1792]{1,0:T(8,128)S(1)}, f32[16,1792]{1,0:T(8,128)}, u32[]{:S(2)}) copy-start(f32[16,1792]{1,0:T(8,128)} %param.10) | copy-start | bytes 344068
  18.5 8.2 %copy-start.6 = (s32[16,1792]{1,0:T(8,128)S(1)}, s32[16,1792]{1,0:T(8,128)}, u32[]{:S(2)}) copy-start(s32[16,1792]{1,0:T(8,128)} %param.11) | copy-start | bytes 344068
  18.8 4.5 %collective-permute-start.2 = (f32[16,1792]{1,0:T(8,128)S(1)}, f32[16,1792]{1,0:T(8,128)S(1)}, u32[]{:S(2)}, u32[]{:S(2)}) collective-permute-start(f32[16,1792]{1,0:T(8,128)S(1)} %fusion.32), channel_id=1, source_target_pairs={{0,8},{8,0},{16,24},{24,16},{1,9},{9,1},{17,25},{25,17},{2,10},{10... | collective-permute-start | bytes 344072 | tf_op jit(solution)/shard_map/ppermute | solution.py:56
  20.6 6.1 %collective-permute-start.3 = (f32[16,1792]{1,0:T(8,128)S(1)}, f32[16,1792]{1,0:T(8,128)S(1)}, u32[]{:S(2)}, u32[]{:S(2)}) collective-permute-start(f32[16,1792]{1,0:T(8,128)S(1)} %fusion.32), channel_id=1, source_target_pairs={{0,16},{8,24},{16,0},{24,8},{1,17},{9,25},{17,1},{25,9},{2,18},{10... | collective-permute-start | bytes 344072 | tf_op jit(solution)/shard_map/ppermute | solution.py:56
  21.8 4.9 %collective-permute-start.4 = (f32[16,1792]{1,0:T(8,128)S(1)}, f32[16,1792]{1,0:T(8,128)S(1)}, u32[]{:S(2)}, u32[]{:S(2)}) collective-permute-start(f32[16,1792]{1,0:T(8,128)S(1)} %fusion.32), channel_id=1, source_target_pairs={{0,24},{8,16},{16,8},{24,0},{1,25},{9,17},{17,9},{25,1},{2,26},{10... | collective-permute-start | bytes 344072 | tf_op jit(solution)/shard_map/ppermute | solution.py:56
  26.9 5.3 %collective-permute-start.5 = (f32[8,4,1792]{2,1,0:T(4,128)S(1)}, f32[8,4,1792]{2,1,0:T(4,128)S(1)}, u32[]{:S(2)}, u32[]{:S(2)}) collective-permute-start(f32[8,4,1792]{2,1,0:T(4,128)S(1)} %get-tuple-element.17), channel_id=1, source_target_pairs={{0,1},{2,3},{4,5},{6,7},{1,0},{3,2},{5,4},{7,6},{8,9},{10,11},{12,... | collective-permute-start | bytes 688136 | tf_op jit(solution)/shard_map/ppermute | solution.py:37
  27.0 10.1 %collective-permute-start.6 = (f32[8,4,1792]{2,1,0:T(4,128)S(1)}, f32[8,4,1792]{2,1,0:T(4,128)S(1)}, u32[]{:S(2)}, u32[]{:S(2)}) collective-permute-start(f32[8,4,1792]{2,1,0:T(4,128)S(1)} %get-tuple-element.16), channel_id=1, source_target_pairs={{1,2},{3,4},{5,6},{2,1},{4,3},{6,5},{9,10},{11,12},{13,14},{10,9},... | collective-permute-start | bytes 688136 | tf_op jit(solution)/shard_map/ppermute | solution.py:36

commit v26 on v22

--- a/solution.py
+++ b/solution.py
@@ -121,7 +121,9 @@
     main, far = lax.optimization_barrier((main, far))
     band = full_band(stacked, near, far, odd)
     coef_band = band[members:]
-    strip = jnp.where(odd, band[:, row_count - STEPS :], band[:, : 3 * STEPS])
+    strip = lax.dynamic_slice_in_dim(
+        band, jnp.where(odd, row_count - STEPS, 0), 3 * STEPS, axis=1
+    )
     edge = localize_inner(strip[:members], strip[members:])
     localized = jnp.where(
         odd,

time: 39.5 us -> 41.3 us (1.046)
  local copies, waits for them, and re-layouts: 0.56 us -> 1.95 us
  starting transfers between devices: 14.1 us -> 12.9 us
  waiting for transfers between devices: 4.17 us -> 5.03 us
  other arithmetic: 19.8 us -> 20.6 us
    ppermute x3, waiting for transfers between devices: 3.47 us -> 4.73 us  [partner(): return lax.ppermute(part, 'mem', [(i, i ^ stride) for i in range(count)])]
    ppermute x2, starting transfers between devices: 10.9 us -> 9.73 us  [split_exchange(): far = lax.ppermute(jnp.where(odd, tail, head), 'tile', pairs(1))]
    select_n x2 -> x1, other arithmetic: 0.49 us -> 1.39 us  [full_band(): jnp.where(odd, near, far)]
    select_n x1, local copies, waits for them, and re-layouts: 0.07 us -> 0.83 us  [split_exchange(): near = lax.ppermute(jnp.where(odd, head, tail), 'tile', pairs(0))]
    unnamed x12, local copies, waits for them, and re-layouts: 0.04 us -> 0.55 us
  transfers between devices with their start and end apart: 7 -> 7, of which waited for: 4 -> 3; matrix products, arithmetic and copies ran while one was open for 27% -> 25% of each run, Pallas kernels for 0% -> 0%
where the time goes in v26:
time: 41.3 us; the launch traced here: 41.1 us
  other arithmetic  20.6 us (50%)
  starting transfers between devices  12.9 us (31%)
  waiting for transfers between devices  5.03 us (12%)
  local copies, waits for them, and re-layouts  1.95 us (5%)
  between operations  0.58 us (1%)
    ppermute x2, starting transfers between devices, split_exchange(): far = lax.ppermute(jnp.where(odd, tail, head), 'tile', pairs(1))  9.73 us
    sub x16, other arithmetic, diffuse(): values + jnp.concatenate([col_flux, zeros_col], -1)  6.2 us
    mul x16, other arithmetic, diffuse(): col_coef[..., :, :-1] * (values[..., :, 1:] - values[..., :, :-1])  5.13 us
    ppermute x3, waiting for transfers between devices, partner(): return lax.ppermute(part, 'mem', [(i, i ^ stride) for i in range(count)])  4.73 us
    ppermute x3, starting transfers between devices, partner(): return lax.ppermute(part, 'mem', [(i, i ^ stride) for i in range(count)])  3.09 us
    mul x16, other arithmetic, diffuse(): row_coef[..., :-1, :] * (values[..., 1:, :] - values[..., :-1, :])  2.37 us
    select_n x2, other arithmetic, split_exchange(): far = lax.ppermute(jnp.where(odd, tail, head), 'tile', pairs(1))  1.43 us
    select_n x1, other arithmetic, full_band(): jnp.where(odd, near, far)  1.39 us
  transfers between devices with their start and end apart: 7, of which 3 were waited for; matrix products, arithmetic and copies ran while one was open for 25% of the time, Pallas kernels for 0%

profile of v26, /device:TPU:1, one launch (start us, length us, event | category | flops | bytes accessed | tf_op | source)
XLA Modules:
  0.0 41.1 jit_solution(11071998330358713004)
XLA Ops:
  0.0 1.0 %select_bitcast_fusion = f32[1,16,1792]{2,1,0:T(8,128)S(1)} fusion(f32[16,1792]{1,0:T(8,128)} %param.12, pred[16]{0:T(512)(128)(4,1)S(1)} %add_compare_fusion), kind=kLoop, calls=%fused_computation.141 | loop fusion | flops 28672 | bytes 229392 | tf_op jit(solution)/shard_map/broadcast_in_dim | solution.py:109
  1.0 1.4 %broadcast_select_fusion.2 = (f32[10,4,1792]{2,1,0:T(4,128)S(1)}, f32[10,4,1792]{2,1,0:T(4,128)S(1)}, f32[10,4,1792]{2,1,0:T(4,128)S(1)}) fusion(pred[]{:T(512)S(6)} %eq.7, f32[1,16,1792]{2,1,0:T(8,128)} %bitcast.49, f32[1,16,1792]{2,1,0:T(8,128)S(1)} %select_bitcast_fusion, f32[8,16,1792]{2,1,0:T(8,128)} %param.7), kind=kLoop, calls=%fused_computation.125 | loop fusion | flops 358400 | bytes 2007041 | tf_op jit(solution)/shard_map/jit(_where)/select_n | solution.py:36
  2.4 0.8 %copy.11 = f32[10,4,1792]{2,0,1:T(8,128)} copy(f32[10,4,1792]{2,1,0:T(4,128)S(1)} %bitcast.57) | data formatting | bytes 573440 | tf_op jit(solution)/shard_map/jit(_where)/select_n | solution.py:37
  3.4 4.5 %collective-permute-start.1 = (f32[10,4,1792]{2,0,1:T(8,128)S(1)}, f32[10,4,1792]{2,0,1:T(8,128)}, u32[]{:S(2)}, u32[]{:S(2)}) collective-permute-start(f32[10,4,1792]{2,0,1:T(8,128)S(1)} %copy.14), channel_id=1, source_target_pairs={{1,2},{3,4},{5,6},{2,1},{4,3},{6,5},{9,10},{11,12},{13,14},{10,9},... | collective-permute-start | bytes 860168 | tf_op jit(solution)/shard_map/ppermute | solution.py:36
  8.0 0.4 multiply_reduce_fusion
  8.4 0.2 broadcast_select_fusion.1
  8.6 0.5 %copy-done = f32[8,16,1792]{2,1,0:T(8,128)S(1)} copy-done((f32[8,16,1792]{2,1,0:T(8,128)S(1)}, f32[8,16,1792]{2,1,0:T(8,128)}, u32[]{:S(2)}) %copy-start) | copy-done | bytes 917528
  9.1 0.2 pad_maximum_fusion
  9.4 0.2 fusion.15
  9.6 0.4 %fusion.14 = f32[8,24,1791]{2,1,0:T(8,128)S(1)} fusion(f32[10,24,1792]{2,1,0:T(8,128)S(1)} %pad_maximum_fusion, f32[24,1791]{1,0:T(8,128)S(1)} %bitcast.45), kind=kLoop, calls=%fused_computation.33 | loop fusion | flops 687744 | bytes 4298400 | tf_op jit(solution)/shard_map/mul | solution.py:72
  10.0 0.5 %fusion.18 = f32[8,24,1792]{2,1,0:T(8,128)S(1)} fusion(f32[10,24,1792]{2,1,0:T(8,128)S(1)} %pad_maximum_fusion, f32[8,24,1791]{2,1,0:T(8,128)S(1)} %fusion.14, f32[8,23,1792]{2,1,0:T(8,128)S(1)} %fusion.15), kind=kLoop, calls=%fused_computation.39 | loop fusion | flops 1376256 | bytes 5446912 | tf_op jit(solution)/shard_map/sub | solution.py:81
  10.5 0.2 fusion.13
  10.7 0.4 %fusion.12 = f32[8,24,1791]{2,1,0:T(8,128)S(1)} fusion(f32[8,24,1792]{2,1,0:T(8,128)S(1)} %fusion.18, f32[24,1791]{1,0:T(8,128)S(1)} %bitcast.46), kind=kLoop, calls=%fused_computation.29 | loop fusion | flops 687744 | bytes 4298400 | tf_op jit(solution)/shard_map/mul | solution.py:72
  11.1 0.5 %pad_subtract_fusion.4 = f32[8,24,1792]{2,1,0:T(8,128)S(1)} fusion(f32[8,24,1791]{2,1,0:T(8,128)S(1)} %fusion.12, f32[8,23,1792]{2,1,0:T(8,128)S(1)} %fusion.13, f32[8,24,1792]{2,1,0:T(8,128)S(1)} %fusion.18), kind=kLoop, calls=%fused_computation.45 | loop fusion | flops 1376256 | bytes 5446912 | tf_op jit(solution)/shard_map/sub | solution.py:81
  11.6 0.2 fusion.11
  11.8 0.4 %fusion.10 = f32[8,24,1791]{2,1,0:T(8,128)S(1)} fusion(f32[8,24,1792]{2,1,0:T(8,128)S(1)} %pad_subtract_fusion.4, f32[24,1791]{1,0:T(8,128)S(1)} %bitcast.47), kind=kLoop, calls=%fused_computation.25 | loop fusion | flops 687744 | bytes 4298400 | tf_op jit(solution)/shard_map/mul | solution.py:72
  12.3 0.5 %pad_subtract_fusion.3 = f32[8,24,1792]{2,1,0:T(8,128)S(1)} fusion(f32[8,24,1791]{2,1,0:T(8,128)S(1)} %fusion.10, f32[8,23,1792]{2,1,0:T(8,128)S(1)} %fusion.11, f32[8,24,1792]{2,1,0:T(8,128)S(1)} %pad_subtract_fusion.4), kind=kLoop, calls=%fused_computation.44 | loop fusion | flops 1376256 | bytes 5446912 | tf_op jit(solution)/shard_map/sub | solution.py:81
  12.7 0.2 fusion.9
  12.9 0.4 %fusion.8 = f32[8,24,1791]{2,1,0:T(8,128)S(1)} fusion(f32[8,24,1792]{2,1,0:T(8,128)S(1)} %pad_subtract_fusion.3, f32[24,1791]{1,0:T(8,128)S(1)} %bitcast.48), kind=kLoop, calls=%fused_computation.21 | loop fusion | flops 687744 | bytes 4298400 | tf_op jit(solution)/shard_map/mul | solution.py:72
  13.4 0.5 %pad_subtract_fusion.7 = f32[8,16,1792]{2,1,0:T(8,128)S(1)} fusion(f32[8,24,1791]{2,1,0:T(8,128)S(1)} %fusion.8, f32[8,23,1792]{2,1,0:T(8,128)S(1)} %fusion.9, f32[8,24,1792]{2,1,0:T(8,128)S(1)} %pad_subtract_fusion.3), kind=kLoop, calls=%fused_computation.66 | loop fusion | flops 917504 | bytes 4529408 | tf_op jit(solution)/shard_map/sub | solution.py:81
  13.9 0.3 collective-permute-done.1
  14.2 1.4 %copy_select_fusion.1 = (f32[10,4,1792]{2,1,0:T(4,128)S(1)}, f32[10,4,1792]{2,1,0:T(4,128)S(1)}) fusion(f32[10,4,1792]{2,0,1:T(8,128)} %collective-permute-done.1, pred[]{:T(512)S(6)} %eq.7, f32[10,4,1792]{2,0,1:T(8,128)S(1)} %collective-permute-done), kind=kLoop, calls=%fused_computation.122 | loop fusion | flops 143360 | bytes 1146881 | tf_op jit(solution)/shard_map/jit(_where)/select_n | solution.py:47
  15.6 0.3 pad_maximum_fusion.2
  16.1 0.2 fusion.25
  16.3 0.3 fusion.24
  16.6 0.5 %fusion.28 = f32[8,12,1792]{2,1,0:T(8,128)S(1)} fusion(f32[10,24,1792]{2,1,0:T(8,128)S(1)} %pad_maximum_fusion.2, s32[]{:T(128)S(6)} %select_n.105, f32[8,12,1791]{2,1,0:T(8,128)S(1)} %fusion.24, f32[8,11,1792]{2,1,0:T(8,128)S(1)} %fusion.25), kind=kLoop, calls=%fused_computation.65 | loop fusion | flops 688128 | bytes 2694788 | tf_op jit(solution)/shard_map/sub | solution.py:81
  17.1 0.2 fusion.20
  17.3 0.3 fusion.19
  17.6 0.4 fusion.23
  18.0 0.1 fusion.42
  18.1 0.2 fusion.41
  18.3 0.2 fusion.45
  18.6 0.1 fusion.40
  18.7 0.2 fusion.39
  18.9 0.1 fusion.47
  19.0 0.2 pad_subtract_fusion.13
  19.2 0.3 fusion.30
  19.5 1.8 %collective-permute-start.2 = (f32[16,1792]{1,0:T(8,128)S(1)}, f32[16,1792]{1,0:T(8,128)S(1)}, u32[]{:S(2)}, u32[]{:S(2)}) collective-permute-start(f32[16,1792]{1,0:T(8,128)S(1)} %fusion.30), channel_id=1, source_target_pairs={{0,8},{8,0},{16,24},{24,16},{1,9},{9,1},{17,25},{25,17},{2,10},{10... | collective-permute-start | bytes 344072 | tf_op jit(solution)/shard_map/ppermute | solution.py:56
  21.4 1.2 %collective-permute-start.3 = (f32[16,1792]{1,0:T(8,128)S(1)}, f32[16,1792]{1,0:T(8,128)S(1)}, u32[]{:S(2)}, u32[]{:S(2)}) collective-permute-start(f32[16,1792]{1,0:T(8,128)S(1)} %fusion.30), channel_id=1, source_target_pairs={{0,16},{8,24},{16,0},{24,8},{1,17},{9,25},{17,1},{25,9},{2,18},{10... | collective-permute-start | bytes 344072 | tf_op jit(solution)/shard_map/ppermute | solution.py:56
  22.7 1.1 %collective-permute-done.2 = f32[16,1792]{1,0:T(8,128)S(1)} collective-permute-done((f32[16,1792]{1,0:T(8,128)S(1)}, f32[16,1792]{1,0:T(8,128)S(1)}, u32[]{:S(2)}, u32[]{:S(2)}) %collective-permute-start.2) | collective-permute-done | bytes 114720 | tf_op jit(solution)/shard_map/ppermute | solution.py:56
  23.8 3.7 %collective-permute-done.3 = f32[16,1792]{1,0:T(8,128)S(1)} collective-permute-done((f32[16,1792]{1,0:T(8,128)S(1)}, f32[16,1792]{1,0:T(8,128)S(1)}, u32[]{:S(2)}, u32[]{:S(2)}) %collective-permute-start.3) | collective-permute-done | bytes 114720 | tf_op jit(solution)/shard_map/ppermute | solution.py:56
  27.8 5.2 %collective-permute-start.6 = (f32[8,4,1792]{2,1,0:T(4,128)S(1)}, f32[8,4,1792]{2,1,0:T(4,128)S(1)}, u32[]{:S(2)}, u32[]{:S(2)}) collective-permute-start(f32[8,4,1792]{2,1,0:T(4,128)S(1)} %get-tuple-element.16), channel_id=1, source_target_pairs={{1,2},{3,4},{5,6},{2,1},{4,3},{6,5},{9,10},{11,12},{13,14},{10,9},... | collective-permute-start | bytes 688136 | tf_op jit(solution)/shard_map/ppermute | solution.py:36
  33.1 0.2 pad_maximum_fusion.3
  33.3 0.2 fusion.7
  33.5 0.4 %fusion.6 = f32[8,24,1791]{2,1,0:T(8,128)S(1)} fusion(f32[8,24,1792]{2,1,0:T(8,128)S(1)} %pad_maximum_fusion.3, f32[24,1791]{1,0:T(8,128)S(1)} %bitcast.41), kind=kLoop, calls=%fused_computation.17 | loop fusion | flops 687744 | bytes 4298400 | tf_op jit(solution)/shard_map/mul | solution.py:72
  33.9 0.6 %pad_subtract_fusion.2 = f32[8,24,1792]{2,1,0:T(8,128)S(1)} fusion(f32[8,24,1791]{2,1,0:T(8,128)S(1)} %fusion.6, f32[8,23,1792]{2,1,0:T(8,128)S(1)} %fusion.7, f32[8,4,1792]{2,1,0:T(4,128)S(1)} %get-tuple-element.27, f32[8,16,1792]{2,1,0:T(8,128)S(1)} %broadcast_multiply_fusion, f32[8,4,1792]{2,1,0:T(4,128)S(1)} %get-tuple-element.26), kind=kLoop, calls=%fused_computation.43 | loop fusion | flops 2064384 | bytes 5446912 | tf_op jit(solution)/shard_map/sub | solution.py:81
  34.5 0.2 fusion.5
  34.7 0.4 %fusion.4 = f32[8,24,1791]{2,1,0:T(8,128)S(1)} fusion(f32[8,24,1792]{2,1,0:T(8,128)S(1)} %pad_subtract_fusion.2, f32[24,1791]{1,0:T(8,128)S(1)} %bitcast.42), kind=kLoop, calls=%fused_computation.13 | loop fusion | flops 687744 | bytes 4298400 | tf_op jit(solution)/shard_map/mul | solution.py:72
  35.1 0.5 %pad_subtract_fusion.1 = f32[8,24,1792]{2,1,0:T(8,128)S(1)} fusion(f32[8,24,1791]{2,1,0:T(8,128)S(1)} %fusion.4, f32[8,23,1792]{2,1,0:T(8,128)S(1)} %fusion.5, f32[8,24,1792]{2,1,0:T(8,128)S(1)} %pad_subtract_fusion.2), kind=kLoop, calls=%fused_computation.42 | loop fusion | flops 1376256 | bytes 5446912 | tf_op jit(solution)/shard_map/sub | solution.py:81
  35.6 0.2 fusion.3
  35.8 0.4 %fusion.2 = f32[8,24,1791]{2,1,0:T(8,128)S(1)} fusion(f32[8,24,1792]{2,1,0:T(8,128)S(1)} %pad_subtract_fusion.1, f32[24,1791]{1,0:T(8,128)S(1)} %bitcast.43), kind=kLoop, calls=%fused_computation.9 | loop fusion | flops 687744 | bytes 4298400 | tf_op jit(solution)/shard_map/mul | solution.py:72
  36.2 0.5 %pad_subtract_fusion = f32[8,24,1792]{2,1,0:T(8,128)S(1)} fusion(f32[8,24,1791]{2,1,0:T(8,128)S(1)} %fusion.2, f32[8,23,1792]{2,1,0:T(8,128)S(1)} %fusion.3, f32[8,24,1792]{2,1,0:T(8,128)S(1)} %pad_subtract_fusion.1), kind=kLoop, calls=%fused_computation.41 | loop fusion | flops 1376256 | bytes 5446912 | tf_op jit(solution)/shard_map/sub | solution.py:81
  36.7 0.2 fusion.1
  36.9 0.4 %fusion = f32[8,24,1791]{2,1,0:T(8,128)S(1)} fusion(f32[8,24,1792]{2,1,0:T(8,128)S(1)} %pad_subtract_fusion, f32[24,1791]{1,0:T(8,128)S(1)} %bitcast.44), kind=kLoop, calls=%fused_computation.5 | loop fusion | flops 687744 | bytes 4298400 | tf_op jit(solution)/shard_map/mul | solution.py:72
  37.3 0.5 %pad_subtract_fusion.5 = f32[8,16,1792]{2,1,0:T(8,128)S(1)} fusion(f32[8,24,1791]{2,1,0:T(8,128)S(1)} %fusion, f32[8,23,1792]{2,1,0:T(8,128)S(1)} %fusion.1, f32[8,24,1792]{2,1,0:T(8,128)S(1)} %pad_subtract_fusion), kind=kLoop, calls=%fused_computation.46 | loop fusion | flops 917504 | bytes 4529408 | tf_op jit(solution)/shard_map/sub | solution.py:81
  38.0 0.2 fusion.37
  38.2 0.2 pad_subtract_fusion.12
  38.5 0.2 fusion.35
  38.7 0.2 pad_subtract_fusion.11
  39.0 0.2 fusion.33
  39.2 0.2 pad_subtract_fusion.10
  39.5 0.2 fusion.31
  39.6 0.2 pad_subtract_fusion.9
  40.0 1.1 %add_add_fusion = f32[8,16,1792]{2,1,0:T(8,128)} fusion(f32[8,16,1792]{2,1,0:T(8,128)S(1)} %copy-done, f32[8,16,1792]{2,1,0:T(8,128)S(1)} %pad_subtract_fusion.5, f32[8,4,1792]{2,1,0:T(4,128)S(1)} %get-tuple-element.23, f32[8,4,1792]{2,1,0:T(4,128)S(1)} %get-tuple-element.22, pred[]{:T(512)S(6)} %eq.7), kind=kLoop, calls=%fused_computation.73 | loop fusion | flops 688128 | bytes 3211265 | tf_op jit(solution)/shard_map/add | solution.py:149
  (47 shorter events, 1.3 us)
Async XLA Ops:
  2.3 5.6 %copy-start.1 = (bf16[8,4,16,1792]{3,2,1,0:T(8,128)(2,1)S(1)}, bf16[8,4,16,1792]{3,2,1,0:T(8,128)(2,1)}, u32[]{:S(2)}) copy-start(bf16[8,4,16,1792]{3,2,1,0:T(8,128)(2,1)} %param.8) | copy-start | bytes 5505028
  2.4 5.6 %copy-start.3 = (f32[4,16,1792]{2,1,0:T(8,128)S(1)}, f32[4,16,1792]{2,1,0:T(8,128)}, u32[]{:S(2)}) copy-start(f32[4,16,1792]{2,1,0:T(8,128)} %param.9) | copy-start | bytes 1376260
  3.2 5.1 %collective-permute-start = (f32[10,4,1792]{2,0,1:T(8,128)}, f32[10,4,1792]{2,0,1:T(8,128)S(1)}, u32[]{:S(2)}, u32[]{:S(2)}) collective-permute-start(f32[10,4,1792]{2,0,1:T(8,128)} %copy.11), channel_id=1, source_target_pairs={{0,1},{2,3},{4,5},{6,7},{1,0},{3,2},{5,4},{7,6},{8,9},{10,11},{12,... | collective-permute-start | bytes 860168 | tf_op jit(solution)/shard_map/ppermute | solution.py:37
  3.4 10.8 %collective-permute-start.1 = (f32[10,4,1792]{2,0,1:T(8,128)S(1)}, f32[10,4,1792]{2,0,1:T(8,128)}, u32[]{:S(2)}, u32[]{:S(2)}) collective-permute-start(f32[10,4,1792]{2,0,1:T(8,128)S(1)} %copy.14), channel_id=1, source_target_pairs={{1,2},{3,4},{5,6},{2,1},{4,3},{6,5},{9,10},{11,12},{13,14},{10,9},... | collective-permute-start | bytes 860168 | tf_op jit(solution)/shard_map/ppermute | solution.py:36
  7.9 1.2 %copy-start = (f32[8,16,1792]{2,1,0:T(8,128)S(1)}, f32[8,16,1792]{2,1,0:T(8,128)}, u32[]{:S(2)}) copy-start(f32[8,16,1792]{2,1,0:T(8,128)} %param.7) | copy-start | bytes 2752516
  8.0 1.2 %copy-start.2 = (f32[16,1792]{1,0:T(8,128)S(1)}, f32[16,1792]{1,0:T(8,128)}, u32[]{:S(2)}) copy-start(f32[16,1792]{1,0:T(8,128)} %param.13) | copy-start | bytes 344068
  19.5 8.0 %copy-start.4 = (f32[16,1792]{1,0:T(8,128)S(1)}, f32[16,1792]{1,0:T(8,128)}, u32[]{:S(2)}) copy-start(f32[16,1792]{1,0:T(8,128)} %param.10) | copy-start | bytes 344068
  19.5 7.9 %copy-start.5 = (s32[16,1792]{1,0:T(8,128)S(1)}, s32[16,1792]{1,0:T(8,128)}, u32[]{:S(2)}) copy-start(s32[16,1792]{1,0:T(8,128)} %param.11) | copy-start | bytes 344068
  19.5 4.2 %collective-permute-start.2 = (f32[16,1792]{1,0:T(8,128)S(1)}, f32[16,1792]{1,0:T(8,128)S(1)}, u32[]{:S(2)}, u32[]{:S(2)}) collective-permute-start(f32[16,1792]{1,0:T(8,128)S(1)} %fusion.30), channel_id=1, source_target_pairs={{0,8},{8,0},{16,24},{24,16},{1,9},{9,1},{17,25},{25,17},{2,10},{10... | collective-permute-start | bytes 344072 | tf_op jit(solution)/shard_map/ppermute | solution.py:56
  21.4 6.1 %collective-permute-start.3 = (f32[16,1792]{1,0:T(8,128)S(1)}, f32[16,1792]{1,0:T(8,128)S(1)}, u32[]{:S(2)}, u32[]{:S(2)}) collective-permute-start(f32[16,1792]{1,0:T(8,128)S(1)} %fusion.30), channel_id=1, source_target_pairs={{0,16},{8,24},{16,0},{24,8},{1,17},{9,25},{17,1},{25,9},{2,18},{10... | collective-permute-start | bytes 344072 | tf_op jit(solution)/shard_map/ppermute | solution.py:56
  22.6 4.9 %collective-permute-start.4 = (f32[16,1792]{1,0:T(8,128)S(1)}, f32[16,1792]{1,0:T(8,128)S(1)}, u32[]{:S(2)}, u32[]{:S(2)}) collective-permute-start(f32[16,1792]{1,0:T(8,128)S(1)} %fusion.30), channel_id=1, source_target_pairs={{0,24},{8,16},{16,8},{24,0},{1,25},{9,17},{17,9},{25,1},{2,26},{10... | collective-permute-start | bytes 344072 | tf_op jit(solution)/shard_map/ppermute | solution.py:56
  27.7 5.3 %collective-permute-start.5 = (f32[8,4,1792]{2,1,0:T(4,128)S(1)}, f32[8,4,1792]{2,1,0:T(4,128)S(1)}, u32[]{:S(2)}, u32[]{:S(2)}) collective-permute-start(f32[8,4,1792]{2,1,0:T(4,128)S(1)} %get-tuple-element.17), channel_id=1, source_target_pairs={{0,1},{2,3},{4,5},{6,7},{1,0},{3,2},{5,4},{7,6},{8,9},{10,11},{12,... | collective-permute-start | bytes 688136 | tf_op jit(solution)/shard_map/ppermute | solution.py:37
  27.8 10.1 %collective-permute-start.6 = (f32[8,4,1792]{2,1,0:T(4,128)S(1)}, f32[8,4,1792]{2,1,0:T(4,128)S(1)}, u32[]{:S(2)}, u32[]{:S(2)}) collective-permute-start(f32[8,4,1792]{2,1,0:T(4,128)S(1)} %get-tuple-element.16), channel_id=1, source_target_pairs={{1,2},{3,4},{5,6},{2,1},{4,3},{6,5},{9,10},{11,12},{13,14},{10,9},... | collective-permute-start | bytes 688136 | tf_op jit(solution)/shard_map/ppermute | solution.py:36

commit v27 on v22

--- a/solution.py
+++ b/solution.py
@@ -118,17 +118,20 @@
     near, far, odd = split_exchange(stacked, STEPS)
     partial = near_band(stacked, near, odd)
     main = localize(partial[:members], partial[members:])[:, STEPS : STEPS + row_count]
-    main, far = lax.optimization_barrier((main, far))
+    inner = jnp.sum(mix * main, 0)
+    inner, far = lax.optimization_barrier((inner, far))
     band = full_band(stacked, near, far, odd)
     coef_band = band[members:]
     strip = jnp.where(odd, band[:, row_count - STEPS :], band[:, : 3 * STEPS])
     edge = localize_inner(strip[:members], strip[members:])
-    localized = jnp.where(
+    edge_mix = jnp.where(odd, mix[:, row_count - STEPS :], mix[:, :STEPS])
+    outer = jnp.sum(edge_mix * edge, 0)
+    partial_sum = jnp.where(
         odd,
-        jnp.concatenate([main[:, : row_count - STEPS], edge], 1),
-        jnp.concatenate([edge, main[:, STEPS:]], 1),
+        jnp.concatenate([inner[: row_count - STEPS], outer], 0),
+        jnp.concatenate([outer, inner[STEPS:]], 0),
     )
-    reflect = mem_sum(jnp.sum(mix * localized, 0))
+    reflect = mem_sum(partial_sum)
     weighted = radar_mask.astype(jnp.float32) * obs_weight * reflect
     near, far, odd = split_exchange(mix * weighted[None], STEPS)
     spread = localize(near_band(mix * weighted[None], near, odd), coef_band)

time: 39.5 us -> 39.2 us (level)
    sub x16 -> x14, other arithmetic: 6.23 us -> 5.47 us  [diffuse(): values + jnp.concatenate([col_flux, zeros_col], -1)]
    reduce_sum x1 -> x2, other arithmetic: 0.27 us -> 0.87 us  [the longest x1 0.56 us: per_device(): inner = jnp.sum(mix * main, 0)]
where the time goes in v27:
time: 39.2 us; the launch traced here: 39 us
  other arithmetic  19.7 us (50%)
  starting transfers between devices  14.1 us (36%)
  waiting for transfers between devices  4.16 us (11%)
  between operations  0.63 us (2%)
  local copies, waits for them, and re-layouts  0.44 us (1%)
    ppermute x2, starting transfers between devices, split_exchange(): far = lax.ppermute(jnp.where(odd, tail, head), 'tile', pairs(1))  10.8 us
    sub x14, other arithmetic, diffuse(): values + jnp.concatenate([col_flux, zeros_col], -1)  5.47 us
    mul x16, other arithmetic, diffuse(): col_coef[..., :, :-1] * (values[..., :, 1:] - values[..., :, :-1])  5.13 us
    ppermute x3, waiting for transfers between devices, partner(): return lax.ppermute(part, 'mem', [(i, i ^ stride) for i in range(count)])  3.48 us
    ppermute x3, starting transfers between devices, partner(): return lax.ppermute(part, 'mem', [(i, i ^ stride) for i in range(count)])  3.1 us
    mul x16, other arithmetic, diffuse(): row_coef[..., :-1, :] * (values[..., 1:, :] - values[..., :-1, :])  2.24 us
    select_n x2, other arithmetic, split_exchange(): far = lax.ppermute(jnp.where(odd, tail, head), 'tile', pairs(1))  1.43 us
    add x1, other arithmetic, per_device(): return controls + (spread + edge)  1.12 us
  transfers between devices with their start and end apart: 7, of which 4 were waited for; matrix products, arithmetic and copies ran while one was open for 27% of the time, Pallas kernels for 0%

profile of v27, /device:TPU:1, one launch (start us, length us, event | category | flops | bytes accessed | tf_op | source)
XLA Modules:
  0.0 39.0 jit_solution(16826362707105181601)
XLA Ops:
  0.0 1.0 %select_bitcast_fusion = f32[1,16,1792]{2,1,0:T(8,128)S(1)} fusion(f32[16,1792]{1,0:T(8,128)} %param.12, pred[16]{0:T(512)(128)(4,1)S(1)} %add_compare_fusion), kind=kLoop, calls=%fused_computation.141 | loop fusion | flops 28672 | bytes 229392 | tf_op jit(solution)/shard_map/broadcast_in_dim | solution.py:109
  1.0 1.4 %broadcast_select_fusion.2 = (f32[10,4,1792]{2,1,0:T(4,128)S(1)}, f32[10,4,1792]{2,1,0:T(4,128)S(1)}, f32[10,4,1792]{2,1,0:T(4,128)S(1)}) fusion(pred[]{:T(512)S(6)} %eq.7, f32[1,16,1792]{2,1,0:T(8,128)} %bitcast.49, f32[1,16,1792]{2,1,0:T(8,128)S(1)} %select_bitcast_fusion, f32[8,16,1792]{2,1,0:T(8,128)} %param.7), kind=kLoop, calls=%fused_computation.130 | loop fusion | flops 358400 | bytes 2007041 | tf_op jit(solution)/shard_map/jit(_where)/select_n | solution.py:36
  2.5 0.1 collective-permute-start
  2.7 4.7 %collective-permute-start.1 = (f32[10,4,1792]{2,0,1:T(8,128)S(1)}, f32[10,4,1792]{2,0,1:T(8,128)S(1)}, u32[]{:S(2)}, u32[]{:S(2)}) collective-permute-start(f32[10,4,1792]{2,0,1:T(8,128)S(1)} %copy.14), channel_id=1, source_target_pairs={{1,2},{3,4},{5,6},{2,1},{4,3},{6,5},{9,10},{11,12},{13,14},{10,9},... | collective-permute-start | bytes 860168 | tf_op jit(solution)/shard_map/ppermute | solution.py:36
  7.4 0.4 multiply_reduce_fusion
  7.8 0.2 broadcast_select_fusion.1
  8.1 0.2 pad_maximum_fusion
  8.4 0.4 %fusion.14 = f32[8,24,1791]{2,1,0:T(8,128)S(1)} fusion(f32[10,24,1792]{2,1,0:T(8,128)S(1)} %pad_maximum_fusion, f32[24,1791]{1,0:T(8,128)S(1)} %bitcast.45), kind=kLoop, calls=%fused_computation.35 | loop fusion | flops 687744 | bytes 4298400 | tf_op jit(solution)/shard_map/mul | solution.py:72
  8.8 0.2 fusion.15
  9.0 0.5 %fusion.18 = f32[8,24,1792]{2,1,0:T(8,128)S(1)} fusion(f32[10,24,1792]{2,1,0:T(8,128)S(1)} %pad_maximum_fusion, f32[8,24,1791]{2,1,0:T(8,128)S(1)} %fusion.14, f32[8,23,1792]{2,1,0:T(8,128)S(1)} %fusion.15), kind=kLoop, calls=%fused_computation.41 | loop fusion | flops 1376256 | bytes 5446912 | tf_op jit(solution)/shard_map/sub | solution.py:81
  9.5 0.4 %fusion.12 = f32[8,24,1791]{2,1,0:T(8,128)S(1)} fusion(f32[8,24,1792]{2,1,0:T(8,128)S(1)} %fusion.18, f32[24,1791]{1,0:T(8,128)S(1)} %bitcast.46), kind=kLoop, calls=%fused_computation.31 | loop fusion | flops 687744 | bytes 4298400 | tf_op jit(solution)/shard_map/mul | solution.py:72
  9.9 0.2 fusion.13
  10.1 0.5 %pad_subtract_fusion.4 = f32[8,24,1792]{2,1,0:T(8,128)S(1)} fusion(f32[8,24,1791]{2,1,0:T(8,128)S(1)} %fusion.12, f32[8,23,1792]{2,1,0:T(8,128)S(1)} %fusion.13, f32[8,24,1792]{2,1,0:T(8,128)S(1)} %fusion.18), kind=kLoop, calls=%fused_computation.47 | loop fusion | flops 1376256 | bytes 5446912 | tf_op jit(solution)/shard_map/sub | solution.py:81
  10.6 0.4 %fusion.10 = f32[8,24,1791]{2,1,0:T(8,128)S(1)} fusion(f32[8,24,1792]{2,1,0:T(8,128)S(1)} %pad_subtract_fusion.4, f32[24,1791]{1,0:T(8,128)S(1)} %bitcast.47), kind=kLoop, calls=%fused_computation.27 | loop fusion | flops 687744 | bytes 4298400 | tf_op jit(solution)/shard_map/mul | solution.py:72
  11.0 0.2 fusion.11
  11.2 0.5 %pad_subtract_fusion.3 = f32[8,24,1792]{2,1,0:T(8,128)S(1)} fusion(f32[8,24,1791]{2,1,0:T(8,128)S(1)} %fusion.10, f32[8,23,1792]{2,1,0:T(8,128)S(1)} %fusion.11, f32[8,24,1792]{2,1,0:T(8,128)S(1)} %pad_subtract_fusion.4), kind=kLoop, calls=%fused_computation.46 | loop fusion | flops 1376256 | bytes 5446912 | tf_op jit(solution)/shard_map/sub | solution.py:81
  11.7 0.4 %fusion.8 = f32[8,24,1791]{2,1,0:T(8,128)S(1)} fusion(f32[8,24,1792]{2,1,0:T(8,128)S(1)} %pad_subtract_fusion.3, f32[24,1791]{1,0:T(8,128)S(1)} %bitcast.48), kind=kLoop, calls=%fused_computation.23 | loop fusion | flops 687744 | bytes 4298400 | tf_op jit(solution)/shard_map/mul | solution.py:72
  12.1 0.2 fusion.9
  12.3 0.6 %fusion.30 = f32[16,1792]{1,0:T(8,128)S(1)} fusion(f32[8,16,1792]{2,1,0:T(8,128)S(1)} %multiply_reduce_fusion, f32[8,24,1791]{2,1,0:T(8,128)S(1)} %fusion.8, f32[8,23,1792]{2,1,0:T(8,128)S(1)} %fusion.9, f32[8,24,1792]{2,1,0:T(8,128)S(1)} %pad_subtract_fusion.3), kind=kLoop, calls=%fused_computation.71 | loop fusion | flops 1347584 | bytes 4644096 | tf_op jit(solution)/shard_map/reduce_sum | solution.py:121
  12.9 0.7 %collective-permute-done.1 = f32[10,4,1792]{2,0,1:T(8,128)S(1)} collective-permute-done((f32[10,4,1792]{2,0,1:T(8,128)S(1)}, f32[10,4,1792]{2,0,1:T(8,128)S(1)}, u32[]{:S(2)}, u32[]{:S(2)}) %collective-permute-start.1) | collective-permute-done | bytes 286752 | tf_op jit(solution)/shard_map/ppermute | solution.py:36
  13.5 0.4 copy_select_fusion.1
  13.9 0.3 pad_maximum_fusion.2
  14.2 0.1 slice_select_fusion
  14.5 0.3 fusion.24
  14.8 0.1 fusion.25
  14.9 0.5 %fusion.28 = f32[8,12,1792]{2,1,0:T(8,128)S(1)} fusion(f32[10,12,1792]{2,1,0:T(8,128)S(1)} %slice_select_fusion, f32[8,12,1791]{2,1,0:T(8,128)S(1)} %fusion.24, f32[8,11,1792]{2,1,0:T(8,128)S(1)} %fusion.25), kind=kLoop, calls=%fused_computation.68 | loop fusion | flops 688128 | bytes 2694784 | tf_op jit(solution)/shard_map/sub | solution.py:81
  15.4 0.3 fusion.19
  15.7 0.2 fusion.20
  15.9 0.4 %fusion.23 = f32[8,10,1792]{2,1,0:T(8,128)S(1)} fusion(f32[8,12,1792]{2,1,0:T(8,128)S(1)} %fusion.28, f32[8,10,1791]{2,1,0:T(8,128)S(1)} %fusion.19, f32[8,9,1792]{2,1,0:T(8,128)S(1)} %fusion.20), kind=kLoop, calls=%fused_computation.60 | loop fusion | flops 573440 | bytes 2236096 | tf_op jit(solution)/shard_map/sub | solution.py:81
  16.3 0.2 fusion.41
  16.5 0.1 fusion.42
  16.6 0.2 fusion.45
  16.9 0.2 fusion.39
  17.2 0.3 fusion.47
  17.5 1.8 %collective-permute-start.3 = (f32[16,1792]{1,0:T(8,128)S(1)}, f32[16,1792]{1,0:T(8,128)S(1)}, u32[]{:S(2)}, u32[]{:S(2)}) collective-permute-start(f32[16,1792]{1,0:T(8,128)S(1)} %maximum_select_fusion.1), channel_id=1, source_target_pairs={{0,16},{8,24},{16,0},{24,8},{1,17},{9,25},{17,1},{25,9},{2,18},{10... | collective-permute-start | bytes 344072 | tf_op jit(solution)/shard_map/ppermute | solution.py:56
  19.4 1.2 %collective-permute-start.4 = (f32[16,1792]{1,0:T(8,128)S(1)}, f32[16,1792]{1,0:T(8,128)S(1)}, u32[]{:S(2)}, u32[]{:S(2)}) collective-permute-start(f32[16,1792]{1,0:T(8,128)S(1)} %maximum_select_fusion.1), channel_id=1, source_target_pairs={{0,24},{8,16},{16,8},{24,0},{1,25},{9,17},{17,9},{25,1},{2,26},{10... | collective-permute-start | bytes 344072 | tf_op jit(solution)/shard_map/ppermute | solution.py:56
  20.5 0.1 collective-permute-start.2
  20.6 0.3 pad_maximum_fusion.3
  21.0 1.8 %collective-permute-done.3 = f32[16,1792]{1,0:T(8,128)S(1)} collective-permute-done((f32[16,1792]{1,0:T(8,128)S(1)}, f32[16,1792]{1,0:T(8,128)S(1)}, u32[]{:S(2)}, u32[]{:S(2)}) %collective-permute-start.3) | collective-permute-done | bytes 114720 | tf_op jit(solution)/shard_map/ppermute | solution.py:56
  22.9 1.4 %collective-permute-done.4 = f32[16,1792]{1,0:T(8,128)S(1)} collective-permute-done((f32[16,1792]{1,0:T(8,128)S(1)}, f32[16,1792]{1,0:T(8,128)S(1)}, u32[]{:S(2)}, u32[]{:S(2)}) %collective-permute-start.4) | collective-permute-done | bytes 114720 | tf_op jit(solution)/shard_map/ppermute | solution.py:56
  24.2 0.3 collective-permute-done.2
  24.8 6.1 %collective-permute-start.6 = (f32[8,4,1792]{2,1,0:T(4,128)S(1)}, f32[8,4,1792]{2,1,0:T(4,128)S(1)}, u32[]{:S(2)}, u32[]{:S(2)}) collective-permute-start(f32[8,4,1792]{2,1,0:T(4,128)S(1)} %get-tuple-element.18), channel_id=1, source_target_pairs={{1,2},{3,4},{5,6},{2,1},{4,3},{6,5},{9,10},{11,12},{13,14},{10,9},... | collective-permute-start | bytes 688136 | tf_op jit(solution)/shard_map/ppermute | solution.py:36
  31.1 0.2 pad_maximum_fusion.4
  31.3 0.4 %fusion.6 = f32[8,24,1791]{2,1,0:T(8,128)S(1)} fusion(f32[8,24,1792]{2,1,0:T(8,128)S(1)} %pad_maximum_fusion.4, f32[24,1791]{1,0:T(8,128)S(1)} %bitcast.41), kind=kLoop, calls=%fused_computation.19 | loop fusion | flops 687744 | bytes 4298400 | tf_op jit(solution)/shard_map/mul | solution.py:72
  31.7 0.2 fusion.7
  31.9 0.6 %pad_subtract_fusion.2 = f32[8,24,1792]{2,1,0:T(8,128)S(1)} fusion(f32[8,24,1791]{2,1,0:T(8,128)S(1)} %fusion.6, f32[8,23,1792]{2,1,0:T(8,128)S(1)} %fusion.7, f32[8,4,1792]{2,1,0:T(4,128)S(1)} %get-tuple-element.27, f32[8,16,1792]{2,1,0:T(8,128)S(1)} %broadcast_multiply_fusion, f32[8,4,1792]{2,1,0:T(4,128)S(1)} %get-tuple-element.26), kind=kLoop, calls=%fused_computation.45 | loop fusion | flops 2064384 | bytes 5446912 | tf_op jit(solution)/shard_map/sub | solution.py:81
  32.5 0.4 %fusion.4 = f32[8,24,1791]{2,1,0:T(8,128)S(1)} fusion(f32[8,24,1792]{2,1,0:T(8,128)S(1)} %pad_subtract_fusion.2, f32[24,1791]{1,0:T(8,128)S(1)} %bitcast.42), kind=kLoop, calls=%fused_computation.15 | loop fusion | flops 687744 | bytes 4298400 | tf_op jit(solution)/shard_map/mul | solution.py:72
  32.9 0.2 fusion.5
  33.1 0.5 %pad_subtract_fusion.1 = f32[8,24,1792]{2,1,0:T(8,128)S(1)} fusion(f32[8,24,1791]{2,1,0:T(8,128)S(1)} %fusion.4, f32[8,23,1792]{2,1,0:T(8,128)S(1)} %fusion.5, f32[8,24,1792]{2,1,0:T(8,128)S(1)} %pad_subtract_fusion.2), kind=kLoop, calls=%fused_computation.44 | loop fusion | flops 1376256 | bytes 5446912 | tf_op jit(solution)/shard_map/sub | solution.py:81
  33.6 0.4 %fusion.2 = f32[8,24,1791]{2,1,0:T(8,128)S(1)} fusion(f32[8,24,1792]{2,1,0:T(8,128)S(1)} %pad_subtract_fusion.1, f32[24,1791]{1,0:T(8,128)S(1)} %bitcast.43), kind=kLoop, calls=%fused_computation.11 | loop fusion | flops 687744 | bytes 4298400 | tf_op jit(solution)/shard_map/mul | solution.py:72
  34.0 0.2 fusion.3
  34.2 0.5 %pad_subtract_fusion = f32[8,24,1792]{2,1,0:T(8,128)S(1)} fusion(f32[8,24,1791]{2,1,0:T(8,128)S(1)} %fusion.2, f32[8,23,1792]{2,1,0:T(8,128)S(1)} %fusion.3, f32[8,24,1792]{2,1,0:T(8,128)S(1)} %pad_subtract_fusion.1), kind=kLoop, calls=%fused_computation.43 | loop fusion | flops 1376256 | bytes 5446912 | tf_op jit(solution)/shard_map/sub | solution.py:81
  34.7 0.4 %fusion = f32[8,24,1791]{2,1,0:T(8,128)S(1)} fusion(f32[8,24,1792]{2,1,0:T(8,128)S(1)} %pad_subtract_fusion, f32[24,1791]{1,0:T(8,128)S(1)} %bitcast.44), kind=kLoop, calls=%fused_computation.7 | loop fusion | flops 687744 | bytes 4298400 | tf_op jit(solution)/shard_map/mul | solution.py:72
  35.1 0.2 fusion.1
  35.3 0.5 %pad_subtract_fusion.5 = f32[8,16,1792]{2,1,0:T(8,128)S(1)} fusion(f32[8,24,1791]{2,1,0:T(8,128)S(1)} %fusion, f32[8,23,1792]{2,1,0:T(8,128)S(1)} %fusion.1, f32[8,24,1792]{2,1,0:T(8,128)S(1)} %pad_subtract_fusion), kind=kLoop, calls=%fused_computation.49 | loop fusion | flops 917504 | bytes 4529408 | tf_op jit(solution)/shard_map/sub | solution.py:81
  35.9 0.2 fusion.37
  36.2 0.2 pad_subtract_fusion.12
  36.4 0.2 fusion.35
  36.6 0.2 pad_subtract_fusion.11
  36.9 0.2 fusion.33
  37.1 0.2 pad_subtract_fusion.10
  37.4 0.2 fusion.31
  37.6 0.2 pad_subtract_fusion.9
  37.9 1.1 %add_add_fusion = f32[8,16,1792]{2,1,0:T(8,128)} fusion(f32[8,16,1792]{2,1,0:T(8,128)S(1)} %copy-done, f32[8,16,1792]{2,1,0:T(8,128)S(1)} %pad_subtract_fusion.5, f32[8,4,1792]{2,1,0:T(4,128)S(1)} %get-tuple-element.23, f32[8,4,1792]{2,1,0:T(4,128)S(1)} %get-tuple-element.22, pred[]{:T(512)S(6)} %eq.7), kind=kLoop, calls=%fused_computation.75 | loop fusion | flops 688128 | bytes 3211265 | tf_op jit(solution)/shard_map/add | solution.py:150
  (49 shorter events, 1.4 us)
Async XLA Ops:
  2.3 5.1 %copy-start.2 = (bf16[8,4,16,1792]{3,2,1,0:T(8,128)(2,1)S(1)}, bf16[8,4,16,1792]{3,2,1,0:T(8,128)(2,1)}, u32[]{:S(2)}) copy-start(bf16[8,4,16,1792]{3,2,1,0:T(8,128)(2,1)} %param.8) | copy-start | bytes 5505028
  2.4 5.1 %copy-start.3 = (f32[4,16,1792]{2,1,0:T(8,128)S(1)}, f32[4,16,1792]{2,1,0:T(8,128)}, u32[]{:S(2)}) copy-start(f32[4,16,1792]{2,1,0:T(8,128)} %param.9) | copy-start | bytes 1376260
  2.5 5.3 %collective-permute-start = (f32[10,4,1792]{2,0,1:T(8,128)S(1)}, f32[10,4,1792]{2,0,1:T(8,128)S(1)}, u32[]{:S(2)}, u32[]{:S(2)}) collective-permute-start(f32[10,4,1792]{2,0,1:T(8,128)S(1)} %copy.11), channel_id=1, source_target_pairs={{0,1},{2,3},{4,5},{6,7},{1,0},{3,2},{5,4},{7,6},{8,9},{10,11},{12,... | collective-permute-start | bytes 860168 | tf_op jit(solution)/shard_map/ppermute | solution.py:37
  2.7 5.4 %copy-start = (f32[8,16,1792]{2,1,0:T(8,128)S(1)}, f32[8,16,1792]{2,1,0:T(8,128)}, u32[]{:S(2)}) copy-start(f32[8,16,1792]{2,1,0:T(8,128)} %param.7) | copy-start | bytes 2752516
  2.7 5.4 %copy-start.1 = (f32[16,1792]{1,0:T(8,128)S(1)}, f32[16,1792]{1,0:T(8,128)}, u32[]{:S(2)}) copy-start(f32[16,1792]{1,0:T(8,128)} %param.13) | copy-start | bytes 344068
  2.7 10.8 %collective-permute-start.1 = (f32[10,4,1792]{2,0,1:T(8,128)S(1)}, f32[10,4,1792]{2,0,1:T(8,128)S(1)}, u32[]{:S(2)}, u32[]{:S(2)}) collective-permute-start(f32[10,4,1792]{2,0,1:T(8,128)S(1)} %copy.14), channel_id=1, source_target_pairs={{1,2},{3,4},{5,6},{2,1},{4,3},{6,5},{9,10},{11,12},{13,14},{10,9},... | collective-permute-start | bytes 860168 | tf_op jit(solution)/shard_map/ppermute | solution.py:36
  17.5 5.3 %collective-permute-start.3 = (f32[16,1792]{1,0:T(8,128)S(1)}, f32[16,1792]{1,0:T(8,128)S(1)}, u32[]{:S(2)}, u32[]{:S(2)}) collective-permute-start(f32[16,1792]{1,0:T(8,128)S(1)} %maximum_select_fusion.1), channel_id=1, source_target_pairs={{0,16},{8,24},{16,0},{24,8},{1,17},{9,25},{17,1},{25,9},{2,18},{10... | collective-permute-start | bytes 344072 | tf_op jit(solution)/shard_map/ppermute | solution.py:56
  19.4 4.9 %collective-permute-start.4 = (f32[16,1792]{1,0:T(8,128)S(1)}, f32[16,1792]{1,0:T(8,128)S(1)}, u32[]{:S(2)}, u32[]{:S(2)}) collective-permute-start(f32[16,1792]{1,0:T(8,128)S(1)} %maximum_select_fusion.1), channel_id=1, source_target_pairs={{0,24},{8,16},{16,8},{24,0},{1,25},{9,17},{17,9},{25,1},{2,26},{10... | collective-permute-start | bytes 344072 | tf_op jit(solution)/shard_map/ppermute | solution.py:56
  20.5 4.0 %collective-permute-start.2 = (f32[16,1792]{1,0:T(8,128)S(1)}, f32[16,1792]{1,0:T(8,128)S(1)}, u32[]{:S(2)}, u32[]{:S(2)}) collective-permute-start(f32[16,1792]{1,0:T(8,128)S(1)} %maximum_select_fusion.1), channel_id=1, source_target_pairs={{0,8},{8,0},{16,24},{24,16},{1,9},{9,1},{17,25},{25,17},{2,10},{10... | collective-permute-start | bytes 344072 | tf_op jit(solution)/shard_map/ppermute | solution.py:56
  20.9 3.6 %copy-start.4 = (f32[16,1792]{1,0:T(8,128)S(1)}, f32[16,1792]{1,0:T(8,128)}, u32[]{:S(2)}) copy-start(f32[16,1792]{1,0:T(8,128)} %param.10) | copy-start | bytes 344068
  20.9 3.6 %copy-start.5 = (s32[16,1792]{1,0:T(8,128)S(1)}, s32[16,1792]{1,0:T(8,128)}, u32[]{:S(2)}) copy-start(s32[16,1792]{1,0:T(8,128)} %param.11) | copy-start | bytes 344068
  24.7 6.2 %collective-permute-start.5 = (f32[8,4,1792]{2,1,0:T(4,128)S(1)}, f32[8,4,1792]{2,1,0:T(4,128)S(1)}, u32[]{:S(2)}, u32[]{:S(2)}) collective-permute-start(f32[8,4,1792]{2,1,0:T(4,128)S(1)} %get-tuple-element.19), channel_id=1, source_target_pairs={{0,1},{2,3},{4,5},{6,7},{1,0},{3,2},{5,4},{7,6},{8,9},{10,11},{12,... | collective-permute-start | bytes 688136 | tf_op jit(solution)/shard_map/ppermute | solution.py:37
  24.8 11.0 %collective-permute-start.6 = (f32[8,4,1792]{2,1,0:T(4,128)S(1)}, f32[8,4,1792]{2,1,0:T(4,128)S(1)}, u32[]{:S(2)}, u32[]{:S(2)}) collective-permute-start(f32[8,4,1792]{2,1,0:T(4,128)S(1)} %get-tuple-element.18), channel_id=1, source_target_pairs={{1,2},{3,4},{5,6},{2,1},{4,3},{6,5},{9,10},{11,12},{13,14},{10,9},... | collective-permute-start | bytes 688136 | tf_op jit(solution)/shard_map/ppermute | solution.py:36

commit v28 on v27

--- a/solution.py
+++ b/solution.py
@@ -120,9 +120,12 @@
     main = localize(partial[:members], partial[members:])[:, STEPS : STEPS + row_count]
     inner = jnp.sum(mix * main, 0)
     inner, far = lax.optimization_barrier((inner, far))
-    band = full_band(stacked, near, far, odd)
-    coef_band = band[members:]
-    strip = jnp.where(odd, band[:, row_count - STEPS :], band[:, : 3 * STEPS])
+    coef_band = full_band(stacked[members:], near[members:], far[members:], odd)
+    strip = jnp.where(
+        odd,
+        jnp.concatenate([stacked[:, row_count - 2 * STEPS :], far], 1),
+        jnp.concatenate([far, stacked[:, : 2 * STEPS]], 1),
+    )
     edge = localize_inner(strip[:members], strip[members:])
     edge_mix = jnp.where(odd, mix[:, row_count - STEPS :], mix[:, :STEPS])
     outer = jnp.sum(edge_mix * edge, 0)

time: 39.2 us -> 38.9 us (level)
  starting transfers between devices: 14.1 us -> 12.8 us
  local copies, waits for them, and re-layouts: 0.44 us -> 1.51 us
  other arithmetic: 19.7 us -> 19.1 us
  waiting for transfers between devices: 4.16 us -> 4.67 us
    concatenate x0 -> x1, other arithmetic: none -> 1.33 us  [per_device(): stacked = jnp.concatenate([controls, row_coef[None], col_faces[None]], 0)]
    select_n x2, other arithmetic: 1.43 us -> 0.19 us  [split_exchange(): far = lax.ppermute(jnp.where(odd, tail, head), 'tile', pairs(1))]
    ppermute x3, waiting for transfers between devices: 3.48 us -> 4.66 us  [partner(): return lax.ppermute(part, 'mem', [(i, i ^ stride) for i in range(count)])]
    ppermute x2, starting transfers between devices: 10.8 us -> 9.91 us  [split_exchange(): far = lax.ppermute(jnp.where(odd, tail, head), 'tile', pairs(1))]
    unnamed x12, local copies, waits for them, and re-layouts: 0.04 us -> 0.87 us
    ppermute x2, waiting for transfers between devices: 0.67 us -> 0.01 us  [split_exchange(): far = lax.ppermute(jnp.where(odd, tail, head), 'tile', pairs(1))]
    concatenate x2 -> x1, other arithmetic: 0.51 us -> 0.05 us  [full_band(): jnp.concatenate([jnp.where(odd, near, far), part, jnp.where(odd, far, nea...]
    mul x16 -> x17, other arithmetic: 2.24 us -> 2.29 us  [diffuse(): row_coef[..., :-1, :] * (values[..., 1:, :] - values[..., :-1, :])]
  transfers between devices with their start and end apart: 7 -> 7, of which waited for: 4 -> 3; matrix products, arithmetic and copies ran while one was open for 27% -> 27% of each run, Pallas kernels for 0% -> 0%
where the time goes in v28:
time: 38.9 us; the launch traced here: 38.7 us
  other arithmetic  19.1 us (49%)
  starting transfers between devices  12.8 us (33%)
  waiting for transfers between devices  4.67 us (12%)
  local copies, waits for them, and re-layouts  1.51 us (4%)
  between operations  0.62 us (2%)
    ppermute x2, starting transfers between devices, split_exchange(): far = lax.ppermute(jnp.where(odd, tail, head), 'tile', pairs(1))  9.91 us
    sub x14, other arithmetic, diffuse(): values + jnp.concatenate([col_flux, zeros_col], -1)  5.49 us
    mul x16, other arithmetic, diffuse(): col_coef[..., :, :-1] * (values[..., :, 1:] - values[..., :, :-1])  5.12 us
    ppermute x3, waiting for transfers between devices, partner(): return lax.ppermute(part, 'mem', [(i, i ^ stride) for i in range(count)])  4.66 us
    ppermute x3, starting transfers between devices, partner(): return lax.ppermute(part, 'mem', [(i, i ^ stride) for i in range(count)])  2.71 us
    mul x17, other arithmetic, diffuse(): row_coef[..., :-1, :] * (values[..., 1:, :] - values[..., :-1, :])  2.29 us
    concatenate x1, other arithmetic, per_device(): stacked = jnp.concatenate([controls, row_coef[None], col_faces[None]], 0)  1.33 us
    add x1, other arithmetic, per_device(): return controls + (spread + edge)  1.12 us
  transfers between devices with their start and end apart: 7, of which 3 were waited for; matrix products, arithmetic and copies ran while one was open for 27% of the time, Pallas kernels for 0%

profile of v28, /device:TPU:1, one launch (start us, length us, event | category | flops | bytes accessed | tf_op | source)
XLA Modules:
  0.0 38.7 jit_solution(9601580405144992838)
XLA Ops:
  0.0 1.0 %select_bitcast_fusion = f32[1,16,1792]{2,1,0:T(8,128)S(1)} fusion(f32[16,1792]{1,0:T(8,128)} %param.12, pred[16]{0:T(512)(128)(4,1)S(1)} %add_compare_fusion), kind=kLoop, calls=%fused_computation.138 | loop fusion | flops 28672 | bytes 229392 | tf_op jit(solution)/shard_map/broadcast_in_dim | solution.py:109
  1.0 1.3 %pad_maximum_fusion.2 = f32[10,16,1792]{2,1,0:T(8,128)S(1)} fusion(f32[1,16,1792]{2,1,0:T(8,128)} %bitcast.46, f32[1,16,1792]{2,1,0:T(8,128)S(1)} %select_bitcast_fusion, f32[8,16,1792]{2,1,0:T(8,128)} %param.7), kind=kLoop, calls=%fused_computation.44 | loop fusion | flops 573440 | bytes 2293760 | tf_op jit(solution)/shard_map/concatenate | solution.py:109
  2.3 0.1 slice_select_fusion
  2.5 0.1 collective-permute-start
  2.7 4.7 %collective-permute-start.1 = (f32[10,4,1792]{2,0,1:T(8,128)S(1)}, f32[10,4,1792]{2,0,1:T(8,128)S(1)}, u32[]{:S(2)}, u32[]{:S(2)}) collective-permute-start(f32[10,4,1792]{2,0,1:T(8,128)S(1)} %copy.14), channel_id=1, source_target_pairs={{1,2},{3,4},{5,6},{2,1},{4,3},{6,5},{9,10},{11,12},{13,14},{10,9},... | collective-permute-start | bytes 860168 | tf_op jit(solution)/shard_map/ppermute | solution.py:36
  7.5 0.4 multiply_reduce_fusion
  7.9 0.2 broadcast_select_fusion.1
  8.2 0.8 %copy-done = f32[8,16,1792]{2,1,0:T(8,128)S(1)} copy-done((f32[8,16,1792]{2,1,0:T(8,128)S(1)}, f32[8,16,1792]{2,1,0:T(8,128)}, u32[]{:S(2)}) %copy-start) | copy-done | bytes 917528
  9.1 0.3 pad_maximum_fusion
  9.4 0.2 fusion.15
  9.6 0.4 %fusion.14 = f32[8,24,1791]{2,1,0:T(8,128)S(1)} fusion(f32[10,24,1792]{2,1,0:T(8,128)S(1)} %pad_maximum_fusion, f32[24,1791]{1,0:T(8,128)S(1)} %bitcast.42), kind=kLoop, calls=%fused_computation.31 | loop fusion | flops 687744 | bytes 4298400 | tf_op jit(solution)/shard_map/mul | solution.py:72
  10.0 0.5 %fusion.18 = f32[8,24,1792]{2,1,0:T(8,128)S(1)} fusion(f32[10,24,1792]{2,1,0:T(8,128)S(1)} %pad_maximum_fusion, f32[8,24,1791]{2,1,0:T(8,128)S(1)} %fusion.14, f32[8,23,1792]{2,1,0:T(8,128)S(1)} %fusion.15), kind=kLoop, calls=%fused_computation.37 | loop fusion | flops 1376256 | bytes 5446912 | tf_op jit(solution)/shard_map/sub | solution.py:81
  10.5 0.2 fusion.13
  10.7 0.4 %fusion.12 = f32[8,24,1791]{2,1,0:T(8,128)S(1)} fusion(f32[8,24,1792]{2,1,0:T(8,128)S(1)} %fusion.18, f32[24,1791]{1,0:T(8,128)S(1)} %bitcast.43), kind=kLoop, calls=%fused_computation.27 | loop fusion | flops 687744 | bytes 4298400 | tf_op jit(solution)/shard_map/mul | solution.py:72
  11.1 0.5 %pad_subtract_fusion.4 = f32[8,24,1792]{2,1,0:T(8,128)S(1)} fusion(f32[8,24,1791]{2,1,0:T(8,128)S(1)} %fusion.12, f32[8,23,1792]{2,1,0:T(8,128)S(1)} %fusion.13, f32[8,24,1792]{2,1,0:T(8,128)S(1)} %fusion.18), kind=kLoop, calls=%fused_computation.43 | loop fusion | flops 1376256 | bytes 5446912 | tf_op jit(solution)/shard_map/sub | solution.py:81
  11.6 0.2 fusion.11
  11.8 0.4 %fusion.10 = f32[8,24,1791]{2,1,0:T(8,128)S(1)} fusion(f32[8,24,1792]{2,1,0:T(8,128)S(1)} %pad_subtract_fusion.4, f32[24,1791]{1,0:T(8,128)S(1)} %bitcast.44), kind=kLoop, calls=%fused_computation.23 | loop fusion | flops 687744 | bytes 4298400 | tf_op jit(solution)/shard_map/mul | solution.py:72
  12.2 0.5 %pad_subtract_fusion.3 = f32[8,24,1792]{2,1,0:T(8,128)S(1)} fusion(f32[8,24,1791]{2,1,0:T(8,128)S(1)} %fusion.10, f32[8,23,1792]{2,1,0:T(8,128)S(1)} %fusion.11, f32[8,24,1792]{2,1,0:T(8,128)S(1)} %pad_subtract_fusion.4), kind=kLoop, calls=%fused_computation.42 | loop fusion | flops 1376256 | bytes 5446912 | tf_op jit(solution)/shard_map/sub | solution.py:81
  12.7 0.2 fusion.9
  12.9 0.4 %fusion.8 = f32[8,24,1791]{2,1,0:T(8,128)S(1)} fusion(f32[8,24,1792]{2,1,0:T(8,128)S(1)} %pad_subtract_fusion.3, f32[24,1791]{1,0:T(8,128)S(1)} %bitcast.45), kind=kLoop, calls=%fused_computation.19 | loop fusion | flops 687744 | bytes 4298400 | tf_op jit(solution)/shard_map/mul | solution.py:72
  13.3 0.6 %fusion.30 = f32[16,1792]{1,0:T(8,128)S(1)} fusion(f32[8,16,1792]{2,1,0:T(8,128)S(1)} %multiply_reduce_fusion, f32[8,24,1791]{2,1,0:T(8,128)S(1)} %fusion.8, f32[8,23,1792]{2,1,0:T(8,128)S(1)} %fusion.9, f32[8,24,1792]{2,1,0:T(8,128)S(1)} %pad_subtract_fusion.3), kind=kLoop, calls=%fused_computation.68 | loop fusion | flops 1347584 | bytes 4644096 | tf_op jit(solution)/shard_map/reduce_sum | solution.py:121
  13.9 0.2 copy.15
  14.1 0.2 maximum_select_fusion
  14.5 0.1 fusion.25
  14.6 0.3 fusion.24
  14.9 0.5 %fusion.28 = f32[8,12,1792]{2,1,0:T(8,128)S(1)} fusion(f32[10,12,1792]{2,1,0:T(8,128)S(1)} %maximum_select_fusion, f32[8,12,1791]{2,1,0:T(8,128)S(1)} %fusion.24, f32[8,11,1792]{2,1,0:T(8,128)S(1)} %fusion.25), kind=kLoop, calls=%fused_computation.65 | loop fusion | flops 688128 | bytes 2694784 | tf_op jit(solution)/shard_map/sub | solution.py:81
  15.4 0.2 fusion.20
  15.6 0.3 fusion.19
  15.9 0.4 %fusion.23 = f32[8,10,1792]{2,1,0:T(8,128)S(1)} fusion(f32[8,12,1792]{2,1,0:T(8,128)S(1)} %fusion.28, f32[8,10,1791]{2,1,0:T(8,128)S(1)} %fusion.19, f32[8,9,1792]{2,1,0:T(8,128)S(1)} %fusion.20), kind=kLoop, calls=%fused_computation.57 | loop fusion | flops 573440 | bytes 2236096 | tf_op jit(solution)/shard_map/sub | solution.py:81
  16.3 0.1 fusion.42
  16.4 0.2 fusion.41
  16.6 0.2 fusion.45
  16.9 0.1 fusion.40
  17.0 0.2 fusion.39
  17.2 0.3 fusion.47
  17.6 1.4 %collective-permute-start.2 = (f32[16,1792]{1,0:T(8,128)S(1)}, f32[16,1792]{1,0:T(8,128)S(1)}, u32[]{:S(2)}, u32[]{:S(2)}) collective-permute-start(f32[16,1792]{1,0:T(8,128)S(1)} %maximum_select_fusion.1), channel_id=1, source_target_pairs={{0,8},{8,0},{16,24},{24,16},{1,9},{9,1},{17,25},{25,17},{2,10},{10... | collective-permute-start | bytes 344072 | tf_op jit(solution)/shard_map/ppermute | solution.py:56
  19.0 1.2 %collective-permute-start.3 = (f32[16,1792]{1,0:T(8,128)S(1)}, f32[16,1792]{1,0:T(8,128)S(1)}, u32[]{:S(2)}, u32[]{:S(2)}) collective-permute-start(f32[16,1792]{1,0:T(8,128)S(1)} %maximum_select_fusion.1), channel_id=1, source_target_pairs={{0,16},{8,24},{16,0},{24,8},{1,17},{9,25},{17,1},{25,9},{2,18},{10... | collective-permute-start | bytes 344072 | tf_op jit(solution)/shard_map/ppermute | solution.py:56
  20.5 1.5 %collective-permute-done.2 = f32[16,1792]{1,0:T(8,128)S(1)} collective-permute-done((f32[16,1792]{1,0:T(8,128)S(1)}, f32[16,1792]{1,0:T(8,128)S(1)}, u32[]{:S(2)}, u32[]{:S(2)}) %collective-permute-start.2) | collective-permute-done | bytes 114720 | tf_op jit(solution)/shard_map/ppermute | solution.py:56
  22.0 2.5 %collective-permute-done.3 = f32[16,1792]{1,0:T(8,128)S(1)} collective-permute-done((f32[16,1792]{1,0:T(8,128)S(1)}, f32[16,1792]{1,0:T(8,128)S(1)}, u32[]{:S(2)}, u32[]{:S(2)}) %collective-permute-start.3) | collective-permute-done | bytes 114720 | tf_op jit(solution)/shard_map/ppermute | solution.py:56
  24.5 0.7 %collective-permute-done.4 = f32[16,1792]{1,0:T(8,128)S(1)} collective-permute-done((f32[16,1792]{1,0:T(8,128)S(1)}, f32[16,1792]{1,0:T(8,128)S(1)}, u32[]{:S(2)}, u32[]{:S(2)}) %collective-permute-start.4) | collective-permute-done | bytes 114720 | tf_op jit(solution)/shard_map/ppermute | solution.py:56
  25.2 0.1 slice_select_fusion.3
  25.4 5.2 %collective-permute-start.6 = (f32[8,4,1792]{2,1,0:T(4,128)S(1)}, f32[8,4,1792]{2,1,0:T(4,128)S(1)}, u32[]{:S(2)}, u32[]{:S(2)}) collective-permute-start(f32[8,4,1792]{2,1,0:T(4,128)S(1)} %get-tuple-element.19), channel_id=1, source_target_pairs={{1,2},{3,4},{5,6},{2,1},{4,3},{6,5},{9,10},{11,12},{13,14},{10,9},... | collective-permute-start | bytes 688136 | tf_op jit(solution)/shard_map/ppermute | solution.py:36
  30.7 0.2 pad_maximum_fusion.1
  30.9 0.2 fusion.7
  31.1 0.4 %fusion.6 = f32[8,24,1791]{2,1,0:T(8,128)S(1)} fusion(f32[8,24,1792]{2,1,0:T(8,128)S(1)} %pad_maximum_fusion.1, f32[24,1791]{1,0:T(8,128)S(1)} %bitcast.38), kind=kLoop, calls=%fused_computation.15 | loop fusion | flops 687744 | bytes 4298400 | tf_op jit(solution)/shard_map/mul | solution.py:72
  31.5 0.6 %pad_subtract_fusion.2 = f32[8,24,1792]{2,1,0:T(8,128)S(1)} fusion(f32[8,24,1791]{2,1,0:T(8,128)S(1)} %fusion.6, f32[8,23,1792]{2,1,0:T(8,128)S(1)} %fusion.7, f32[8,4,1792]{2,1,0:T(4,128)S(1)} %get-tuple-element.26, f32[8,16,1792]{2,1,0:T(8,128)S(1)} %broadcast_multiply_fusion, f32[8,4,1792]{2,1,0:T(4,128)S(1)} %get-tuple-element.25), kind=kLoop, calls=%fused_computation.41 | loop fusion | flops 2064384 | bytes 5446912 | tf_op jit(solution)/shard_map/sub | solution.py:81
  32.1 0.2 fusion.5
  32.3 0.4 %fusion.4 = f32[8,24,1791]{2,1,0:T(8,128)S(1)} fusion(f32[8,24,1792]{2,1,0:T(8,128)S(1)} %pad_subtract_fusion.2, f32[24,1791]{1,0:T(8,128)S(1)} %bitcast.39), kind=kLoop, calls=%fused_computation.11 | loop fusion | flops 687744 | bytes 4298400 | tf_op jit(solution)/shard_map/mul | solution.py:72
  32.7 0.5 %pad_subtract_fusion.1 = f32[8,24,1792]{2,1,0:T(8,128)S(1)} fusion(f32[8,24,1791]{2,1,0:T(8,128)S(1)} %fusion.4, f32[8,23,1792]{2,1,0:T(8,128)S(1)} %fusion.5, f32[8,24,1792]{2,1,0:T(8,128)S(1)} %pad_subtract_fusion.2), kind=kLoop, calls=%fused_computation.40 | loop fusion | flops 1376256 | bytes 5446912 | tf_op jit(solution)/shard_map/sub | solution.py:81
  33.2 0.2 fusion.3
  33.4 0.4 %fusion.2 = f32[8,24,1791]{2,1,0:T(8,128)S(1)} fusion(f32[8,24,1792]{2,1,0:T(8,128)S(1)} %pad_subtract_fusion.1, f32[24,1791]{1,0:T(8,128)S(1)} %bitcast.40), kind=kLoop, calls=%fused_computation.7 | loop fusion | flops 687744 | bytes 4298400 | tf_op jit(solution)/shard_map/mul | solution.py:72
  33.8 0.5 %pad_subtract_fusion = f32[8,24,1792]{2,1,0:T(8,128)S(1)} fusion(f32[8,24,1791]{2,1,0:T(8,128)S(1)} %fusion.2, f32[8,23,1792]{2,1,0:T(8,128)S(1)} %fusion.3, f32[8,24,1792]{2,1,0:T(8,128)S(1)} %pad_subtract_fusion.1), kind=kLoop, calls=%fused_computation.39 | loop fusion | flops 1376256 | bytes 5446912 | tf_op jit(solution)/shard_map/sub | solution.py:81
  34.3 0.2 fusion.1
  34.5 0.4 %fusion = f32[8,24,1791]{2,1,0:T(8,128)S(1)} fusion(f32[8,24,1792]{2,1,0:T(8,128)S(1)} %pad_subtract_fusion, f32[24,1791]{1,0:T(8,128)S(1)} %bitcast.41), kind=kLoop, calls=%fused_computation.3 | loop fusion | flops 687744 | bytes 4298400 | tf_op jit(solution)/shard_map/mul | solution.py:72
  35.0 0.5 %pad_subtract_fusion.5 = f32[8,16,1792]{2,1,0:T(8,128)S(1)} fusion(f32[8,24,1791]{2,1,0:T(8,128)S(1)} %fusion, f32[8,23,1792]{2,1,0:T(8,128)S(1)} %fusion.1, f32[8,24,1792]{2,1,0:T(8,128)S(1)} %pad_subtract_fusion), kind=kLoop, calls=%fused_computation.46 | loop fusion | flops 917504 | bytes 4529408 | tf_op jit(solution)/shard_map/sub | solution.py:81
  35.6 0.2 fusion.37
  35.8 0.2 pad_subtract_fusion.12
  36.1 0.2 fusion.35
  36.3 0.2 pad_subtract_fusion.11
  36.6 0.2 fusion.33
  36.8 0.2 pad_subtract_fusion.10
  37.1 0.2 fusion.31
  37.3 0.2 pad_subtract_fusion.9
  37.6 1.1 %add_add_fusion = f32[8,16,1792]{2,1,0:T(8,128)} fusion(f32[8,16,1792]{2,1,0:T(8,128)S(1)} %copy-done, f32[8,16,1792]{2,1,0:T(8,128)S(1)} %pad_subtract_fusion.5, f32[8,4,1792]{2,1,0:T(4,128)S(1)} %get-tuple-element.24, f32[8,4,1792]{2,1,0:T(4,128)S(1)} %get-tuple-element.23, pred[]{:T(512)S(6)} %eq.7), kind=kLoop, calls=%fused_computation.72 | loop fusion | flops 688128 | bytes 3211265 | tf_op jit(solution)/shard_map/add | solution.py:153
  (51 shorter events, 1.4 us)
Async XLA Ops:
  2.5 5.4 %collective-permute-start = (f32[10,4,1792]{2,0,1:T(8,128)S(1)}, f32[10,4,1792]{2,0,1:T(8,128)S(1)}, u32[]{:S(2)}, u32[]{:S(2)}) collective-permute-start(f32[10,4,1792]{2,0,1:T(8,128)S(1)} %copy.11), channel_id=1, source_target_pairs={{0,1},{2,3},{4,5},{6,7},{1,0},{3,2},{5,4},{7,6},{8,9},{10,11},{12,... | collective-permute-start | bytes 860168 | tf_op jit(solution)/shard_map/ppermute | solution.py:37
  2.6 4.9 %copy-start.2 = (bf16[8,4,16,1792]{3,2,1,0:T(8,128)(2,1)S(1)}, bf16[8,4,16,1792]{3,2,1,0:T(8,128)(2,1)}, u32[]{:S(2)}) copy-start(bf16[8,4,16,1792]{3,2,1,0:T(8,128)(2,1)} %param.8) | copy-start | bytes 5505028
  2.6 4.9 %copy-start.3 = (f32[4,16,1792]{2,1,0:T(8,128)S(1)}, f32[4,16,1792]{2,1,0:T(8,128)}, u32[]{:S(2)}) copy-start(f32[4,16,1792]{2,1,0:T(8,128)} %param.9) | copy-start | bytes 1376260
  2.7 11.2 %collective-permute-start.1 = (f32[10,4,1792]{2,0,1:T(8,128)S(1)}, f32[10,4,1792]{2,0,1:T(8,128)S(1)}, u32[]{:S(2)}, u32[]{:S(2)}) collective-permute-start(f32[10,4,1792]{2,0,1:T(8,128)S(1)} %copy.14), channel_id=1, source_target_pairs={{1,2},{3,4},{5,6},{2,1},{4,3},{6,5},{9,10},{11,12},{13,14},{10,9},... | collective-permute-start | bytes 860168 | tf_op jit(solution)/shard_map/ppermute | solution.py:36
  7.9 1.2 %copy-start = (f32[8,16,1792]{2,1,0:T(8,128)S(1)}, f32[8,16,1792]{2,1,0:T(8,128)}, u32[]{:S(2)}) copy-start(f32[8,16,1792]{2,1,0:T(8,128)} %param.7) | copy-start | bytes 2752516
  7.9 1.2 %copy-start.1 = (f32[16,1792]{1,0:T(8,128)S(1)}, f32[16,1792]{1,0:T(8,128)}, u32[]{:S(2)}) copy-start(f32[16,1792]{1,0:T(8,128)} %param.13) | copy-start | bytes 344068
  17.5 7.6 %copy-start.4 = (f32[16,1792]{1,0:T(8,128)S(1)}, f32[16,1792]{1,0:T(8,128)}, u32[]{:S(2)}) copy-start(f32[16,1792]{1,0:T(8,128)} %param.10) | copy-start | bytes 344068
  17.5 7.6 %copy-start.5 = (s32[16,1792]{1,0:T(8,128)S(1)}, s32[16,1792]{1,0:T(8,128)}, u32[]{:S(2)}) copy-start(s32[16,1792]{1,0:T(8,128)} %param.11) | copy-start | bytes 344068
  17.6 4.4 %collective-permute-start.2 = (f32[16,1792]{1,0:T(8,128)S(1)}, f32[16,1792]{1,0:T(8,128)S(1)}, u32[]{:S(2)}, u32[]{:S(2)}) collective-permute-start(f32[16,1792]{1,0:T(8,128)S(1)} %maximum_select_fusion.1), channel_id=1, source_target_pairs={{0,8},{8,0},{16,24},{24,16},{1,9},{9,1},{17,25},{25,17},{2,10},{10... | collective-permute-start | bytes 344072 | tf_op jit(solution)/shard_map/ppermute | solution.py:56
  19.0 5.4 %collective-permute-start.3 = (f32[16,1792]{1,0:T(8,128)S(1)}, f32[16,1792]{1,0:T(8,128)S(1)}, u32[]{:S(2)}, u32[]{:S(2)}) collective-permute-start(f32[16,1792]{1,0:T(8,128)S(1)} %maximum_select_fusion.1), channel_id=1, source_target_pairs={{0,16},{8,24},{16,0},{24,8},{1,17},{9,25},{17,1},{25,9},{2,18},{10... | collective-permute-start | bytes 344072 | tf_op jit(solution)/shard_map/ppermute | solution.py:56
  20.3 4.9 %collective-permute-start.4 = (f32[16,1792]{1,0:T(8,128)S(1)}, f32[16,1792]{1,0:T(8,128)S(1)}, u32[]{:S(2)}, u32[]{:S(2)}) collective-permute-start(f32[16,1792]{1,0:T(8,128)S(1)} %maximum_select_fusion.1), channel_id=1, source_target_pairs={{0,24},{8,16},{16,8},{24,0},{1,25},{9,17},{17,9},{25,1},{2,26},{10... | collective-permute-start | bytes 344072 | tf_op jit(solution)/shard_map/ppermute | solution.py:56
  25.3 5.3 %collective-permute-start.5 = (f32[8,4,1792]{2,1,0:T(4,128)S(1)}, f32[8,4,1792]{2,1,0:T(4,128)S(1)}, u32[]{:S(2)}, u32[]{:S(2)}) collective-permute-start(f32[8,4,1792]{2,1,0:T(4,128)S(1)} %get-tuple-element.20), channel_id=1, source_target_pairs={{0,1},{2,3},{4,5},{6,7},{1,0},{3,2},{5,4},{7,6},{8,9},{10,11},{12,... | collective-permute-start | bytes 688136 | tf_op jit(solution)/shard_map/ppermute | solution.py:37
  25.4 10.1 %collective-permute-start.6 = (f32[8,4,1792]{2,1,0:T(4,128)S(1)}, f32[8,4,1792]{2,1,0:T(4,128)S(1)}, u32[]{:S(2)}, u32[]{:S(2)}) collective-permute-start(f32[8,4,1792]{2,1,0:T(4,128)S(1)} %get-tuple-element.19), channel_id=1, source_target_pairs={{1,2},{3,4},{5,6},{2,1},{4,3},{6,5},{9,10},{11,12},{13,14},{10,9},... | collective-permute-start | bytes 688136 | tf_op jit(solution)/shard_map/ppermute | solution.py:36

commit v29 on v28

--- a/solution.py
+++ b/solution.py
@@ -136,13 +136,18 @@
     )
     reflect = mem_sum(partial_sum)
     weighted = radar_mask.astype(jnp.float32) * obs_weight * reflect
+    coef_far = far[members:]
     near, far, odd = split_exchange(mix * weighted[None], STEPS)
     spread = localize(near_band(mix * weighted[None], near, odd), coef_band)
     spread = spread[:, STEPS : STEPS + row_count]
     spread, far = lax.optimization_barrier((spread, far))
     zero = jnp.zeros_like(far)
     strip = jnp.where(odd, jnp.concatenate([zero, far], 1), jnp.concatenate([far, zero], 1))
-    strip_coef = jnp.where(odd, coef_band[:, row_count:], coef_band[:, : 2 * STEPS])
+    strip_coef = jnp.where(
+        odd,
+        jnp.concatenate([stacked[members:, row_count - STEPS :], coef_far], 1),
+        jnp.concatenate([coef_far, stacked[members:, :STEPS]], 1),
+    )
     edge = localize(strip, strip_coef)
     rest = jnp.zeros_like(spread[:, STEPS:])
     edge = jnp.where(

time: 38.9 us -> 38.9 us (level)
  no operation moved by 1% of the time
where the time goes in v29:
time: 38.9 us; the launch traced here: 38.7 us
  other arithmetic  19.1 us (49%)
  starting transfers between devices  12.8 us (33%)
  waiting for transfers between devices  4.67 us (12%)
  local copies, waits for them, and re-layouts  1.51 us (4%)
  between operations  0.63 us (2%)
    ppermute x2, starting transfers between devices, split_exchange(): far = lax.ppermute(jnp.where(odd, tail, head), 'tile', pairs(1))  9.91 us
    sub x14, other arithmetic, diffuse(): values + jnp.concatenate([col_flux, zeros_col], -1)  5.49 us
    mul x16, other arithmetic, diffuse(): col_coef[..., :, :-1] * (values[..., :, 1:] - values[..., :, :-1])  5.12 us
    ppermute x3, waiting for transfers between devices, partner(): return lax.ppermute(part, 'mem', [(i, i ^ stride) for i in range(count)])  4.65 us
    ppermute x3, starting transfers between devices, partner(): return lax.ppermute(part, 'mem', [(i, i ^ stride) for i in range(count)])  2.71 us
    mul x17, other arithmetic, diffuse(): row_coef[..., :-1, :] * (values[..., 1:, :] - values[..., :-1, :])  2.29 us
    concatenate x1, other arithmetic, per_device(): stacked = jnp.concatenate([controls, row_coef[None], col_faces[None]], 0)  1.33 us
    add x1, other arithmetic, per_device(): return controls + (spread + edge)  1.12 us
  transfers between devices with their start and end apart: 7, of which 3 were waited for; matrix products, arithmetic and copies ran while one was open for 27% of the time, Pallas kernels for 0%

profile of v29, /device:TPU:1, one launch (start us, length us, event | category | flops | bytes accessed | tf_op | source)
XLA Modules:
  0.0 38.7 jit_solution(13828726102406544769)
XLA Ops:
  0.0 1.0 %select_bitcast_fusion = f32[1,16,1792]{2,1,0:T(8,128)S(1)} fusion(f32[16,1792]{1,0:T(8,128)} %param.12, pred[16]{0:T(512)(128)(4,1)S(1)} %add_compare_fusion), kind=kLoop, calls=%fused_computation.138 | loop fusion | flops 28672 | bytes 229392 | tf_op jit(solution)/shard_map/broadcast_in_dim | solution.py:109
  1.0 1.3 %pad_maximum_fusion.2 = f32[10,16,1792]{2,1,0:T(8,128)S(1)} fusion(f32[1,16,1792]{2,1,0:T(8,128)} %bitcast.46, f32[1,16,1792]{2,1,0:T(8,128)S(1)} %select_bitcast_fusion, f32[8,16,1792]{2,1,0:T(8,128)} %param.7), kind=kLoop, calls=%fused_computation.44 | loop fusion | flops 573440 | bytes 2293760 | tf_op jit(solution)/shard_map/concatenate | solution.py:109
  2.3 0.1 slice_select_fusion
  2.5 0.1 collective-permute-start
  2.7 4.7 %collective-permute-start.1 = (f32[10,4,1792]{2,0,1:T(8,128)S(1)}, f32[10,4,1792]{2,0,1:T(8,128)S(1)}, u32[]{:S(2)}, u32[]{:S(2)}) collective-permute-start(f32[10,4,1792]{2,0,1:T(8,128)S(1)} %copy.14), channel_id=1, source_target_pairs={{1,2},{3,4},{5,6},{2,1},{4,3},{6,5},{9,10},{11,12},{13,14},{10,9},... | collective-permute-start | bytes 860168 | tf_op jit(solution)/shard_map/ppermute | solution.py:36
  7.5 0.4 multiply_reduce_fusion
  7.9 0.2 broadcast_select_fusion.1
  8.2 0.8 %copy-done = f32[8,16,1792]{2,1,0:T(8,128)S(1)} copy-done((f32[8,16,1792]{2,1,0:T(8,128)S(1)}, f32[8,16,1792]{2,1,0:T(8,128)}, u32[]{:S(2)}) %copy-start) | copy-done | bytes 917528
  9.1 0.3 pad_maximum_fusion
  9.4 0.2 fusion.15
  9.6 0.4 %fusion.14 = f32[8,24,1791]{2,1,0:T(8,128)S(1)} fusion(f32[10,24,1792]{2,1,0:T(8,128)S(1)} %pad_maximum_fusion, f32[24,1791]{1,0:T(8,128)S(1)} %bitcast.42), kind=kLoop, calls=%fused_computation.31 | loop fusion | flops 687744 | bytes 4298400 | tf_op jit(solution)/shard_map/mul | solution.py:72
  10.0 0.5 %fusion.18 = f32[8,24,1792]{2,1,0:T(8,128)S(1)} fusion(f32[10,24,1792]{2,1,0:T(8,128)S(1)} %pad_maximum_fusion, f32[8,24,1791]{2,1,0:T(8,128)S(1)} %fusion.14, f32[8,23,1792]{2,1,0:T(8,128)S(1)} %fusion.15), kind=kLoop, calls=%fused_computation.37 | loop fusion | flops 1376256 | bytes 5446912 | tf_op jit(solution)/shard_map/sub | solution.py:81
  10.5 0.2 fusion.13
  10.7 0.4 %fusion.12 = f32[8,24,1791]{2,1,0:T(8,128)S(1)} fusion(f32[8,24,1792]{2,1,0:T(8,128)S(1)} %fusion.18, f32[24,1791]{1,0:T(8,128)S(1)} %bitcast.43), kind=kLoop, calls=%fused_computation.27 | loop fusion | flops 687744 | bytes 4298400 | tf_op jit(solution)/shard_map/mul | solution.py:72
  11.1 0.5 %pad_subtract_fusion.4 = f32[8,24,1792]{2,1,0:T(8,128)S(1)} fusion(f32[8,24,1791]{2,1,0:T(8,128)S(1)} %fusion.12, f32[8,23,1792]{2,1,0:T(8,128)S(1)} %fusion.13, f32[8,24,1792]{2,1,0:T(8,128)S(1)} %fusion.18), kind=kLoop, calls=%fused_computation.43 | loop fusion | flops 1376256 | bytes 5446912 | tf_op jit(solution)/shard_map/sub | solution.py:81
  11.6 0.2 fusion.11
  11.8 0.4 %fusion.10 = f32[8,24,1791]{2,1,0:T(8,128)S(1)} fusion(f32[8,24,1792]{2,1,0:T(8,128)S(1)} %pad_subtract_fusion.4, f32[24,1791]{1,0:T(8,128)S(1)} %bitcast.44), kind=kLoop, calls=%fused_computation.23 | loop fusion | flops 687744 | bytes 4298400 | tf_op jit(solution)/shard_map/mul | solution.py:72
  12.2 0.5 %pad_subtract_fusion.3 = f32[8,24,1792]{2,1,0:T(8,128)S(1)} fusion(f32[8,24,1791]{2,1,0:T(8,128)S(1)} %fusion.10, f32[8,23,1792]{2,1,0:T(8,128)S(1)} %fusion.11, f32[8,24,1792]{2,1,0:T(8,128)S(1)} %pad_subtract_fusion.4), kind=kLoop, calls=%fused_computation.42 | loop fusion | flops 1376256 | bytes 5446912 | tf_op jit(solution)/shard_map/sub | solution.py:81
  12.7 0.2 fusion.9
  12.9 0.4 %fusion.8 = f32[8,24,1791]{2,1,0:T(8,128)S(1)} fusion(f32[8,24,1792]{2,1,0:T(8,128)S(1)} %pad_subtract_fusion.3, f32[24,1791]{1,0:T(8,128)S(1)} %bitcast.45), kind=kLoop, calls=%fused_computation.19 | loop fusion | flops 687744 | bytes 4298400 | tf_op jit(solution)/shard_map/mul | solution.py:72
  13.3 0.6 %fusion.30 = f32[16,1792]{1,0:T(8,128)S(1)} fusion(f32[8,16,1792]{2,1,0:T(8,128)S(1)} %multiply_reduce_fusion, f32[8,24,1791]{2,1,0:T(8,128)S(1)} %fusion.8, f32[8,23,1792]{2,1,0:T(8,128)S(1)} %fusion.9, f32[8,24,1792]{2,1,0:T(8,128)S(1)} %pad_subtract_fusion.3), kind=kLoop, calls=%fused_computation.68 | loop fusion | flops 1347584 | bytes 4644096 | tf_op jit(solution)/shard_map/reduce_sum | solution.py:121
  13.9 0.2 copy.15
  14.2 0.2 maximum_select_fusion
  14.5 0.1 fusion.25
  14.6 0.3 fusion.24
  14.9 0.5 %fusion.28 = f32[8,12,1792]{2,1,0:T(8,128)S(1)} fusion(f32[10,12,1792]{2,1,0:T(8,128)S(1)} %maximum_select_fusion, f32[8,12,1791]{2,1,0:T(8,128)S(1)} %fusion.24, f32[8,11,1792]{2,1,0:T(8,128)S(1)} %fusion.25), kind=kLoop, calls=%fused_computation.65 | loop fusion | flops 688128 | bytes 2694784 | tf_op jit(solution)/shard_map/sub | solution.py:81
  15.4 0.2 fusion.20
  15.6 0.3 fusion.19
  15.9 0.4 %fusion.23 = f32[8,10,1792]{2,1,0:T(8,128)S(1)} fusion(f32[8,12,1792]{2,1,0:T(8,128)S(1)} %fusion.28, f32[8,10,1791]{2,1,0:T(8,128)S(1)} %fusion.19, f32[8,9,1792]{2,1,0:T(8,128)S(1)} %fusion.20), kind=kLoop, calls=%fused_computation.57 | loop fusion | flops 573440 | bytes 2236096 | tf_op jit(solution)/shard_map/sub | solution.py:81
  16.3 0.1 fusion.42
  16.4 0.2 fusion.41
  16.6 0.2 fusion.45
  16.9 0.1 fusion.40
  17.0 0.2 fusion.39
  17.2 0.3 fusion.47
  17.6 1.4 %collective-permute-start.2 = (f32[16,1792]{1,0:T(8,128)S(1)}, f32[16,1792]{1,0:T(8,128)S(1)}, u32[]{:S(2)}, u32[]{:S(2)}) collective-permute-start(f32[16,1792]{1,0:T(8,128)S(1)} %maximum_select_fusion.1), channel_id=1, source_target_pairs={{0,8},{8,0},{16,24},{24,16},{1,9},{9,1},{17,25},{25,17},{2,10},{10... | collective-permute-start | bytes 344072 | tf_op jit(solution)/shard_map/ppermute | solution.py:56
  19.0 1.2 %collective-permute-start.3 = (f32[16,1792]{1,0:T(8,128)S(1)}, f32[16,1792]{1,0:T(8,128)S(1)}, u32[]{:S(2)}, u32[]{:S(2)}) collective-permute-start(f32[16,1792]{1,0:T(8,128)S(1)} %maximum_select_fusion.1), channel_id=1, source_target_pairs={{0,16},{8,24},{16,0},{24,8},{1,17},{9,25},{17,1},{25,9},{2,18},{10... | collective-permute-start | bytes 344072 | tf_op jit(solution)/shard_map/ppermute | solution.py:56
  20.5 1.5 %collective-permute-done.2 = f32[16,1792]{1,0:T(8,128)S(1)} collective-permute-done((f32[16,1792]{1,0:T(8,128)S(1)}, f32[16,1792]{1,0:T(8,128)S(1)}, u32[]{:S(2)}, u32[]{:S(2)}) %collective-permute-start.2) | collective-permute-done | bytes 114720 | tf_op jit(solution)/shard_map/ppermute | solution.py:56
  22.0 2.5 %collective-permute-done.3 = f32[16,1792]{1,0:T(8,128)S(1)} collective-permute-done((f32[16,1792]{1,0:T(8,128)S(1)}, f32[16,1792]{1,0:T(8,128)S(1)}, u32[]{:S(2)}, u32[]{:S(2)}) %collective-permute-start.3) | collective-permute-done | bytes 114720 | tf_op jit(solution)/shard_map/ppermute | solution.py:56
  24.5 0.7 %collective-permute-done.4 = f32[16,1792]{1,0:T(8,128)S(1)} collective-permute-done((f32[16,1792]{1,0:T(8,128)S(1)}, f32[16,1792]{1,0:T(8,128)S(1)}, u32[]{:S(2)}, u32[]{:S(2)}) %collective-permute-start.4) | collective-permute-done | bytes 114720 | tf_op jit(solution)/shard_map/ppermute | solution.py:56
  25.2 0.1 slice_select_fusion.3
  25.4 5.2 %collective-permute-start.6 = (f32[8,4,1792]{2,1,0:T(4,128)S(1)}, f32[8,4,1792]{2,1,0:T(4,128)S(1)}, u32[]{:S(2)}, u32[]{:S(2)}) collective-permute-start(f32[8,4,1792]{2,1,0:T(4,128)S(1)} %get-tuple-element.19), channel_id=1, source_target_pairs={{1,2},{3,4},{5,6},{2,1},{4,3},{6,5},{9,10},{11,12},{13,14},{10,9},... | collective-permute-start | bytes 688136 | tf_op jit(solution)/shard_map/ppermute | solution.py:36
  30.7 0.2 pad_maximum_fusion.1
  30.9 0.2 fusion.7
  31.1 0.4 %fusion.6 = f32[8,24,1791]{2,1,0:T(8,128)S(1)} fusion(f32[8,24,1792]{2,1,0:T(8,128)S(1)} %pad_maximum_fusion.1, f32[24,1791]{1,0:T(8,128)S(1)} %bitcast.38), kind=kLoop, calls=%fused_computation.15 | loop fusion | flops 687744 | bytes 4298400 | tf_op jit(solution)/shard_map/mul | solution.py:72
  31.6 0.6 %pad_subtract_fusion.2 = f32[8,24,1792]{2,1,0:T(8,128)S(1)} fusion(f32[8,24,1791]{2,1,0:T(8,128)S(1)} %fusion.6, f32[8,23,1792]{2,1,0:T(8,128)S(1)} %fusion.7, f32[8,4,1792]{2,1,0:T(4,128)S(1)} %get-tuple-element.27, f32[8,16,1792]{2,1,0:T(8,128)S(1)} %broadcast_multiply_fusion, f32[8,4,1792]{2,1,0:T(4,128)S(1)} %get-tuple-element.26), kind=kLoop, calls=%fused_computation.41 | loop fusion | flops 2064384 | bytes 5446912 | tf_op jit(solution)/shard_map/sub | solution.py:81
  32.1 0.2 fusion.5
  32.3 0.4 %fusion.4 = f32[8,24,1791]{2,1,0:T(8,128)S(1)} fusion(f32[8,24,1792]{2,1,0:T(8,128)S(1)} %pad_subtract_fusion.2, f32[24,1791]{1,0:T(8,128)S(1)} %bitcast.39), kind=kLoop, calls=%fused_computation.11 | loop fusion | flops 687744 | bytes 4298400 | tf_op jit(solution)/shard_map/mul | solution.py:72
  32.7 0.5 %pad_subtract_fusion.1 = f32[8,24,1792]{2,1,0:T(8,128)S(1)} fusion(f32[8,24,1791]{2,1,0:T(8,128)S(1)} %fusion.4, f32[8,23,1792]{2,1,0:T(8,128)S(1)} %fusion.5, f32[8,24,1792]{2,1,0:T(8,128)S(1)} %pad_subtract_fusion.2), kind=kLoop, calls=%fused_computation.40 | loop fusion | flops 1376256 | bytes 5446912 | tf_op jit(solution)/shard_map/sub | solution.py:81
  33.2 0.2 fusion.3
  33.4 0.4 %fusion.2 = f32[8,24,1791]{2,1,0:T(8,128)S(1)} fusion(f32[8,24,1792]{2,1,0:T(8,128)S(1)} %pad_subtract_fusion.1, f32[24,1791]{1,0:T(8,128)S(1)} %bitcast.40), kind=kLoop, calls=%fused_computation.7 | loop fusion | flops 687744 | bytes 4298400 | tf_op jit(solution)/shard_map/mul | solution.py:72
  33.9 0.5 %pad_subtract_fusion = f32[8,24,1792]{2,1,0:T(8,128)S(1)} fusion(f32[8,24,1791]{2,1,0:T(8,128)S(1)} %fusion.2, f32[8,23,1792]{2,1,0:T(8,128)S(1)} %fusion.3, f32[8,24,1792]{2,1,0:T(8,128)S(1)} %pad_subtract_fusion.1), kind=kLoop, calls=%fused_computation.39 | loop fusion | flops 1376256 | bytes 5446912 | tf_op jit(solution)/shard_map/sub | solution.py:81
  34.3 0.2 fusion.1
  34.5 0.4 %fusion = f32[8,24,1791]{2,1,0:T(8,128)S(1)} fusion(f32[8,24,1792]{2,1,0:T(8,128)S(1)} %pad_subtract_fusion, f32[24,1791]{1,0:T(8,128)S(1)} %bitcast.41), kind=kLoop, calls=%fused_computation.3 | loop fusion | flops 687744 | bytes 4298400 | tf_op jit(solution)/shard_map/mul | solution.py:72
  35.0 0.5 %pad_subtract_fusion.5 = f32[8,16,1792]{2,1,0:T(8,128)S(1)} fusion(f32[8,24,1791]{2,1,0:T(8,128)S(1)} %fusion, f32[8,23,1792]{2,1,0:T(8,128)S(1)} %fusion.1, f32[8,24,1792]{2,1,0:T(8,128)S(1)} %pad_subtract_fusion), kind=kLoop, calls=%fused_computation.46 | loop fusion | flops 917504 | bytes 4529408 | tf_op jit(solution)/shard_map/sub | solution.py:81
  35.6 0.2 fusion.37
  35.8 0.2 pad_subtract_fusion.12
  36.1 0.2 fusion.35
  36.3 0.2 pad_subtract_fusion.11
  36.6 0.2 fusion.33
  36.8 0.2 pad_subtract_fusion.10
  37.1 0.2 fusion.31
  37.3 0.2 pad_subtract_fusion.9
  37.6 1.1 %add_add_fusion = f32[8,16,1792]{2,1,0:T(8,128)} fusion(f32[8,16,1792]{2,1,0:T(8,128)S(1)} %copy-done, f32[8,16,1792]{2,1,0:T(8,128)S(1)} %pad_subtract_fusion.5, f32[8,4,1792]{2,1,0:T(4,128)S(1)} %get-tuple-element.24, f32[8,4,1792]{2,1,0:T(4,128)S(1)} %get-tuple-element.23, pred[]{:T(512)S(6)} %eq.7), kind=kLoop, calls=%fused_computation.72 | loop fusion | flops 688128 | bytes 3211265 | tf_op jit(solution)/shard_map/add | solution.py:158
  (51 shorter events, 1.4 us)
Async XLA Ops:
  2.5 5.4 %collective-permute-start = (f32[10,4,1792]{2,0,1:T(8,128)S(1)}, f32[10,4,1792]{2,0,1:T(8,128)S(1)}, u32[]{:S(2)}, u32[]{:S(2)}) collective-permute-start(f32[10,4,1792]{2,0,1:T(8,128)S(1)} %copy.11), channel_id=1, source_target_pairs={{0,1},{2,3},{4,5},{6,7},{1,0},{3,2},{5,4},{7,6},{8,9},{10,11},{12,... | collective-permute-start | bytes 860168 | tf_op jit(solution)/shard_map/ppermute | solution.py:37
  2.6 4.9 %copy-start.2 = (bf16[8,4,16,1792]{3,2,1,0:T(8,128)(2,1)S(1)}, bf16[8,4,16,1792]{3,2,1,0:T(8,128)(2,1)}, u32[]{:S(2)}) copy-start(bf16[8,4,16,1792]{3,2,1,0:T(8,128)(2,1)} %param.8) | copy-start | bytes 5505028
  2.6 4.9 %copy-start.3 = (f32[4,16,1792]{2,1,0:T(8,128)S(1)}, f32[4,16,1792]{2,1,0:T(8,128)}, u32[]{:S(2)}) copy-start(f32[4,16,1792]{2,1,0:T(8,128)} %param.9) | copy-start | bytes 1376260
  2.7 11.2 %collective-permute-start.1 = (f32[10,4,1792]{2,0,1:T(8,128)S(1)}, f32[10,4,1792]{2,0,1:T(8,128)S(1)}, u32[]{:S(2)}, u32[]{:S(2)}) collective-permute-start(f32[10,4,1792]{2,0,1:T(8,128)S(1)} %copy.14), channel_id=1, source_target_pairs={{1,2},{3,4},{5,6},{2,1},{4,3},{6,5},{9,10},{11,12},{13,14},{10,9},... | collective-permute-start | bytes 860168 | tf_op jit(solution)/shard_map/ppermute | solution.py:36
  7.9 1.2 %copy-start = (f32[8,16,1792]{2,1,0:T(8,128)S(1)}, f32[8,16,1792]{2,1,0:T(8,128)}, u32[]{:S(2)}) copy-start(f32[8,16,1792]{2,1,0:T(8,128)} %param.7) | copy-start | bytes 2752516
  7.9 1.2 %copy-start.1 = (f32[16,1792]{1,0:T(8,128)S(1)}, f32[16,1792]{1,0:T(8,128)}, u32[]{:S(2)}) copy-start(f32[16,1792]{1,0:T(8,128)} %param.13) | copy-start | bytes 344068
  17.5 7.6 %copy-start.4 = (f32[16,1792]{1,0:T(8,128)S(1)}, f32[16,1792]{1,0:T(8,128)}, u32[]{:S(2)}) copy-start(f32[16,1792]{1,0:T(8,128)} %param.10) | copy-start | bytes 344068
  17.5 7.6 %copy-start.5 = (s32[16,1792]{1,0:T(8,128)S(1)}, s32[16,1792]{1,0:T(8,128)}, u32[]{:S(2)}) copy-start(s32[16,1792]{1,0:T(8,128)} %param.11) | copy-start | bytes 344068
  17.6 4.4 %collective-permute-start.2 = (f32[16,1792]{1,0:T(8,128)S(1)}, f32[16,1792]{1,0:T(8,128)S(1)}, u32[]{:S(2)}, u32[]{:S(2)}) collective-permute-start(f32[16,1792]{1,0:T(8,128)S(1)} %maximum_select_fusion.1), channel_id=1, source_target_pairs={{0,8},{8,0},{16,24},{24,16},{1,9},{9,1},{17,25},{25,17},{2,10},{10... | collective-permute-start | bytes 344072 | tf_op jit(solution)/shard_map/ppermute | solution.py:56
  19.0 5.4 %collective-permute-start.3 = (f32[16,1792]{1,0:T(8,128)S(1)}, f32[16,1792]{1,0:T(8,128)S(1)}, u32[]{:S(2)}, u32[]{:S(2)}) collective-permute-start(f32[16,1792]{1,0:T(8,128)S(1)} %maximum_select_fusion.1), channel_id=1, source_target_pairs={{0,16},{8,24},{16,0},{24,8},{1,17},{9,25},{17,1},{25,9},{2,18},{10... | collective-permute-start | bytes 344072 | tf_op jit(solution)/shard_map/ppermute | solution.py:56
  20.3 4.9 %collective-permute-start.4 = (f32[16,1792]{1,0:T(8,128)S(1)}, f32[16,1792]{1,0:T(8,128)S(1)}, u32[]{:S(2)}, u32[]{:S(2)}) collective-permute-start(f32[16,1792]{1,0:T(8,128)S(1)} %maximum_select_fusion.1), channel_id=1, source_target_pairs={{0,24},{8,16},{16,8},{24,0},{1,25},{9,17},{17,9},{25,1},{2,26},{10... | collective-permute-start | bytes 344072 | tf_op jit(solution)/shard_map/ppermute | solution.py:56
  25.3 5.3 %collective-permute-start.5 = (f32[8,4,1792]{2,1,0:T(4,128)S(1)}, f32[8,4,1792]{2,1,0:T(4,128)S(1)}, u32[]{:S(2)}, u32[]{:S(2)}) collective-permute-start(f32[8,4,1792]{2,1,0:T(4,128)S(1)} %get-tuple-element.20), channel_id=1, source_target_pairs={{0,1},{2,3},{4,5},{6,7},{1,0},{3,2},{5,4},{7,6},{8,9},{10,11},{12,... | collective-permute-start | bytes 688136 | tf_op jit(solution)/shard_map/ppermute | solution.py:37
  25.4 10.1 %collective-permute-start.6 = (f32[8,4,1792]{2,1,0:T(4,128)S(1)}, f32[8,4,1792]{2,1,0:T(4,128)S(1)}, u32[]{:S(2)}, u32[]{:S(2)}) collective-permute-start(f32[8,4,1792]{2,1,0:T(4,128)S(1)} %get-tuple-element.19), channel_id=1, source_target_pairs={{1,2},{3,4},{5,6},{2,1},{4,3},{6,5},{9,10},{11,12},{13,14},{10,9},... | collective-permute-start | bytes 688136 | tf_op jit(solution)/shard_map/ppermute | solution.py:36
